TPU v7x, 32 devices: a whole 2x2x4 slice. The times are simulated.
32 devices in a mesh: gx: 8 (over z, y), gy: 4 (over x, core).
Axes of the slice: x: 2, y: 2, z: 4, core: 2. Of those that a mesh axis runs over, the one named last changes fastest.
Arguments:
- conc_prev: float32 [128, 64, 128], P('gx', 'gy'), may hold values from 0.5 to 2
- right_side: float32 [128, 64, 128], P('gx', 'gy'), may hold values from -5 to 7
- soil_id: int32 [128, 64, 128], P('gx', 'gy'), may hold values from 0 to 7
- soil_table: float32 [5, 8], replicated, may hold values from 0.3 to 3
Outputs:
- correction: float32 [128, 64, 128], P('gx', 'gy')
All inputs are finite; a program needn't handle non-finite values.
Results may differ from a plain program's by a relative error of at most 0.00002.
Values sent between devices are 32-bit elements; how exact they have to be, the bound alone decides.
No kernel may reach another device: no remote copies, remote signals or barrier semaphores. Data moves between devices by JAX's collectives and lax.ppermute only.
A program may use at most 128 MiB of HBM per device.

v0:
```python
import jax
import jax.numpy as jnp
from jax import lax
from jax.sharding import PartitionSpec as P

CHEB = 3
COARSE_SWEEPS = 8


storage_scale = 0.05
cheb_centre = 1.1
cheb_half = 0.9
cheb_ratio = cheb_centre / cheb_half
jacobi_weight = 0.8


def padded_2(cells, sides, width):
    for axis, dim in sides:
        count = lax.axis_size(axis)
        ends = count - 1
        head = lax.slice_in_dim(cells, 0, width, axis=dim)
        tail = lax.slice_in_dim(cells, cells.shape[dim] - width, cells.shape[dim], axis=dim)
        cells = jnp.concatenate(
            [
                lax.ppermute(tail, axis, [(i, (i + 1) % count) for i in range(ends)]),
                cells,
                lax.ppermute(head, axis, [((i + 1) % count, i) for i in range(ends)]),
            ],
            axis=dim,
        )
    return cells


def harmonic(first, second):
    return first * second / jnp.maximum(0.5 * (first + second), 0.1)


def face_terms(coeffs, spacing):
    eastward = coeffs[0]
    northward = coeffs[1]
    upward = coeffs[2]
    centre_x = eastward[1:-1, 1:-1]
    centre_y = northward[1:-1, 1:-1]
    centre_z = upward[1:-1, 1:-1]
    east_face = harmonic(eastward[2:, 1:-1], centre_x) * spacing
    west_face = harmonic(eastward[:-2, 1:-1], centre_x) * spacing
    north_face = harmonic(northward[1:-1, 2:], centre_y) * spacing
    south_face = harmonic(northward[1:-1, :-2], centre_y) * spacing
    vertical = harmonic(centre_z[:, :, 1:], centre_z[:, :, :-1]) * spacing
    closed = jnp.zeros_like(centre_z[:, :, :1])
    above_face = jnp.concatenate([vertical, closed], axis=2)
    below_face = jnp.concatenate([closed, vertical], axis=2)
    storage = coeffs[3, 1:-1, 1:-1]
    return (east_face, west_face, north_face, south_face, above_face, below_face, storage)


def main_diagonal(coeffs, spacing):
    east_face, west_face, north_face, south_face, above_face, below_face, storage = face_terms(
        coeffs, spacing
    )
    return jnp.maximum(
        storage + east_face + west_face + north_face + south_face + above_face + below_face, 0.01
    )


def operate(values, coeffs, spacing):
    east_face, west_face, north_face, south_face, above_face, below_face, storage = face_terms(
        coeffs, spacing
    )
    centre = values[1:-1, 1:-1]
    upper_cell = jnp.concatenate([centre[:, :, 1:], centre[:, :, :1]], axis=2)
    lower_cell = jnp.concatenate([centre[:, :, -1:], centre[:, :, :-1]], axis=2)
    fluxes = east_face * (centre - values[2:, 1:-1]) + west_face * (centre - values[:-2, 1:-1])
    fluxes = (
        fluxes
        + north_face * (centre - values[1:-1, 2:])
        + south_face * (centre - values[1:-1, :-2])
    )
    fluxes = fluxes + above_face * (centre - upper_cell) + below_face * (centre - lower_cell)
    return storage * centre + fluxes


def coarsen(values):
    lead = values.shape[:-3]
    size_x, size_y, size_z = values.shape[-3:]
    split = values.reshape(lead + (size_x // 2, 2, size_y // 2, 2, size_z // 2, 2))
    return jnp.mean(split, axis=(-5, -3, -1))


def prolong(values):
    return jnp.repeat(jnp.repeat(jnp.repeat(values, 2, axis=0), 2, axis=1), 2, axis=2)


def shrink(values, amount):
    if amount == 0:
        return values
    return values[..., amount:-amount, amount:-amount, :]


def tile_halo(layers, amount):
    return padded_2(layers, (("gx", 1), ("gy", 2)), amount)


def expand(values):
    return (tile_halo(values[None], 1)[0], 1)


def smooth(target, target_margin, initial, coeffs, coeff_margin, spacing):
    if initial is None:
        current = target_margin
        diagonal = main_diagonal(shrink(coeffs, coeff_margin - current - 1), spacing)
        update = target / diagonal * (1.0 / cheb_centre)
        iterate = update
    else:
        padded, padded_margin = expand(initial)
        applied = operate(padded, shrink(coeffs, coeff_margin - padded_margin), spacing)
        current = padded_margin - 1
        diagonal = main_diagonal(shrink(coeffs, coeff_margin - current - 1), spacing)
        misfit = shrink(target, target_margin - current) - applied
        update = misfit / diagonal * (1.0 / cheb_centre)
        iterate = shrink(padded, 1) + update
    diagonal_margin = current
    factor = 1.0 / cheb_ratio
    for repeat in range(CHEB - 1):
        padded, padded_margin = expand(iterate)
        applied = operate(padded, shrink(coeffs, coeff_margin - padded_margin), spacing)
        next_margin = padded_margin - 1
        misfit = shrink(target, target_margin - next_margin) - applied
        factor_new = 1.0 / (2.0 * cheb_ratio - factor)
        update = factor_new * factor * shrink(
            update, current - next_margin
        ) + 2.0 * factor_new / cheb_half * (
            misfit / shrink(diagonal, diagonal_margin - next_margin)
        )
        iterate = shrink(iterate, current - next_margin) + update
        current = next_margin
        factor = factor_new
    return (iterate, current)


def leftover(target, target_margin, iterate, coeffs, coeff_margin, spacing):
    padded, padded_margin = expand(iterate)
    applied = operate(padded, shrink(coeffs, coeff_margin - padded_margin), spacing)
    return shrink(target, target_margin - padded_margin + 1) - applied


def local_fields(conc_prev, soil_id, soil_table):
    fields = []
    for record in range(5):
        looked = jnp.zeros(soil_id.shape, jnp.float32)
        for material in range(soil_table.shape[1]):
            looked = looked + jnp.where(soil_id == material, soil_table[record, material], 0.0)
        fields.append(looked)
    storage = storage_scale * (1.0 + fields[3] * jnp.exp((fields[4] - 1.0) * jnp.log(conc_prev)))
    return jnp.stack([fields[0], fields[1], fields[2], storage])


def local(conc_prev, right_side, soil_id, soil_table):
    halo_depth = 0
    fine_margin = max(4, 2 * halo_depth + 2)
    own_coeffs = local_fields(conc_prev, soil_id, soil_table)
    fine_coeffs = padded_2(own_coeffs, (("gx", 1), ("gy", 2)), fine_margin)
    mid_margin = fine_margin // 2
    mid_coeffs = coarsen(fine_coeffs)
    coarse_coeffs = coarsen(shrink(mid_coeffs, mid_margin - 2))
    fine_iterate, current = smooth(right_side, halo_depth, None, fine_coeffs, fine_margin, 1.0)
    fine_misfit = leftover(right_side, halo_depth, fine_iterate, fine_coeffs, fine_margin, 1.0)
    fine_iterate = shrink(fine_iterate, current)
    mid_plain = coarsen(fine_misfit)
    mid_iterate, current = smooth(mid_plain, halo_depth, None, mid_coeffs, mid_margin, 0.25)
    mid_misfit = leftover(mid_plain, halo_depth, mid_iterate, mid_coeffs, mid_margin, 0.25)
    mid_iterate = shrink(mid_iterate, current)
    coarse_source = coarsen(mid_misfit)
    narrow = coarse_coeffs[:, :, 1:-1]
    group_source, group_coeffs = (
        lax.all_gather(coarse_source, "gy", axis=1, tiled=True),
        lax.all_gather(narrow, "gy", axis=2, tiled=True),
    )
    line_total = jnp.sum(group_source, axis=1)
    line_store = jnp.sum(group_coeffs[3, 1:-1], axis=1)
    line_mean = line_total / line_store
    group_coeffs = jnp.pad(group_coeffs, ((0, 0), (0, 0), (1, 1), (0, 0)))
    diagonal = main_diagonal(group_coeffs, 0.0625)
    coarse_value = jnp.broadcast_to(line_mean[:, None, :], group_source.shape)
    for sweeps in range(COARSE_SWEEPS):
        padded = padded_2(coarse_value, (("gx", 0),), 1)
        padded = jnp.pad(padded, ((0, 0), (1, 1), (0, 0)))
        applied = operate(padded, group_coeffs, 0.0625)
        coarse_value = coarse_value + jacobi_weight * ((group_source - applied) / diagonal)
    tile_width = coarse_source.shape[1]
    coarse_value = lax.dynamic_slice_in_dim(
        coarse_value, lax.axis_index("gy") * tile_width, tile_width, 1
    )
    mid_start = mid_iterate + prolong(coarse_value)
    mid_result, current = smooth(mid_plain, halo_depth, mid_start, mid_coeffs, mid_margin, 0.25)
    fine_start = fine_iterate + prolong(mid_result)
    fine_result, current = smooth(right_side, halo_depth, fine_start, fine_coeffs, fine_margin, 1.0)
    return fine_result


def solution(mesh):
    placed = (P("gx", "gy", None), P("gx", "gy", None), P("gx", "gy", None), P())
    return jax.shard_map(
        local, mesh=mesh, in_specs=placed, out_specs=P("gx", "gy", None), check_vma=False
    )
```

profile of v0, /device:TPU:26, one launch (start us, length us, event | category | flops | bytes accessed | tf_op | source)
XLA Modules:
  0.0 402.7 jit_solution(15851466285160394497)
XLA Ops:
  5.6 6.3 %add_bitcast_fusion.3 = (f32[1,16,16,128]{3,2,1,0:T(8,128)S(1)}, pred[16,16,128]{2,1,0:T(8,128)(4,1)S(1)}, pred[16,16,128]{2,1,0:T(8,128)(4,1)S(1)}, pred[16,16,...) fusion(f32[]{:T(128)} %bitcast.23, f32[]{:T(128)} %bitcast.22, ...), kind=kLoop, calls=%fused_computation.162 | loop fusion | flops 753664 | bytes 524320 | tf_op jit(solution)/shard_map/stack | solution.py:155
  11.9 5.3 %add_bitcast_fusion.1 = f32[1,16,16,128]{3,2,1,0:T(8,128)S(1)} fusion(pred[16,16,128]{2,1,0:T(8,128)(4,1)S(1)} %get-tuple-element.49, pred[16,16,128]{2,1,0:T(8,128)(4,1)S(1)} %get-tuple-element.48, pred[16,16,128]{2,1,0:T(8,128)(4,1)S(1)} %get-tuple-element.47, pred[16,16,128]{2,1,0:T(8,128)(4,1)S(1)} %get-tuple-element.46, ...), kind=kLoop, calls=%fused_computation.160 | loop fusion | flops 491520 | bytes 393248 | tf_op jit(solution)/shard_map/stack | solution.py:155
  17.2 5.0 %add_bitcast_fusion.2 = f32[1,16,16,128]{3,2,1,0:T(8,128)S(1)} fusion(pred[16,16,128]{2,1,0:T(8,128)(4,1)S(1)} %get-tuple-element.49, pred[16,16,128]{2,1,0:T(8,128)(4,1)S(1)} %get-tuple-element.48, pred[16,16,128]{2,1,0:T(8,128)(4,1)S(1)} %get-tuple-element.47, pred[16,16,128]{2,1,0:T(8,128)(4,1)S(1)} %get-tuple-element.46, ...), kind=kLoop, calls=%fused_computation.161 | loop fusion | flops 491520 | bytes 393248 | tf_op jit(solution)/shard_map/stack | solution.py:155
  22.1 10.1 %add_multiply_fusion = f32[16,16,128]{2,1,0:T(8,128)S(1)} fusion(f32[16,16,128]{2,1,0:T(8,128)S(1)} %copy-done.1, pred[16,16,128]{2,1,0:T(8,128)(4,1)S(1)} %get-tuple-element.49, pred[16,16,128]{2,1,0:T(8,128)(4,1)S(1)} %get-tuple-element.48, pred[16,16,128]{2,1,0:T(8,128)(4,1)S(1)} %get-tuple-element.47, pred[16,16,128]{2,1,0:T(8,128)(4,1)S(1)} %get-tuple-element.46, ...), kind=kLoop, calls=%fused_computation.163 | loop fusion | flops 1146880 | bytes 524352 | tf_op jit(solution)/shard_map/mul | solution.py:154
  32.3 3.3 collective-permute-start.1
  39.5 4.0 collective-permute-done
  48.6 3.8 collective-permute-done.2
  53.8 3.2 collective-permute-start.5
  57.0 2.6 collective-permute-start.4
  59.7 3.8 collective-permute-done.4
  72.8 3.9 collective-permute-start.8
  76.7 18.2 %copy.868 = f32[4,24,24,128]{0,3,2,1:T(8,128)} copy(f32[4,24,24,128]{3,2,1,0:T(8,128)S(1)} %pad_maximum_fusion) | data formatting | bytes 2359296 | tf_op jit(solution)/shard_map/concatenate | solution.py:23
  94.9 27.0 %reduce_sum.55 = f32[4,12,12,64]{0,3,2,1:T(8,128)} reduce(f32[4,12,2,12,2,64,2]{0,6,5,4,3,2,1:T(2,128)} %bitcast.161, f32[]{:T(128)} %constant.27.clone.1), dimensions={2,4,6}, to_apply=%region_1.2 | reduce | flops 258048 | bytes 1327108 | tf_op jit(solution)/shard_map/reduce_sum | solution.py:87
  121.9 3.7 copy.869
  133.1 2.8 collective-permute-start.13
  136.0 3.0 collective-permute-start.12
  139.0 3.4 collective-permute-done.12
  149.8 9.8 %reshape.56 = f32[8,2,8,2,64,2]{5,4,3,2,1,0:T(8,128)} reshape(f32[16,16,128]{2,1,0:T(8,128)S(1)} %fusion.41) | data formatting | bytes 262144 | tf_op jit(solution)/shard_map/reshape | solution.py:86
  159.6 4.0 reduce_sum.54
  165.7 4.0 collective-permute-start.16
  169.7 3.1 copy.880
  172.8 5.3 %reduce_sum.58 = f32[4,6,6,32]{0,3,2,1:T(8,128)S(1)} reduce(f32[4,6,2,6,2,32,2]{0,6,5,4,3,2,1:T(2,128)} %bitcast.162, f32[]{:T(128)} %constant.27.clone.1), dimensions={2,4,6}, to_apply=%region_4.5 | reduce | flops 32256 | bytes 165892 | tf_op jit(solution)/shard_map/reduce_sum | solution.py:87
  185.5 2.9 collective-permute-start.21
  188.4 2.9 collective-permute-start.20
  191.3 10.7 %all_gather.7 = f32[4,6,16,32]{0,3,2,1:T(8,128)S(1)} all-gather(f32[4,6,4,32]{0,3,2,1:T(8,128)S(1)} %slice_multiply_fusion), channel_id=1, replica_groups=mesh['gx'=8,'gy'=4] {'gy'}, dimensions={2}, use_global_device_ids=true | all-gather | bytes 61440 | tf_op jit(solution)/shard_map/all_gather | solution.py:177
  202.0 4.6 %collective-permute-start.23 = (f32[1,10,1,64]{3,2,1,0:T(1,128)S(1)}, f32[1,10,1,64]{3,2,1,0:T(1,128)S(1)}, u32[]{:S(2)}, u32[]{:S(2)}) collective-permute-start(f32[1,10,1,64]{3,2,1,0:T(1,128)S(1)} %get-tuple-element.143), channel_id=1, source_target_pairs={{1,0},{2,1},{3,2},{5,4},{6,5},{7,6},{9,8},{10,9},{11,10},{13,12},{... | collective-permute-start | bytes 7688 | tf_op jit(solution)/shard_map/ppermute | solution.py:27
  211.9 3.8 collective-permute-start.25
  217.9 4.3 %collective-permute-done.24 = f32[1,1,8,64]{3,2,1,0:T(8,128)S(1)} collective-permute-done((f32[1,1,8,64]{3,2,1,0:T(8,128)S(1)}, f32[1,1,8,64]{3,2,1,0:T(8,128)S(1)}, u32[]{:S(2)}, u32[]{:S(2)}) %collective-permute-start.24) | collective-permute-done | bytes 2080 | tf_op jit(solution)/shard_map/ppermute | solution.py:25
  230.6 5.2 %all_gather.6 = f32[4,16,32]{2,0,1:T(4,128)S(1)} all-gather(f32[4,4,32]{2,0,1:T(4,128)S(1)} %copy.879), channel_id=1, replica_groups=mesh['gx'=8,'gy'=4] {'gy'}, dimensions={1}, use_global_device_ids=true | all-gather | bytes 10240 | tf_op jit(solution)/shard_map/all_gather | solution.py:176
  237.9 3.9 collective-permute-start.29
  244.7 2.9 collective-permute-start.30
  247.6 2.9 collective-permute-start.31
  250.6 3.4 collective-permute-done.31
  256.2 3.9 collective-permute-start.33
  262.8 2.8 collective-permute-start.34
  265.7 3.0 collective-permute-start.35
  268.8 3.3 collective-permute-done.35
  274.2 3.9 collective-permute-start.37
  282.8 3.9 collective-permute-start.39
  291.4 3.9 collective-permute-start.41
  300.1 3.9 collective-permute-start.43
  309.0 3.9 collective-permute-start.44
  317.3 2.6 collective-permute-start.46
  324.5 3.9 collective-permute-start.48
  340.1 3.9 collective-permute-start.52
  356.6 3.9 collective-permute-start.56
  372.4 3.9 collective-permute-start.60
  388.2 3.9 collective-permute-start.64
  (279 shorter events, 163.1 us)
Async XLA Ops:
  32.3 7.1 %collective-permute-start.1 = (f32[4,4,16,128]{3,2,1,0:T(8,128)S(1)}, f32[4,4,16,128]{3,2,1,0:T(8,128)S(1)}, u32[]{:S(2)}, u32[]{:S(2)}) collective-permute-start(f32[4,4,16,128]{3,2,1,0:T(8,128)S(1)} %get-tuple-element.56), channel_id=1, source_target_pairs={{4,0},{8,4},{12,8},{16,12},{20,16},{24,20},{28,24},{5,1},{9,5},{13... | collective-permute-start | bytes 393224 | tf_op jit(solution)/shard_map/ppermute | solution.py:27
  35.6 7.8 %collective-permute-start = (f32[4,4,16,128]{3,2,1,0:T(8,128)S(1)}, f32[4,4,16,128]{3,2,1,0:T(8,128)S(1)}, u32[]{:S(2)}, u32[]{:S(2)}) collective-permute-start(f32[4,4,16,128]{3,2,1,0:T(8,128)S(1)} %get-tuple-element.55), channel_id=1, source_target_pairs={{0,4},{4,8},{8,12},{12,16},{16,20},{20,24},{24,28},{1,5},{5,9},{9,... | collective-permute-start | bytes 393224 | tf_op jit(solution)/shard_map/ppermute | solution.py:25
  43.5 5.1 %collective-permute-start.3 = (f32[4,24,4,128]{3,1,2,0:T(8,128)S(1)}, f32[4,24,4,128]{3,1,2,0:T(8,128)S(1)}, u32[]{:S(2)}, u32[]{:S(2)}) collective-permute-start(f32[4,24,4,128]{3,1,2,0:T(8,128)S(1)} %copy.913), channel_id=1, source_target_pairs={{1,0},{2,1},{3,2},{5,4},{6,5},{7,6},{9,8},{10,9},{11,10},{13,12},{... | collective-permute-start | bytes 589832 | tf_op jit(solution)/shard_map/ppermute | solution.py:27
  45.5 7.0 %collective-permute-start.2 = (f32[4,24,4,128]{3,1,2,0:T(8,128)S(1)}, f32[4,24,4,128]{3,1,2,0:T(8,128)S(1)}, u32[]{:S(2)}, u32[]{:S(2)}) collective-permute-start(f32[4,24,4,128]{3,1,2,0:T(8,128)S(1)} %copy.912), channel_id=1, source_target_pairs={{0,1},{1,2},{2,3},{4,5},{5,6},{6,7},{8,9},{9,10},{10,11},{12,13},{... | collective-permute-start | bytes 589832 | tf_op jit(solution)/shard_map/ppermute | solution.py:25
  53.8 5.9 %collective-permute-start.5 = (f32[1,1,16,128]{3,2,1,0:T(8,128)S(1)}, f32[1,1,16,128]{3,2,1,0:T(8,128)S(1)}, u32[]{:S(2)}, u32[]{:S(2)}) collective-permute-start(f32[1,1,16,128]{3,2,1,0:T(8,128)S(1)} %get-tuple-element.109), channel_id=1, source_target_pairs={{4,0},{8,4},{12,8},{16,12},{20,16},{24,20},{28,24},{5,1},{9,5},{13... | collective-permute-start | bytes 24584 | tf_op jit(solution)/shard_map/ppermute | solution.py:27
  57.0 6.4 %collective-permute-start.4 = (f32[1,1,16,128]{3,2,1,0:T(8,128)S(1)}, f32[1,1,16,128]{3,2,1,0:T(8,128)S(1)}, u32[]{:S(2)}, u32[]{:S(2)}) collective-permute-start(f32[1,1,16,128]{3,2,1,0:T(8,128)S(1)} %get-tuple-element.108), channel_id=1, source_target_pairs={{0,4},{4,8},{8,12},{12,16},{16,20},{20,24},{24,28},{1,5},{5,9},{9,... | collective-permute-start | bytes 24584 | tf_op jit(solution)/shard_map/ppermute | solution.py:25
  65.4 5.0 %collective-permute-start.6 = (f32[1,18,1,128]{3,2,1,0:T(1,128)S(1)}, f32[1,18,1,128]{3,2,1,0:T(1,128)S(1)}, u32[]{:S(2)}, u32[]{:S(2)}) collective-permute-start(f32[1,18,1,128]{3,2,1,0:T(1,128)S(1)} %get-tuple-element.96), channel_id=1, source_target_pairs={{0,1},{1,2},{2,3},{4,5},{5,6},{6,7},{8,9},{9,10},{10,11},{12,13},{... | collective-permute-start | bytes 27656 | tf_op jit(solution)/shard_map/ppermute | solution.py:25
  70.9 54.8 %collective-permute-start.9 = (f32[1,1,16,128]{3,2,1,0:T(8,128)S(1)}, f32[1,1,16,128]{3,2,1,0:T(8,128)S(1)}, u32[]{:S(2)}, u32[]{:S(2)}) collective-permute-start(f32[1,1,16,128]{3,2,1,0:T(8,128)S(1)} %get-tuple-element.107), channel_id=1, source_target_pairs={{4,0},{8,4},{12,8},{16,12},{20,16},{24,20},{28,24},{5,1},{9,5},{13... | collective-permute-start | bytes 24584 | tf_op jit(solution)/shard_map/ppermute | solution.py:27
  72.8 52.9 %collective-permute-start.8 = (f32[1,1,16,128]{3,2,1,0:T(8,128)S(1)}, f32[1,1,16,128]{3,2,1,0:T(8,128)S(1)}, u32[]{:S(2)}, u32[]{:S(2)}) collective-permute-start(f32[1,1,16,128]{3,2,1,0:T(8,128)S(1)} %get-tuple-element.106), channel_id=1, source_target_pairs={{0,4},{4,8},{8,12},{12,16},{16,20},{20,24},{24,28},{1,5},{5,9},{9,... | collective-permute-start | bytes 24584 | tf_op jit(solution)/shard_map/ppermute | solution.py:25
  127.6 5.0 %collective-permute-start.10 = (f32[1,18,1,128]{3,2,1,0:T(1,128)S(1)}, f32[1,18,1,128]{3,2,1,0:T(1,128)S(1)}, u32[]{:S(2)}, u32[]{:S(2)}) collective-permute-start(f32[1,18,1,128]{3,2,1,0:T(1,128)S(1)} %get-tuple-element.94), channel_id=1, source_target_pairs={{0,1},{1,2},{2,3},{4,5},{5,6},{6,7},{8,9},{9,10},{10,11},{12,13},{... | collective-permute-start | bytes 27656 | tf_op jit(solution)/shard_map/ppermute | solution.py:25
  133.1 5.9 %collective-permute-start.13 = (f32[1,1,16,128]{3,2,1,0:T(8,128)S(1)}, f32[1,1,16,128]{3,2,1,0:T(8,128)S(1)}, u32[]{:S(2)}, u32[]{:S(2)}) collective-permute-start(f32[1,1,16,128]{3,2,1,0:T(8,128)S(1)} %get-tuple-element.105), channel_id=1, source_target_pairs={{4,0},{8,4},{12,8},{16,12},{20,16},{24,20},{28,24},{5,1},{9,5},{13... | collective-permute-start | bytes 24584 | tf_op jit(solution)/shard_map/ppermute | solution.py:27
  136.0 6.4 %collective-permute-start.12 = (f32[1,1,16,128]{3,2,1,0:T(8,128)S(1)}, f32[1,1,16,128]{3,2,1,0:T(8,128)S(1)}, u32[]{:S(2)}, u32[]{:S(2)}) collective-permute-start(f32[1,1,16,128]{3,2,1,0:T(8,128)S(1)} %get-tuple-element.104), channel_id=1, source_target_pairs={{0,4},{4,8},{8,12},{12,16},{16,20},{20,24},{24,28},{1,5},{5,9},{9,... | collective-permute-start | bytes 24584 | tf_op jit(solution)/shard_map/ppermute | solution.py:25
  163.7 14.5 %collective-permute-start.17 = (f32[1,1,8,64]{3,2,1,0:T(8,128)S(1)}, f32[1,1,8,64]{3,2,1,0:T(8,128)S(1)}, u32[]{:S(2)}, u32[]{:S(2)}) collective-permute-start(f32[1,1,8,64]{3,2,1,0:T(8,128)S(1)} %get-tuple-element.201), channel_id=1, source_target_pairs={{4,0},{8,4},{12,8},{16,12},{20,16},{24,20},{28,24},{5,1},{9,5},{13... | collective-permute-start | bytes 6152 | tf_op jit(solution)/shard_map/ppermute | solution.py:27
  165.7 12.5 %collective-permute-start.16 = (f32[1,1,8,64]{3,2,1,0:T(8,128)S(1)}, f32[1,1,8,64]{3,2,1,0:T(8,128)S(1)}, u32[]{:S(2)}, u32[]{:S(2)}) collective-permute-start(f32[1,1,8,64]{3,2,1,0:T(8,128)S(1)} %get-tuple-element.200), channel_id=1, source_target_pairs={{0,4},{4,8},{8,12},{12,16},{16,20},{20,24},{24,28},{1,5},{5,9},{9,... | collective-permute-start | bytes 6152 | tf_op jit(solution)/shard_map/ppermute | solution.py:25
  185.5 16.6 %collective-permute-start.21 = (f32[1,1,8,64]{3,2,1,0:T(8,128)S(1)}, f32[1,1,8,64]{3,2,1,0:T(8,128)S(1)}, u32[]{:S(2)}, u32[]{:S(2)}) collective-permute-start(f32[1,1,8,64]{3,2,1,0:T(8,128)S(1)} %get-tuple-element.199), channel_id=1, source_target_pairs={{4,0},{8,4},{12,8},{16,12},{20,16},{24,20},{28,24},{5,1},{9,5},{13... | collective-permute-start | bytes 6152 | tf_op jit(solution)/shard_map/ppermute | solution.py:27
  188.4 13.6 %collective-permute-start.20 = (f32[1,1,8,64]{3,2,1,0:T(8,128)S(1)}, f32[1,1,8,64]{3,2,1,0:T(8,128)S(1)}, u32[]{:S(2)}, u32[]{:S(2)}) collective-permute-start(f32[1,1,8,64]{3,2,1,0:T(8,128)S(1)} %get-tuple-element.198), channel_id=1, source_target_pairs={{0,4},{4,8},{8,12},{12,16},{16,20},{20,24},{24,28},{1,5},{5,9},{9,... | collective-permute-start | bytes 6152 | tf_op jit(solution)/shard_map/ppermute | solution.py:25
  202.0 8.8 %collective-permute-start.23 = (f32[1,10,1,64]{3,2,1,0:T(1,128)S(1)}, f32[1,10,1,64]{3,2,1,0:T(1,128)S(1)}, u32[]{:S(2)}, u32[]{:S(2)}) collective-permute-start(f32[1,10,1,64]{3,2,1,0:T(1,128)S(1)} %get-tuple-element.143), channel_id=1, source_target_pairs={{1,0},{2,1},{3,2},{5,4},{6,5},{7,6},{9,8},{10,9},{11,10},{13,12},{... | collective-permute-start | bytes 7688 | tf_op jit(solution)/shard_map/ppermute | solution.py:27
  211.9 6.0 %collective-permute-start.25 = (f32[1,1,8,64]{3,2,1,0:T(8,128)S(1)}, f32[1,1,8,64]{3,2,1,0:T(8,128)S(1)}, u32[]{:S(2)}, u32[]{:S(2)}) collective-permute-start(f32[1,1,8,64]{3,2,1,0:T(8,128)S(1)} %get-tuple-element.197), channel_id=1, source_target_pairs={{4,0},{8,4},{12,8},{16,12},{20,16},{24,20},{28,24},{5,1},{9,5},{13... | collective-permute-start | bytes 6152 | tf_op jit(solution)/shard_map/ppermute | solution.py:27
  215.7 6.4 %collective-permute-start.24 = (f32[1,1,8,64]{3,2,1,0:T(8,128)S(1)}, f32[1,1,8,64]{3,2,1,0:T(8,128)S(1)}, u32[]{:S(2)}, u32[]{:S(2)}) collective-permute-start(f32[1,1,8,64]{3,2,1,0:T(8,128)S(1)} %get-tuple-element.196), channel_id=1, source_target_pairs={{0,4},{4,8},{8,12},{12,16},{16,20},{20,24},{24,28},{1,5},{5,9},{9,... | collective-permute-start | bytes 6152 | tf_op jit(solution)/shard_map/ppermute | solution.py:25
  222.2 5.0 %collective-permute-start.27 = (f32[1,10,1,64]{3,2,1,0:T(1,128)S(1)}, f32[1,10,1,64]{3,2,1,0:T(1,128)S(1)}, u32[]{:S(2)}, u32[]{:S(2)}) collective-permute-start(f32[1,10,1,64]{3,2,1,0:T(1,128)S(1)} %get-tuple-element.141), channel_id=1, source_target_pairs={{1,0},{2,1},{3,2},{5,4},{6,5},{7,6},{9,8},{10,9},{11,10},{13,12},{... | collective-permute-start | bytes 7688 | tf_op jit(solution)/shard_map/ppermute | solution.py:27
  235.9 6.0 %collective-permute-start.28 = (f32[1,16,32]{2,1,0:T(8,128)S(1)}, f32[1,16,32]{2,1,0:T(8,128)S(1)}, u32[]{:S(2)}, u32[]{:S(2)}) collective-permute-start(f32[1,16,32]{2,1,0:T(8,128)S(1)} %broadcast_in_dim.284), channel_id=1, source_target_pairs={{4,0},{8,4},{12,8},{16,12},{20,16},{24,20},{28,24},{5,1},{9,5},{13... | collective-permute-start | bytes 6152 | tf_op jit(solution)/shard_map/ppermute | solution.py:27
  237.9 6.4 %collective-permute-start.29 = (f32[1,16,32]{2,1,0:T(8,128)S(1)}, f32[1,16,32]{2,1,0:T(8,128)S(1)}, u32[]{:S(2)}, u32[]{:S(2)}) collective-permute-start(f32[1,16,32]{2,1,0:T(8,128)S(1)} %broadcast_in_dim.285), channel_id=1, source_target_pairs={{0,4},{4,8},{8,12},{12,16},{16,20},{20,24},{24,28},{1,5},{5,9},{9,... | collective-permute-start | bytes 6152 | tf_op jit(solution)/shard_map/ppermute | solution.py:25
  244.7 5.9 %collective-permute-start.30 = (f32[1,16,32]{2,1,0:T(8,128)S(1)}, f32[1,16,32]{2,1,0:T(8,128)S(1)}, u32[]{:S(2)}, u32[]{:S(2)}) collective-permute-start(f32[1,16,32]{2,1,0:T(8,128)S(1)} %get-tuple-element.191), channel_id=1, source_target_pairs={{4,0},{8,4},{12,8},{16,12},{20,16},{24,20},{28,24},{5,1},{9,5},{13... | collective-permute-start | bytes 6152 | tf_op jit(solution)/shard_map/ppermute | solution.py:27
  247.6 6.4 %collective-permute-start.31 = (f32[1,16,32]{2,1,0:T(8,128)S(1)}, f32[1,16,32]{2,1,0:T(8,128)S(1)}, u32[]{:S(2)}, u32[]{:S(2)}) collective-permute-start(f32[1,16,32]{2,1,0:T(8,128)S(1)} %get-tuple-element.190), channel_id=1, source_target_pairs={{0,4},{4,8},{8,12},{12,16},{16,20},{20,24},{24,28},{1,5},{5,9},{9,... | collective-permute-start | bytes 6152 | tf_op jit(solution)/shard_map/ppermute | solution.py:25
  254.3 5.9 %collective-permute-start.32 = (f32[1,16,32]{2,1,0:T(8,128)S(1)}, f32[1,16,32]{2,1,0:T(8,128)S(1)}, u32[]{:S(2)}, u32[]{:S(2)}) collective-permute-start(f32[1,16,32]{2,1,0:T(8,128)S(1)} %get-tuple-element.185), channel_id=1, source_target_pairs={{4,0},{8,4},{12,8},{16,12},{20,16},{24,20},{28,24},{5,1},{9,5},{13... | collective-permute-start | bytes 6152 | tf_op jit(solution)/shard_map/ppermute | solution.py:27
  256.2 6.4 %collective-permute-start.33 = (f32[1,16,32]{2,1,0:T(8,128)S(1)}, f32[1,16,32]{2,1,0:T(8,128)S(1)}, u32[]{:S(2)}, u32[]{:S(2)}) collective-permute-start(f32[1,16,32]{2,1,0:T(8,128)S(1)} %get-tuple-element.184), channel_id=1, source_target_pairs={{0,4},{4,8},{8,12},{12,16},{16,20},{20,24},{24,28},{1,5},{5,9},{9,... | collective-permute-start | bytes 6152 | tf_op jit(solution)/shard_map/ppermute | solution.py:25
  262.8 5.9 %collective-permute-start.34 = (f32[1,16,32]{2,1,0:T(8,128)S(1)}, f32[1,16,32]{2,1,0:T(8,128)S(1)}, u32[]{:S(2)}, u32[]{:S(2)}) collective-permute-start(f32[1,16,32]{2,1,0:T(8,128)S(1)} %get-tuple-element.179), channel_id=1, source_target_pairs={{4,0},{8,4},{12,8},{16,12},{20,16},{24,20},{28,24},{5,1},{9,5},{13... | collective-permute-start | bytes 6152 | tf_op jit(solution)/shard_map/ppermute | solution.py:27
  265.7 6.4 %collective-permute-start.35 = (f32[1,16,32]{2,1,0:T(8,128)S(1)}, f32[1,16,32]{2,1,0:T(8,128)S(1)}, u32[]{:S(2)}, u32[]{:S(2)}) collective-permute-start(f32[1,16,32]{2,1,0:T(8,128)S(1)} %get-tuple-element.178), channel_id=1, source_target_pairs={{0,4},{4,8},{8,12},{12,16},{16,20},{20,24},{24,28},{1,5},{5,9},{9,... | collective-permute-start | bytes 6152 | tf_op jit(solution)/shard_map/ppermute | solution.py:25
  272.3 5.9 %collective-permute-start.36 = (f32[1,16,32]{2,1,0:T(8,128)S(1)}, f32[1,16,32]{2,1,0:T(8,128)S(1)}, u32[]{:S(2)}, u32[]{:S(2)}) collective-permute-start(f32[1,16,32]{2,1,0:T(8,128)S(1)} %get-tuple-element.173), channel_id=1, source_target_pairs={{4,0},{8,4},{12,8},{16,12},{20,16},{24,20},{28,24},{5,1},{9,5},{13... | collective-permute-start | bytes 6152 | tf_op jit(solution)/shard_map/ppermute | solution.py:27
  274.2 6.4 %collective-permute-start.37 = (f32[1,16,32]{2,1,0:T(8,128)S(1)}, f32[1,16,32]{2,1,0:T(8,128)S(1)}, u32[]{:S(2)}, u32[]{:S(2)}) collective-permute-start(f32[1,16,32]{2,1,0:T(8,128)S(1)} %get-tuple-element.172), channel_id=1, source_target_pairs={{0,4},{4,8},{8,12},{12,16},{16,20},{20,24},{24,28},{1,5},{5,9},{9,... | collective-permute-start | bytes 6152 | tf_op jit(solution)/shard_map/ppermute | solution.py:25
  280.9 5.9 %collective-permute-start.38 = (f32[1,16,32]{2,1,0:T(8,128)S(1)}, f32[1,16,32]{2,1,0:T(8,128)S(1)}, u32[]{:S(2)}, u32[]{:S(2)}) collective-permute-start(f32[1,16,32]{2,1,0:T(8,128)S(1)} %get-tuple-element.167), channel_id=1, source_target_pairs={{4,0},{8,4},{12,8},{16,12},{20,16},{24,20},{28,24},{5,1},{9,5},{13... | collective-permute-start | bytes 6152 | tf_op jit(solution)/shard_map/ppermute | solution.py:27
  282.8 6.4 %collective-permute-start.39 = (f32[1,16,32]{2,1,0:T(8,128)S(1)}, f32[1,16,32]{2,1,0:T(8,128)S(1)}, u32[]{:S(2)}, u32[]{:S(2)}) collective-permute-start(f32[1,16,32]{2,1,0:T(8,128)S(1)} %get-tuple-element.166), channel_id=1, source_target_pairs={{0,4},{4,8},{8,12},{12,16},{16,20},{20,24},{24,28},{1,5},{5,9},{9,... | collective-permute-start | bytes 6152 | tf_op jit(solution)/shard_map/ppermute | solution.py:25
  289.5 5.9 %collective-permute-start.40 = (f32[1,16,32]{2,1,0:T(8,128)S(1)}, f32[1,16,32]{2,1,0:T(8,128)S(1)}, u32[]{:S(2)}, u32[]{:S(2)}) collective-permute-start(f32[1,16,32]{2,1,0:T(8,128)S(1)} %get-tuple-element.161), channel_id=1, source_target_pairs={{4,0},{8,4},{12,8},{16,12},{20,16},{24,20},{28,24},{5,1},{9,5},{13... | collective-permute-start | bytes 6152 | tf_op jit(solution)/shard_map/ppermute | solution.py:27
  291.4 6.4 %collective-permute-start.41 = (f32[1,16,32]{2,1,0:T(8,128)S(1)}, f32[1,16,32]{2,1,0:T(8,128)S(1)}, u32[]{:S(2)}, u32[]{:S(2)}) collective-permute-start(f32[1,16,32]{2,1,0:T(8,128)S(1)} %get-tuple-element.160), channel_id=1, source_target_pairs={{0,4},{4,8},{8,12},{12,16},{16,20},{20,24},{24,28},{1,5},{5,9},{9,... | collective-permute-start | bytes 6152 | tf_op jit(solution)/shard_map/ppermute | solution.py:25
  298.2 5.9 %collective-permute-start.42 = (f32[1,16,32]{2,1,0:T(8,128)S(1)}, f32[1,16,32]{2,1,0:T(8,128)S(1)}, u32[]{:S(2)}, u32[]{:S(2)}) collective-permute-start(f32[1,16,32]{2,1,0:T(8,128)S(1)} %get-tuple-element.159), channel_id=1, source_target_pairs={{4,0},{8,4},{12,8},{16,12},{20,16},{24,20},{28,24},{5,1},{9,5},{13... | collective-permute-start | bytes 6152 | tf_op jit(solution)/shard_map/ppermute | solution.py:27
  300.1 6.4 %collective-permute-start.43 = (f32[1,16,32]{2,1,0:T(8,128)S(1)}, f32[1,16,32]{2,1,0:T(8,128)S(1)}, u32[]{:S(2)}, u32[]{:S(2)}) collective-permute-start(f32[1,16,32]{2,1,0:T(8,128)S(1)} %get-tuple-element.158), channel_id=1, source_target_pairs={{0,4},{4,8},{8,12},{12,16},{16,20},{20,24},{24,28},{1,5},{5,9},{9,... | collective-permute-start | bytes 6152 | tf_op jit(solution)/shard_map/ppermute | solution.py:25
  307.0 5.9 %collective-permute-start.45 = (f32[1,1,8,64]{3,2,1,0:T(8,128)S(1)}, f32[1,1,8,64]{3,2,1,0:T(8,128)S(1)}, u32[]{:S(2)}, u32[]{:S(2)}) collective-permute-start(f32[1,1,8,64]{3,2,1,0:T(8,128)S(1)} %get-tuple-element.151), channel_id=1, source_target_pairs={{4,0},{8,4},{12,8},{16,12},{20,16},{24,20},{28,24},{5,1},{9,5},{13... | collective-permute-start | bytes 6152 | tf_op jit(solution)/shard_map/ppermute | solution.py:27
  309.0 6.4 %collective-permute-start.44 = (f32[1,1,8,64]{3,2,1,0:T(8,128)S(1)}, f32[1,1,8,64]{3,2,1,0:T(8,128)S(1)}, u32[]{:S(2)}, u32[]{:S(2)}) collective-permute-start(f32[1,1,8,64]{3,2,1,0:T(8,128)S(1)} %get-tuple-element.150), channel_id=1, source_target_pairs={{0,4},{4,8},{8,12},{12,16},{16,20},{20,24},{24,28},{1,5},{5,9},{9,... | collective-permute-start | bytes 6152 | tf_op jit(solution)/shard_map/ppermute | solution.py:25
  322.6 5.9 %collective-permute-start.49 = (f32[1,1,8,64]{3,2,1,0:T(8,128)S(1)}, f32[1,1,8,64]{3,2,1,0:T(8,128)S(1)}, u32[]{:S(2)}, u32[]{:S(2)}) collective-permute-start(f32[1,1,8,64]{3,2,1,0:T(8,128)S(1)} %get-tuple-element.149), channel_id=1, source_target_pairs={{4,0},{8,4},{12,8},{16,12},{20,16},{24,20},{28,24},{5,1},{9,5},{13... | collective-permute-start | bytes 6152 | tf_op jit(solution)/shard_map/ppermute | solution.py:27
  324.5 6.4 %collective-permute-start.48 = (f32[1,1,8,64]{3,2,1,0:T(8,128)S(1)}, f32[1,1,8,64]{3,2,1,0:T(8,128)S(1)}, u32[]{:S(2)}, u32[]{:S(2)}) collective-permute-start(f32[1,1,8,64]{3,2,1,0:T(8,128)S(1)} %get-tuple-element.148), channel_id=1, source_target_pairs={{0,4},{4,8},{8,12},{12,16},{16,20},{20,24},{24,28},{1,5},{5,9},{9,... | collective-permute-start | bytes 6152 | tf_op jit(solution)/shard_map/ppermute | solution.py:25
  338.2 5.9 %collective-permute-start.53 = (f32[1,1,8,64]{3,2,1,0:T(8,128)S(1)}, f32[1,1,8,64]{3,2,1,0:T(8,128)S(1)}, u32[]{:S(2)}, u32[]{:S(2)}) collective-permute-start(f32[1,1,8,64]{3,2,1,0:T(8,128)S(1)} %get-tuple-element.147), channel_id=1, source_target_pairs={{4,0},{8,4},{12,8},{16,12},{20,16},{24,20},{28,24},{5,1},{9,5},{13... | collective-permute-start | bytes 6152 | tf_op jit(solution)/shard_map/ppermute | solution.py:27
  340.1 6.4 %collective-permute-start.52 = (f32[1,1,8,64]{3,2,1,0:T(8,128)S(1)}, f32[1,1,8,64]{3,2,1,0:T(8,128)S(1)}, u32[]{:S(2)}, u32[]{:S(2)}) collective-permute-start(f32[1,1,8,64]{3,2,1,0:T(8,128)S(1)} %get-tuple-element.146), channel_id=1, source_target_pairs={{0,4},{4,8},{8,12},{12,16},{16,20},{20,24},{24,28},{1,5},{5,9},{9,... | collective-permute-start | bytes 6152 | tf_op jit(solution)/shard_map/ppermute | solution.py:25
  354.6 5.9 %collective-permute-start.57 = (f32[1,1,16,128]{3,2,1,0:T(8,128)S(1)}, f32[1,1,16,128]{3,2,1,0:T(8,128)S(1)}, u32[]{:S(2)}, u32[]{:S(2)}) collective-permute-start(f32[1,1,16,128]{3,2,1,0:T(8,128)S(1)} %get-tuple-element.103), channel_id=1, source_target_pairs={{4,0},{8,4},{12,8},{16,12},{20,16},{24,20},{28,24},{5,1},{9,5},{13... | collective-permute-start | bytes 24584 | tf_op jit(solution)/shard_map/ppermute | solution.py:27
  356.6 6.4 %collective-permute-start.56 = (f32[1,1,16,128]{3,2,1,0:T(8,128)S(1)}, f32[1,1,16,128]{3,2,1,0:T(8,128)S(1)}, u32[]{:S(2)}, u32[]{:S(2)}) collective-permute-start(f32[1,1,16,128]{3,2,1,0:T(8,128)S(1)} %get-tuple-element.102), channel_id=1, source_target_pairs={{0,4},{4,8},{8,12},{12,16},{16,20},{20,24},{24,28},{1,5},{5,9},{9,... | collective-permute-start | bytes 24584 | tf_op jit(solution)/shard_map/ppermute | solution.py:25
  370.4 5.9 %collective-permute-start.61 = (f32[1,1,16,128]{3,2,1,0:T(8,128)S(1)}, f32[1,1,16,128]{3,2,1,0:T(8,128)S(1)}, u32[]{:S(2)}, u32[]{:S(2)}) collective-permute-start(f32[1,1,16,128]{3,2,1,0:T(8,128)S(1)} %get-tuple-element.101), channel_id=1, source_target_pairs={{4,0},{8,4},{12,8},{16,12},{20,16},{24,20},{28,24},{5,1},{9,5},{13... | collective-permute-start | bytes 24584 | tf_op jit(solution)/shard_map/ppermute | solution.py:27
  372.4 6.4 %collective-permute-start.60 = (f32[1,1,16,128]{3,2,1,0:T(8,128)S(1)}, f32[1,1,16,128]{3,2,1,0:T(8,128)S(1)}, u32[]{:S(2)}, u32[]{:S(2)}) collective-permute-start(f32[1,1,16,128]{3,2,1,0:T(8,128)S(1)} %get-tuple-element.100), channel_id=1, source_target_pairs={{0,4},{4,8},{8,12},{12,16},{16,20},{20,24},{24,28},{1,5},{5,9},{9,... | collective-permute-start | bytes 24584 | tf_op jit(solution)/shard_map/ppermute | solution.py:25
  386.3 5.9 %collective-permute-start.65 = (f32[1,1,16,128]{3,2,1,0:T(8,128)S(1)}, f32[1,1,16,128]{3,2,1,0:T(8,128)S(1)}, u32[]{:S(2)}, u32[]{:S(2)}) collective-permute-start(f32[1,1,16,128]{3,2,1,0:T(8,128)S(1)} %get-tuple-element.99), channel_id=1, source_target_pairs={{4,0},{8,4},{12,8},{16,12},{20,16},{24,20},{28,24},{5,1},{9,5},{13... | collective-permute-start | bytes 24584 | tf_op jit(solution)/shard_map/ppermute | solution.py:27
  388.2 6.4 %collective-permute-start.64 = (f32[1,1,16,128]{3,2,1,0:T(8,128)S(1)}, f32[1,1,16,128]{3,2,1,0:T(8,128)S(1)}, u32[]{:S(2)}, u32[]{:S(2)}) collective-permute-start(f32[1,1,16,128]{3,2,1,0:T(8,128)S(1)} %get-tuple-element.98), channel_id=1, source_target_pairs={{0,4},{4,8},{8,12},{12,16},{16,20},{20,24},{24,28},{1,5},{5,9},{9,... | collective-permute-start | bytes 24584 | tf_op jit(solution)/shard_map/ppermute | solution.py:25
  (22 other events, 116.4 us)
where the time goes:
time: 405 us; the launch traced here: 403 us
  starting transfers between devices  181 us (45%)
  waiting for transfers between devices  85.1 us (21%)
  other arithmetic  69.4 us (17%)
  local copies, waits for them, and re-layouts  49.5 us (12%)
  blocking collectives  15.9 us (4%)
    ppermute x34, starting transfers between devices, padded_2(): lax.ppermute(tail, axis, [(i, (i + 1) % count) for i in range(ends)])  105 us
    ppermute x34, waiting for transfers between devices, padded_2(): lax.ppermute(tail, axis, [(i, (i + 1) % count) for i in range(ends)])  83 us
    ppermute x34, starting transfers between devices, padded_2(): lax.ppermute(head, axis, [((i + 1) % count, i) for i in range(ends)])  76.4 us
    reduce_sum x4, other arithmetic, coarsen(): return jnp.mean(split, axis=(-5, -3, -1))  36.5 us
    concatenate x1, local copies, waits for them, and re-layouts, padded_2(): jnp.concatenate([lax.ppermute(tail, axis, [(i, (i + 1) % count) for i in...  18.2 us
    another operation x3, other arithmetic, local_fields(): return jnp.stack([fields[0], fields[1], fields[2], storage])  16.5 us
    reshape x2, local copies, waits for them, and re-layouts, coarsen(): values.reshape(lead + (size_x // 2, 2, size_y // 2, 2, size_z // 2, 2))  10.9 us
    all_gather x1, blocking collectives, local(): lax.all_gather(narrow, 'gy', axis=2, tiled=True)  10.7 us
  transfers between devices with their start and end apart: 68, of which 33 were waited for; matrix products, arithmetic and copies ran while one was open for 15% of the time, Pallas kernels for 0%

commit v1 on v0

v1 whole, which is shorter than its diff:
```python
import jax
import jax.numpy as jnp
from jax import lax
from jax.sharding import PartitionSpec as P

CHEB = 3
COARSE_SWEEPS = 8

storage_scale = 0.05
cheb_centre = 1.1
cheb_half = 0.9
cheb_ratio = cheb_centre / cheb_half
jacobi_weight = 0.8

FINE_HALO = 10
MID_HALO = 5
HIGH = lax.Precision.HIGHEST


def shift_from(cells, axis, offset):
    count = lax.axis_size(axis)
    if offset > 0:
        pairs = [(i + offset, i) for i in range(count - offset)]
    else:
        pairs = [(i, i - offset) for i in range(count + offset)]
    if not pairs:
        return jnp.zeros_like(cells)
    return lax.ppermute(cells, axis, pairs)


def halo(cells, sides, width):
    for axis, dim in sides:
        size = cells.shape[dim]
        head = lax.slice_in_dim(cells, 0, width, axis=dim)
        tail = lax.slice_in_dim(cells, size - width, size, axis=dim)
        cells = jnp.concatenate(
            [shift_from(tail, axis, -1), cells, shift_from(head, axis, 1)], axis=dim
        )
    return cells


def harmonic(first, second):
    return first * second / jnp.maximum(0.5 * (first + second), 0.1)


def win(a, n, margin, r, dx=0, dy=0):
    lo = margin - r
    hi = margin + n + r
    return a[..., lo + dx : hi + dx, lo + dy : hi + dy, :]


def pair_matrix(size, dtype=jnp.float32):
    rows = jnp.arange(size)[:, None] // 2
    cols = jnp.arange(size // 2)[None, :]
    return (rows == cols).astype(dtype)


def coarsen(values):
    lead = values.shape[:-3]
    sx, sy, sz = values.shape[-3:]
    v = values.reshape(lead + (sx // 2, 2, sy, sz))
    v = v[..., 0, :, :] + v[..., 1, :, :]
    v = jnp.einsum("...yz,zw->...yw", v, pair_matrix(sz), precision=HIGH)
    v = jnp.einsum("...yw,yv->...vw", v, pair_matrix(sy), precision=HIGH)
    return v * 0.125


def prolong(values):
    sx, sy, sz = values.shape
    v = jnp.einsum("xyz,wz->xyw", values, pair_matrix(2 * sz), precision=HIGH)
    v = jnp.einsum("xyw,vy->xvw", v, pair_matrix(2 * sy), precision=HIGH)
    v = jnp.broadcast_to(v[:, None], (sx, 2) + v.shape[1:]).reshape((2 * sx,) + v.shape[1:])
    return v


def build_level(coeffs, n, margin, spacing):
    kx, ky, kz, store = coeffs[0], coeffs[1], coeffs[2], coeffs[3]
    fx = harmonic(kx[1:], kx[:-1]) * spacing
    fy = harmonic(ky[:, 1:], ky[:, :-1]) * spacing
    vertical = harmonic(kz[:, :, 1:], kz[:, :, :-1]) * spacing
    closed = jnp.zeros_like(kz[:, :, :1])
    above = jnp.concatenate([vertical, closed], axis=2)
    below = jnp.concatenate([closed, vertical], axis=2)
    level = dict(n=n, m=margin, fx=fx, fy=fy, above=above, below=below, store=store)
    r = margin - 1
    level["diag"] = jnp.maximum(faces_sum(level, r) + win(store, n, margin, r), 0.01)
    level["dm"] = r
    return level


def faces_sum(level, r):
    n, m = level["n"], level["m"]
    east = win(level["fx"], n, m, r)
    west = win(level["fx"], n, m, r, dx=-1)
    north = win(level["fy"], n, m, r)
    south = win(level["fy"], n, m, r, dy=-1)
    above = win(level["above"], n, m, r)
    below = win(level["below"], n, m, r)
    return east + west + north + south + above + below


def operate(values, vm, level):
    n, m = level["n"], level["m"]
    r = vm - 1
    centre = win(values, n, vm, r)
    upper = jnp.concatenate([centre[:, :, 1:], centre[:, :, :1]], axis=2)
    lower = jnp.concatenate([centre[:, :, -1:], centre[:, :, :-1]], axis=2)
    fx, fy = level["fx"], level["fy"]
    fluxes = win(fx, n, m, r) * (centre - win(values, n, vm, r, dx=1))
    fluxes = fluxes + win(fx, n, m, r, dx=-1) * (centre - win(values, n, vm, r, dx=-1))
    fluxes = fluxes + win(fy, n, m, r) * (centre - win(values, n, vm, r, dy=1))
    fluxes = fluxes + win(fy, n, m, r, dy=-1) * (centre - win(values, n, vm, r, dy=-1))
    fluxes = fluxes + win(level["above"], n, m, r) * (centre - upper)
    fluxes = fluxes + win(level["below"], n, m, r) * (centre - lower)
    return win(level["store"], n, m, r) * centre + fluxes


def chebyshev(target, tm, initial, im, level):
    n = level["n"]
    diag, dm = level["diag"], level["dm"]
    if initial is None:
        cur = min(tm, dm)
        misfit = win(target, n, tm, cur)
        update = misfit / win(diag, n, dm, cur) * (1.0 / cheb_centre)
        iterate = update
    else:
        applied = operate(initial, im, level)
        cur = im - 1
        misfit = win(target, n, tm, cur) - applied
        update = misfit / win(diag, n, dm, cur) * (1.0 / cheb_centre)
        iterate = win(initial, n, im, cur) + update
    factor = 1.0 / cheb_ratio
    for repeat in range(CHEB - 1):
        applied = operate(iterate, cur, level)
        nxt = cur - 1
        misfit = win(target, n, tm, nxt) - applied
        factor_new = 1.0 / (2.0 * cheb_ratio - factor)
        update = factor_new * factor * win(update, n, cur, nxt) + 2.0 * factor_new / cheb_half * (
            misfit / win(diag, n, dm, nxt)
        )
        iterate = win(iterate, n, cur, nxt) + update
        cur = nxt
        factor = factor_new
    return iterate, cur


def lookup(soil_id, soil_table, record):
    looked = jnp.full(soil_id.shape, soil_table[record, soil_table.shape[1] - 1])
    for material in range(soil_table.shape[1] - 2, -1, -1):
        looked = jnp.where(soil_id == material, soil_table[record, material], looked)
    return looked


def local(conc_prev, right_side, soil_id, soil_table):
    n = conc_prev.shape[0]
    ny = conc_prev.shape[1]
    hf = FINE_HALO
    gx_count = lax.axis_size("gx")
    gy_count = lax.axis_size("gy")
    ix = lax.axis_index("gx")
    iy = lax.axis_index("gy")

    stacked = jnp.stack([conc_prev, right_side, soil_id.astype(jnp.float32)])
    ext = halo(stacked, (("gx", 1), ("gy", 2)), hf)
    conc, rhs, idf = ext[0], ext[1], ext[2]
    ids = idf.astype(jnp.int32)
    gxi = ix * n - hf + jnp.arange(n + 2 * hf)
    gyi = iy * ny - hf + jnp.arange(ny + 2 * hf)
    inside = ((gxi >= 0) & (gxi < gx_count * n))[:, None, None] & (
        (gyi >= 0) & (gyi < gy_count * ny)
    )[None, :, None]
    kx = jnp.where(inside, lookup(ids, soil_table, 0), 0.0)
    ky = jnp.where(inside, lookup(ids, soil_table, 1), 0.0)
    kz = jnp.where(inside, lookup(ids, soil_table, 2), 0.0)
    s3 = lookup(ids, soil_table, 3)
    s4 = lookup(ids, soil_table, 4)
    store = storage_scale * (1.0 + s3 * jnp.exp((s4 - 1.0) * jnp.log(conc)))
    store = jnp.where(inside, store, 0.0)
    fine_c = jnp.stack([kx, ky, kz, store])
    fine = build_level(fine_c, n, hf, 1.0)

    x0, x0m = chebyshev(rhs, hf, None, 0, fine)
    r0 = win(rhs, n, hf, x0m - 1) - operate(x0, x0m, fine)
    r0m = x0m - 1
    nm = n // 2
    mm = hf // 2
    mid_c = coarsen(fine_c)
    mid = build_level(mid_c, nm, mm, 0.25)
    b1 = coarsen(win(r0, n, r0m, 2 * (r0m // 2)))
    b1m = r0m // 2
    x1, x1m = chebyshev(b1, b1m, None, 0, mid)
    r1 = win(b1, nm, b1m, x1m - 1) - operate(x1, x1m, mid)
    r1m = x1m - 1
    b2 = coarsen(win(r1, nm, r1m, 0))
    coarse_own = coarsen(win(mid_c, nm, mm, 0))

    nc = b2.shape[0]
    reach = 2
    cpack = jnp.concatenate([b2[None], coarse_own], axis=0)
    cpack = lax.all_gather(cpack, "gy", axis=2, tiled=True)
    parts = [shift_from(cpack, "gx", -d) for d in range(reach, 0, -1)]
    parts += [cpack]
    parts += [shift_from(cpack, "gx", d) for d in range(1, reach + 1)]
    cpack = jnp.concatenate(parts, axis=1)
    cm = reach * nc
    source = cpack[0]
    cc = cpack[1:]
    line_total = jnp.sum(source, axis=1)
    line_store = jnp.sum(cc[3], axis=1)
    line_mean = jnp.where(line_store > 0, line_total / jnp.where(line_store > 0, line_store, 1.0), 0.0)
    width = source.shape[0]
    ccp = jnp.pad(cc, ((0, 0), (0, 0), (1, 1), (0, 0)))
    kx_, ky_, kz_, st_ = ccp[0], ccp[1], ccp[2], ccp[3]
    q = 0.0625
    cx = kx_[1:-1, 1:-1]
    cy = ky_[1:-1, 1:-1]
    cz = kz_[1:-1, 1:-1]
    east = harmonic(kx_[2:, 1:-1], cx) * q
    west = harmonic(kx_[:-2, 1:-1], cx) * q
    north = harmonic(ky_[1:-1, 2:], cy) * q
    south = harmonic(ky_[1:-1, :-2], cy) * q
    vert = harmonic(cz[:, :, 1:], cz[:, :, :-1]) * q
    closed = jnp.zeros_like(cz[:, :, :1])
    above = jnp.concatenate([vert, closed], axis=2)
    below = jnp.concatenate([closed, vert], axis=2)
    cst = st_[1:-1, 1:-1]
    cdiag = jnp.maximum(cst + east + west + north + south + above + below, 0.01)
    csrc = source[1:-1]
    u = jnp.broadcast_to(line_mean[:, None, :], source.shape)
    for sweep in range(COARSE_SWEEPS):
        lo = sweep
        cur = u
        up = jnp.pad(cur, ((0, 0), (1, 1), (0, 0)))
        centre = up[1:-1, 1:-1]
        sl = slice(lo, width - 2 - lo)
        upper = jnp.concatenate([centre[:, :, 1:], centre[:, :, :1]], axis=2)
        lower = jnp.concatenate([centre[:, :, -1:], centre[:, :, :-1]], axis=2)
        fl = east[sl] * (centre - up[2:, 1:-1]) + west[sl] * (centre - up[:-2, 1:-1])
        fl = fl + north[sl] * (centre - up[1:-1, 2:]) + south[sl] * (centre - up[1:-1, :-2])
        fl = fl + above[sl] * (centre - upper) + below[sl] * (centre - lower)
        applied = cst[sl] * centre + fl
        u = centre + jacobi_weight * ((csrc[sl] - applied) / cdiag[sl])
    ncy = nc
    u = lax.dynamic_slice_in_dim(u, iy * ncy, ncy, 1)

    s1 = win(x1, nm, x1m, 0) + prolong(u)
    mpack = jnp.stack([s1, win(b1, nm, b1m, 0)])
    mpack = halo(mpack, (("gx", 1), ("gy", 2)), MID_HALO)
    s1e, b1e = mpack[0], mpack[1]
    y1, y1m = chebyshev(b1e, MID_HALO, s1e, MID_HALO, mid)
    fm = 2 * y1m
    s0 = win(x0, n, x0m, fm) + prolong(y1)
    fs = min(fm, CHEB)
    s0 = win(s0, n, fm, fs)
    out, om = chebyshev(rhs, hf, s0, fs, fine)
    return out


def solution(mesh):
    placed = (P("gx", "gy", None), P("gx", "gy", None), P("gx", "gy", None), P())
    return jax.shard_map(
        local, mesh=mesh, in_specs=placed, out_specs=P("gx", "gy", None), check_vma=False
    )
```

time: 405 us -> 163 us (0.40)
  the two profiles are of different devices: /device:TPU:26 before, /device:TPU:1 now
where the time goes in v1:
time: 163 us; the launch traced here: 162 us
  other arithmetic  64.4 us (40%)
  starting transfers between devices  36.6 us (22%)
  waiting for transfers between devices  35 us (21%)
  local copies, waits for them, and re-layouts  16.8 us (10%)
  blocking collectives  4.37 us (3%)
  matrix products  4.22 us (3%)
    ppermute x12, starting transfers between devices, shift_from(): return lax.ppermute(cells, axis, pairs)  36.6 us
    ppermute x12, waiting for transfers between devices, shift_from(): return lax.ppermute(cells, axis, pairs)  35 us
    select_n x2, other arithmetic, local(): kx = jnp.where(inside, lookup(ids, soil_table, 0), 0.0)  11.7 us
    select_n x2, other arithmetic, local(): kz = jnp.where(inside, lookup(ids, soil_table, 2), 0.0)  11.4 us
    select_n x1, other arithmetic, local(): store = jnp.where(inside, store, 0.0)  11 us
    select_n x2, other arithmetic, local(): ky = jnp.where(inside, lookup(ids, soil_table, 1), 0.0)  11 us
    all_gather x1, blocking collectives, local(): cpack = lax.all_gather(cpack, 'gy', axis=2, tiled=True)  4.37 us
    add x7, other arithmetic, chebyshev(): iterate = win(iterate, n, cur, nxt) + update  3.87 us
  transfers between devices with their start and end apart: 12, of which 7 were waited for; matrix products, arithmetic and copies ran while one was open for 2% of the time, Pallas kernels for 0%

profile of v1, /device:TPU:1, one launch (start us, length us, event | category | flops | bytes accessed | tf_op | source)
XLA Modules:
  0.0 162.3 jit_solution(11000969976232683504)
XLA Ops:
  0.0 1.0 fusion.164
  1.0 1.1 copy_bitcast_fusion
  2.1 4.0 %collective-permute-start = (f32[3,10,16,128]{3,1,2,0:T(8,128)S(1)}, f32[3,10,16,128]{3,1,2,0:T(8,128)S(1)}, u32[]{:S(2)}, u32[]{:S(2)}) collective-permute-start(f32[3,10,16,128]{3,1,2,0:T(8,128)S(1)} %get-tuple-element.62), channel_id=1, source_target_pairs={{0,4},{4,8},{8,12},{12,16},{16,20},{20,24},{24,28},{1,5},{5,9},{9,... | collective-permute-start | bytes 737288 | tf_op jit(solution)/shard_map/ppermute | solution.py:28
  6.1 1.3 collective-permute-start.1
  9.2 13.1 %collective-permute-done = f32[3,10,16,128]{3,1,2,0:T(8,128)S(1)} collective-permute-done((f32[3,10,16,128]{3,1,2,0:T(8,128)S(1)}, f32[3,10,16,128]{3,1,2,0:T(8,128)S(1)}, u32[]{:S(2)}, u32[]{:S(2)}) %collective-permute-start) | collective-permute-done | bytes 245792 | tf_op jit(solution)/shard_map/ppermute | solution.py:28
  22.5 4.6 %collective-permute-start.2 = (f32[3,36,10,128]{3,1,2,0:T(8,128)S(1)}, f32[3,36,10,128]{3,1,2,0:T(8,128)S(1)}, u32[]{:S(2)}, u32[]{:S(2)}) collective-permute-start(f32[3,36,10,128]{3,1,2,0:T(8,128)S(1)} %get-tuple-element.37), channel_id=1, source_target_pairs={{0,1},{1,2},{2,3},{4,5},{5,6},{6,7},{8,9},{9,10},{10,11},{12,13},{... | collective-permute-start | bytes 1658888 | tf_op jit(solution)/shard_map/ppermute | solution.py:28
  27.1 1.9 %collective-permute-start.3 = (f32[3,36,10,128]{3,1,2,0:T(8,128)S(1)}, f32[3,36,10,128]{3,1,2,0:T(8,128)S(1)}, u32[]{:S(2)}, u32[]{:S(2)}) collective-permute-start(f32[3,36,10,128]{3,1,2,0:T(8,128)S(1)} %get-tuple-element.38), channel_id=1, source_target_pairs={{1,0},{2,1},{3,2},{5,4},{6,5},{7,6},{9,8},{10,9},{11,10},{13,12},{... | collective-permute-start | bytes 1658888 | tf_op jit(solution)/shard_map/ppermute | solution.py:28
  29.0 0.7 fusion.463
  29.7 0.7 fusion.462
  30.5 3.6 %collective-permute-done.2 = f32[3,36,10,128]{3,1,2,0:T(8,128)S(1)} collective-permute-done((f32[3,36,10,128]{3,1,2,0:T(8,128)S(1)}, f32[3,36,10,128]{3,1,2,0:T(8,128)S(1)}, u32[]{:S(2)}, u32[]{:S(2)}) %collective-permute-start.2) | collective-permute-done | bytes 552992 | tf_op jit(solution)/shard_map/ppermute | solution.py:28
  34.1 4.4 %collective-permute-done.3 = f32[3,36,10,128]{3,1,2,0:T(8,128)S(1)} collective-permute-done((f32[3,36,10,128]{3,1,2,0:T(8,128)S(1)}, f32[3,36,10,128]{3,1,2,0:T(8,128)S(1)}, u32[]{:S(2)}, u32[]{:S(2)}) %collective-permute-start.3) | collective-permute-done | bytes 552992 | tf_op jit(solution)/shard_map/ppermute | solution.py:28
  38.7 6.1 %broadcast_select_fusion.3 = (f32[1,36,36,128]{3,1,2,0:T(8,128)S(1)}, pred[1,36,36,128]{3,1,2,0:T(8,128)(4,1)S(1)}, pred[1,36,36,128]{3,1,2,0:T(8,128)(4,1)S(1)}...) fusion(pred[36,36]{0,1:T(8,128)(4,1)S(1)} %broadcast_and_fusion, ...), kind=kLoop, calls=%fused_computation.137 | loop fusion | flops 2654208 | bytes 3816752 | tf_op jit(solution)/shard_map/jit(_where)/select_n | solution.py:172
  44.8 5.5 %broadcast_select_fusion.2 = f32[1,36,36,128]{3,1,2,0:T(8,128)S(1)} fusion(pred[36,36]{0,1:T(8,128)(4,1)S(1)} %broadcast_and_fusion, pred[1,36,36,128]{3,1,2,0:T(8,128)(4,1)S(1)} %get-tuple-element.33, pred[1,36,36,128]{3,1,2,0:T(8,128)(4,1)S(1)} %get-tuple-element.32, pred[1,36,36,128]{3,1,2,0:T(8,128)(4,1)S(1)} %get-tuple-element.31, ...), kind=kLoop, calls=%fused_computation.136 | loop fusion | flops 1327104 | bytes 1826096 | tf_op jit(solution)/shard_map/jit(_where)/select_n | solution.py:173
  50.3 5.5 %bitcast_select_fusion.2 = f32[36,36,128]{2,0,1:T(8,128)S(1)} fusion(pred[36,36]{0,1:T(8,128)(4,1)S(1)} %broadcast_and_fusion, pred[1,36,36,128]{3,1,2,0:T(8,128)(4,1)S(1)} %get-tuple-element.33, pred[1,36,36,128]{3,1,2,0:T(8,128)(4,1)S(1)} %get-tuple-element.32, pred[1,36,36,128]{3,1,2,0:T(8,128)(4,1)S(1)} %get-tuple-element.31, ...), kind=kLoop, calls=%fused_computation.31 | loop fusion | flops 1327104 | bytes 1826096 | tf_op jit(solution)/shard_map/jit(_where)/select_n | solution.py:173
  55.8 5.7 %broadcast_select_fusion.1 = f32[1,36,36,128]{3,1,2,0:T(8,128)S(1)} fusion(pred[36,36]{0,1:T(8,128)(4,1)S(1)} %broadcast_and_fusion, pred[1,36,36,128]{3,1,2,0:T(8,128)(4,1)S(1)} %get-tuple-element.33, pred[1,36,36,128]{3,1,2,0:T(8,128)(4,1)S(1)} %get-tuple-element.32, pred[1,36,36,128]{3,1,2,0:T(8,128)(4,1)S(1)} %get-tuple-element.31, ...), kind=kLoop, calls=%fused_computation.135 | loop fusion | flops 1327104 | bytes 1826096 | tf_op jit(solution)/shard_map/jit(_where)/select_n | solution.py:174
  61.5 5.7 %bitcast_select_fusion.1 = f32[36,36,128]{2,0,1:T(8,128)S(1)} fusion(pred[36,36]{0,1:T(8,128)(4,1)S(1)} %broadcast_and_fusion, pred[1,36,36,128]{3,1,2,0:T(8,128)(4,1)S(1)} %get-tuple-element.33, pred[1,36,36,128]{3,1,2,0:T(8,128)(4,1)S(1)} %get-tuple-element.32, pred[1,36,36,128]{3,1,2,0:T(8,128)(4,1)S(1)} %get-tuple-element.31, ...), kind=kLoop, calls=%fused_computation.30 | loop fusion | flops 1327104 | bytes 1826096 | tf_op jit(solution)/shard_map/jit(_where)/select_n | solution.py:174
  67.3 0.7 copy.30
  68.0 11.0 %broadcast_select_fusion = (f32[1,36,36,128]{3,1,2,0:T(8,128)S(1)}, f32[1,36,36,128]{3,1,2,0:T(8,128)S(1)}) fusion(pred[36,36]{0,1:T(8,128)(4,1)S(1)} %broadcast_and_fusion, f32[3,36,36,128]{3,1,2,0:T(8,128)S(1)} %pad_maximum_fusion.1, pred[1,36,36,128]{3,1,2,0:T(8,128)(4,1)S(1)} %get-tuple-element.33, pred[1,36,36,128]{3,1,2,0:T(8,128)(4,1)S(1)} %get-tuple-element.32, ...), kind=kLoop, calls=%fused_computation.134 | loop fusion | flops 3317760 | bytes 3153232 | tf_op jit(solution)/shard_map/jit(_where)/select_n | solution.py:178
  79.0 0.7 copy.33
  80.4 0.7 copy.32
  81.1 2.7 %pad_maximum_fusion = f32[4,18,2,36,128]{4,0,3,2,1:T(4,128)S(1)} fusion(f32[1,18,2,36,128]{4,0,3,2,1:T(1,128)S(1)} %bitcast.252, f32[1,18,2,36,128]{4,0,3,2,1:T(1,128)S(1)} %bitcast.254, f32[1,18,2,36,128]{4,0,3,2,1:T(1,128)S(1)} %bitcast.253, f32[1,18,2,36,128]{4,0,3,2,1:T(1,128)S(1)} %bitcast.251), kind=kLoop, calls=%fused_computation | loop fusion | flops 1990656 | bytes 5308416 | tf_op jit(solution)/shard_map/stack | solution.py:179
  84.2 0.8 fusion
  85.7 0.7 multiply_bitcast_fusion
  86.4 0.7 slice_bitcast_fusion.4
  87.3 5.6 %bitcast_select_fusion.3 = (f32[36,36,128]{2,0,1:T(8,128)S(1)}, f32[36,36,128]{2,0,1:T(8,128)S(1)}) fusion(pred[36,36]{0,1:T(8,128)(4,1)S(1)} %broadcast_and_fusion, pred[1,36,36,128]{3,1,2,0:T(8,128)(4,1)S(1)} %get-tuple-element.33, pred[1,36,36,128]{3,1,2,0:T(8,128)(4,1)S(1)} %get-tuple-element.32, pred[1,36,36,128]{3,1,2,0:T(8,128)(4,1)S(1)} %get-tuple-element.31, ...), kind=kLoop, calls=%fused_computation.32 | loop fusion | flops 1492992 | bytes 3153200 | tf_op jit(solution)/shard_map/jit(_where)/select_n | solution.py:172
  93.4 0.8 fusion.15
  94.6 1.2 slice_add_fusion.5
  96.2 1.1 fusion.33
  97.8 0.8 divide_multiply_fusion
  98.6 0.8 divide_multiply_fusion.1
  99.4 1.7 %fusion.58 = f32[28,28,128]{2,0,1:T(8,128)} fusion(f32[36,36,127]{2,0,1:T(8,128)S(1)} %maximum_divide_fusion, f32[30,30,128]{2,0,1:T(8,128)S(1)} %fusion.33, f32[36,35,128]{2,0,1:T(8,128)S(1)} %maximum_divide_fusion.2, f32[35,36,128]{2,0,1:T(8,128)S(1)} %maximum_divide_fusion.1, f32[36,36,128]{2,0,1:T(8,128)S(1)} %get-tuple-element.151, ...), kind=kLoop, calls=%fused_computation.116 | loop fusion | flops 2207744 | bytes 6278080 | tf_op jit(solution)/shard_map/sub | solution.py:183
  101.1 2.0 %reshape.377 = f32[14,2,28,128]{3,1,0,2:T(2,128)} reshape(f32[28,28,128]{2,0,1:T(8,128)} %fusion.58) | data formatting | bytes 802816 | tf_op jit(solution)/shard_map/reshape | solution.py:61
  103.1 1.5 fusion.426
  104.6 0.9 fusion.87
  105.5 1.5 add_maximum_fusion.1
  109.1 4.4 %all_gather.3 = f32[5,4,16,32]{3,1,0,2:T(4,128)S(1)} all-gather(f32[5,4,4,32]{3,1,0,2:T(4,128)S(1)} %copy.39), channel_id=1, replica_groups=mesh['gx'=8,'gy'=4] {'gy'}, dimensions={2}, use_global_device_ids=true | all-gather | bytes 51200 | tf_op jit(solution)/shard_map/all_gather | solution.py:200
  113.4 5.1 %collective-permute-start.4 = (f32[5,4,16,32]{3,2,1,0:T(8,128)S(1)}, f32[5,4,16,32]{3,2,1,0:T(8,128)S(1)}, u32[]{:S(2)}, u32[]{:S(2)}) collective-permute-start(f32[5,4,16,32]{3,2,1,0:T(8,128)S(1)} %copy.40), channel_id=1, source_target_pairs={{0,8},{4,12},{8,16},{12,20},{16,24},{20,28},{1,9},{5,13},{9,17},{1... | collective-permute-start | bytes 122888 | tf_op jit(solution)/shard_map/ppermute | solution.py:28
  118.5 1.3 collective-permute-start.7
  119.8 1.3 collective-permute-start.6
  121.1 4.2 %collective-permute-start.5 = (f32[5,4,16,32]{3,2,1,0:T(8,128)S(1)}, f32[5,4,16,32]{3,2,1,0:T(8,128)S(1)}, u32[]{:S(2)}, u32[]{:S(2)}) collective-permute-start(f32[5,4,16,32]{3,2,1,0:T(8,128)S(1)} %copy.40), channel_id=1, source_target_pairs={{0,4},{4,8},{8,12},{12,16},{16,20},{20,24},{24,28},{1,5},{5,9},{9,... | collective-permute-start | bytes 122888 | tf_op jit(solution)/shard_map/ppermute | solution.py:28
  125.4 6.0 %collective-permute-done.5 = f32[5,4,16,32]{3,2,1,0:T(8,128)S(1)} collective-permute-done((f32[5,4,16,32]{3,2,1,0:T(8,128)S(1)}, f32[5,4,16,32]{3,2,1,0:T(8,128)S(1)}, u32[]{:S(2)}, u32[]{:S(2)}) %collective-permute-start.5) | collective-permute-done | bytes 40992 | tf_op jit(solution)/shard_map/ppermute | solution.py:28
  135.8 4.1 %collective-permute-start.8 = (f32[2,5,8,64]{3,2,1,0:T(8,128)S(1)}, f32[2,5,8,64]{3,2,1,0:T(8,128)S(1)}, u32[]{:S(2)}, u32[]{:S(2)}) collective-permute-start(f32[2,5,8,64]{3,2,1,0:T(8,128)S(1)} %get-tuple-element.135), channel_id=1, source_target_pairs={{0,4},{4,8},{8,12},{12,16},{16,20},{20,24},{24,28},{1,5},{5,9},{9,... | collective-permute-start | bytes 61448 | tf_op jit(solution)/shard_map/ppermute | solution.py:28
  140.0 1.3 collective-permute-start.9
  141.3 3.4 %collective-permute-done.9 = f32[2,5,8,64]{3,2,1,0:T(8,128)S(1)} collective-permute-done((f32[2,5,8,64]{3,2,1,0:T(8,128)S(1)}, f32[2,5,8,64]{3,2,1,0:T(8,128)S(1)}, u32[]{:S(2)}, u32[]{:S(2)}) %collective-permute-start.9) | collective-permute-done | bytes 20512 | tf_op jit(solution)/shard_map/ppermute | solution.py:28
  144.7 5.6 %collective-permute-start.10 = (f32[2,18,5,64]{3,2,1,0:T(8,128)S(1)}, f32[2,18,5,64]{3,2,1,0:T(8,128)S(1)}, u32[]{:S(2)}, u32[]{:S(2)}) collective-permute-start(f32[2,18,5,64]{3,2,1,0:T(8,128)S(1)} %get-tuple-element.91), channel_id=1, source_target_pairs={{0,1},{1,2},{2,3},{4,5},{5,6},{6,7},{8,9},{9,10},{10,11},{12,13},{... | collective-permute-start | bytes 138248 | tf_op jit(solution)/shard_map/ppermute | solution.py:28
  150.4 1.9 %collective-permute-start.11 = (f32[2,18,5,64]{3,2,1,0:T(8,128)S(1)}, f32[2,18,5,64]{3,2,1,0:T(8,128)S(1)}, u32[]{:S(2)}, u32[]{:S(2)}) collective-permute-start(f32[2,18,5,64]{3,2,1,0:T(8,128)S(1)} %get-tuple-element.92), channel_id=1, source_target_pairs={{1,0},{2,1},{3,2},{5,4},{6,5},{7,6},{9,8},{10,9},{11,10},{13,12},{... | collective-permute-start | bytes 138248 | tf_op jit(solution)/shard_map/ppermute | solution.py:28
  152.4 4.4 %collective-permute-done.11 = f32[2,18,5,64]{3,2,1,0:T(8,128)S(1)} collective-permute-done((f32[2,18,5,64]{3,2,1,0:T(8,128)S(1)}, f32[2,18,5,64]{3,2,1,0:T(8,128)S(1)}, u32[]{:S(2)}, u32[]{:S(2)}) %collective-permute-start.11) | collective-permute-done | bytes 46112 | tf_op jit(solution)/shard_map/ppermute | solution.py:28
  161.7 0.7 copy.48
  (152 shorter events, 16.9 us)
Async XLA Ops:
  0.0 8.6 %copy-start.8 = (f32[5,8]{1,0:T(8,128)S(1)}, f32[5,8]{1,0:T(8,128)}, u32[]{:S(2)}) copy-start(f32[5,8]{1,0:T(8,128)} %param.7) | copy-start | bytes 484
  2.1 20.2 %collective-permute-start = (f32[3,10,16,128]{3,1,2,0:T(8,128)S(1)}, f32[3,10,16,128]{3,1,2,0:T(8,128)S(1)}, u32[]{:S(2)}, u32[]{:S(2)}) collective-permute-start(f32[3,10,16,128]{3,1,2,0:T(8,128)S(1)} %get-tuple-element.62), channel_id=1, source_target_pairs={{0,4},{4,8},{8,12},{12,16},{16,20},{20,24},{24,28},{1,5},{5,9},{9,... | collective-permute-start | bytes 737288 | tf_op jit(solution)/shard_map/ppermute | solution.py:28
  6.1 16.2 %collective-permute-start.1 = (f32[3,10,16,128]{3,1,2,0:T(8,128)S(1)}, f32[3,10,16,128]{3,1,2,0:T(8,128)S(1)}, u32[]{:S(2)}, u32[]{:S(2)}) collective-permute-start(f32[3,10,16,128]{3,1,2,0:T(8,128)S(1)} %get-tuple-element.63), channel_id=1, source_target_pairs={{4,0},{8,4},{12,8},{16,12},{20,16},{24,20},{28,24},{5,1},{9,5},{13... | collective-permute-start | bytes 737288 | tf_op jit(solution)/shard_map/ppermute | solution.py:28
  7.4 76.7 %copy-start.9 = (s32[128]{0:T(128)}, s32[128]{0:T(128)S(1)}, u32[]{:S(2)}) copy-start(s32[128]{0:T(128)S(1)} %and_select_fusion.3) | copy-start | bytes 1540
  22.5 11.6 %collective-permute-start.2 = (f32[3,36,10,128]{3,1,2,0:T(8,128)S(1)}, f32[3,36,10,128]{3,1,2,0:T(8,128)S(1)}, u32[]{:S(2)}, u32[]{:S(2)}) collective-permute-start(f32[3,36,10,128]{3,1,2,0:T(8,128)S(1)} %get-tuple-element.37), channel_id=1, source_target_pairs={{0,1},{1,2},{2,3},{4,5},{5,6},{6,7},{8,9},{9,10},{10,11},{12,13},{... | collective-permute-start | bytes 1658888 | tf_op jit(solution)/shard_map/ppermute | solution.py:28
  27.1 11.5 %collective-permute-start.3 = (f32[3,36,10,128]{3,1,2,0:T(8,128)S(1)}, f32[3,36,10,128]{3,1,2,0:T(8,128)S(1)}, u32[]{:S(2)}, u32[]{:S(2)}) collective-permute-start(f32[3,36,10,128]{3,1,2,0:T(8,128)S(1)} %get-tuple-element.38), channel_id=1, source_target_pairs={{1,0},{2,1},{3,2},{5,4},{6,5},{7,6},{9,8},{10,9},{11,10},{13,12},{... | collective-permute-start | bytes 1658888 | tf_op jit(solution)/shard_map/ppermute | solution.py:28
  92.9 6.5 %copy-start = (f32[36,36,128]{2,0,1:T(8,128)}, f32[36,36,128]{2,0,1:T(8,128)S(1)}, u32[]{:S(2)}) copy-start(f32[36,36,128]{2,0,1:T(8,128)S(1)} %get-tuple-element.151) | copy-start | bytes 1990660
  94.1 2.1 %copy-start.5 = (f32[34,34,128]{2,0,1:T(8,128)}, f32[34,34,128]{2,0,1:T(8,128)S(1)}, u32[]{:S(2)}) copy-start(f32[34,34,128]{2,0,1:T(8,128)S(1)} %get-tuple-element.25) | copy-start | bytes 1775620
  103.1 4.0 %copy-start.12 = (s32[28]{0:T(128)S(1)}, s32[28]{0:T(128)}, u32[]{:S(2)}) copy-start(s32[28]{0:T(128)} %and_select_fusion.4) | copy-start | bytes 340
  103.1 4.4 %copy-start.2 = (f32[18,18,63]{2,1,0:T(8,128)S(1)}, f32[18,18,63]{2,1,0:T(8,128)}, u32[]{:S(2)}) copy-start(f32[18,18,63]{2,1,0:T(8,128)} %divide_multiply_fusion) | copy-start | bytes 244948
  103.1 4.4 %copy-start.3 = (f32[17,18,64]{2,1,0:T(8,128)S(1)}, f32[17,18,64]{2,1,0:T(8,128)}, u32[]{:S(2)}) copy-start(f32[17,18,64]{2,1,0:T(8,128)} %multiply_bitcast_fusion) | copy-start | bytes 235012
  103.1 4.4 %copy-start.4 = (f32[18,17,64]{2,1,0:T(8,128)S(1)}, f32[18,17,64]{2,1,0:T(8,128)}, u32[]{:S(2)}) copy-start(f32[18,17,64]{2,1,0:T(8,128)} %divide_multiply_fusion.1) | copy-start | bytes 235012
  103.1 4.4 %copy-start.7 = (f32[18,18,64]{2,1,0:T(8,128)S(1)}, f32[18,18,64]{2,1,0:T(8,128)}, u32[]{:S(2)}) copy-start(f32[18,18,64]{2,1,0:T(8,128)} %get-tuple-element.40) | copy-start | bytes 248836
  107.5 0.8 copy-start.11
  113.4 11.9 %collective-permute-start.4 = (f32[5,4,16,32]{3,2,1,0:T(8,128)S(1)}, f32[5,4,16,32]{3,2,1,0:T(8,128)S(1)}, u32[]{:S(2)}, u32[]{:S(2)}) collective-permute-start(f32[5,4,16,32]{3,2,1,0:T(8,128)S(1)} %copy.40), channel_id=1, source_target_pairs={{0,8},{4,12},{8,16},{12,20},{16,24},{20,28},{1,9},{5,13},{9,17},{1... | collective-permute-start | bytes 122888 | tf_op jit(solution)/shard_map/ppermute | solution.py:28
  118.5 13.0 %collective-permute-start.7 = (f32[5,4,16,32]{3,2,1,0:T(8,128)S(1)}, f32[5,4,16,32]{3,2,1,0:T(8,128)S(1)}, u32[]{:S(2)}, u32[]{:S(2)}) collective-permute-start(f32[5,4,16,32]{3,2,1,0:T(8,128)S(1)} %copy.40), channel_id=1, source_target_pairs={{8,0},{12,4},{16,8},{20,12},{24,16},{28,20},{9,1},{13,5},{17,9},{2... | collective-permute-start | bytes 122888 | tf_op jit(solution)/shard_map/ppermute | solution.py:28
  119.8 11.6 %collective-permute-start.6 = (f32[5,4,16,32]{3,2,1,0:T(8,128)S(1)}, f32[5,4,16,32]{3,2,1,0:T(8,128)S(1)}, u32[]{:S(2)}, u32[]{:S(2)}) collective-permute-start(f32[5,4,16,32]{3,2,1,0:T(8,128)S(1)} %copy.40), channel_id=1, source_target_pairs={{4,0},{8,4},{12,8},{16,12},{20,16},{24,20},{28,24},{5,1},{9,5},{13... | collective-permute-start | bytes 122888 | tf_op jit(solution)/shard_map/ppermute | solution.py:28
  121.1 10.3 %collective-permute-start.5 = (f32[5,4,16,32]{3,2,1,0:T(8,128)S(1)}, f32[5,4,16,32]{3,2,1,0:T(8,128)S(1)}, u32[]{:S(2)}, u32[]{:S(2)}) collective-permute-start(f32[5,4,16,32]{3,2,1,0:T(8,128)S(1)} %copy.40), channel_id=1, source_target_pairs={{0,4},{4,8},{8,12},{12,16},{16,20},{20,24},{24,28},{1,5},{5,9},{9,... | collective-permute-start | bytes 122888 | tf_op jit(solution)/shard_map/ppermute | solution.py:28
  135.8 5.4 %collective-permute-start.8 = (f32[2,5,8,64]{3,2,1,0:T(8,128)S(1)}, f32[2,5,8,64]{3,2,1,0:T(8,128)S(1)}, u32[]{:S(2)}, u32[]{:S(2)}) collective-permute-start(f32[2,5,8,64]{3,2,1,0:T(8,128)S(1)} %get-tuple-element.135), channel_id=1, source_target_pairs={{0,4},{4,8},{8,12},{12,16},{16,20},{20,24},{24,28},{1,5},{5,9},{9,... | collective-permute-start | bytes 61448 | tf_op jit(solution)/shard_map/ppermute | solution.py:28
  140.0 4.7 %collective-permute-start.9 = (f32[2,5,8,64]{3,2,1,0:T(8,128)S(1)}, f32[2,5,8,64]{3,2,1,0:T(8,128)S(1)}, u32[]{:S(2)}, u32[]{:S(2)}) collective-permute-start(f32[2,5,8,64]{3,2,1,0:T(8,128)S(1)} %get-tuple-element.136), channel_id=1, source_target_pairs={{4,0},{8,4},{12,8},{16,12},{20,16},{24,20},{28,24},{5,1},{9,5},{13... | collective-permute-start | bytes 61448 | tf_op jit(solution)/shard_map/ppermute | solution.py:28
  144.7 7.7 %collective-permute-start.10 = (f32[2,18,5,64]{3,2,1,0:T(8,128)S(1)}, f32[2,18,5,64]{3,2,1,0:T(8,128)S(1)}, u32[]{:S(2)}, u32[]{:S(2)}) collective-permute-start(f32[2,18,5,64]{3,2,1,0:T(8,128)S(1)} %get-tuple-element.91), channel_id=1, source_target_pairs={{0,1},{1,2},{2,3},{4,5},{5,6},{6,7},{8,9},{9,10},{10,11},{12,13},{... | collective-permute-start | bytes 138248 | tf_op jit(solution)/shard_map/ppermute | solution.py:28
  150.4 6.5 %collective-permute-start.11 = (f32[2,18,5,64]{3,2,1,0:T(8,128)S(1)}, f32[2,18,5,64]{3,2,1,0:T(8,128)S(1)}, u32[]{:S(2)}, u32[]{:S(2)}) collective-permute-start(f32[2,18,5,64]{3,2,1,0:T(8,128)S(1)} %get-tuple-element.92), channel_id=1, source_target_pairs={{1,0},{2,1},{3,2},{5,4},{6,5},{7,6},{9,8},{10,9},{11,10},{13,12},{... | collective-permute-start | bytes 138248 | tf_op jit(solution)/shard_map/ppermute | solution.py:28
  157.5 0.7 copy-start.10
  158.6 1.1 copy-start.1
  158.6 1.3 copy-start.6

commit v2 on v1

--- a/solution.py
+++ b/solution.py
@@ -2,6 +2,8 @@
 import jax.numpy as jnp
 from jax import lax
 from jax.sharding import PartitionSpec as P
+from jax.experimental import pallas as pl
+from jax.experimental.pallas import tpu as pltpu
 
 CHEB = 3
 COARSE_SWEEPS = 8
@@ -60,15 +62,15 @@
     sx, sy, sz = values.shape[-3:]
     v = values.reshape(lead + (sx // 2, 2, sy, sz))
     v = v[..., 0, :, :] + v[..., 1, :, :]
+    v = v[..., 0::2, :] + v[..., 1::2, :]
     v = jnp.einsum("...yz,zw->...yw", v, pair_matrix(sz), precision=HIGH)
-    v = jnp.einsum("...yw,yv->...vw", v, pair_matrix(sy), precision=HIGH)
     return v * 0.125
 
 
 def prolong(values):
     sx, sy, sz = values.shape
     v = jnp.einsum("xyz,wz->xyw", values, pair_matrix(2 * sz), precision=HIGH)
-    v = jnp.einsum("xyw,vy->xvw", v, pair_matrix(2 * sy), precision=HIGH)
+    v = jnp.repeat(v, 2, axis=1)
     v = jnp.broadcast_to(v[:, None], (sx, 2) + v.shape[1:]).reshape((2 * sx,) + v.shape[1:])
     return v
 
@@ -144,11 +146,50 @@
     return iterate, cur
 
 
-def lookup(soil_id, soil_table, record):
-    looked = jnp.full(soil_id.shape, soil_table[record, soil_table.shape[1] - 1])
-    for material in range(soil_table.shape[1] - 2, -1, -1):
-        looked = jnp.where(soil_id == material, soil_table[record, material], looked)
-    return looked
+def fields_kernel(bounds_ref, table_ref, conc_ref, idf_ref, out_ref):
+    rows = conc_ref.shape[0]
+    shape = conc_ref.shape[1:]
+    mats = table_ref.shape[1]
+    col = lax.broadcasted_iota(jnp.int32, shape, 0)
+    col_ok = (col >= bounds_ref[2]) & (col < bounds_ref[3])
+
+    def body(i, carry):
+        ids = idf_ref[i]
+        conc = conc_ref[i]
+        row = jnp.zeros(shape, jnp.int32) + i
+        ok = col_ok & (row >= bounds_ref[0]) & (row < bounds_ref[1])
+        vals = []
+        for record in range(5):
+            acc = jnp.zeros(shape, jnp.float32) + table_ref[record, mats - 1]
+            for material in range(mats - 2, -1, -1):
+                acc = jnp.where(ids == float(material), table_ref[record, material], acc)
+            vals.append(acc)
+        store = storage_scale * (1.0 + vals[3] * jnp.exp((vals[4] - 1.0) * jnp.log(conc)))
+        out_ref[0, i] = jnp.where(ok, vals[0], 0.0)
+        out_ref[1, i] = jnp.where(ok, vals[1], 0.0)
+        out_ref[2, i] = jnp.where(ok, vals[2], 0.0)
+        out_ref[3, i] = jnp.where(ok, store, 0.0)
+        return carry
+
+    lax.fori_loop(0, rows, body, 0)
+
+
+def soil_fields(bounds, soil_table, conc, idf):
+    cells = conc.size
+    return pl.pallas_call(
+        fields_kernel,
+        out_shape=jax.ShapeDtypeStruct((4,) + conc.shape, jnp.float32),
+        in_specs=[
+            pl.BlockSpec(memory_space=pltpu.SMEM),
+            pl.BlockSpec(memory_space=pltpu.SMEM),
+            pl.BlockSpec(memory_space=pltpu.VMEM),
+            pl.BlockSpec(memory_space=pltpu.VMEM),
+        ],
+        out_specs=pl.BlockSpec(memory_space=pltpu.VMEM),
+        cost_estimate=pl.CostEstimate(
+            flops=100 * cells, transcendentals=2 * cells, bytes_accessed=24 * cells
+        ),
+    )(bounds, soil_table, conc, idf)
 
 
 def local(conc_prev, right_side, soil_id, soil_table):
@@ -163,20 +204,10 @@
     stacked = jnp.stack([conc_prev, right_side, soil_id.astype(jnp.float32)])
     ext = halo(stacked, (("gx", 1), ("gy", 2)), hf)
     conc, rhs, idf = ext[0], ext[1], ext[2]
-    ids = idf.astype(jnp.int32)
-    gxi = ix * n - hf + jnp.arange(n + 2 * hf)
-    gyi = iy * ny - hf + jnp.arange(ny + 2 * hf)
-    inside = ((gxi >= 0) & (gxi < gx_count * n))[:, None, None] & (
-        (gyi >= 0) & (gyi < gy_count * ny)
-    )[None, :, None]
-    kx = jnp.where(inside, lookup(ids, soil_table, 0), 0.0)
-    ky = jnp.where(inside, lookup(ids, soil_table, 1), 0.0)
-    kz = jnp.where(inside, lookup(ids, soil_table, 2), 0.0)
-    s3 = lookup(ids, soil_table, 3)
-    s4 = lookup(ids, soil_table, 4)
-    store = storage_scale * (1.0 + s3 * jnp.exp((s4 - 1.0) * jnp.log(conc)))
-    store = jnp.where(inside, store, 0.0)
-    fine_c = jnp.stack([kx, ky, kz, store])
+    x_lo = hf - ix * n
+    y_lo = hf - iy * ny
+    bounds = jnp.stack([x_lo, x_lo + gx_count * n, y_lo, y_lo + gy_count * ny]).astype(jnp.int32)
+    fine_c = soil_fields(bounds, soil_table, conc, idf)
     fine = build_level(fine_c, n, hf, 1.0)
 
     x0, x0m = chebyshev(rhs, hf, None, 0, fine)

time: 163 us -> 136 us (0.83)
  other arithmetic: 64.4 us -> 24.3 us
  local copies, waits for them, and re-layouts: 16.8 us -> 26.2 us
  waiting for transfers between devices: 35 us -> 28 us
  Pallas kernels: 0 us -> 5.47 us
  blocking collectives: 4.37 us -> 6.43 us
  starting transfers between devices: 36.6 us -> 38.3 us
    select_n x7 -> x0, other arithmetic: 45.1 us -> none  [the longest x2 11.7 us: local(): kx = jnp.where(inside, lookup(ids, soil_table, 0), 0.0)]
    slice x4 -> x9, local copies, waits for them, and re-layouts: 3.66 us -> 14.1 us  [the longest x8 13.9 us: coarsen(): v = v[..., 0::2, :] + v[..., 1::2, :]]
    ppermute x12, waiting for transfers between devices: 35 us -> 28 us  [shift_from(): return lax.ppermute(cells, axis, pairs)]
    pallas_call x0 -> x1, Pallas kernels: none -> 5.47 us  [soil_fields(): pl.pallas_call(fields_kernel, out_shape=jax.ShapeDtypeStruct((4,) + conc....]
    add x1 -> x4, other arithmetic: 0.34 us -> 3.35 us  [coarsen(): v = v[..., 0, :, :] + v[..., 1, :, :]]
    select_n x4 -> x0, local copies, waits for them, and re-layouts: 2.73 us -> none  [the longest x1 0.68 us: local(): kz = jnp.where(inside, lookup(ids, soil_table, 2), 0.0)]
    dot_general x4, matrix products: 2.01 us -> 4.64 us  [coarsen(): v = jnp.einsum('...yz,zw->...yw', v, pair_matrix(sz), precision=HIGH)]
    another operation x1, other arithmetic: 2.74 us -> 0.6 us  [local(): jnp.stack([x_lo, x_lo + gx_count * n, y_lo, y_lo + gy_count * ny])]
  transfers between devices with their start and end apart: 12 -> 12, of which waited for: 7 -> 8; matrix products, arithmetic and copies ran while one was open for 2% -> 1% of each run, Pallas kernels for 0% -> 0%
where the time goes in v2:
time: 136 us; the launch traced here: 135 us
  starting transfers between devices  38.3 us (28%)
  waiting for transfers between devices  28 us (21%)
  local copies, waits for them, and re-layouts  26.2 us (19%)
  other arithmetic  24.3 us (18%)
  blocking collectives  6.43 us (5%)
  Pallas kernels  5.47 us (4%)
  matrix products  5.22 us (4%)
    ppermute x12, starting transfers between devices, shift_from(): return lax.ppermute(cells, axis, pairs)  38.3 us
    ppermute x12, waiting for transfers between devices, shift_from(): return lax.ppermute(cells, axis, pairs)  28 us
    slice x8, local copies, waits for them, and re-layouts, coarsen(): v = v[..., 0::2, :] + v[..., 1::2, :]  13.9 us
    all_gather x1, blocking collectives, local(): cpack = lax.all_gather(cpack, 'gy', axis=2, tiled=True)  6.43 us
    pallas_call x1, Pallas kernels, soil_fields(): pl.pallas_call(fields_kernel, out_shape=jax.ShapeDtypeStruct((4,) + conc....  5.47 us
    dot_general x4, matrix products, coarsen(): v = jnp.einsum('...yz,zw->...yw', v, pair_matrix(sz), precision=HIGH)  4.64 us
    add x7, other arithmetic, chebyshev(): iterate = win(iterate, n, cur, nxt) + update  4.6 us
    add x4, other arithmetic, coarsen(): v = v[..., 0, :, :] + v[..., 1, :, :]  3.35 us
  transfers between devices with their start and end apart: 12, of which 8 were waited for; matrix products, arithmetic and copies ran while one was open for 1% of the time, Pallas kernels for 0%

profile of v2, /device:TPU:1, one launch (start us, length us, event | category | flops | bytes accessed | tf_op | source)
XLA Modules:
  0.0 135.0 jit_solution(16410792709510935093)
XLA Ops:
  0.0 0.9 convert_bitcast_fusion
  0.9 1.0 pad_maximum_fusion.3
  2.0 4.0 %collective-permute-start = (f32[3,10,16,128]{3,2,1,0:T(8,128)S(1)}, f32[3,10,16,128]{3,2,1,0:T(8,128)S(1)}, u32[]{:S(2)}, u32[]{:S(2)}) collective-permute-start(f32[3,10,16,128]{3,2,1,0:T(8,128)S(1)} %get-tuple-element.55), channel_id=1, source_target_pairs={{0,4},{4,8},{8,12},{12,16},{16,20},{20,24},{24,28},{1,5},{5,9},{9,... | collective-permute-start | bytes 737288 | tf_op jit(solution)/shard_map/ppermute | solution.py:30
  6.0 1.3 collective-permute-start.1
  7.3 3.3 %collective-permute-done = f32[3,10,16,128]{3,2,1,0:T(8,128)S(1)} collective-permute-done((f32[3,10,16,128]{3,2,1,0:T(8,128)S(1)}, f32[3,10,16,128]{3,2,1,0:T(8,128)S(1)}, u32[]{:S(2)}, u32[]{:S(2)}) %collective-permute-start) | collective-permute-done | bytes 245792 | tf_op jit(solution)/shard_map/ppermute | solution.py:30
  10.6 3.8 %collective-permute-done.1 = f32[3,10,16,128]{3,2,1,0:T(8,128)S(1)} collective-permute-done((f32[3,10,16,128]{3,2,1,0:T(8,128)S(1)}, f32[3,10,16,128]{3,2,1,0:T(8,128)S(1)}, u32[]{:S(2)}, u32[]{:S(2)}) %collective-permute-start.1) | collective-permute-done | bytes 245792 | tf_op jit(solution)/shard_map/ppermute | solution.py:30
  14.4 1.1 pad_maximum_fusion.1
  15.9 5.0 %collective-permute-start.3 = (f32[3,36,10,128]{3,1,2,0:T(8,128)S(1)}, f32[3,36,10,128]{3,1,2,0:T(8,128)S(1)}, u32[]{:S(2)}, u32[]{:S(2)}) collective-permute-start(f32[3,36,10,128]{3,1,2,0:T(8,128)S(1)} %copy.40), channel_id=1, source_target_pairs={{1,0},{2,1},{3,2},{5,4},{6,5},{7,6},{9,8},{10,9},{11,10},{13,12},{... | collective-permute-start | bytes 1658888 | tf_op jit(solution)/shard_map/ppermute | solution.py:30
  20.9 1.0 copy.39
  21.9 3.1 %collective-permute-start.2 = (f32[3,36,10,128]{3,1,2,0:T(8,128)}, f32[3,36,10,128]{3,1,2,0:T(8,128)}, u32[]{:S(2)}, u32[]{:S(2)}) collective-permute-start(f32[3,36,10,128]{3,1,2,0:T(8,128)} %copy.39), channel_id=1, source_target_pairs={{0,1},{1,2},{2,3},{4,5},{5,6},{6,7},{8,9},{9,10},{10,11},{12,13},{... | collective-permute-start | bytes 1658888 | tf_op jit(solution)/shard_map/ppermute | solution.py:30
  25.7 4.1 %collective-permute-done.3 = f32[3,36,10,128]{3,1,2,0:T(8,128)S(1)} collective-permute-done((f32[3,36,10,128]{3,1,2,0:T(8,128)S(1)}, f32[3,36,10,128]{3,1,2,0:T(8,128)S(1)}, u32[]{:S(2)}, u32[]{:S(2)}) %collective-permute-start.3) | collective-permute-done | bytes 552992 | tf_op jit(solution)/shard_map/ppermute | solution.py:30
  29.9 2.5 %collective-permute-done.2 = f32[3,36,10,128]{3,1,2,0:T(8,128)} collective-permute-done((f32[3,36,10,128]{3,1,2,0:T(8,128)}, f32[3,36,10,128]{3,1,2,0:T(8,128)}, u32[]{:S(2)}, u32[]{:S(2)}) %collective-permute-start.2) | collective-permute-done | bytes 552992 | tf_op jit(solution)/shard_map/ppermute | solution.py:30
  32.5 1.2 copy.41
  34.0 1.3 slice_bitcast_fusion.5
  35.3 5.5 %shard_map.46 = f32[4,36,36,128]{3,2,1,0:T(8,128)} custom-call(s32[4]{0:T(128)} %pad_add_fusion.bounds_ref, f32[5,8]{1,0:T(8,128)} %table_ref.1, f32[36,36,128]{2,1,0:T(8,128)} %get-tuple-element.30.conc_ref, f32[36,36,128]{2,1,0:T(8,128)} %get-tuple-element.29.idf_ref), custom_call_target="tpu_custom_call" | custom-call | flops 16588800 | bytes 3981312 | tf_op jit(solution)/shard_map/pallas_call | solution.py:179
  40.8 1.5 %divide_bitcast_fusion = f32[35,36,128]{2,1,0:T(8,128)S(1)} fusion(f32[4,36,36,128]{3,2,1,0:T(8,128)} %shard_map.46), kind=kLoop, calls=%fused_computation.24 | loop fusion | flops 806400 | bytes 1935360 | tf_op jit(solution)/shard_map/div | solution.py:45
  42.3 2.0 %fusion.1 = f32[4,18,36,128]{3,2,1,0:T(8,128)S(1)} fusion(f32[4,18,2,36,128]{4,3,2,1,0:T(8,128)} %bitcast.191), kind=kLoop, calls=%fused_computation.3 | loop fusion | flops 331776 | bytes 3981312 | tf_op jit(solution)/shard_map/add | solution.py:64
  44.3 2.8 %slice.1560 = f32[4,18,18,128]{3,2,1,0:T(8,128)} slice(f32[4,18,36,128]{3,2,1,0:T(8,128)S(1)} %fusion.1), slice={[0:4:1], [0:18:1], [1:36:2], [0:128:1]} | slice | bytes 1327104 | tf_op jit(solution)/shard_map/slice | solution.py:65
  47.1 2.8 %slice.1559 = f32[4,18,18,128]{3,2,1,0:T(8,128)} slice(f32[4,18,36,128]{3,2,1,0:T(8,128)S(1)} %fusion.1), slice={[0:4:1], [0:18:1], [0:36:2], [0:128:1]} | slice | bytes 1327104 | tf_op jit(solution)/shard_map/slice | solution.py:65
  49.8 2.0 %convolution_multiply_fusion = f32[4,18,18,64]{3,2,1,0:T(8,128)S(1)} fusion(f32[4,18,18,128]{3,2,1,0:T(8,128)} %slice.1559, f32[4,18,18,128]{3,2,1,0:T(8,128)} %slice.1560, s32[128]{0:T(128)S(1)} %and_select_fusion.1), kind=kOutput, calls=%fused_computation.5 | convolution fusion | flops 127659008 | bytes 1659392 | tf_op jit(solution)/shard_map/...yz,zw->...yw/dot_general | solution.py:66
  51.9 1.3 slice.1640
  53.1 1.2 slice.1639
  56.0 1.7 %slice_bitcast_fusion.4 = (f32[36,36,128]{2,1,0:T(8,128)S(1)}, f32[36,36,128]{2,1,0:T(8,128)S(1)}, f32[36,36,128]{2,1,0:T(8,128)S(1)}) fusion(f32[4,36,36,128]{3,2,1,0:T(8,128)} %shard_map.46), kind=kLoop, calls=%fused_computation.18 | loop fusion | bytes 3981312 | tf_op jit(solution)/shard_map/squeeze | solution.py:79
  59.4 1.2 slice_add_fusion.4
  61.0 1.2 fusion.25
  62.6 0.9 fusion.43
  64.3 1.6 %slice.1556 = f32[14,14,128]{2,1,0:T(8,128)} slice(f32[14,28,128]{2,1,0:T(8,128)} %fusion.72), slice={[0:14:1], [1:28:2], [0:128:1]} | slice | bytes 200704 | tf_op jit(solution)/shard_map/slice | solution.py:65
  65.9 1.6 %slice.1555 = f32[14,14,128]{2,1,0:T(8,128)} slice(f32[14,28,128]{2,1,0:T(8,128)} %fusion.72), slice={[0:14:1], [0:28:2], [0:128:1]} | slice | bytes 200704 | tf_op jit(solution)/shard_map/slice | solution.py:65
  67.5 1.2 divide_multiply_fusion
  68.8 1.2 divide_multiply_fusion.1
  70.0 1.3 add_maximum_fusion.1
  74.5 1.3 slice.1635
  75.8 1.3 slice.1634
  77.1 0.9 convolution_multiply_fusion.2
  79.0 6.4 %all_gather.3 = f32[5,4,16,32]{3,1,0,2:T(4,128)S(1)} all-gather(f32[5,4,4,32]{3,1,0,2:T(4,128)S(1)} %copy.51), channel_id=1, replica_groups=mesh['gx'=8,'gy'=4] {'gy'}, dimensions={2}, use_global_device_ids=true | all-gather | bytes 51200 | tf_op jit(solution)/shard_map/all_gather | solution.py:231
  85.4 5.1 %collective-permute-start.4 = (f32[5,4,16,32]{3,2,1,0:T(8,128)S(1)}, f32[5,4,16,32]{3,2,1,0:T(8,128)S(1)}, u32[]{:S(2)}, u32[]{:S(2)}) collective-permute-start(f32[5,4,16,32]{3,2,1,0:T(8,128)S(1)} %copy.52), channel_id=1, source_target_pairs={{0,8},{4,12},{8,16},{12,20},{16,24},{20,28},{1,9},{5,13},{9,17},{1... | collective-permute-start | bytes 122888 | tf_op jit(solution)/shard_map/ppermute | solution.py:30
  90.5 1.3 collective-permute-start.7
  91.8 1.3 collective-permute-start.6
  93.1 4.2 %collective-permute-start.5 = (f32[5,4,16,32]{3,2,1,0:T(8,128)S(1)}, f32[5,4,16,32]{3,2,1,0:T(8,128)S(1)}, u32[]{:S(2)}, u32[]{:S(2)}) collective-permute-start(f32[5,4,16,32]{3,2,1,0:T(8,128)S(1)} %copy.52), channel_id=1, source_target_pairs={{0,4},{4,8},{8,12},{12,16},{16,20},{20,24},{24,28},{1,5},{5,9},{9,... | collective-permute-start | bytes 122888 | tf_op jit(solution)/shard_map/ppermute | solution.py:30
  97.4 6.3 %collective-permute-done.5 = f32[5,4,16,32]{3,2,1,0:T(8,128)S(1)} collective-permute-done((f32[5,4,16,32]{3,2,1,0:T(8,128)S(1)}, f32[5,4,16,32]{3,2,1,0:T(8,128)S(1)}, u32[]{:S(2)}, u32[]{:S(2)}) %collective-permute-start.5) | collective-permute-done | bytes 40992 | tf_op jit(solution)/shard_map/ppermute | solution.py:30
  107.9 0.9 bitcast_add_fusion
  108.8 4.1 %collective-permute-start.8 = (f32[2,5,8,64]{3,2,1,0:T(8,128)S(1)}, f32[2,5,8,64]{3,2,1,0:T(8,128)S(1)}, u32[]{:S(2)}, u32[]{:S(2)}) collective-permute-start(f32[2,5,8,64]{3,2,1,0:T(8,128)S(1)} %get-tuple-element.128), channel_id=1, source_target_pairs={{0,4},{4,8},{8,12},{12,16},{16,20},{20,24},{24,28},{1,5},{5,9},{9,... | collective-permute-start | bytes 61448 | tf_op jit(solution)/shard_map/ppermute | solution.py:30
  112.9 1.3 collective-permute-start.9
  114.2 3.4 %collective-permute-done.9 = f32[2,5,8,64]{3,2,1,0:T(8,128)S(1)} collective-permute-done((f32[2,5,8,64]{3,2,1,0:T(8,128)S(1)}, f32[2,5,8,64]{3,2,1,0:T(8,128)S(1)}, u32[]{:S(2)}, u32[]{:S(2)}) %collective-permute-start.9) | collective-permute-done | bytes 20512 | tf_op jit(solution)/shard_map/ppermute | solution.py:30
  117.7 5.7 %collective-permute-start.10 = (f32[2,18,5,64]{3,2,1,0:T(8,128)S(1)}, f32[2,18,5,64]{3,2,1,0:T(8,128)S(1)}, u32[]{:S(2)}, u32[]{:S(2)}) collective-permute-start(f32[2,18,5,64]{3,2,1,0:T(8,128)S(1)} %get-tuple-element.84), channel_id=1, source_target_pairs={{0,1},{1,2},{2,3},{4,5},{5,6},{6,7},{8,9},{9,10},{10,11},{12,13},{... | collective-permute-start | bytes 138248 | tf_op jit(solution)/shard_map/ppermute | solution.py:30
  123.4 1.9 %collective-permute-start.11 = (f32[2,18,5,64]{3,2,1,0:T(8,128)S(1)}, f32[2,18,5,64]{3,2,1,0:T(8,128)S(1)}, u32[]{:S(2)}, u32[]{:S(2)}) collective-permute-start(f32[2,18,5,64]{3,2,1,0:T(8,128)S(1)} %get-tuple-element.85), channel_id=1, source_target_pairs={{1,0},{2,1},{3,2},{5,4},{6,5},{7,6},{9,8},{10,9},{11,10},{13,12},{... | collective-permute-start | bytes 138248 | tf_op jit(solution)/shard_map/ppermute | solution.py:30
  125.5 4.4 %collective-permute-done.11 = f32[2,18,5,64]{3,2,1,0:T(8,128)S(1)} collective-permute-done((f32[2,18,5,64]{3,2,1,0:T(8,128)S(1)}, f32[2,18,5,64]{3,2,1,0:T(8,128)S(1)}, u32[]{:S(2)}, u32[]{:S(2)}) %collective-permute-start.11) | collective-permute-done | bytes 46112 | tf_op jit(solution)/shard_map/ppermute | solution.py:30
  134.0 1.0 fusion.127
  (162 shorter events, 18.4 us)
Async XLA Ops:
  2.0 8.6 %collective-permute-start = (f32[3,10,16,128]{3,2,1,0:T(8,128)S(1)}, f32[3,10,16,128]{3,2,1,0:T(8,128)S(1)}, u32[]{:S(2)}, u32[]{:S(2)}) collective-permute-start(f32[3,10,16,128]{3,2,1,0:T(8,128)S(1)} %get-tuple-element.55), channel_id=1, source_target_pairs={{0,4},{4,8},{8,12},{12,16},{16,20},{20,24},{24,28},{1,5},{5,9},{9,... | collective-permute-start | bytes 737288 | tf_op jit(solution)/shard_map/ppermute | solution.py:30
  6.0 8.4 %collective-permute-start.1 = (f32[3,10,16,128]{3,2,1,0:T(8,128)S(1)}, f32[3,10,16,128]{3,2,1,0:T(8,128)S(1)}, u32[]{:S(2)}, u32[]{:S(2)}) collective-permute-start(f32[3,10,16,128]{3,2,1,0:T(8,128)S(1)} %get-tuple-element.56), channel_id=1, source_target_pairs={{4,0},{8,4},{12,8},{16,12},{20,16},{24,20},{28,24},{5,1},{9,5},{13... | collective-permute-start | bytes 737288 | tf_op jit(solution)/shard_map/ppermute | solution.py:30
  10.6 5.1 %copy-start.15 = (f32[3,10,16,128]{3,2,1,0:T(8,128)}, f32[3,10,16,128]{3,2,1,0:T(8,128)S(1)}, u32[]{:S(2)}) copy-start(f32[3,10,16,128]{3,2,1,0:T(8,128)S(1)} %collective-permute-done) | copy-start | bytes 737284
  14.4 1.3 copy-start.17
  15.9 13.9 %collective-permute-start.3 = (f32[3,36,10,128]{3,1,2,0:T(8,128)S(1)}, f32[3,36,10,128]{3,1,2,0:T(8,128)S(1)}, u32[]{:S(2)}, u32[]{:S(2)}) collective-permute-start(f32[3,36,10,128]{3,1,2,0:T(8,128)S(1)} %copy.40), channel_id=1, source_target_pairs={{1,0},{2,1},{3,2},{5,4},{6,5},{7,6},{9,8},{10,9},{11,10},{13,12},{... | collective-permute-start | bytes 1658888 | tf_op jit(solution)/shard_map/ppermute | solution.py:30
  20.9 12.8 %copy-start.13 = (f32[16,16,128]{2,1,0:T(8,128)S(1)}, f32[16,16,128]{2,1,0:T(8,128)}, u32[]{:S(2)}) copy-start(f32[16,16,128]{2,1,0:T(8,128)} %param.5) | copy-start | bytes 393220
  20.9 12.8 %copy-start.14 = (f32[16,16,128]{2,1,0:T(8,128)S(1)}, f32[16,16,128]{2,1,0:T(8,128)}, u32[]{:S(2)}) copy-start(f32[16,16,128]{2,1,0:T(8,128)} %param.4) | copy-start | bytes 393220
  21.9 11.8 %copy-start.16 = (f32[3,10,16,128]{3,2,1,0:T(8,128)S(1)}, f32[3,10,16,128]{3,2,1,0:T(8,128)}, u32[]{:S(2)}) copy-start(f32[3,10,16,128]{3,2,1,0:T(8,128)} %copy-done.15) | copy-start | bytes 737284
  21.9 11.8 %copy-start.18 = (f32[3,10,16,128]{3,2,1,0:T(8,128)S(1)}, f32[3,10,16,128]{3,2,1,0:T(8,128)}, u32[]{:S(2)}) copy-start(f32[3,10,16,128]{3,2,1,0:T(8,128)} %copy-done.17) | copy-start | bytes 737284
  21.9 10.5 %collective-permute-start.2 = (f32[3,36,10,128]{3,1,2,0:T(8,128)}, f32[3,36,10,128]{3,1,2,0:T(8,128)}, u32[]{:S(2)}, u32[]{:S(2)}) collective-permute-start(f32[3,36,10,128]{3,1,2,0:T(8,128)} %copy.39), channel_id=1, source_target_pairs={{0,1},{1,2},{2,3},{4,5},{5,6},{6,7},{8,9},{9,10},{10,11},{12,13},{... | collective-permute-start | bytes 1658888 | tf_op jit(solution)/shard_map/ppermute | solution.py:30
  25.1 24.7 %copy-start.22 = (s32[128]{0:T(128)}, s32[128]{0:T(128)S(1)}, u32[]{:S(2)}) copy-start(s32[128]{0:T(128)S(1)} %and_select_fusion.1) | copy-start | bytes 1540
  57.7 4.9 %copy-start = (f32[36,36,128]{2,1,0:T(8,128)}, f32[36,36,128]{2,1,0:T(8,128)S(1)}, u32[]{:S(2)}) copy-start(f32[36,36,128]{2,1,0:T(8,128)S(1)} %get-tuple-element.27) | copy-start | bytes 1990660
  58.9 2.1 %copy-start.8 = (f32[34,34,128]{2,1,0:T(8,128)}, f32[34,34,128]{2,1,0:T(8,128)S(1)}, u32[]{:S(2)}) copy-start(f32[34,34,128]{2,1,0:T(8,128)S(1)} %get-tuple-element.25) | copy-start | bytes 1775620
  67.5 3.8 %copy-start.20 = (f32[14,14,128]{2,1,0:T(8,128)S(1)}, f32[14,14,128]{2,1,0:T(8,128)}, u32[]{:S(2)}) copy-start(f32[14,14,128]{2,1,0:T(8,128)} %slice.1556) | copy-start | bytes 301060
  67.5 3.8 %copy-start.21 = (f32[14,14,128]{2,1,0:T(8,128)S(1)}, f32[14,14,128]{2,1,0:T(8,128)}, u32[]{:S(2)}) copy-start(f32[14,14,128]{2,1,0:T(8,128)} %slice.1555) | copy-start | bytes 301060
  67.5 4.9 %copy-start.4 = (f32[17,18,64]{2,1,0:T(8,128)S(1)}, f32[17,18,64]{2,1,0:T(8,128)}, u32[]{:S(2)}) copy-start(f32[17,18,64]{2,1,0:T(8,128)} %multiply_bitcast_fusion) | copy-start | bytes 235012
  67.5 4.9 %copy-start.10 = (f32[18,18,64]{2,1,0:T(8,128)S(1)}, f32[18,18,64]{2,1,0:T(8,128)}, u32[]{:S(2)}) copy-start(f32[18,18,64]{2,1,0:T(8,128)} %get-tuple-element.33) | copy-start | bytes 248836
  68.8 4.5 %copy-start.2 = (f32[18,18,63]{2,1,0:T(8,128)}, f32[18,18,63]{2,1,0:T(8,128)S(1)}, u32[]{:S(2)}) copy-start(f32[18,18,63]{2,1,0:T(8,128)S(1)} %divide_multiply_fusion) | copy-start | bytes 244948
  70.0 3.3 %copy-start.6 = (f32[18,17,64]{2,1,0:T(8,128)}, f32[18,17,64]{2,1,0:T(8,128)S(1)}, u32[]{:S(2)}) copy-start(f32[18,17,64]{2,1,0:T(8,128)S(1)} %divide_multiply_fusion.1) | copy-start | bytes 235012
  73.0 0.8 copy-start.12
  85.4 11.9 %collective-permute-start.4 = (f32[5,4,16,32]{3,2,1,0:T(8,128)S(1)}, f32[5,4,16,32]{3,2,1,0:T(8,128)S(1)}, u32[]{:S(2)}, u32[]{:S(2)}) collective-permute-start(f32[5,4,16,32]{3,2,1,0:T(8,128)S(1)} %copy.52), channel_id=1, source_target_pairs={{0,8},{4,12},{8,16},{12,20},{16,24},{20,28},{1,9},{5,13},{9,17},{1... | collective-permute-start | bytes 122888 | tf_op jit(solution)/shard_map/ppermute | solution.py:30
  90.5 13.2 %collective-permute-start.7 = (f32[5,4,16,32]{3,2,1,0:T(8,128)S(1)}, f32[5,4,16,32]{3,2,1,0:T(8,128)S(1)}, u32[]{:S(2)}, u32[]{:S(2)}) collective-permute-start(f32[5,4,16,32]{3,2,1,0:T(8,128)S(1)} %copy.52), channel_id=1, source_target_pairs={{8,0},{12,4},{16,8},{20,12},{24,16},{28,20},{9,1},{13,5},{17,9},{2... | collective-permute-start | bytes 122888 | tf_op jit(solution)/shard_map/ppermute | solution.py:30
  91.8 11.9 %collective-permute-start.6 = (f32[5,4,16,32]{3,2,1,0:T(8,128)S(1)}, f32[5,4,16,32]{3,2,1,0:T(8,128)S(1)}, u32[]{:S(2)}, u32[]{:S(2)}) collective-permute-start(f32[5,4,16,32]{3,2,1,0:T(8,128)S(1)} %copy.52), channel_id=1, source_target_pairs={{4,0},{8,4},{12,8},{16,12},{20,16},{24,20},{28,24},{5,1},{9,5},{13... | collective-permute-start | bytes 122888 | tf_op jit(solution)/shard_map/ppermute | solution.py:30
  93.1 10.5 %collective-permute-start.5 = (f32[5,4,16,32]{3,2,1,0:T(8,128)S(1)}, f32[5,4,16,32]{3,2,1,0:T(8,128)S(1)}, u32[]{:S(2)}, u32[]{:S(2)}) collective-permute-start(f32[5,4,16,32]{3,2,1,0:T(8,128)S(1)} %copy.52), channel_id=1, source_target_pairs={{0,4},{4,8},{8,12},{12,16},{16,20},{20,24},{24,28},{1,5},{5,9},{9,... | collective-permute-start | bytes 122888 | tf_op jit(solution)/shard_map/ppermute | solution.py:30
  106.8 2.0 %copy-start.19 = (f32[1,8,8,64]{3,2,1,0:T(8,128)S(1)}, f32[1,8,8,64]{3,2,1,0:T(8,128)}, u32[]{:S(2)}) copy-start(f32[1,8,8,64]{3,2,1,0:T(8,128)} %get-tuple-element.107) | copy-start | bytes 49156
  107.5 22.7 %copy-start.3 = (f32[18,18,63]{2,1,0:T(8,128)S(1)}, f32[18,18,63]{2,1,0:T(8,128)}, u32[]{:S(2)}) copy-start(f32[18,18,63]{2,1,0:T(8,128)} %copy-done.2) | copy-start | bytes 244948
  107.5 22.7 %copy-start.5 = (f32[17,18,64]{2,1,0:T(8,128)S(1)}, f32[17,18,64]{2,1,0:T(8,128)}, u32[]{:S(2)}) copy-start(f32[17,18,64]{2,1,0:T(8,128)} %multiply_bitcast_fusion) | copy-start | bytes 235012
  107.5 22.7 %copy-start.7 = (f32[18,17,64]{2,1,0:T(8,128)S(1)}, f32[18,17,64]{2,1,0:T(8,128)}, u32[]{:S(2)}) copy-start(f32[18,17,64]{2,1,0:T(8,128)} %copy-done.6) | copy-start | bytes 235012
  107.6 22.7 %copy-start.11 = (f32[18,18,64]{2,1,0:T(8,128)S(1)}, f32[18,18,64]{2,1,0:T(8,128)}, u32[]{:S(2)}) copy-start(f32[18,18,64]{2,1,0:T(8,128)} %get-tuple-element.33) | copy-start | bytes 248836
  108.8 5.4 %collective-permute-start.8 = (f32[2,5,8,64]{3,2,1,0:T(8,128)S(1)}, f32[2,5,8,64]{3,2,1,0:T(8,128)S(1)}, u32[]{:S(2)}, u32[]{:S(2)}) collective-permute-start(f32[2,5,8,64]{3,2,1,0:T(8,128)S(1)} %get-tuple-element.128), channel_id=1, source_target_pairs={{0,4},{4,8},{8,12},{12,16},{16,20},{20,24},{24,28},{1,5},{5,9},{9,... | collective-permute-start | bytes 61448 | tf_op jit(solution)/shard_map/ppermute | solution.py:30
  112.9 4.7 %collective-permute-start.9 = (f32[2,5,8,64]{3,2,1,0:T(8,128)S(1)}, f32[2,5,8,64]{3,2,1,0:T(8,128)S(1)}, u32[]{:S(2)}, u32[]{:S(2)}) collective-permute-start(f32[2,5,8,64]{3,2,1,0:T(8,128)S(1)} %get-tuple-element.129), channel_id=1, source_target_pairs={{4,0},{8,4},{12,8},{16,12},{20,16},{24,20},{28,24},{5,1},{9,5},{13... | collective-permute-start | bytes 61448 | tf_op jit(solution)/shard_map/ppermute | solution.py:30
  117.7 7.8 %collective-permute-start.10 = (f32[2,18,5,64]{3,2,1,0:T(8,128)S(1)}, f32[2,18,5,64]{3,2,1,0:T(8,128)S(1)}, u32[]{:S(2)}, u32[]{:S(2)}) collective-permute-start(f32[2,18,5,64]{3,2,1,0:T(8,128)S(1)} %get-tuple-element.84), channel_id=1, source_target_pairs={{0,1},{1,2},{2,3},{4,5},{5,6},{6,7},{8,9},{9,10},{10,11},{12,13},{... | collective-permute-start | bytes 138248 | tf_op jit(solution)/shard_map/ppermute | solution.py:30
  123.4 6.5 %collective-permute-start.11 = (f32[2,18,5,64]{3,2,1,0:T(8,128)S(1)}, f32[2,18,5,64]{3,2,1,0:T(8,128)S(1)}, u32[]{:S(2)}, u32[]{:S(2)}) collective-permute-start(f32[2,18,5,64]{3,2,1,0:T(8,128)S(1)} %get-tuple-element.85), channel_id=1, source_target_pairs={{1,0},{2,1},{3,2},{5,4},{6,5},{7,6},{9,8},{10,9},{11,10},{13,12},{... | collective-permute-start | bytes 138248 | tf_op jit(solution)/shard_map/ppermute | solution.py:30
  130.6 0.7 copy-start.23
  131.3 1.1 copy-start.1
  131.3 1.3 copy-start.9

commit v3 on v2

--- a/solution.py
+++ b/solution.py
@@ -62,8 +62,11 @@
     sx, sy, sz = values.shape[-3:]
     v = values.reshape(lead + (sx // 2, 2, sy, sz))
     v = v[..., 0, :, :] + v[..., 1, :, :]
-    v = v[..., 0::2, :] + v[..., 1::2, :]
     v = jnp.einsum("...yz,zw->...yw", v, pair_matrix(sz), precision=HIGH)
+    rows = v.reshape((-1, sy, sz // 2))
+    pick = jnp.broadcast_to(pair_matrix(sy).T, (rows.shape[0], sy // 2, sy))
+    rows = lax.dot_general(pick, rows, (((2,), (1,)), ((0,), (0,))), precision=HIGH)
+    v = rows.reshape(lead + (sx // 2, sy // 2, sz // 2))
     return v * 0.125
 
 
@@ -226,14 +229,26 @@
     coarse_own = coarsen(win(mid_c, nm, mm, 0))
 
     nc = b2.shape[0]
-    reach = 2
     cpack = jnp.concatenate([b2[None], coarse_own], axis=0)
-    cpack = lax.all_gather(cpack, "gy", axis=2, tiled=True)
-    parts = [shift_from(cpack, "gx", -d) for d in range(reach, 0, -1)]
-    parts += [cpack]
-    parts += [shift_from(cpack, "gx", d) for d in range(1, reach + 1)]
+    mpack = jnp.stack([win(x1, nm, x1m, 0), win(b1, nm, b1m, 0)])
+    hm = MID_HALO
+    blocks = [cpack]
+    for step in range(1, gy_count):
+        pairs = [(j, (j - step) % gy_count) for j in range(gy_count)]
+        blocks.append(lax.ppermute(cpack, "gy", pairs))
+    north = shift_from(mpack[:, :, :hm], "gy", 1)
+    south = shift_from(mpack[:, :, nm - hm :], "gy", -1)
+    mext = jnp.concatenate([south, mpack, north], axis=2)
+    full = jnp.concatenate(blocks, axis=2)
+    full = jnp.roll(full, iy * nc, axis=2)
+    reach = 3
+    parts = [shift_from(full, "gx", -d) for d in range(reach, 0, -1)]
+    parts += [full]
+    parts += [shift_from(full, "gx", d) for d in range(1, reach + 1)]
     cpack = jnp.concatenate(parts, axis=1)
-    cm = reach * nc
+    west_m = shift_from(mext[:, nm - hm :], "gx", -1)
+    east_m = shift_from(mext[:, :hm], "gx", 1)
+    mext = jnp.concatenate([west_m, mext, east_m], axis=1)
     source = cpack[0]
     cc = cpack[1:]
     line_total = jnp.sum(source, axis=1)
@@ -260,8 +275,7 @@
     u = jnp.broadcast_to(line_mean[:, None, :], source.shape)
     for sweep in range(COARSE_SWEEPS):
         lo = sweep
-        cur = u
-        up = jnp.pad(cur, ((0, 0), (1, 1), (0, 0)))
+        up = jnp.pad(u, ((0, 0), (1, 1), (0, 0)))
         centre = up[1:-1, 1:-1]
         sl = slice(lo, width - 2 - lo)
         upper = jnp.concatenate([centre[:, :, 1:], centre[:, :, :1]], axis=2)
@@ -271,14 +285,14 @@
         fl = fl + above[sl] * (centre - upper) + below[sl] * (centre - lower)
         applied = cst[sl] * centre + fl
         u = centre + jacobi_weight * ((csrc[sl] - applied) / cdiag[sl])
-    ncy = nc
-    u = lax.dynamic_slice_in_dim(u, iy * ncy, ncy, 1)
-
-    s1 = win(x1, nm, x1m, 0) + prolong(u)
-    mpack = jnp.stack([s1, win(b1, nm, b1m, 0)])
-    mpack = halo(mpack, (("gx", 1), ("gy", 2)), MID_HALO)
-    s1e, b1e = mpack[0], mpack[1]
-    y1, y1m = chebyshev(b1e, MID_HALO, s1e, MID_HALO, mid)
+    um = (hm + 1) // 2
+    have = reach * nc - COARSE_SWEEPS
+    u = u[have - um : u.shape[0] - (have - um)]
+    u = jnp.pad(u, ((0, 0), (um, um), (0, 0)))
+    u = lax.dynamic_slice_in_dim(u, iy * nc, nc + 2 * um, 1)
+    s1e = win(mext[0], nm, hm, hm) + win(prolong(u), nm, 2 * um, hm)
+    b1e = mext[1]
+    y1, y1m = chebyshev(b1e, hm, s1e, hm, mid)
     fm = 2 * y1m
     s0 = win(x0, n, x0m, fm) + prolong(y1)
     fs = min(fm, CHEB)

time: 136 us -> 119 us (0.88)
  the two profiles are of different devices: /device:TPU:1 before, /device:TPU:4 now
where the time goes in v3:
time: 119 us; the launch traced here: 118 us
  starting transfers between devices  47.1 us (40%)
  local copies, waits for them, and re-layouts  24.7 us (21%)
  other arithmetic  19.8 us (17%)
  waiting for transfers between devices  14.7 us (12%)
  Pallas kernels  5.47 us (5%)
  matrix products  5.12 us (4%)
    ppermute x14, starting transfers between devices, shift_from(): return lax.ppermute(cells, axis, pairs)  38.3 us
    ppermute x14, waiting for transfers between devices, shift_from(): return lax.ppermute(cells, axis, pairs)  14.7 us
    ppermute x3, starting transfers between devices, local(): blocks.append(lax.ppermute(cpack, 'gy', pairs))  8.81 us
    concatenate x1, local copies, waits for them, and re-layouts, local(): full = jnp.roll(full, iy * nc, axis=2)  5.87 us
    add x7, other arithmetic, chebyshev(): iterate = win(iterate, n, cur, nxt) + update  5.54 us
    pallas_call x1, Pallas kernels, soil_fields(): pl.pallas_call(fields_kernel, out_shape=jax.ShapeDtypeStruct((4,) + conc....  5.47 us
    unnamed x63, local copies, waits for them, and re-layouts  4.66 us
    broadcast_in_dim x2, local copies, waits for them, and re-layouts, prolong(): jnp.broadcast_to(v[:, None], (sx, 2) + v.shape[1:])  2.6 us
  transfers between devices with their start and end apart: 17, of which 4 were waited for; matrix products, arithmetic and copies ran while one was open for 16% of the time, Pallas kernels for 0%

profile of v3, /device:TPU:4, one launch (start us, length us, event | category | flops | bytes accessed | tf_op | source)
XLA Modules:
  0.0 118.2 jit_solution(3772320266780749870)
XLA Ops:
  0.0 1.0 convert_bitcast_fusion
  1.0 1.0 pad_maximum_fusion.3
  2.0 1.9 %collective-permute-start.1 = (f32[3,10,16,128]{3,2,1,0:T(8,128)S(1)}, f32[3,10,16,128]{3,2,1,0:T(8,128)S(1)}, u32[]{:S(2)}, u32[]{:S(2)}) collective-permute-start(f32[3,10,16,128]{3,2,1,0:T(8,128)S(1)} %get-tuple-element.51), channel_id=1, source_target_pairs={{4,0},{8,4},{12,8},{16,12},{20,16},{24,20},{28,24},{5,1},{9,5},{13... | collective-permute-start | bytes 737288 | tf_op jit(solution)/shard_map/ppermute | solution.py:30
  3.9 4.8 %collective-permute-start = (f32[3,10,16,128]{3,2,1,0:T(8,128)S(1)}, f32[3,10,16,128]{3,2,1,0:T(8,128)S(1)}, u32[]{:S(2)}, u32[]{:S(2)}) collective-permute-start(f32[3,10,16,128]{3,2,1,0:T(8,128)S(1)} %get-tuple-element.50), channel_id=1, source_target_pairs={{0,4},{4,8},{8,12},{12,16},{16,20},{20,24},{24,28},{1,5},{5,9},{9,... | collective-permute-start | bytes 737288 | tf_op jit(solution)/shard_map/ppermute | solution.py:30
  9.3 3.3 %collective-permute-done.1 = f32[3,10,16,128]{3,2,1,0:T(8,128)S(1)} collective-permute-done((f32[3,10,16,128]{3,2,1,0:T(8,128)S(1)}, f32[3,10,16,128]{3,2,1,0:T(8,128)S(1)}, u32[]{:S(2)}, u32[]{:S(2)}) %collective-permute-start.1) | collective-permute-done | bytes 245792 | tf_op jit(solution)/shard_map/ppermute | solution.py:30
  12.6 5.2 %collective-permute-done = f32[3,10,16,128]{3,2,1,0:T(8,128)S(1)} collective-permute-done((f32[3,10,16,128]{3,2,1,0:T(8,128)S(1)}, f32[3,10,16,128]{3,2,1,0:T(8,128)S(1)}, u32[]{:S(2)}, u32[]{:S(2)}) %collective-permute-start) | collective-permute-done | bytes 245792 | tf_op jit(solution)/shard_map/ppermute | solution.py:30
  17.8 0.7 copy-done.17
  18.9 1.3 %collective-permute-start.3 = (f32[3,36,10,128]{3,1,2,0:T(8,128)S(1)}, f32[3,36,10,128]{3,1,2,0:T(8,128)S(1)}, u32[]{:S(2)}, u32[]{:S(2)}) collective-permute-start(f32[3,36,10,128]{3,1,2,0:T(8,128)S(1)} %copy.16), channel_id=1, source_target_pairs={{1,0},{2,1},{3,2},{5,4},{6,5},{7,6},{9,8},{10,9},{11,10},{13,12},{... | collective-permute-start | bytes 1658888 | tf_op jit(solution)/shard_map/ppermute | solution.py:30
  20.4 3.1 %collective-permute-start.2 = (f32[3,36,10,128]{3,1,2,0:T(8,128)S(1)}, f32[3,36,10,128]{3,1,2,0:T(8,128)S(1)}, u32[]{:S(2)}, u32[]{:S(2)}) collective-permute-start(f32[3,36,10,128]{3,1,2,0:T(8,128)S(1)} %copy.15), channel_id=1, source_target_pairs={{0,1},{1,2},{2,3},{4,5},{5,6},{6,7},{8,9},{9,10},{10,11},{12,13},{... | collective-permute-start | bytes 1658888 | tf_op jit(solution)/shard_map/ppermute | solution.py:30
  23.4 0.6 pad_add_fusion.bounds_ref
  26.0 1.3 %slice_bitcast_fusion.3 = (f32[36,36,128]{2,1,0:T(8,128)}, f32[36,36,128]{2,1,0:T(8,128)}, f32[36,36,128]{2,1,0:T(8,128)S(1)}) fusion(f32[3,36,36,128]{3,2,1,0:T(8,128)S(1)} %pad_maximum_fusion), kind=kLoop, calls=%fused_computation.15 | loop fusion | bytes 3981312 | tf_op jit(solution)/shard_map/squeeze | solution.py:209
  27.3 5.5 %shard_map.46 = f32[4,36,36,128]{3,2,1,0:T(8,128)} custom-call(s32[4]{0:T(128)} %pad_add_fusion.bounds_ref, f32[5,8]{1,0:T(8,128)} %table_ref.1, f32[36,36,128]{2,1,0:T(8,128)} %get-tuple-element.30.conc_ref, f32[36,36,128]{2,1,0:T(8,128)} %get-tuple-element.29.idf_ref), custom_call_target="tpu_custom_call" | custom-call | flops 16588800 | bytes 3981312 | tf_op jit(solution)/shard_map/pallas_call | solution.py:182
  32.8 1.9 %slice_bitcast_fusion.2 = (f32[36,36,128]{2,1,0:T(8,128)S(1)}, f32[36,36,128]{2,1,0:T(8,128)S(1)}, f32[36,36,128]{2,1,0:T(8,128)S(1)}) fusion(f32[4,36,36,128]{3,2,1,0:T(8,128)} %shard_map.46), kind=kLoop, calls=%fused_computation.14 | loop fusion | bytes 3981312 | tf_op jit(solution)/shard_map/squeeze | solution.py:82
  34.6 0.6 copy-done
  35.9 0.7 fusion.4
  37.1 1.2 %slice_add_fusion.5 = (f32[32,32,128]{2,1,0:T(8,128)S(1)}, f32[32,32,128]{2,1,0:T(8,128)S(1)}) fusion(f32[34,34,128]{2,1,0:T(8,128)S(1)} %get-tuple-element.24, f32[34,34,128]{2,1,0:T(8,128)S(1)} %get-tuple-element.25, f32[32,32,127]{2,1,0:T(8,128)S(1)} %get-tuple-element.39, f32[32,32,1]{2,1,0:T(8,128)S(1)} %get-tuple-element.41, ...), kind=kLoop, calls=%fused_computation.55 | loop fusion | flops 3538944 | bytes 9046976 | tf_op jit(solution)/shard_map/add | solution.py:146
  38.9 0.8 fusion.335
  39.7 1.5 %convolution_multiply_fusion = f32[72,18,64]{2,1,0:T(8,128)S(1)} fusion(f32[72,36,64]{2,1,0:T(8,128)S(1)} %fusion.335, f32[18,36]{1,0:T(8,128)S(1)} %fusion.357), kind=kOutput, calls=%fused_computation.6 | convolution fusion | flops 35914752 | bytes 997920 | tf_op jit(solution)/shard_map/dot_general | solution.py:68
  41.7 1.2 fusion.22
  43.3 0.9 fusion.40
  46.9 1.0 collective-permute-start.8
  47.9 7.6 %collective-permute-start.9 = (f32[5,4,4,32]{3,2,1,0:T(4,128)S(1)}, f32[5,4,4,32]{3,2,1,0:T(4,128)S(1)}, u32[]{:S(2)}, u32[]{:S(2)}) collective-permute-start(f32[5,4,4,32]{3,2,1,0:T(4,128)S(1)} %pad_maximum_fusion.8), channel_id=1, source_target_pairs={{0,2},{1,3},{2,0},{3,1},{4,6},{5,7},{6,4},{7,5},{8,10},{9,11},{10,... | collective-permute-start | bytes 30728 | tf_op jit(solution)/shard_map/ppermute | solution.py:238
  55.7 0.7 slice_maximum_fusion
  56.4 1.3 %collective-permute-start.5 = (f32[2,8,5,64]{3,2,1,0:T(8,128)}, f32[2,8,5,64]{3,2,1,0:T(8,128)}, u32[]{:S(2)}, u32[]{:S(2)}) collective-permute-start(f32[2,8,5,64]{3,2,1,0:T(8,128)} %get-tuple-element.138), channel_id=1, source_target_pairs={{1,0},{2,1},{3,2},{5,4},{6,5},{7,6},{9,8},{10,9},{11,10},{13,12},{... | collective-permute-start | bytes 61448 | tf_op jit(solution)/shard_map/ppermute | solution.py:30
  57.7 3.7 %collective-permute-start.4 = (f32[2,8,5,64]{3,2,1,0:T(8,128)}, f32[2,8,5,64]{3,2,1,0:T(8,128)}, u32[]{:S(2)}, u32[]{:S(2)}) collective-permute-start(f32[2,8,5,64]{3,2,1,0:T(8,128)} %get-tuple-element.137), channel_id=1, source_target_pairs={{0,1},{1,2},{2,3},{4,5},{5,6},{6,7},{8,9},{9,10},{10,11},{12,13},{... | collective-permute-start | bytes 61448 | tf_op jit(solution)/shard_map/ppermute | solution.py:30
  61.3 0.6 copy-done.22
  62.6 5.9 %concatenate.192 = f32[5,4,32,32]{3,2,1,0:T(8,128)} concatenate(f32[5,4,4,32]{3,2,1,0:T(4,128)} %copy-done.21, f32[5,4,4,32]{3,2,1,0:T(4,128)} %copy-done.22, f32[5,4,4,32]{3,2,1,0:T(4,128)} %copy-done.23, f32[5,4,4,32]{3,2,1,0:T(4,128)} %collective-permute-done.10, f32[5,4,4,32]{3,2,1,0:T(4,128)} %copy-done.21, f32[5,4,4,32]{3,2,1,0:T(4,128)} %copy-done.22, ...), dimensions={2} | concatenate | bytes 163840 | tf_op jit(solution)/shard_map/jit(_roll_dynamic)/concatenate | solution.py:243
  68.4 1.0 constant_dynamic-slice_fusion
  69.4 3.5 %collective-permute-start.12 = (f32[5,4,16,32]{3,2,1,0:T(8,128)S(1)}, f32[5,4,16,32]{3,2,1,0:T(8,128)S(1)}, u32[]{:S(2)}, u32[]{:S(2)}) collective-permute-start(f32[5,4,16,32]{3,2,1,0:T(8,128)S(1)} %constant_dynamic-slice_fusion), channel_id=1, source_target_pairs={{0,8},{4,12},{8,16},{12,20},{16,24},{20,28},{1,9},{5,13},{9,17},{1... | collective-permute-start | bytes 122888 | tf_op jit(solution)/shard_map/ppermute | solution.py:30
  72.9 3.5 %collective-permute-start.11 = (f32[5,4,16,32]{3,2,1,0:T(8,128)S(1)}, f32[5,4,16,32]{3,2,1,0:T(8,128)S(1)}, u32[]{:S(2)}, u32[]{:S(2)}) collective-permute-start(f32[5,4,16,32]{3,2,1,0:T(8,128)S(1)} %constant_dynamic-slice_fusion), channel_id=1, source_target_pairs={{0,12},{4,16},{8,20},{12,24},{16,28},{1,13},{5,17},{9,21},{13,25},... | collective-permute-start | bytes 122888 | tf_op jit(solution)/shard_map/ppermute | solution.py:30
  76.4 2.8 %collective-permute-start.13 = (f32[5,4,16,32]{3,2,1,0:T(8,128)S(1)}, f32[5,4,16,32]{3,2,1,0:T(8,128)S(1)}, u32[]{:S(2)}, u32[]{:S(2)}) collective-permute-start(f32[5,4,16,32]{3,2,1,0:T(8,128)S(1)} %constant_dynamic-slice_fusion), channel_id=1, source_target_pairs={{0,4},{4,8},{8,12},{12,16},{16,20},{20,24},{24,28},{1,5},{5,9},{9,... | collective-permute-start | bytes 122888 | tf_op jit(solution)/shard_map/ppermute | solution.py:30
  79.3 3.2 %collective-permute-start.14 = (f32[5,4,16,32]{3,2,1,0:T(8,128)S(1)}, f32[5,4,16,32]{3,2,1,0:T(8,128)S(1)}, u32[]{:S(2)}, u32[]{:S(2)}) collective-permute-start(f32[5,4,16,32]{3,2,1,0:T(8,128)S(1)} %constant_dynamic-slice_fusion), channel_id=1, source_target_pairs={{4,0},{8,4},{12,8},{16,12},{20,16},{24,20},{28,24},{5,1},{9,5},{13... | collective-permute-start | bytes 122888 | tf_op jit(solution)/shard_map/ppermute | solution.py:30
  82.5 1.3 %collective-permute-start.15 = (f32[5,4,16,32]{3,2,1,0:T(8,128)S(1)}, f32[5,4,16,32]{3,2,1,0:T(8,128)S(1)}, u32[]{:S(2)}, u32[]{:S(2)}) collective-permute-start(f32[5,4,16,32]{3,2,1,0:T(8,128)S(1)} %constant_dynamic-slice_fusion), channel_id=1, source_target_pairs={{8,0},{12,4},{16,8},{20,12},{24,16},{28,20},{9,1},{13,5},{17,9},{2... | collective-permute-start | bytes 122888 | tf_op jit(solution)/shard_map/ppermute | solution.py:30
  83.8 1.0 pad_maximum_fusion.4
  84.7 0.7 fusion.394
  85.4 1.3 %collective-permute-start.16 = (f32[5,4,16,32]{3,2,1,0:T(8,128)S(1)}, f32[5,4,16,32]{3,2,1,0:T(8,128)S(1)}, u32[]{:S(2)}, u32[]{:S(2)}) collective-permute-start(f32[5,4,16,32]{3,2,1,0:T(8,128)S(1)} %constant_dynamic-slice_fusion), channel_id=1, source_target_pairs={{12,0},{16,4},{20,8},{24,12},{28,16},{13,1},{17,5},{21,9},{25,13},... | collective-permute-start | bytes 122888 | tf_op jit(solution)/shard_map/ppermute | solution.py:30
  86.8 1.9 %collective-permute-start.7 = (f32[2,5,18,64]{3,2,1,0:T(8,128)}, f32[2,5,18,64]{3,2,1,0:T(8,128)}, u32[]{:S(2)}, u32[]{:S(2)}) collective-permute-start(f32[2,5,18,64]{3,2,1,0:T(8,128)} %get-tuple-element.78), channel_id=1, source_target_pairs={{4,0},{8,4},{12,8},{16,12},{20,16},{24,20},{28,24},{5,1},{9,5},{13... | collective-permute-start | bytes 138248 | tf_op jit(solution)/shard_map/ppermute | solution.py:30
  88.7 4.8 %collective-permute-start.6 = (f32[2,5,18,64]{3,2,1,0:T(8,128)}, f32[2,5,18,64]{3,2,1,0:T(8,128)}, u32[]{:S(2)}, u32[]{:S(2)}) collective-permute-start(f32[2,5,18,64]{3,2,1,0:T(8,128)} %get-tuple-element.77), channel_id=1, source_target_pairs={{0,4},{4,8},{8,12},{12,16},{16,20},{20,24},{24,28},{1,5},{5,9},{9,... | collective-permute-start | bytes 138248 | tf_op jit(solution)/shard_map/ppermute | solution.py:30
  93.7 6.1 %collective-permute-done.16 = f32[5,4,16,32]{3,2,1,0:T(8,128)S(1)} collective-permute-done((f32[5,4,16,32]{3,2,1,0:T(8,128)S(1)}, f32[5,4,16,32]{3,2,1,0:T(8,128)S(1)}, u32[]{:S(2)}, u32[]{:S(2)}) %collective-permute-start.16) | collective-permute-done | bytes 40992 | tf_op jit(solution)/shard_map/ppermute | solution.py:30
  105.6 0.7 broadcast_in_dim.94
  106.2 1.6 %broadcast_in_dim.95 = f32[10,20,64]{2,1,0:T(8,128)} reshape(f32[10,10,2,64]{3,2,1,0:T(2,128)} %broadcast_in_dim.94) | data formatting | bytes 102400 | tf_op jit(solution)/shard_map/broadcast_in_dim | solution.py:77
  107.9 1.1 pad_maximum_fusion.2
  109.0 1.0 broadcast_in_dim.96
  110.3 1.2 %slice_add_fusion.10 = (f32[16,16,64]{2,1,0:T(8,128)S(1)}, f32[16,16,64]{2,1,0:T(8,128)S(1)}) fusion(f32[18,18,64]{2,1,0:T(8,128)S(1)} %slice_add_fusion.8, f32[16,16,64]{2,1,0:T(8,128)S(1)} %add_maximum_fusion.1, f32[16,16,63]{2,1,0:T(8,128)S(1)} %get-tuple-element.70, f32[16,16,1]{2,1,0:T(8,128)S(1)} %get-tuple-element.72, ...), kind=kLoop, calls=%fused_computation.387 | loop fusion | flops 409600 | bytes 1130224 | tf_op jit(solution)/shard_map/add | solution.py:136
  111.7 1.2 %slice_add_fusion.11 = (f32[14,14,64]{2,1,0:T(8,128)S(1)}, f32[14,14,64]{2,1,0:T(8,128)S(1)}) fusion(f32[16,16,64]{2,1,0:T(8,128)S(1)} %get-tuple-element.15, f32[16,16,64]{2,1,0:T(8,128)S(1)} %add_maximum_fusion.1, f32[14,14,63]{2,1,0:T(8,128)S(1)} %get-tuple-element.106, f32[14,14,1]{2,1,0:T(8,128)S(1)} %get-tuple-element.108, ...), kind=kLoop, calls=%fused_computation.438 | loop fusion | flops 338688 | bytes 934640 | tf_op jit(solution)/shard_map/add | solution.py:146
  113.1 1.3 %fusion.266 = f32[12,12,128]{2,1,0:T(8,128)S(1)} fusion(f32[14,14,64]{2,1,0:T(8,128)S(1)} %get-tuple-element.14, f32[14,14,64]{2,1,0:T(8,128)S(1)} %get-tuple-element.13, f32[18,18,64]{2,1,0:T(8,128)S(1)} %slice_bitcast_fusion.9, f32[12,12,1]{2,1,0:T(8,128)S(1)} %get-tuple-element.114, f32[12,12,63]{2,1,0:T(8,128)S(1)} %get-tuple-element.116, ...), kind=kOutput, calls=%fused_computation.469 | convolution fusion | flops 14412800 | bytes 1966592 | tf_op jit(solution)/shard_map/xyz,wz->xyw/dot_general | solution.py:75
  114.9 0.7 copy-done.2
  117.2 1.0 fusion.191
  (185 shorter events, 17.0 us)
Async XLA Ops:
  0.0 18.5 %copy-start.13 = (f32[16,16,128]{2,1,0:T(8,128)S(1)}, f32[16,16,128]{2,1,0:T(8,128)}, u32[]{:S(2)}) copy-start(f32[16,16,128]{2,1,0:T(8,128)} %param.5) | copy-start | bytes 393220
  0.0 18.5 %copy-start.14 = (f32[16,16,128]{2,1,0:T(8,128)S(1)}, f32[16,16,128]{2,1,0:T(8,128)}, u32[]{:S(2)}) copy-start(f32[16,16,128]{2,1,0:T(8,128)} %param.4) | copy-start | bytes 393220
  2.0 10.6 %collective-permute-start.1 = (f32[3,10,16,128]{3,2,1,0:T(8,128)S(1)}, f32[3,10,16,128]{3,2,1,0:T(8,128)S(1)}, u32[]{:S(2)}, u32[]{:S(2)}) collective-permute-start(f32[3,10,16,128]{3,2,1,0:T(8,128)S(1)} %get-tuple-element.51), channel_id=1, source_target_pairs={{4,0},{8,4},{12,8},{16,12},{20,16},{24,20},{28,24},{5,1},{9,5},{13... | collective-permute-start | bytes 737288 | tf_op jit(solution)/shard_map/ppermute | solution.py:30
  3.9 13.8 %collective-permute-start = (f32[3,10,16,128]{3,2,1,0:T(8,128)S(1)}, f32[3,10,16,128]{3,2,1,0:T(8,128)S(1)}, u32[]{:S(2)}, u32[]{:S(2)}) collective-permute-start(f32[3,10,16,128]{3,2,1,0:T(8,128)S(1)} %get-tuple-element.50), channel_id=1, source_target_pairs={{0,4},{4,8},{8,12},{12,16},{16,20},{20,24},{24,28},{1,5},{5,9},{9,... | collective-permute-start | bytes 737288 | tf_op jit(solution)/shard_map/ppermute | solution.py:30
  8.8 35.4 %copy-start.27 = (s32[128]{0:T(128)}, s32[128]{0:T(128)S(1)}, u32[]{:S(2)}) copy-start(s32[128]{0:T(128)S(1)} %and_select_fusion.3) | copy-start | bytes 1540
  12.6 6.1 %copy-start.15 = (f32[3,10,16,128]{3,2,1,0:T(8,128)}, f32[3,10,16,128]{3,2,1,0:T(8,128)S(1)}, u32[]{:S(2)}) copy-start(f32[3,10,16,128]{3,2,1,0:T(8,128)S(1)} %collective-permute-done.1) | copy-start | bytes 737284
  17.8 0.7 copy-start.17
  18.9 5.8 %collective-permute-start.3 = (f32[3,36,10,128]{3,1,2,0:T(8,128)S(1)}, f32[3,36,10,128]{3,1,2,0:T(8,128)S(1)}, u32[]{:S(2)}, u32[]{:S(2)}) collective-permute-start(f32[3,36,10,128]{3,1,2,0:T(8,128)S(1)} %copy.16), channel_id=1, source_target_pairs={{1,0},{2,1},{3,2},{5,4},{6,5},{7,6},{9,8},{10,9},{11,10},{13,12},{... | collective-permute-start | bytes 1658888 | tf_op jit(solution)/shard_map/ppermute | solution.py:30
  20.4 4.7 %collective-permute-start.2 = (f32[3,36,10,128]{3,1,2,0:T(8,128)S(1)}, f32[3,36,10,128]{3,1,2,0:T(8,128)S(1)}, u32[]{:S(2)}, u32[]{:S(2)}) collective-permute-start(f32[3,36,10,128]{3,1,2,0:T(8,128)S(1)} %copy.15), channel_id=1, source_target_pairs={{0,1},{1,2},{2,3},{4,5},{5,6},{6,7},{8,9},{9,10},{10,11},{12,13},{... | collective-permute-start | bytes 1658888 | tf_op jit(solution)/shard_map/ppermute | solution.py:30
  24.7 0.9 copy-start.16
  24.7 1.1 copy-start.18
  32.8 2.5 %copy-start = (f32[4,36,36,128]{3,2,1,0:T(8,128)S(1)}, f32[4,36,36,128]{3,2,1,0:T(8,128)}, u32[]{:S(2)}) copy-start(f32[4,36,36,128]{3,2,1,0:T(8,128)} %shard_map.46) | copy-start | bytes 7962628
  35.3 8.0 %copy-start.1 = (f32[36,36,128]{2,1,0:T(8,128)}, f32[36,36,128]{2,1,0:T(8,128)S(1)}, u32[]{:S(2)}) copy-start(f32[36,36,128]{2,1,0:T(8,128)S(1)} %get-tuple-element.27) | copy-start | bytes 1990660
  36.7 5.0 %copy-start.10 = (f32[34,34,128]{2,1,0:T(8,128)}, f32[34,34,128]{2,1,0:T(8,128)S(1)}, u32[]{:S(2)}) copy-start(f32[34,34,128]{2,1,0:T(8,128)S(1)} %get-tuple-element.25) | copy-start | bytes 1775620
  41.3 4.8 %copy-start.5 = (f32[72,18,64]{2,1,0:T(8,128)}, f32[72,18,64]{2,1,0:T(8,128)S(1)}, u32[]{:S(2)}) copy-start(f32[72,18,64]{2,1,0:T(8,128)S(1)} %convolution_multiply_fusion) | copy-start | bytes 995332
  41.4 4.8 %copy-start.8 = (f32[18,17,64]{2,1,0:T(8,128)}, f32[18,17,64]{2,1,0:T(8,128)S(1)}, u32[]{:S(2)}) copy-start(f32[18,17,64]{2,1,0:T(8,128)S(1)} %divide_multiply_fusion.1) | copy-start | bytes 235012
  41.5 4.7 %copy-start.6 = (f32[17,18,64]{2,1,0:T(8,128)}, f32[17,18,64]{2,1,0:T(8,128)S(1)}, u32[]{:S(2)}) copy-start(f32[17,18,64]{2,1,0:T(8,128)S(1)} %multiply_bitcast_fusion) | copy-start | bytes 235012
  41.6 4.5 %copy-start.3 = (f32[18,18,63]{2,1,0:T(8,128)}, f32[18,18,63]{2,1,0:T(8,128)S(1)}, u32[]{:S(2)}) copy-start(f32[18,18,63]{2,1,0:T(8,128)S(1)} %divide_multiply_fusion) | copy-start | bytes 244948
  43.3 1.3 %copy-start.24 = (f32[14,28]{1,0:T(8,128)S(1)}, f32[14,28]{1,0:T(8,128)}, u32[]{:S(2)}) copy-start(f32[14,28]{1,0:T(8,128)} %fusion.361) | copy-start | bytes 4708
  45.3 0.6 copy-start.25
  46.3 9.4 %copy-start.19 = (f32[1,8,8,64]{3,2,1,0:T(8,128)}, f32[1,8,8,64]{3,2,1,0:T(8,128)S(1)}, u32[]{:S(2)}) copy-start(f32[1,8,8,64]{3,2,1,0:T(8,128)S(1)} %get-tuple-element.117) | copy-start | bytes 49156
  46.3 10.1 %copy-start.20 = (f32[1,8,8,64]{3,2,1,0:T(8,128)}, f32[1,8,8,64]{3,2,1,0:T(8,128)S(1)}, u32[]{:S(2)}) copy-start(f32[1,8,8,64]{3,2,1,0:T(8,128)S(1)} %get-tuple-element.132) | copy-start | bytes 49156
  46.9 9.5 %copy-start.21 = (f32[5,4,4,32]{3,2,1,0:T(4,128)}, f32[5,4,4,32]{3,2,1,0:T(4,128)S(1)}, u32[]{:S(2)}) copy-start(f32[5,4,4,32]{3,2,1,0:T(4,128)S(1)} %pad_maximum_fusion.8) | copy-start | bytes 30724
  46.9 14.4 %collective-permute-start.8 = (f32[5,4,4,32]{3,2,1,0:T(4,128)S(1)}, f32[5,4,4,32]{3,2,1,0:T(4,128)S(1)}, u32[]{:S(2)}, u32[]{:S(2)}) collective-permute-start(f32[5,4,4,32]{3,2,1,0:T(4,128)S(1)} %pad_maximum_fusion.8), channel_id=1, source_target_pairs={{0,3},{1,0},{2,1},{3,2},{4,7},{5,4},{6,5},{7,6},{8,11},{9,8},{10,9... | collective-permute-start | bytes 30728 | tf_op jit(solution)/shard_map/ppermute | solution.py:238
  47.9 13.4 %collective-permute-start.9 = (f32[5,4,4,32]{3,2,1,0:T(4,128)S(1)}, f32[5,4,4,32]{3,2,1,0:T(4,128)S(1)}, u32[]{:S(2)}, u32[]{:S(2)}) collective-permute-start(f32[5,4,4,32]{3,2,1,0:T(4,128)S(1)} %pad_maximum_fusion.8), channel_id=1, source_target_pairs={{0,2},{1,3},{2,0},{3,1},{4,6},{5,7},{6,4},{7,5},{8,10},{9,11},{10,... | collective-permute-start | bytes 30728 | tf_op jit(solution)/shard_map/ppermute | solution.py:238
  55.5 7.0 %collective-permute-start.10 = (f32[5,4,4,32]{3,2,1,0:T(4,128)S(1)}, f32[5,4,4,32]{3,2,1,0:T(4,128)}, u32[]{:S(2)}, u32[]{:S(2)}) collective-permute-start(f32[5,4,4,32]{3,2,1,0:T(4,128)S(1)} %pad_maximum_fusion.8), channel_id=1, source_target_pairs={{0,1},{1,2},{2,3},{3,0},{4,5},{5,6},{6,7},{7,4},{8,9},{9,10},{10,1... | collective-permute-start | bytes 30728 | tf_op jit(solution)/shard_map/ppermute | solution.py:238
  56.4 22.9 %collective-permute-start.5 = (f32[2,8,5,64]{3,2,1,0:T(8,128)}, f32[2,8,5,64]{3,2,1,0:T(8,128)}, u32[]{:S(2)}, u32[]{:S(2)}) collective-permute-start(f32[2,8,5,64]{3,2,1,0:T(8,128)} %get-tuple-element.138), channel_id=1, source_target_pairs={{1,0},{2,1},{3,2},{5,4},{6,5},{7,6},{9,8},{10,9},{11,10},{13,12},{... | collective-permute-start | bytes 61448 | tf_op jit(solution)/shard_map/ppermute | solution.py:30
  57.7 24.8 %collective-permute-start.4 = (f32[2,8,5,64]{3,2,1,0:T(8,128)}, f32[2,8,5,64]{3,2,1,0:T(8,128)}, u32[]{:S(2)}, u32[]{:S(2)}) collective-permute-start(f32[2,8,5,64]{3,2,1,0:T(8,128)} %get-tuple-element.137), channel_id=1, source_target_pairs={{0,1},{1,2},{2,3},{4,5},{5,6},{6,7},{8,9},{9,10},{10,11},{12,13},{... | collective-permute-start | bytes 61448 | tf_op jit(solution)/shard_map/ppermute | solution.py:30
  61.3 0.6 copy-start.22
  61.9 0.6 copy-start.23
  68.4 25.2 %copy-start.12 = (f32[5,4,32,32]{3,2,1,0:T(8,128)S(1)}, f32[5,4,32,32]{3,2,1,0:T(8,128)}, u32[]{:S(2)}) copy-start(f32[5,4,32,32]{3,2,1,0:T(8,128)} %concatenate.192) | copy-start | bytes 245764
  69.4 17.3 %collective-permute-start.12 = (f32[5,4,16,32]{3,2,1,0:T(8,128)S(1)}, f32[5,4,16,32]{3,2,1,0:T(8,128)S(1)}, u32[]{:S(2)}, u32[]{:S(2)}) collective-permute-start(f32[5,4,16,32]{3,2,1,0:T(8,128)S(1)} %constant_dynamic-slice_fusion), channel_id=1, source_target_pairs={{0,8},{4,12},{8,16},{12,20},{16,24},{20,28},{1,9},{5,13},{9,17},{1... | collective-permute-start | bytes 122888 | tf_op jit(solution)/shard_map/ppermute | solution.py:30
  72.9 12.5 %collective-permute-start.11 = (f32[5,4,16,32]{3,2,1,0:T(8,128)S(1)}, f32[5,4,16,32]{3,2,1,0:T(8,128)S(1)}, u32[]{:S(2)}, u32[]{:S(2)}) collective-permute-start(f32[5,4,16,32]{3,2,1,0:T(8,128)S(1)} %constant_dynamic-slice_fusion), channel_id=1, source_target_pairs={{0,12},{4,16},{8,20},{12,24},{16,28},{1,13},{5,17},{9,21},{13,25},... | collective-permute-start | bytes 122888 | tf_op jit(solution)/shard_map/ppermute | solution.py:30
  76.4 12.3 %collective-permute-start.13 = (f32[5,4,16,32]{3,2,1,0:T(8,128)S(1)}, f32[5,4,16,32]{3,2,1,0:T(8,128)S(1)}, u32[]{:S(2)}, u32[]{:S(2)}) collective-permute-start(f32[5,4,16,32]{3,2,1,0:T(8,128)S(1)} %constant_dynamic-slice_fusion), channel_id=1, source_target_pairs={{0,4},{4,8},{8,12},{12,16},{16,20},{20,24},{24,28},{1,5},{5,9},{9,... | collective-permute-start | bytes 122888 | tf_op jit(solution)/shard_map/ppermute | solution.py:30
  79.3 14.4 %collective-permute-start.14 = (f32[5,4,16,32]{3,2,1,0:T(8,128)S(1)}, f32[5,4,16,32]{3,2,1,0:T(8,128)S(1)}, u32[]{:S(2)}, u32[]{:S(2)}) collective-permute-start(f32[5,4,16,32]{3,2,1,0:T(8,128)S(1)} %constant_dynamic-slice_fusion), channel_id=1, source_target_pairs={{4,0},{8,4},{12,8},{16,12},{20,16},{24,20},{28,24},{5,1},{9,5},{13... | collective-permute-start | bytes 122888 | tf_op jit(solution)/shard_map/ppermute | solution.py:30
  82.5 11.2 %collective-permute-start.15 = (f32[5,4,16,32]{3,2,1,0:T(8,128)S(1)}, f32[5,4,16,32]{3,2,1,0:T(8,128)S(1)}, u32[]{:S(2)}, u32[]{:S(2)}) collective-permute-start(f32[5,4,16,32]{3,2,1,0:T(8,128)S(1)} %constant_dynamic-slice_fusion), channel_id=1, source_target_pairs={{8,0},{12,4},{16,8},{20,12},{24,16},{28,20},{9,1},{13,5},{17,9},{2... | collective-permute-start | bytes 122888 | tf_op jit(solution)/shard_map/ppermute | solution.py:30
  85.4 14.4 %collective-permute-start.16 = (f32[5,4,16,32]{3,2,1,0:T(8,128)S(1)}, f32[5,4,16,32]{3,2,1,0:T(8,128)S(1)}, u32[]{:S(2)}, u32[]{:S(2)}) collective-permute-start(f32[5,4,16,32]{3,2,1,0:T(8,128)S(1)} %constant_dynamic-slice_fusion), channel_id=1, source_target_pairs={{12,0},{16,4},{20,8},{24,12},{28,16},{13,1},{17,5},{21,9},{25,13},... | collective-permute-start | bytes 122888 | tf_op jit(solution)/shard_map/ppermute | solution.py:30
  86.8 21.1 %collective-permute-start.7 = (f32[2,5,18,64]{3,2,1,0:T(8,128)}, f32[2,5,18,64]{3,2,1,0:T(8,128)}, u32[]{:S(2)}, u32[]{:S(2)}) collective-permute-start(f32[2,5,18,64]{3,2,1,0:T(8,128)} %get-tuple-element.78), channel_id=1, source_target_pairs={{4,0},{8,4},{12,8},{16,12},{20,16},{24,20},{28,24},{5,1},{9,5},{13... | collective-permute-start | bytes 138248 | tf_op jit(solution)/shard_map/ppermute | solution.py:30
  88.7 19.1 %collective-permute-start.6 = (f32[2,5,18,64]{3,2,1,0:T(8,128)}, f32[2,5,18,64]{3,2,1,0:T(8,128)}, u32[]{:S(2)}, u32[]{:S(2)}) collective-permute-start(f32[2,5,18,64]{3,2,1,0:T(8,128)} %get-tuple-element.77), channel_id=1, source_target_pairs={{0,4},{4,8},{8,12},{12,16},{16,20},{20,24},{24,28},{1,5},{5,9},{9,... | collective-permute-start | bytes 138248 | tf_op jit(solution)/shard_map/ppermute | solution.py:30
  104.8 0.6 copy-start.26
  109.0 1.3 %copy-start.4 = (f32[18,18,63]{2,1,0:T(8,128)S(1)}, f32[18,18,63]{2,1,0:T(8,128)}, u32[]{:S(2)}) copy-start(f32[18,18,63]{2,1,0:T(8,128)} %copy-done.3) | copy-start | bytes 244948
  109.0 1.3 %copy-start.7 = (f32[17,18,64]{2,1,0:T(8,128)S(1)}, f32[17,18,64]{2,1,0:T(8,128)}, u32[]{:S(2)}) copy-start(f32[17,18,64]{2,1,0:T(8,128)} %copy-done.6) | copy-start | bytes 235012
  109.0 1.3 %copy-start.9 = (f32[18,17,64]{2,1,0:T(8,128)S(1)}, f32[18,17,64]{2,1,0:T(8,128)}, u32[]{:S(2)}) copy-start(f32[18,17,64]{2,1,0:T(8,128)} %copy-done.8) | copy-start | bytes 235012
  111.7 1.4 %copy-start.28 = (s32[128]{0:T(128)S(1)}, s32[128]{0:T(128)}, u32[]{:S(2)}) copy-start(s32[128]{0:T(128)} %copy-done.27) | copy-start | bytes 1540
  114.5 1.1 copy-start.2
  114.5 1.3 %copy-start.11 = (f32[34,34,128]{2,1,0:T(8,128)S(1)}, f32[34,34,128]{2,1,0:T(8,128)}, u32[]{:S(2)}) copy-start(f32[34,34,128]{2,1,0:T(8,128)} %copy-done.10) | copy-start | bytes 1775620

commit v4 on v3

--- a/solution.py
+++ b/solution.py
@@ -39,6 +39,18 @@
             [shift_from(tail, axis, -1), cells, shift_from(head, axis, 1)], axis=dim
         )
     return cells
+
+
+def pack(pieces):
+    return jnp.concatenate([p.reshape(-1) for p in pieces])
+
+
+def unpack(flat, pieces):
+    out, at = [], 0
+    for p in pieces:
+        out.append(flat[at : at + p.size].reshape(p.shape))
+        at += p.size
+    return out
 
 
 def harmonic(first, second):
@@ -232,22 +244,50 @@
     cpack = jnp.concatenate([b2[None], coarse_own], axis=0)
     mpack = jnp.stack([win(x1, nm, x1m, 0), win(b1, nm, b1m, 0)])
     hm = MID_HALO
+    north_slab = mpack[:, :, :hm]
+    south_slab = mpack[:, :, nm - hm :]
     blocks = [cpack]
+    north = south = None
     for step in range(1, gy_count):
         pairs = [(j, (j - step) % gy_count) for j in range(gy_count)]
-        blocks.append(lax.ppermute(cpack, "gy", pairs))
-    north = shift_from(mpack[:, :, :hm], "gy", 1)
-    south = shift_from(mpack[:, :, nm - hm :], "gy", -1)
+        pieces = [cpack]
+        if step == 1:
+            pieces.append(north_slab)
+        if step == gy_count - 1:
+            pieces.append(south_slab)
+        got = unpack(lax.ppermute(pack(pieces), "gy", pairs), pieces)
+        blocks.append(got[0])
+        if step == 1:
+            north = got[1]
+        if step == gy_count - 1:
+            south = got[-1]
+    if gy_count == 1:
+        north = jnp.zeros_like(north_slab)
+        south = jnp.zeros_like(south_slab)
+    north = jnp.where(iy < gy_count - 1, north, 0.0)
+    south = jnp.where(iy > 0, south, 0.0)
     mext = jnp.concatenate([south, mpack, north], axis=2)
-    full = jnp.concatenate(blocks, axis=2)
-    full = jnp.roll(full, iy * nc, axis=2)
+    full = jnp.zeros(cpack.shape[:2] + (nc * gy_count,) + cpack.shape[3:], cpack.dtype)
+    for step, block in enumerate(blocks):
+        at = ((iy + step) % gy_count) * nc
+        full = lax.dynamic_update_slice_in_dim(full, block, at, axis=2)
     reach = 3
-    parts = [shift_from(full, "gx", -d) for d in range(reach, 0, -1)]
-    parts += [full]
-    parts += [shift_from(full, "gx", d) for d in range(1, reach + 1)]
-    cpack = jnp.concatenate(parts, axis=1)
-    west_m = shift_from(mext[:, nm - hm :], "gx", -1)
-    east_m = shift_from(mext[:, :hm], "gx", 1)
+    west_slab = mext[:, nm - hm :]
+    east_slab = mext[:, :hm]
+    before, after = [], []
+    west_m = east_m = None
+    for d in range(1, reach + 1):
+        if d == 1:
+            got = unpack(shift_from(pack([full, west_slab]), "gx", -1), [full, west_slab])
+            before.append(got[0])
+            west_m = got[1]
+            got = unpack(shift_from(pack([full, east_slab]), "gx", 1), [full, east_slab])
+            after.append(got[0])
+            east_m = got[1]
+        else:
+            before.append(shift_from(full, "gx", -d))
+            after.append(shift_from(full, "gx", d))
+    cpack = jnp.concatenate(before[::-1] + [full] + after, axis=1)
     mext = jnp.concatenate([west_m, mext, east_m], axis=1)
     source = cpack[0]
     cc = cpack[1:]

time: 119 us -> 163 us (1.37)
  the two profiles are of different devices: /device:TPU:4 before, /device:TPU:26 now
where the time goes in v4:
time: 163 us; the launch traced here: 160 us
  local copies, waits for them, and re-layouts  64.3 us (39%)
  starting transfers between devices  32.2 us (20%)
  other arithmetic  32 us (20%)
  waiting for transfers between devices  20.1 us (12%)
  Pallas kernels  5.46 us (3%)
  matrix products  5.12 us (3%)
    ppermute x10, starting transfers between devices, shift_from(): return lax.ppermute(cells, axis, pairs)  31.7 us
    ppermute x10, waiting for transfers between devices, shift_from(): return lax.ppermute(cells, axis, pairs)  16 us
    unnamed x59, local copies, waits for them, and re-layouts  11.7 us
    reshape x7, local copies, waits for them, and re-layouts, unpack(): out.append(flat[at:at + p.size].reshape(p.shape))  10.4 us
    reshape x6, local copies, waits for them, and re-layouts, pack(): return jnp.concatenate([p.reshape(-1) for p in pieces])  9.32 us
    slice x6, local copies, waits for them, and re-layouts, unpack(): out.append(flat[at:at + p.size].reshape(p.shape))  7.46 us
    add x7, other arithmetic, chebyshev(): iterate = win(iterate, n, cur, nxt) + update  5.54 us
    pallas_call x1, Pallas kernels, soil_fields(): pl.pallas_call(fields_kernel, out_shape=jax.ShapeDtypeStruct((4,) + conc....  5.46 us
  transfers between devices with their start and end apart: 13, of which 4 were waited for; matrix products, arithmetic and copies ran while one was open for 22% of the time, Pallas kernels for 0%

profile of v4, /device:TPU:26, one launch (start us, length us, event | category | flops | bytes accessed | tf_op | source)
XLA Modules:
  0.0 160.2 jit_solution(5341065370674873443)
XLA Ops:
  2.0 3.3 %collective-permute-start.1 = (f32[3,10,16,128]{3,2,1,0:T(8,128)S(1)}, f32[3,10,16,128]{3,2,1,0:T(8,128)S(1)}, u32[]{:S(2)}, u32[]{:S(2)}) collective-permute-start(f32[3,10,16,128]{3,2,1,0:T(8,128)S(1)} %get-tuple-element.51), channel_id=1, source_target_pairs={{4,0},{8,4},{12,8},{16,12},{20,16},{24,20},{28,24},{5,1},{9,5},{13... | collective-permute-start | bytes 737288 | tf_op jit(solution)/shard_map/ppermute | solution.py:30
  5.3 2.5 %collective-permute-start = (f32[3,10,16,128]{3,2,1,0:T(8,128)S(1)}, f32[3,10,16,128]{3,2,1,0:T(8,128)S(1)}, u32[]{:S(2)}, u32[]{:S(2)}) collective-permute-start(f32[3,10,16,128]{3,2,1,0:T(8,128)S(1)} %get-tuple-element.50), channel_id=1, source_target_pairs={{0,4},{4,8},{8,12},{12,16},{16,20},{20,24},{24,28},{1,5},{5,9},{9,... | collective-permute-start | bytes 737288 | tf_op jit(solution)/shard_map/ppermute | solution.py:30
  8.5 8.4 %collective-permute-done.1 = f32[3,10,16,128]{3,2,1,0:T(8,128)S(1)} collective-permute-done((f32[3,10,16,128]{3,2,1,0:T(8,128)S(1)}, f32[3,10,16,128]{3,2,1,0:T(8,128)S(1)}, u32[]{:S(2)}, u32[]{:S(2)}) %collective-permute-start.1) | collective-permute-done | bytes 245792 | tf_op jit(solution)/shard_map/ppermute | solution.py:30
  18.0 1.9 %collective-permute-start.3 = (f32[3,36,10,128]{3,1,2,0:T(8,128)S(1)}, f32[3,36,10,128]{3,1,2,0:T(8,128)S(1)}, u32[]{:S(2)}, u32[]{:S(2)}) collective-permute-start(f32[3,36,10,128]{3,1,2,0:T(8,128)S(1)} %copy.26), channel_id=1, source_target_pairs={{1,0},{2,1},{3,2},{5,4},{6,5},{7,6},{9,8},{10,9},{11,10},{13,12},{... | collective-permute-start | bytes 1658888 | tf_op jit(solution)/shard_map/ppermute | solution.py:30
  20.2 2.4 %collective-permute-start.2 = (f32[3,36,10,128]{3,1,2,0:T(8,128)S(1)}, f32[3,36,10,128]{3,1,2,0:T(8,128)S(1)}, u32[]{:S(2)}, u32[]{:S(2)}) collective-permute-start(f32[3,36,10,128]{3,1,2,0:T(8,128)S(1)} %copy.25), channel_id=1, source_target_pairs={{0,1},{1,2},{2,3},{4,5},{5,6},{6,7},{8,9},{9,10},{10,11},{12,13},{... | collective-permute-start | bytes 1658888 | tf_op jit(solution)/shard_map/ppermute | solution.py:30
  23.8 3.8 %collective-permute-done.3 = f32[3,36,10,128]{3,1,2,0:T(8,128)S(1)} collective-permute-done((f32[3,36,10,128]{3,1,2,0:T(8,128)S(1)}, f32[3,36,10,128]{3,1,2,0:T(8,128)S(1)}, u32[]{:S(2)}, u32[]{:S(2)}) %collective-permute-start.3) | collective-permute-done | bytes 552992 | tf_op jit(solution)/shard_map/ppermute | solution.py:30
  27.7 3.9 %collective-permute-done.2 = f32[3,36,10,128]{3,1,2,0:T(8,128)S(1)} collective-permute-done((f32[3,36,10,128]{3,1,2,0:T(8,128)S(1)}, f32[3,36,10,128]{3,1,2,0:T(8,128)S(1)}, u32[]{:S(2)}, u32[]{:S(2)}) %collective-permute-start.2) | collective-permute-done | bytes 552992 | tf_op jit(solution)/shard_map/ppermute | solution.py:30
  33.3 5.5 %shard_map.46 = f32[4,36,36,128]{3,2,1,0:T(8,128)} custom-call(s32[4]{0:T(128)} %pad_add_fusion.bounds_ref, f32[5,8]{1,0:T(8,128)} %table_ref.1, f32[36,36,128]{2,1,0:T(8,128)} %get-tuple-element.30.conc_ref, f32[36,36,128]{2,1,0:T(8,128)} %get-tuple-element.29.idf_ref), custom_call_target="tpu_custom_call" | custom-call | flops 16588800 | bytes 3981312 | tf_op jit(solution)/shard_map/pallas_call | solution.py:194
  38.8 1.9 %slice_bitcast_fusion.2 = (f32[36,36,128]{2,1,0:T(8,128)S(1)}, f32[36,36,128]{2,1,0:T(8,128)S(1)}, f32[36,36,128]{2,1,0:T(8,128)S(1)}) fusion(f32[4,36,36,128]{3,2,1,0:T(8,128)} %shard_map.46), kind=kLoop, calls=%fused_computation.14 | loop fusion | bytes 3981312 | tf_op jit(solution)/shard_map/squeeze | solution.py:94
  45.8 1.5 convolution_multiply_fusion
  54.8 1.5 reshape.366
  56.2 1.5 pad_maximum_fusion.9
  57.7 1.5 reshape.370
  59.3 1.5 reshape.367
  60.8 1.4 pad_maximum_fusion.10
  62.7 4.0 %collective-permute-done.5 = f32[2560]{0:T(1024)} collective-permute-done((f32[2560]{0:T(1024)}, f32[2560]{0:T(1024)}, u32[]{:S(2)}, u32[]{:S(2)}) %collective-permute-start.5) | collective-permute-done | bytes 10272 | tf_op jit(solution)/shard_map/ppermute | solution.py:258
  66.7 1.4 reshape.369
  69.4 1.4 reshape.368
  72.1 1.4 reshape.371
  73.5 1.4 constant_dynamic-update-slice_fusion.14
  74.9 1.4 constant_dynamic-update-slice_fusion.13
  76.3 1.4 constant_dynamic-update-slice_fusion.12
  80.3 1.6 %reshape.372 = f32[10240]{0:T(1024)} reshape(f32[5,4,16,32]{3,2,1,0:T(8,128)} %constant_dynamic-update-slice_fusion.12) | data formatting | bytes 81920 | tf_op jit(solution)/shard_map/reshape | solution.py:45
  82.0 5.9 %collective-permute-start.11 = (f32[5,4,16,32]{3,2,1,0:T(8,128)}, f32[5,4,16,32]{3,2,1,0:T(8,128)}, u32[]{:S(2)}, u32[]{:S(2)}) collective-permute-start(f32[5,4,16,32]{3,2,1,0:T(8,128)} %constant_dynamic-update-slice_fusion.12), channel_id=1, source_target_pairs={{8,0},{12,4},{16,8},{20,12},{24,16},{28,20},{9,1},{13,5},{17,9},{2... | collective-permute-start | bytes 122888 | tf_op jit(solution)/shard_map/ppermute | solution.py:30
  87.8 6.3 %collective-permute-start.12 = (f32[5,4,16,32]{3,2,1,0:T(8,128)}, f32[5,4,16,32]{3,2,1,0:T(8,128)}, u32[]{:S(2)}, u32[]{:S(2)}) collective-permute-start(f32[5,4,16,32]{3,2,1,0:T(8,128)} %constant_dynamic-update-slice_fusion.12), channel_id=1, source_target_pairs={{12,0},{16,4},{20,8},{24,12},{28,16},{13,1},{17,5},{21,9},{25,13},... | collective-permute-start | bytes 122888 | tf_op jit(solution)/shard_map/ppermute | solution.py:30
  95.5 1.4 select_n.164
  98.3 1.4 select_n.161
  101.4 1.6 reshape.375
  103.0 1.6 reshape.373
  104.6 1.5 pad_maximum_fusion.5
  106.1 2.0 %collective-permute-start.7 = (f32[21760]{0:T(1024)S(1)}, f32[21760]{0:T(1024)S(1)}, u32[]{:S(2)}, u32[]{:S(2)}) collective-permute-start(f32[21760]{0:T(1024)S(1)} %get-tuple-element.140), channel_id=1, source_target_pairs={{0,4},{4,8},{8,12},{12,16},{16,20},{20,24},{24,28},{1,5},{5,9},{9,... | collective-permute-start | bytes 261128 | tf_op jit(solution)/shard_map/ppermute | solution.py:30
  108.0 4.8 %collective-permute-start.8 = (f32[21760]{0:T(1024)}, f32[21760]{0:T(1024)}, u32[]{:S(2)}, u32[]{:S(2)}) collective-permute-start(f32[21760]{0:T(1024)} %get-tuple-element.139), channel_id=1, source_target_pairs={{4,0},{8,4},{12,8},{16,12},{20,16},{24,20},{28,24},{5,1},{9,5},{13... | collective-permute-start | bytes 261128 | tf_op jit(solution)/shard_map/ppermute | solution.py:30
  112.8 1.6 constant_dynamic-update-slice_fusion.6
  114.4 1.7 %constant_dynamic-update-slice_fusion.11 = (f32[5,20,16,32]{3,2,1,0:T(8,128)}, f32[5,28,16,32]{3,2,1,0:T(8,128)}) fusion(f32[5,4,16,32]{3,2,1,0:T(8,128)} %collective-permute-done.10, f32[5,28,16,32]{3,2,1,0:T(8,128)} %constant_dynamic-update-slice_fusion.6), kind=kLoop, calls=%fused_computation.593 | loop fusion | bytes 491520
  117.3 1.5 reshape.377
  118.9 1.4 slice.2102
  120.3 1.5 reshape.378
  121.8 1.7 %constant_dynamic-update-slice_fusion.10 = (f32[5,20,16,32]{3,2,1,0:T(8,128)}, f32[5,28,16,32]{3,2,1,0:T(8,128)}) fusion(f32[5,20,16,32]{3,2,1,0:T(8,128)} %get-tuple-element.99, f32[5,4,16,32]{3,2,1,0:T(8,128)} %reshape.377, f32[5,28,16,32]{3,2,1,0:T(8,128)} %get-tuple-element.100), kind=kLoop, calls=%fused_computation.592 | loop fusion | bytes 491520
  123.5 1.7 %constant_dynamic-update-slice_fusion.9 = (f32[5,20,16,32]{3,2,1,0:T(8,128)}, f32[5,28,16,32]{3,2,1,0:T(8,128)}) fusion(f32[5,20,16,32]{3,2,1,0:T(8,128)} %get-tuple-element.97, f32[5,4,16,32]{3,2,1,0:T(8,128)} %constant_dynamic-update-slice_fusion.12, f32[5,28,16,32]{3,2,1,0:T(8,128)} %get-tuple-element.98), kind=kLoop, calls=%fused_computation.591 | loop fusion | bytes 491520
  125.2 1.7 %constant_dynamic-update-slice_fusion.8 = (f32[5,20,16,32]{3,2,1,0:T(8,128)}, f32[5,28,16,32]{3,2,1,0:T(8,128)}) fusion(f32[5,20,16,32]{3,2,1,0:T(8,128)} %get-tuple-element.95, f32[5,4,16,32]{3,2,1,0:T(8,128)} %reshape.378, f32[5,28,16,32]{3,2,1,0:T(8,128)} %get-tuple-element.96), kind=kLoop, calls=%fused_computation.590 | loop fusion | bytes 491520
  126.9 1.7 %constant_dynamic-update-slice_fusion.7 = (f32[5,20,16,32]{3,2,1,0:T(8,128)}, f32[5,28,16,32]{3,2,1,0:T(8,128)}) fusion(f32[5,20,16,32]{3,2,1,0:T(8,128)} %get-tuple-element.93, f32[5,4,16,32]{3,2,1,0:T(8,128)} %collective-permute-done.11, f32[5,28,16,32]{3,2,1,0:T(8,128)} %get-tuple-element.94), kind=kLoop, calls=%fused_computation.589 | loop fusion | bytes 491520 | tf_op jit(solution)/shard_map/concatenate | solution.py:290
  128.6 1.6 %constant_dynamic-update-slice_fusion = f32[5,28,16,32]{3,2,1,0:T(8,128)} fusion(f32[5,28,16,32]{3,2,1,0:T(8,128)} %get-tuple-element.92, f32[5,4,16,32]{3,2,1,0:T(8,128)} %collective-permute-done.12), kind=kLoop, calls=%fused_computation.582 | loop fusion | bytes 327680 | tf_op jit(solution)/shard_map/concatenate | solution.py:290
  134.3 1.5 multiply_add_fusion
  142.4 1.6 %broadcast_in_dim.105 = f32[10,20,64]{2,1,0:T(8,128)} reshape(f32[10,10,2,64]{3,2,1,0:T(2,128)} %broadcast_in_dim.104) | data formatting | bytes 102400 | tf_op jit(solution)/shard_map/broadcast_in_dim | solution.py:89
  144.0 1.4 slice.2099
  145.4 1.5 reshape.376
  147.0 1.4 slice.2097
  148.4 1.5 reshape.374
  (200 shorter events, 51.1 us)
Async XLA Ops:
  0.0 17.6 %copy-start.14 = (f32[16,16,128]{2,1,0:T(8,128)S(1)}, f32[16,16,128]{2,1,0:T(8,128)}, u32[]{:S(2)}) copy-start(f32[16,16,128]{2,1,0:T(8,128)} %param.5) | copy-start | bytes 393220
  0.0 17.6 %copy-start.15 = (f32[16,16,128]{2,1,0:T(8,128)S(1)}, f32[16,16,128]{2,1,0:T(8,128)}, u32[]{:S(2)}) copy-start(f32[16,16,128]{2,1,0:T(8,128)} %param.4) | copy-start | bytes 393220
  2.0 14.9 %collective-permute-start.1 = (f32[3,10,16,128]{3,2,1,0:T(8,128)S(1)}, f32[3,10,16,128]{3,2,1,0:T(8,128)S(1)}, u32[]{:S(2)}, u32[]{:S(2)}) collective-permute-start(f32[3,10,16,128]{3,2,1,0:T(8,128)S(1)} %get-tuple-element.51), channel_id=1, source_target_pairs={{4,0},{8,4},{12,8},{16,12},{20,16},{24,20},{28,24},{5,1},{9,5},{13... | collective-permute-start | bytes 737288 | tf_op jit(solution)/shard_map/ppermute | solution.py:30
  5.3 11.5 %collective-permute-start = (f32[3,10,16,128]{3,2,1,0:T(8,128)S(1)}, f32[3,10,16,128]{3,2,1,0:T(8,128)S(1)}, u32[]{:S(2)}, u32[]{:S(2)}) collective-permute-start(f32[3,10,16,128]{3,2,1,0:T(8,128)S(1)} %get-tuple-element.50), channel_id=1, source_target_pairs={{0,4},{4,8},{8,12},{12,16},{16,20},{20,24},{24,28},{1,5},{5,9},{9,... | collective-permute-start | bytes 737288 | tf_op jit(solution)/shard_map/ppermute | solution.py:30
  7.9 42.3 %copy-start.25 = (s32[128]{0:T(128)}, s32[128]{0:T(128)S(1)}, u32[]{:S(2)}) copy-start(s32[128]{0:T(128)S(1)} %and_select_fusion.2) | copy-start | bytes 1540
  16.9 1.0 copy-start.16
  16.9 0.7 copy-start.18
  18.0 9.6 %collective-permute-start.3 = (f32[3,36,10,128]{3,1,2,0:T(8,128)S(1)}, f32[3,36,10,128]{3,1,2,0:T(8,128)S(1)}, u32[]{:S(2)}, u32[]{:S(2)}) collective-permute-start(f32[3,36,10,128]{3,1,2,0:T(8,128)S(1)} %copy.26), channel_id=1, source_target_pairs={{1,0},{2,1},{3,2},{5,4},{6,5},{7,6},{9,8},{10,9},{11,10},{13,12},{... | collective-permute-start | bytes 1658888 | tf_op jit(solution)/shard_map/ppermute | solution.py:30
  20.2 11.5 %collective-permute-start.2 = (f32[3,36,10,128]{3,1,2,0:T(8,128)S(1)}, f32[3,36,10,128]{3,1,2,0:T(8,128)S(1)}, u32[]{:S(2)}, u32[]{:S(2)}) collective-permute-start(f32[3,36,10,128]{3,1,2,0:T(8,128)S(1)} %copy.25), channel_id=1, source_target_pairs={{0,1},{1,2},{2,3},{4,5},{5,6},{6,7},{8,9},{9,10},{10,11},{12,13},{... | collective-permute-start | bytes 1658888 | tf_op jit(solution)/shard_map/ppermute | solution.py:30
  23.8 7.9 %copy-start.17 = (f32[3,10,16,128]{3,2,1,0:T(8,128)S(1)}, f32[3,10,16,128]{3,2,1,0:T(8,128)}, u32[]{:S(2)}) copy-start(f32[3,10,16,128]{3,2,1,0:T(8,128)} %copy-done.16) | copy-start | bytes 737284
  23.8 8.0 %copy-start.19 = (f32[3,10,16,128]{3,2,1,0:T(8,128)S(1)}, f32[3,10,16,128]{3,2,1,0:T(8,128)}, u32[]{:S(2)}) copy-start(f32[3,10,16,128]{3,2,1,0:T(8,128)} %copy-done.18) | copy-start | bytes 737284
  38.8 2.5 %copy-start = (f32[4,36,36,128]{3,2,1,0:T(8,128)S(1)}, f32[4,36,36,128]{3,2,1,0:T(8,128)}, u32[]{:S(2)}) copy-start(f32[4,36,36,128]{3,2,1,0:T(8,128)} %shard_map.46) | copy-start | bytes 7962628
  41.3 8.0 %copy-start.1 = (f32[36,36,128]{2,1,0:T(8,128)}, f32[36,36,128]{2,1,0:T(8,128)S(1)}, u32[]{:S(2)}) copy-start(f32[36,36,128]{2,1,0:T(8,128)S(1)} %get-tuple-element.27) | copy-start | bytes 1990660
  42.7 5.0 %copy-start.10 = (f32[34,34,128]{2,1,0:T(8,128)}, f32[34,34,128]{2,1,0:T(8,128)S(1)}, u32[]{:S(2)}) copy-start(f32[34,34,128]{2,1,0:T(8,128)S(1)} %get-tuple-element.25) | copy-start | bytes 1775620
  47.3 4.9 %copy-start.5 = (f32[72,18,64]{2,1,0:T(8,128)}, f32[72,18,64]{2,1,0:T(8,128)S(1)}, u32[]{:S(2)}) copy-start(f32[72,18,64]{2,1,0:T(8,128)S(1)} %convolution_multiply_fusion) | copy-start | bytes 995332
  47.4 4.8 %copy-start.8 = (f32[18,17,64]{2,1,0:T(8,128)}, f32[18,17,64]{2,1,0:T(8,128)S(1)}, u32[]{:S(2)}) copy-start(f32[18,17,64]{2,1,0:T(8,128)S(1)} %divide_multiply_fusion.1) | copy-start | bytes 235012
  47.5 4.7 %copy-start.6 = (f32[17,18,64]{2,1,0:T(8,128)}, f32[17,18,64]{2,1,0:T(8,128)S(1)}, u32[]{:S(2)}) copy-start(f32[17,18,64]{2,1,0:T(8,128)S(1)} %multiply_bitcast_fusion) | copy-start | bytes 235012
  47.6 4.6 %copy-start.3 = (f32[18,18,63]{2,1,0:T(8,128)}, f32[18,18,63]{2,1,0:T(8,128)S(1)}, u32[]{:S(2)}) copy-start(f32[18,18,63]{2,1,0:T(8,128)S(1)} %divide_multiply_fusion) | copy-start | bytes 244948
  49.3 1.3 copy-start.22
  51.3 0.7 copy-start.23
  62.2 5.9 %collective-permute-start.4 = (f32[7680]{0:T(1024)}, f32[7680]{0:T(1024)}, u32[]{:S(2)}, u32[]{:S(2)}) collective-permute-start(f32[7680]{0:T(1024)} %get-tuple-element.148), channel_id=1, source_target_pairs={{0,3},{1,0},{2,1},{3,2},{4,7},{5,4},{6,5},{7,6},{8,11},{9,8},{10,9... | collective-permute-start | bytes 92168 | tf_op jit(solution)/shard_map/ppermute | solution.py:258
  62.2 8.6 %collective-permute-start.6 = (f32[7680]{0:T(1024)}, f32[7680]{0:T(1024)}, u32[]{:S(2)}, u32[]{:S(2)}) collective-permute-start(f32[7680]{0:T(1024)} %get-tuple-element.147), channel_id=1, source_target_pairs={{0,1},{1,2},{2,3},{3,0},{4,5},{5,6},{6,7},{7,4},{8,9},{9,10},{10,1... | collective-permute-start | bytes 92168 | tf_op jit(solution)/shard_map/ppermute | solution.py:258
  62.7 4.0 %collective-permute-start.5 = (f32[2560]{0:T(1024)}, f32[2560]{0:T(1024)}, u32[]{:S(2)}, u32[]{:S(2)}) collective-permute-start(f32[2560]{0:T(1024)} %reshape.366), channel_id=1, source_target_pairs={{0,2},{1,3},{2,0},{3,1},{4,6},{5,7},{6,4},{7,5},{8,10},{9,11},{10,... | collective-permute-start | bytes 30728 | tf_op jit(solution)/shard_map/ppermute | solution.py:258
  77.7 36.7 %collective-permute-start.10 = (f32[5,4,16,32]{3,2,1,0:T(8,128)}, f32[5,4,16,32]{3,2,1,0:T(8,128)}, u32[]{:S(2)}, u32[]{:S(2)}) collective-permute-start(f32[5,4,16,32]{3,2,1,0:T(8,128)} %constant_dynamic-update-slice_fusion.12), channel_id=1, source_target_pairs={{0,8},{4,12},{8,16},{12,20},{16,24},{20,28},{1,9},{5,13},{9,17},{1... | collective-permute-start | bytes 122888 | tf_op jit(solution)/shard_map/ppermute | solution.py:30
  79.0 29.0 %collective-permute-start.9 = (f32[5,4,16,32]{3,2,1,0:T(8,128)}, f32[5,4,16,32]{3,2,1,0:T(8,128)}, u32[]{:S(2)}, u32[]{:S(2)}) collective-permute-start(f32[5,4,16,32]{3,2,1,0:T(8,128)} %constant_dynamic-update-slice_fusion.12), channel_id=1, source_target_pairs={{0,12},{4,16},{8,20},{12,24},{16,28},{1,13},{5,17},{9,21},{13,25},... | collective-permute-start | bytes 122888 | tf_op jit(solution)/shard_map/ppermute | solution.py:30
  82.0 44.9 %collective-permute-start.11 = (f32[5,4,16,32]{3,2,1,0:T(8,128)}, f32[5,4,16,32]{3,2,1,0:T(8,128)}, u32[]{:S(2)}, u32[]{:S(2)}) collective-permute-start(f32[5,4,16,32]{3,2,1,0:T(8,128)} %constant_dynamic-update-slice_fusion.12), channel_id=1, source_target_pairs={{8,0},{12,4},{16,8},{20,12},{24,16},{28,20},{9,1},{13,5},{17,9},{2... | collective-permute-start | bytes 122888 | tf_op jit(solution)/shard_map/ppermute | solution.py:30
  87.8 40.7 %collective-permute-start.12 = (f32[5,4,16,32]{3,2,1,0:T(8,128)}, f32[5,4,16,32]{3,2,1,0:T(8,128)}, u32[]{:S(2)}, u32[]{:S(2)}) collective-permute-start(f32[5,4,16,32]{3,2,1,0:T(8,128)} %constant_dynamic-update-slice_fusion.12), channel_id=1, source_target_pairs={{12,0},{16,4},{20,8},{24,12},{28,16},{13,1},{17,5},{21,9},{25,13},... | collective-permute-start | bytes 122888 | tf_op jit(solution)/shard_map/ppermute | solution.py:30
  106.1 10.0 %collective-permute-start.7 = (f32[21760]{0:T(1024)S(1)}, f32[21760]{0:T(1024)S(1)}, u32[]{:S(2)}, u32[]{:S(2)}) collective-permute-start(f32[21760]{0:T(1024)S(1)} %get-tuple-element.140), channel_id=1, source_target_pairs={{0,4},{4,8},{8,12},{12,16},{16,20},{20,24},{24,28},{1,5},{5,9},{9,... | collective-permute-start | bytes 261128 | tf_op jit(solution)/shard_map/ppermute | solution.py:30
  108.0 10.8 %collective-permute-start.8 = (f32[21760]{0:T(1024)}, f32[21760]{0:T(1024)}, u32[]{:S(2)}, u32[]{:S(2)}) collective-permute-start(f32[21760]{0:T(1024)} %get-tuple-element.139), channel_id=1, source_target_pairs={{4,0},{8,4},{12,8},{16,12},{20,16},{24,20},{28,24},{5,1},{9,5},{13... | collective-permute-start | bytes 261128 | tf_op jit(solution)/shard_map/ppermute | solution.py:30
  116.1 0.6 copy-start.21
  128.6 4.4 %copy-start.12 = (f32[5,4,16,32]{3,2,1,0:T(8,128)S(1)}, f32[5,4,16,32]{3,2,1,0:T(8,128)}, u32[]{:S(2)}) copy-start(f32[5,4,16,32]{3,2,1,0:T(8,128)} %reshape.377) | copy-start | bytes 122884
  128.6 4.4 %copy-start.13 = (f32[5,4,16,32]{3,2,1,0:T(8,128)S(1)}, f32[5,4,16,32]{3,2,1,0:T(8,128)}, u32[]{:S(2)}) copy-start(f32[5,4,16,32]{3,2,1,0:T(8,128)} %reshape.378) | copy-start | bytes 122884
  137.7 1.5 copy-start.20
  140.9 0.7 copy-start.24
  151.0 1.3 copy-start.4
  151.0 1.3 copy-start.7
  151.0 1.3 copy-start.9
  153.8 1.4 copy-start.26
  156.5 1.1 copy-start.2
  156.5 1.3 copy-start.11

commit v5 on v3

--- a/solution.py
+++ b/solution.py
@@ -73,7 +73,8 @@
 def prolong(values):
     sx, sy, sz = values.shape
     v = jnp.einsum("xyz,wz->xyw", values, pair_matrix(2 * sz), precision=HIGH)
-    v = jnp.repeat(v, 2, axis=1)
+    pick = jnp.broadcast_to(pair_matrix(2 * sy), (sx, 2 * sy, sy))
+    v = lax.dot_general(pick, v, (((2,), (1,)), ((0,), (0,))), precision=HIGH)
     v = jnp.broadcast_to(v[:, None], (sx, 2) + v.shape[1:]).reshape((2 * sx,) + v.shape[1:])
     return v
 
@@ -240,7 +241,6 @@
     south = shift_from(mpack[:, :, nm - hm :], "gy", -1)
     mext = jnp.concatenate([south, mpack, north], axis=2)
     full = jnp.concatenate(blocks, axis=2)
-    full = jnp.roll(full, iy * nc, axis=2)
     reach = 3
     parts = [shift_from(full, "gx", -d) for d in range(reach, 0, -1)]
     parts += [full]
@@ -255,41 +255,51 @@
     line_store = jnp.sum(cc[3], axis=1)
     line_mean = jnp.where(line_store > 0, line_total / jnp.where(line_store > 0, line_store, 1.0), 0.0)
     width = source.shape[0]
-    ccp = jnp.pad(cc, ((0, 0), (0, 0), (1, 1), (0, 0)))
-    kx_, ky_, kz_, st_ = ccp[0], ccp[1], ccp[2], ccp[3]
+    lines = source.shape[1]
+    gline = (iy * nc + jnp.arange(lines)) % lines
+    kx_, ky_, kz_, st_ = cc[0], cc[1], cc[2], cc[3]
     q = 0.0625
-    cx = kx_[1:-1, 1:-1]
-    cy = ky_[1:-1, 1:-1]
-    cz = kz_[1:-1, 1:-1]
-    east = harmonic(kx_[2:, 1:-1], cx) * q
-    west = harmonic(kx_[:-2, 1:-1], cx) * q
-    north = harmonic(ky_[1:-1, 2:], cy) * q
-    south = harmonic(ky_[1:-1, :-2], cy) * q
+    cx = kx_[1:-1]
+    cy = ky_[1:-1]
+    cz = kz_[1:-1]
+    east = harmonic(kx_[2:], cx) * q
+    west = harmonic(kx_[:-2], cx) * q
+    north = harmonic(jnp.roll(cy, -1, axis=1), cy) * q
+    north = jnp.where((gline != lines - 1)[None, :, None], north, 0.0)
+    south = jnp.roll(north, 1, axis=1)
     vert = harmonic(cz[:, :, 1:], cz[:, :, :-1]) * q
     closed = jnp.zeros_like(cz[:, :, :1])
     above = jnp.concatenate([vert, closed], axis=2)
     below = jnp.concatenate([closed, vert], axis=2)
-    cst = st_[1:-1, 1:-1]
+    cst = st_[1:-1]
     cdiag = jnp.maximum(cst + east + west + north + south + above + below, 0.01)
     csrc = source[1:-1]
     u = jnp.broadcast_to(line_mean[:, None, :], source.shape)
     for sweep in range(COARSE_SWEEPS):
         lo = sweep
-        up = jnp.pad(u, ((0, 0), (1, 1), (0, 0)))
-        centre = up[1:-1, 1:-1]
+        centre = u[1:-1]
         sl = slice(lo, width - 2 - lo)
         upper = jnp.concatenate([centre[:, :, 1:], centre[:, :, :1]], axis=2)
         lower = jnp.concatenate([centre[:, :, -1:], centre[:, :, :-1]], axis=2)
-        fl = east[sl] * (centre - up[2:, 1:-1]) + west[sl] * (centre - up[:-2, 1:-1])
-        fl = fl + north[sl] * (centre - up[1:-1, 2:]) + south[sl] * (centre - up[1:-1, :-2])
+        fl = east[sl] * (centre - u[2:]) + west[sl] * (centre - u[:-2])
+        fl = fl + north[sl] * (centre - jnp.roll(centre, -1, axis=1))
+        fl = fl + south[sl] * (centre - jnp.roll(centre, 1, axis=1))
         fl = fl + above[sl] * (centre - upper) + below[sl] * (centre - lower)
         applied = cst[sl] * centre + fl
         u = centre + jacobi_weight * ((csrc[sl] - applied) / cdiag[sl])
     um = (hm + 1) // 2
     have = reach * nc - COARSE_SWEEPS
     u = u[have - um : u.shape[0] - (have - um)]
-    u = jnp.pad(u, ((0, 0), (um, um), (0, 0)))
-    u = lax.dynamic_slice_in_dim(u, iy * nc, nc + 2 * um, 1)
+    rows = [(k % lines) for k in range(-um, nc + um)]
+    runs = []
+    for r in rows:
+        if runs and runs[-1][1] == r:
+            runs[-1][1] = r + 1
+        else:
+            runs.append([r, r + 1])
+    u = jnp.concatenate([u[:, a:b] for a, b in runs], axis=1)
+    kept = iy * nc + jnp.arange(-um, nc + um)
+    u = jnp.where(((kept >= 0) & (kept < lines))[None, :, None], u, 0.0)
     s1e = win(mext[0], nm, hm, hm) + win(prolong(u), nm, 2 * um, hm)
     b1e = mext[1]
     y1, y1m = chebyshev(b1e, hm, s1e, hm, mid)

time: 119 us -> 103 us (0.87)
  local copies, waits for them, and re-layouts: 24.7 us -> 10.7 us
  other arithmetic: 19.8 us -> 14.5 us
  waiting for transfers between devices: 14.7 us -> 17.1 us
    concatenate x1 -> x0, local copies, waits for them, and re-layouts: 5.87 us -> none  [local(): full = jnp.roll(full, iy * nc, axis=2)]
    unnamed x63 -> x14, local copies, waits for them, and re-layouts: 4.66 us -> 1.43 us
    broadcast_in_dim x2 -> x1, local copies, waits for them, and re-layouts: 2.6 us -> 0.02 us  [prolong(): jnp.broadcast_to(v[:, None], (sx, 2) + v.shape[1:])]
    ppermute x14, waiting for transfers between devices: 14.7 us -> 17.1 us  [shift_from(): return lax.ppermute(cells, axis, pairs)]
    ppermute x3, starting transfers between devices: 8.81 us -> 10.6 us  [local(): blocks.append(lax.ppermute(cpack, 'gy', pairs))]
  transfers between devices with their start and end apart: 17 -> 17, of which waited for: 4 -> 4; matrix products, arithmetic and copies ran while one was open for 16% -> 7% of each run, Pallas kernels for 0% -> 0%
where the time goes in v5:
time: 103 us; the launch traced here: 102 us
  starting transfers between devices  48.1 us (47%)
  waiting for transfers between devices  17.1 us (17%)
  other arithmetic  14.5 us (14%)
  local copies, waits for them, and re-layouts  10.7 us (10%)
  Pallas kernels  5.47 us (5%)
  matrix products  5.17 us (5%)
  between operations  1.18 us (1%)
    ppermute x14, starting transfers between devices, shift_from(): return lax.ppermute(cells, axis, pairs)  37.5 us
    ppermute x14, waiting for transfers between devices, shift_from(): return lax.ppermute(cells, axis, pairs)  17.1 us
    ppermute x3, starting transfers between devices, local(): blocks.append(lax.ppermute(cpack, 'gy', pairs))  10.6 us
    pallas_call x1, Pallas kernels, soil_fields(): pl.pallas_call(fields_kernel, out_shape=jax.ShapeDtypeStruct((4,) + conc....  5.47 us
    add x7, other arithmetic, chebyshev(): iterate = win(iterate, n, cur, nxt) + update  4.56 us
    add x8, other arithmetic, local(): u = centre + jacobi_weight * ((csrc[sl] - applied) / cdiag[sl])  2.49 us
    dot_general x4, matrix products, coarsen(): lax.dot_general(pick, rows, (((2,), (1,)), ((0,), (0,))), precision=HIGH)  2.25 us
  transfers between devices with their start and end apart: 17, of which 4 were waited for; matrix products, arithmetic and copies ran while one was open for 7% of the time, Pallas kernels for 0%

profile of v5, /device:TPU:4, one launch (start us, length us, event | category | flops | bytes accessed | tf_op | source)
XLA Modules:
  0.0 102.2 jit_solution(10335162208743763347)
XLA Ops:
  0.0 1.0 convert_bitcast_fusion
  1.0 1.0 pad_maximum_fusion.4
  2.0 1.9 %collective-permute-start.1 = (f32[3,10,16,128]{3,2,1,0:T(8,128)S(1)}, f32[3,10,16,128]{3,2,1,0:T(8,128)S(1)}, u32[]{:S(2)}, u32[]{:S(2)}) collective-permute-start(f32[3,10,16,128]{3,2,1,0:T(8,128)S(1)} %get-tuple-element.49), channel_id=1, source_target_pairs={{4,0},{8,4},{12,8},{16,12},{20,16},{24,20},{28,24},{5,1},{9,5},{13... | collective-permute-start | bytes 737288 | tf_op jit(solution)/shard_map/ppermute | solution.py:30
  4.0 4.8 %collective-permute-start = (f32[3,10,16,128]{3,2,1,0:T(8,128)S(1)}, f32[3,10,16,128]{3,2,1,0:T(8,128)S(1)}, u32[]{:S(2)}, u32[]{:S(2)}) collective-permute-start(f32[3,10,16,128]{3,2,1,0:T(8,128)S(1)} %get-tuple-element.48), channel_id=1, source_target_pairs={{0,4},{4,8},{8,12},{12,16},{16,20},{20,24},{24,28},{1,5},{5,9},{9,... | collective-permute-start | bytes 737288 | tf_op jit(solution)/shard_map/ppermute | solution.py:30
  8.9 3.7 %collective-permute-done.1 = f32[3,10,16,128]{3,2,1,0:T(8,128)S(1)} collective-permute-done((f32[3,10,16,128]{3,2,1,0:T(8,128)S(1)}, f32[3,10,16,128]{3,2,1,0:T(8,128)S(1)}, u32[]{:S(2)}, u32[]{:S(2)}) %collective-permute-start.1) | collective-permute-done | bytes 245792 | tf_op jit(solution)/shard_map/ppermute | solution.py:30
  12.6 5.2 %collective-permute-done = f32[3,10,16,128]{3,2,1,0:T(8,128)S(1)} collective-permute-done((f32[3,10,16,128]{3,2,1,0:T(8,128)S(1)}, f32[3,10,16,128]{3,2,1,0:T(8,128)S(1)}, u32[]{:S(2)}, u32[]{:S(2)}) %collective-permute-start) | collective-permute-done | bytes 245792 | tf_op jit(solution)/shard_map/ppermute | solution.py:30
  17.8 0.7 copy-done.3
  18.9 1.3 %collective-permute-start.3 = (f32[3,36,10,128]{3,1,2,0:T(8,128)S(1)}, f32[3,36,10,128]{3,1,2,0:T(8,128)S(1)}, u32[]{:S(2)}, u32[]{:S(2)}) collective-permute-start(f32[3,36,10,128]{3,1,2,0:T(8,128)S(1)} %copy.20), channel_id=1, source_target_pairs={{1,0},{2,1},{3,2},{5,4},{6,5},{7,6},{9,8},{10,9},{11,10},{13,12},{... | collective-permute-start | bytes 1658888 | tf_op jit(solution)/shard_map/ppermute | solution.py:30
  20.4 3.1 %collective-permute-start.2 = (f32[3,36,10,128]{3,1,2,0:T(8,128)S(1)}, f32[3,36,10,128]{3,1,2,0:T(8,128)S(1)}, u32[]{:S(2)}, u32[]{:S(2)}) collective-permute-start(f32[3,36,10,128]{3,1,2,0:T(8,128)S(1)} %copy.19), channel_id=1, source_target_pairs={{0,1},{1,2},{2,3},{4,5},{5,6},{6,7},{8,9},{9,10},{10,11},{12,13},{... | collective-permute-start | bytes 1658888 | tf_op jit(solution)/shard_map/ppermute | solution.py:30
  23.4 0.7 pad_add_fusion.bounds_ref
  24.3 0.8 collective-permute-done.2
  25.5 1.3 %slice_bitcast_fusion.3 = (f32[36,36,128]{2,1,0:T(8,128)}, f32[36,36,128]{2,1,0:T(8,128)}, f32[36,36,128]{2,1,0:T(8,128)S(1)}) fusion(f32[3,36,36,128]{3,2,1,0:T(8,128)S(1)} %pad_maximum_fusion), kind=kLoop, calls=%fused_computation.19 | loop fusion | bytes 3981312 | tf_op jit(solution)/shard_map/squeeze | solution.py:210
  26.7 5.5 %shard_map.46 = f32[4,36,36,128]{3,2,1,0:T(8,128)} custom-call(s32[4]{0:T(128)} %pad_add_fusion.bounds_ref, f32[5,8]{1,0:T(8,128)} %table_ref.1, f32[36,36,128]{2,1,0:T(8,128)} %get-tuple-element.27.conc_ref, f32[36,36,128]{2,1,0:T(8,128)} %get-tuple-element.26.idf_ref), custom_call_target="tpu_custom_call" | custom-call | flops 16588800 | bytes 3981312 | tf_op jit(solution)/shard_map/pallas_call | solution.py:183
  32.2 1.9 %slice_bitcast_fusion.2 = (f32[36,36,128]{2,1,0:T(8,128)S(1)}, f32[36,36,128]{2,1,0:T(8,128)S(1)}, f32[36,36,128]{2,1,0:T(8,128)S(1)}) fusion(f32[4,36,36,128]{3,2,1,0:T(8,128)} %shard_map.46), kind=kLoop, calls=%fused_computation.18 | loop fusion | bytes 3981312 | tf_op jit(solution)/shard_map/squeeze | solution.py:83
  34.1 0.6 copy-done
  35.4 0.7 fusion.4
  36.5 1.2 %slice_add_fusion.5 = (f32[32,32,128]{2,1,0:T(8,128)S(1)}, f32[32,32,128]{2,1,0:T(8,128)S(1)}) fusion(f32[34,34,128]{2,1,0:T(8,128)S(1)} %get-tuple-element.21, f32[34,34,128]{2,1,0:T(8,128)S(1)} %get-tuple-element.22, f32[32,32,127]{2,1,0:T(8,128)S(1)} %get-tuple-element.37, f32[32,32,1]{2,1,0:T(8,128)S(1)} %get-tuple-element.39, ...), kind=kLoop, calls=%fused_computation.57 | loop fusion | flops 3538944 | bytes 9046976 | tf_op jit(solution)/shard_map/add | solution.py:147
  38.3 0.8 fusion.336
  39.1 1.5 %convolution_multiply_fusion = f32[72,18,64]{2,1,0:T(8,128)S(1)} fusion(f32[72,36,64]{2,1,0:T(8,128)S(1)} %fusion.336, f32[18,36]{1,0:T(8,128)S(1)} %fusion.357), kind=kOutput, calls=%fused_computation.2 | convolution fusion | flops 35914752 | bytes 997920 | tf_op jit(solution)/shard_map/dot_general | solution.py:68
  40.9 1.2 %fusion.22 = f32[30,30,128]{2,1,0:T(8,128)S(1)} fusion(f32[34,34,128]{2,1,0:T(8,128)S(1)} %get-tuple-element.22, f32[32,32,128]{2,1,0:T(8,128)S(1)} %get-tuple-element.19, f32[36,35,128]{2,1,0:T(8,128)S(1)} %maximum_divide_fusion.1, f32[35,36,128]{2,1,0:T(8,128)S(1)} %divide_bitcast_fusion, f32[36,36,128]{2,1,0:T(8,128)S(1)} %get-tuple-element.24, ...), kind=kLoop, calls=%fused_computation.61 | loop fusion | flops 3110400 | bytes 8031168 | tf_op jit(solution)/shard_map/add | solution.py:147
  42.5 0.9 fusion.40
  43.8 0.3 divide_multiply_fusion.3
  46.0 6.7 %collective-permute-start.10 = (f32[5,4,4,32]{3,2,1,0:T(4,128)S(1)}, f32[5,4,4,32]{3,2,1,0:T(4,128)S(1)}, u32[]{:S(2)}, u32[]{:S(2)}) collective-permute-start(f32[5,4,4,32]{3,2,1,0:T(4,128)S(1)} %pad_maximum_fusion.20), channel_id=1, source_target_pairs={{0,1},{1,2},{2,3},{3,0},{4,5},{5,6},{6,7},{7,4},{8,9},{9,10},{10,1... | collective-permute-start | bytes 30728 | tf_op jit(solution)/shard_map/ppermute | solution.py:239
  52.7 2.4 %collective-permute-start.9 = (f32[5,4,4,32]{3,2,1,0:T(4,128)S(1)}, f32[5,4,4,32]{3,2,1,0:T(4,128)S(1)}, u32[]{:S(2)}, u32[]{:S(2)}) collective-permute-start(f32[5,4,4,32]{3,2,1,0:T(4,128)S(1)} %pad_maximum_fusion.20), channel_id=1, source_target_pairs={{0,2},{1,3},{2,0},{3,1},{4,6},{5,7},{6,4},{7,5},{8,10},{9,11},{10,... | collective-permute-start | bytes 30728 | tf_op jit(solution)/shard_map/ppermute | solution.py:239
  55.2 1.4 %collective-permute-start.8 = (f32[5,4,4,32]{3,2,1,0:T(4,128)S(1)}, f32[5,4,4,32]{3,2,1,0:T(4,128)S(1)}, u32[]{:S(2)}, u32[]{:S(2)}) collective-permute-start(f32[5,4,4,32]{3,2,1,0:T(4,128)S(1)} %pad_maximum_fusion.20), channel_id=1, source_target_pairs={{0,3},{1,0},{2,1},{3,2},{4,7},{5,4},{6,5},{7,6},{8,11},{9,8},{10,9... | collective-permute-start | bytes 30728 | tf_op jit(solution)/shard_map/ppermute | solution.py:239
  56.6 1.3 %collective-permute-start.5 = (f32[2,8,5,64]{3,2,1,0:T(8,128)S(1)}, f32[2,8,5,64]{3,2,1,0:T(8,128)S(1)}, u32[]{:S(2)}, u32[]{:S(2)}) collective-permute-start(f32[2,8,5,64]{3,2,1,0:T(8,128)S(1)} %get-tuple-element.158), channel_id=1, source_target_pairs={{1,0},{2,1},{3,2},{5,4},{6,5},{7,6},{9,8},{10,9},{11,10},{13,12},{... | collective-permute-start | bytes 61448 | tf_op jit(solution)/shard_map/ppermute | solution.py:30
  57.9 3.0 %collective-permute-start.4 = (f32[2,8,5,64]{3,2,1,0:T(8,128)S(1)}, f32[2,8,5,64]{3,2,1,0:T(8,128)S(1)}, u32[]{:S(2)}, u32[]{:S(2)}) collective-permute-start(f32[2,8,5,64]{3,2,1,0:T(8,128)S(1)} %get-tuple-element.157), channel_id=1, source_target_pairs={{0,1},{1,2},{2,3},{4,5},{5,6},{6,7},{8,9},{9,10},{10,11},{12,13},{... | collective-permute-start | bytes 61448 | tf_op jit(solution)/shard_map/ppermute | solution.py:30
  61.0 3.5 %collective-permute-start.12 = (f32[5,4,16,32]{3,2,1,0:T(8,128)S(1)}, f32[5,4,16,32]{3,2,1,0:T(8,128)S(1)}, u32[]{:S(2)}, u32[]{:S(2)}) collective-permute-start(f32[5,4,16,32]{3,2,1,0:T(8,128)S(1)} %pad_maximum_fusion.6), channel_id=1, source_target_pairs={{0,8},{4,12},{8,16},{12,20},{16,24},{20,28},{1,9},{5,13},{9,17},{1... | collective-permute-start | bytes 122888 | tf_op jit(solution)/shard_map/ppermute | solution.py:30
  64.5 3.4 %collective-permute-start.11 = (f32[5,4,16,32]{3,2,1,0:T(8,128)S(1)}, f32[5,4,16,32]{3,2,1,0:T(8,128)S(1)}, u32[]{:S(2)}, u32[]{:S(2)}) collective-permute-start(f32[5,4,16,32]{3,2,1,0:T(8,128)S(1)} %pad_maximum_fusion.6), channel_id=1, source_target_pairs={{0,12},{4,16},{8,20},{12,24},{16,28},{1,13},{5,17},{9,21},{13,25},... | collective-permute-start | bytes 122888 | tf_op jit(solution)/shard_map/ppermute | solution.py:30
  67.9 2.9 %collective-permute-start.13 = (f32[5,4,16,32]{3,2,1,0:T(8,128)S(1)}, f32[5,4,16,32]{3,2,1,0:T(8,128)S(1)}, u32[]{:S(2)}, u32[]{:S(2)}) collective-permute-start(f32[5,4,16,32]{3,2,1,0:T(8,128)S(1)} %pad_maximum_fusion.6), channel_id=1, source_target_pairs={{0,4},{4,8},{8,12},{12,16},{16,20},{20,24},{24,28},{1,5},{5,9},{9,... | collective-permute-start | bytes 122888 | tf_op jit(solution)/shard_map/ppermute | solution.py:30
  70.8 3.0 %collective-permute-start.14 = (f32[5,4,16,32]{3,2,1,0:T(8,128)S(1)}, f32[5,4,16,32]{3,2,1,0:T(8,128)S(1)}, u32[]{:S(2)}, u32[]{:S(2)}) collective-permute-start(f32[5,4,16,32]{3,2,1,0:T(8,128)S(1)} %pad_maximum_fusion.6), channel_id=1, source_target_pairs={{4,0},{8,4},{12,8},{16,12},{20,16},{24,20},{28,24},{5,1},{9,5},{13... | collective-permute-start | bytes 122888 | tf_op jit(solution)/shard_map/ppermute | solution.py:30
  73.8 1.3 %collective-permute-start.15 = (f32[5,4,16,32]{3,2,1,0:T(8,128)S(1)}, f32[5,4,16,32]{3,2,1,0:T(8,128)S(1)}, u32[]{:S(2)}, u32[]{:S(2)}) collective-permute-start(f32[5,4,16,32]{3,2,1,0:T(8,128)S(1)} %pad_maximum_fusion.6), channel_id=1, source_target_pairs={{8,0},{12,4},{16,8},{20,12},{24,16},{28,20},{9,1},{13,5},{17,9},{2... | collective-permute-start | bytes 122888 | tf_op jit(solution)/shard_map/ppermute | solution.py:30
  75.2 1.3 %collective-permute-start.16 = (f32[5,4,16,32]{3,2,1,0:T(8,128)S(1)}, f32[5,4,16,32]{3,2,1,0:T(8,128)S(1)}, u32[]{:S(2)}, u32[]{:S(2)}) collective-permute-start(f32[5,4,16,32]{3,2,1,0:T(8,128)S(1)} %pad_maximum_fusion.6), channel_id=1, source_target_pairs={{12,0},{16,4},{20,8},{24,12},{28,16},{13,1},{17,5},{21,9},{25,13},... | collective-permute-start | bytes 122888 | tf_op jit(solution)/shard_map/ppermute | solution.py:30
  76.5 2.1 %collective-permute-start.7 = (f32[2,5,18,64]{3,2,1,0:T(8,128)S(1)}, f32[2,5,18,64]{3,2,1,0:T(8,128)S(1)}, u32[]{:S(2)}, u32[]{:S(2)}) collective-permute-start(f32[2,5,18,64]{3,2,1,0:T(8,128)S(1)} %get-tuple-element.75), channel_id=1, source_target_pairs={{4,0},{8,4},{12,8},{16,12},{20,16},{24,20},{28,24},{5,1},{9,5},{13... | collective-permute-start | bytes 138248 | tf_op jit(solution)/shard_map/ppermute | solution.py:30
  78.7 4.6 %collective-permute-start.6 = (f32[2,5,18,64]{3,2,1,0:T(8,128)S(1)}, f32[2,5,18,64]{3,2,1,0:T(8,128)S(1)}, u32[]{:S(2)}, u32[]{:S(2)}) collective-permute-start(f32[2,5,18,64]{3,2,1,0:T(8,128)S(1)} %get-tuple-element.74), channel_id=1, source_target_pairs={{0,4},{4,8},{8,12},{12,16},{16,20},{20,24},{24,28},{1,5},{5,9},{9,... | collective-permute-start | bytes 138248 | tf_op jit(solution)/shard_map/ppermute | solution.py:30
  83.5 7.5 %collective-permute-done.16 = f32[5,4,16,32]{3,2,1,0:T(8,128)S(1)} collective-permute-done((f32[5,4,16,32]{3,2,1,0:T(8,128)S(1)}, f32[5,4,16,32]{3,2,1,0:T(8,128)S(1)}, u32[]{:S(2)}, u32[]{:S(2)}) %collective-permute-start.16) | collective-permute-done | bytes 40992 | tf_op jit(solution)/shard_map/ppermute | solution.py:30
  92.2 0.5 fusion.87
  93.0 0.4 multiply_add_fusion
  93.6 0.3 multiply_add_fusion.1
  94.3 0.3 multiply_add_fusion.2
  96.8 0.4 fusion.318
  97.6 0.3 slice_add_fusion.10
  98.1 0.3 slice_add_fusion.11
  98.6 0.4 fusion.258
  99.0 0.5 fusion.315
  99.8 0.4 slice_add_fusion.7
  100.5 0.5 slice_add_fusion.9
  101.3 1.0 fusion.181
  (156 shorter events, 11.4 us)
Async XLA Ops:
  0.0 18.5 %copy-start.1 = (f32[16,16,128]{2,1,0:T(8,128)S(1)}, f32[16,16,128]{2,1,0:T(8,128)}, u32[]{:S(2)}) copy-start(f32[16,16,128]{2,1,0:T(8,128)} %param.5) | copy-start | bytes 393220
  0.0 18.5 %copy-start.2 = (f32[16,16,128]{2,1,0:T(8,128)S(1)}, f32[16,16,128]{2,1,0:T(8,128)}, u32[]{:S(2)}) copy-start(f32[16,16,128]{2,1,0:T(8,128)} %param.4) | copy-start | bytes 393220
  2.0 10.6 %collective-permute-start.1 = (f32[3,10,16,128]{3,2,1,0:T(8,128)S(1)}, f32[3,10,16,128]{3,2,1,0:T(8,128)S(1)}, u32[]{:S(2)}, u32[]{:S(2)}) collective-permute-start(f32[3,10,16,128]{3,2,1,0:T(8,128)S(1)} %get-tuple-element.49), channel_id=1, source_target_pairs={{4,0},{8,4},{12,8},{16,12},{20,16},{24,20},{28,24},{5,1},{9,5},{13... | collective-permute-start | bytes 737288 | tf_op jit(solution)/shard_map/ppermute | solution.py:30
  4.0 13.8 %collective-permute-start = (f32[3,10,16,128]{3,2,1,0:T(8,128)S(1)}, f32[3,10,16,128]{3,2,1,0:T(8,128)S(1)}, u32[]{:S(2)}, u32[]{:S(2)}) collective-permute-start(f32[3,10,16,128]{3,2,1,0:T(8,128)S(1)} %get-tuple-element.48), channel_id=1, source_target_pairs={{0,4},{4,8},{8,12},{12,16},{16,20},{20,24},{24,28},{1,5},{5,9},{9,... | collective-permute-start | bytes 737288 | tf_op jit(solution)/shard_map/ppermute | solution.py:30
  17.8 0.7 copy-start.3
  18.9 5.3 %collective-permute-start.3 = (f32[3,36,10,128]{3,1,2,0:T(8,128)S(1)}, f32[3,36,10,128]{3,1,2,0:T(8,128)S(1)}, u32[]{:S(2)}, u32[]{:S(2)}) collective-permute-start(f32[3,36,10,128]{3,1,2,0:T(8,128)S(1)} %copy.20), channel_id=1, source_target_pairs={{1,0},{2,1},{3,2},{5,4},{6,5},{7,6},{9,8},{10,9},{11,10},{13,12},{... | collective-permute-start | bytes 1658888 | tf_op jit(solution)/shard_map/ppermute | solution.py:30
  20.4 4.7 %collective-permute-start.2 = (f32[3,36,10,128]{3,1,2,0:T(8,128)S(1)}, f32[3,36,10,128]{3,1,2,0:T(8,128)S(1)}, u32[]{:S(2)}, u32[]{:S(2)}) collective-permute-start(f32[3,36,10,128]{3,1,2,0:T(8,128)S(1)} %copy.19), channel_id=1, source_target_pairs={{0,1},{1,2},{2,3},{4,5},{5,6},{6,7},{8,9},{9,10},{10,11},{12,13},{... | collective-permute-start | bytes 1658888 | tf_op jit(solution)/shard_map/ppermute | solution.py:30
  24.1 1.1 %copy-start.4 = (f32[3,10,16,128]{3,2,1,0:T(8,128)S(1)}, f32[3,10,16,128]{3,2,1,0:T(8,128)}, u32[]{:S(2)}) copy-start(f32[3,10,16,128]{3,2,1,0:T(8,128)} %copy-done.3) | copy-start | bytes 737284
  32.2 2.5 %copy-start = (f32[4,36,36,128]{3,2,1,0:T(8,128)S(1)}, f32[4,36,36,128]{3,2,1,0:T(8,128)}, u32[]{:S(2)}) copy-start(f32[4,36,36,128]{3,2,1,0:T(8,128)} %shard_map.46) | copy-start | bytes 7962628
  46.0 14.9 %collective-permute-start.10 = (f32[5,4,4,32]{3,2,1,0:T(4,128)S(1)}, f32[5,4,4,32]{3,2,1,0:T(4,128)S(1)}, u32[]{:S(2)}, u32[]{:S(2)}) collective-permute-start(f32[5,4,4,32]{3,2,1,0:T(4,128)S(1)} %pad_maximum_fusion.20), channel_id=1, source_target_pairs={{0,1},{1,2},{2,3},{3,0},{4,5},{5,6},{6,7},{7,4},{8,9},{9,10},{10,1... | collective-permute-start | bytes 30728 | tf_op jit(solution)/shard_map/ppermute | solution.py:239
  52.7 8.2 %collective-permute-start.9 = (f32[5,4,4,32]{3,2,1,0:T(4,128)S(1)}, f32[5,4,4,32]{3,2,1,0:T(4,128)S(1)}, u32[]{:S(2)}, u32[]{:S(2)}) collective-permute-start(f32[5,4,4,32]{3,2,1,0:T(4,128)S(1)} %pad_maximum_fusion.20), channel_id=1, source_target_pairs={{0,2},{1,3},{2,0},{3,1},{4,6},{5,7},{6,4},{7,5},{8,10},{9,11},{10,... | collective-permute-start | bytes 30728 | tf_op jit(solution)/shard_map/ppermute | solution.py:239
  55.2 5.8 %collective-permute-start.8 = (f32[5,4,4,32]{3,2,1,0:T(4,128)S(1)}, f32[5,4,4,32]{3,2,1,0:T(4,128)S(1)}, u32[]{:S(2)}, u32[]{:S(2)}) collective-permute-start(f32[5,4,4,32]{3,2,1,0:T(4,128)S(1)} %pad_maximum_fusion.20), channel_id=1, source_target_pairs={{0,3},{1,0},{2,1},{3,2},{4,7},{5,4},{6,5},{7,6},{8,11},{9,8},{10,9... | collective-permute-start | bytes 30728 | tf_op jit(solution)/shard_map/ppermute | solution.py:239
  56.6 14.3 %collective-permute-start.5 = (f32[2,8,5,64]{3,2,1,0:T(8,128)S(1)}, f32[2,8,5,64]{3,2,1,0:T(8,128)S(1)}, u32[]{:S(2)}, u32[]{:S(2)}) collective-permute-start(f32[2,8,5,64]{3,2,1,0:T(8,128)S(1)} %get-tuple-element.158), channel_id=1, source_target_pairs={{1,0},{2,1},{3,2},{5,4},{6,5},{7,6},{9,8},{10,9},{11,10},{13,12},{... | collective-permute-start | bytes 61448 | tf_op jit(solution)/shard_map/ppermute | solution.py:30
  57.9 15.9 %collective-permute-start.4 = (f32[2,8,5,64]{3,2,1,0:T(8,128)S(1)}, f32[2,8,5,64]{3,2,1,0:T(8,128)S(1)}, u32[]{:S(2)}, u32[]{:S(2)}) collective-permute-start(f32[2,8,5,64]{3,2,1,0:T(8,128)S(1)} %get-tuple-element.157), channel_id=1, source_target_pairs={{0,1},{1,2},{2,3},{4,5},{5,6},{6,7},{8,9},{9,10},{10,11},{12,13},{... | collective-permute-start | bytes 61448 | tf_op jit(solution)/shard_map/ppermute | solution.py:30
  61.0 15.5 %collective-permute-start.12 = (f32[5,4,16,32]{3,2,1,0:T(8,128)S(1)}, f32[5,4,16,32]{3,2,1,0:T(8,128)S(1)}, u32[]{:S(2)}, u32[]{:S(2)}) collective-permute-start(f32[5,4,16,32]{3,2,1,0:T(8,128)S(1)} %pad_maximum_fusion.6), channel_id=1, source_target_pairs={{0,8},{4,12},{8,16},{12,20},{16,24},{20,28},{1,9},{5,13},{9,17},{1... | collective-permute-start | bytes 122888 | tf_op jit(solution)/shard_map/ppermute | solution.py:30
  64.5 10.7 %collective-permute-start.11 = (f32[5,4,16,32]{3,2,1,0:T(8,128)S(1)}, f32[5,4,16,32]{3,2,1,0:T(8,128)S(1)}, u32[]{:S(2)}, u32[]{:S(2)}) collective-permute-start(f32[5,4,16,32]{3,2,1,0:T(8,128)S(1)} %pad_maximum_fusion.6), channel_id=1, source_target_pairs={{0,12},{4,16},{8,20},{12,24},{16,28},{1,13},{5,17},{9,21},{13,25},... | collective-permute-start | bytes 122888 | tf_op jit(solution)/shard_map/ppermute | solution.py:30
  67.9 10.7 %collective-permute-start.13 = (f32[5,4,16,32]{3,2,1,0:T(8,128)S(1)}, f32[5,4,16,32]{3,2,1,0:T(8,128)S(1)}, u32[]{:S(2)}, u32[]{:S(2)}) collective-permute-start(f32[5,4,16,32]{3,2,1,0:T(8,128)S(1)} %pad_maximum_fusion.6), channel_id=1, source_target_pairs={{0,4},{4,8},{8,12},{12,16},{16,20},{20,24},{24,28},{1,5},{5,9},{9,... | collective-permute-start | bytes 122888 | tf_op jit(solution)/shard_map/ppermute | solution.py:30
  70.8 12.6 %collective-permute-start.14 = (f32[5,4,16,32]{3,2,1,0:T(8,128)S(1)}, f32[5,4,16,32]{3,2,1,0:T(8,128)S(1)}, u32[]{:S(2)}, u32[]{:S(2)}) collective-permute-start(f32[5,4,16,32]{3,2,1,0:T(8,128)S(1)} %pad_maximum_fusion.6), channel_id=1, source_target_pairs={{4,0},{8,4},{12,8},{16,12},{20,16},{24,20},{28,24},{5,1},{9,5},{13... | collective-permute-start | bytes 122888 | tf_op jit(solution)/shard_map/ppermute | solution.py:30
  73.8 9.7 %collective-permute-start.15 = (f32[5,4,16,32]{3,2,1,0:T(8,128)S(1)}, f32[5,4,16,32]{3,2,1,0:T(8,128)S(1)}, u32[]{:S(2)}, u32[]{:S(2)}) collective-permute-start(f32[5,4,16,32]{3,2,1,0:T(8,128)S(1)} %pad_maximum_fusion.6), channel_id=1, source_target_pairs={{8,0},{12,4},{16,8},{20,12},{24,16},{28,20},{9,1},{13,5},{17,9},{2... | collective-permute-start | bytes 122888 | tf_op jit(solution)/shard_map/ppermute | solution.py:30
  75.2 15.8 %collective-permute-start.16 = (f32[5,4,16,32]{3,2,1,0:T(8,128)S(1)}, f32[5,4,16,32]{3,2,1,0:T(8,128)S(1)}, u32[]{:S(2)}, u32[]{:S(2)}) collective-permute-start(f32[5,4,16,32]{3,2,1,0:T(8,128)S(1)} %pad_maximum_fusion.6), channel_id=1, source_target_pairs={{12,0},{16,4},{20,8},{24,12},{28,16},{13,1},{17,5},{21,9},{25,13},... | collective-permute-start | bytes 122888 | tf_op jit(solution)/shard_map/ppermute | solution.py:30
  76.5 20.7 %collective-permute-start.7 = (f32[2,5,18,64]{3,2,1,0:T(8,128)S(1)}, f32[2,5,18,64]{3,2,1,0:T(8,128)S(1)}, u32[]{:S(2)}, u32[]{:S(2)}) collective-permute-start(f32[2,5,18,64]{3,2,1,0:T(8,128)S(1)} %get-tuple-element.75), channel_id=1, source_target_pairs={{4,0},{8,4},{12,8},{16,12},{20,16},{24,20},{28,24},{5,1},{9,5},{13... | collective-permute-start | bytes 138248 | tf_op jit(solution)/shard_map/ppermute | solution.py:30
  78.7 18.6 %collective-permute-start.6 = (f32[2,5,18,64]{3,2,1,0:T(8,128)S(1)}, f32[2,5,18,64]{3,2,1,0:T(8,128)S(1)}, u32[]{:S(2)}, u32[]{:S(2)}) collective-permute-start(f32[2,5,18,64]{3,2,1,0:T(8,128)S(1)} %get-tuple-element.74), channel_id=1, source_target_pairs={{0,4},{4,8},{8,12},{12,16},{16,20},{20,24},{24,28},{1,5},{5,9},{9,... | collective-permute-start | bytes 138248 | tf_op jit(solution)/shard_map/ppermute | solution.py:30

commit v6 on v5

--- a/solution.py
+++ b/solution.py
@@ -150,50 +150,53 @@
     return iterate, cur
 
 
-def fields_kernel(bounds_ref, table_ref, conc_ref, idf_ref, out_ref):
-    rows = conc_ref.shape[0]
-    shape = conc_ref.shape[1:]
+def fields_kernel(bounds_ref, table_ref, ext_ref, kx_ref, ky_ref, kz_ref, st_ref):
+    rows = ext_ref.shape[1]
+    shape = ext_ref.shape[2:]
     mats = table_ref.shape[1]
     col = lax.broadcasted_iota(jnp.int32, shape, 0)
     col_ok = (col >= bounds_ref[2]) & (col < bounds_ref[3])
+    table = [[table_ref[record, material] for material in range(mats)] for record in range(5)]
+    outs = (kx_ref, ky_ref, kz_ref)
 
     def body(i, carry):
-        ids = idf_ref[i]
-        conc = conc_ref[i]
+        conc = ext_ref[0, i]
+        ids = ext_ref[2, i]
         row = jnp.zeros(shape, jnp.int32) + i
         ok = col_ok & (row >= bounds_ref[0]) & (row < bounds_ref[1])
+        masks = [ids == float(material) for material in range(mats - 1)]
         vals = []
         for record in range(5):
-            acc = jnp.zeros(shape, jnp.float32) + table_ref[record, mats - 1]
+            acc = jnp.zeros(shape, jnp.float32) + table[record][mats - 1]
             for material in range(mats - 2, -1, -1):
-                acc = jnp.where(ids == float(material), table_ref[record, material], acc)
+                acc = jnp.where(masks[material], table[record][material], acc)
             vals.append(acc)
         store = storage_scale * (1.0 + vals[3] * jnp.exp((vals[4] - 1.0) * jnp.log(conc)))
-        out_ref[0, i] = jnp.where(ok, vals[0], 0.0)
-        out_ref[1, i] = jnp.where(ok, vals[1], 0.0)
-        out_ref[2, i] = jnp.where(ok, vals[2], 0.0)
-        out_ref[3, i] = jnp.where(ok, store, 0.0)
+        for record in range(3):
+            outs[record][i] = jnp.where(ok, vals[record], 0.0)
+        st_ref[i] = jnp.where(ok, store, 0.0)
         return carry
 
     lax.fori_loop(0, rows, body, 0)
 
 
-def soil_fields(bounds, soil_table, conc, idf):
-    cells = conc.size
+def soil_fields(bounds, soil_table, ext):
+    frame = ext.shape[1:]
+    cells = ext[0].size
+    field = jax.ShapeDtypeStruct(frame, jnp.float32)
     return pl.pallas_call(
         fields_kernel,
-        out_shape=jax.ShapeDtypeStruct((4,) + conc.shape, jnp.float32),
+        out_shape=(field, field, field, field),
         in_specs=[
             pl.BlockSpec(memory_space=pltpu.SMEM),
             pl.BlockSpec(memory_space=pltpu.SMEM),
             pl.BlockSpec(memory_space=pltpu.VMEM),
-            pl.BlockSpec(memory_space=pltpu.VMEM),
         ],
-        out_specs=pl.BlockSpec(memory_space=pltpu.VMEM),
+        out_specs=tuple(pl.BlockSpec(memory_space=pltpu.VMEM) for _ in range(4)),
         cost_estimate=pl.CostEstimate(
-            flops=100 * cells, transcendentals=2 * cells, bytes_accessed=24 * cells
+            flops=100 * cells, transcendentals=2 * cells, bytes_accessed=28 * cells
         ),
-    )(bounds, soil_table, conc, idf)
+    )(bounds, soil_table, ext)
 
 
 def local(conc_prev, right_side, soil_id, soil_table):
@@ -207,11 +210,11 @@
 
     stacked = jnp.stack([conc_prev, right_side, soil_id.astype(jnp.float32)])
     ext = halo(stacked, (("gx", 1), ("gy", 2)), hf)
-    conc, rhs, idf = ext[0], ext[1], ext[2]
+    rhs = ext[1]
     x_lo = hf - ix * n
     y_lo = hf - iy * ny
     bounds = jnp.stack([x_lo, x_lo + gx_count * n, y_lo, y_lo + gy_count * ny]).astype(jnp.int32)
-    fine_c = soil_fields(bounds, soil_table, conc, idf)
+    fine_c = jnp.stack(soil_fields(bounds, soil_table, ext))
     fine = build_level(fine_c, n, hf, 1.0)
 
     x0, x0m = chebyshev(rhs, hf, None, 0, fine)

time: 103 us -> 104 us (level)
  other arithmetic: 14.5 us -> 16.3 us
  local copies, waits for them, and re-layouts: 10.7 us -> 9.52 us
    squeeze x2 -> x1, local copies, waits for them, and re-layouts: 3.14 us -> 0.05 us  [local(): rhs = ext[1]]
    unnamed x14 -> x18, local copies, waits for them, and re-layouts: 1.43 us -> 3.27 us
    div x3, other arithmetic: 0.62 us -> 2.03 us  [harmonic(): return first * second / jnp.maximum(0.5 * (first + second), 0.1)]
where the time goes in v6:
time: 104 us; the launch traced here: 103 us
  starting transfers between devices  48.3 us (46%)
  waiting for transfers between devices  17 us (16%)
  other arithmetic  16.3 us (16%)
  local copies, waits for them, and re-layouts  9.52 us (9%)
  Pallas kernels  5.62 us (5%)
  matrix products  5.18 us (5%)
  between operations  1.21 us (1%)
    ppermute x14, starting transfers between devices, shift_from(): return lax.ppermute(cells, axis, pairs)  37.7 us
    ppermute x14, waiting for transfers between devices, shift_from(): return lax.ppermute(cells, axis, pairs)  17 us
    ppermute x3, starting transfers between devices, local(): blocks.append(lax.ppermute(cpack, 'gy', pairs))  10.6 us
    pallas_call x1, Pallas kernels, soil_fields(): pl.pallas_call(fields_kernel, out_shape=(field, field, field, field), in_...  5.62 us
    add x7, other arithmetic, chebyshev(): iterate = win(iterate, n, cur, nxt) + update  4.58 us
    unnamed x18, local copies, waits for them, and re-layouts  3.27 us
    add x8, other arithmetic, local(): u = centre + jacobi_weight * ((csrc[sl] - applied) / cdiag[sl])  2.63 us
    dot_general x4, matrix products, coarsen(): lax.dot_general(pick, rows, (((2,), (1,)), ((0,), (0,))), precision=HIGH)  2.26 us
  transfers between devices with their start and end apart: 17, of which 4 were waited for; matrix products, arithmetic and copies ran while one was open for 7% of the time, Pallas kernels for 0%

profile of v6, /device:TPU:4, one launch (start us, length us, event | category | flops | bytes accessed | tf_op | source)
XLA Modules:
  0.0 103.1 jit_solution(14035195994008977466)
XLA Ops:
  0.0 1.0 convert_bitcast_fusion
  1.0 1.0 pad_maximum_fusion.5
  2.0 1.9 %collective-permute-start.1 = (f32[3,10,16,128]{3,2,1,0:T(8,128)S(1)}, f32[3,10,16,128]{3,2,1,0:T(8,128)S(1)}, u32[]{:S(2)}, u32[]{:S(2)}) collective-permute-start(f32[3,10,16,128]{3,2,1,0:T(8,128)S(1)} %get-tuple-element.51), channel_id=1, source_target_pairs={{4,0},{8,4},{12,8},{16,12},{20,16},{24,20},{28,24},{5,1},{9,5},{13... | collective-permute-start | bytes 737288 | tf_op jit(solution)/shard_map/ppermute | solution.py:30
  3.9 4.8 %collective-permute-start = (f32[3,10,16,128]{3,2,1,0:T(8,128)S(1)}, f32[3,10,16,128]{3,2,1,0:T(8,128)S(1)}, u32[]{:S(2)}, u32[]{:S(2)}) collective-permute-start(f32[3,10,16,128]{3,2,1,0:T(8,128)S(1)} %get-tuple-element.50), channel_id=1, source_target_pairs={{0,4},{4,8},{8,12},{12,16},{16,20},{20,24},{24,28},{1,5},{5,9},{9,... | collective-permute-start | bytes 737288 | tf_op jit(solution)/shard_map/ppermute | solution.py:30
  8.9 3.7 %collective-permute-done.1 = f32[3,10,16,128]{3,2,1,0:T(8,128)S(1)} collective-permute-done((f32[3,10,16,128]{3,2,1,0:T(8,128)S(1)}, f32[3,10,16,128]{3,2,1,0:T(8,128)S(1)}, u32[]{:S(2)}, u32[]{:S(2)}) %collective-permute-start.1) | collective-permute-done | bytes 245792 | tf_op jit(solution)/shard_map/ppermute | solution.py:30
  12.6 5.2 %collective-permute-done = f32[3,10,16,128]{3,2,1,0:T(8,128)S(1)} collective-permute-done((f32[3,10,16,128]{3,2,1,0:T(8,128)S(1)}, f32[3,10,16,128]{3,2,1,0:T(8,128)S(1)}, u32[]{:S(2)}, u32[]{:S(2)}) %collective-permute-start) | collective-permute-done | bytes 245792 | tf_op jit(solution)/shard_map/ppermute | solution.py:30
  18.2 1.3 %collective-permute-start.3 = (f32[3,36,10,128]{3,1,2,0:T(8,128)S(1)}, f32[3,36,10,128]{3,1,2,0:T(8,128)S(1)}, u32[]{:S(2)}, u32[]{:S(2)}) collective-permute-start(f32[3,36,10,128]{3,1,2,0:T(8,128)S(1)} %copy.20), channel_id=1, source_target_pairs={{1,0},{2,1},{3,2},{5,4},{6,5},{7,6},{9,8},{10,9},{11,10},{13,12},{... | collective-permute-start | bytes 1658888 | tf_op jit(solution)/shard_map/ppermute | solution.py:30
  19.7 3.1 %collective-permute-start.2 = (f32[3,36,10,128]{3,1,2,0:T(8,128)S(1)}, f32[3,36,10,128]{3,1,2,0:T(8,128)S(1)}, u32[]{:S(2)}, u32[]{:S(2)}) collective-permute-start(f32[3,36,10,128]{3,1,2,0:T(8,128)S(1)} %copy.19), channel_id=1, source_target_pairs={{0,1},{1,2},{2,3},{4,5},{5,6},{6,7},{8,9},{9,10},{10,11},{12,13},{... | collective-permute-start | bytes 1658888 | tf_op jit(solution)/shard_map/ppermute | solution.py:30
  22.7 0.6 pad_add_fusion.bounds_ref
  23.5 0.9 collective-permute-done.2
  24.8 1.3 %copy-done.1 = f32[3,36,36,128]{3,2,1,0:T(8,128)} copy-done((f32[3,36,36,128]{3,2,1,0:T(8,128)}, f32[3,36,36,128]{3,2,1,0:T(8,128)S(1)}, u32[]{:S(2)}) %copy-start.1) | copy-done | bytes 1990680
  26.1 5.6 %shard_map.46 = (f32[36,36,128]{2,1,0:T(8,128)}, f32[36,36,128]{2,1,0:T(8,128)}, f32[36,36,128]{2,1,0:T(8,128)}, f32[36,36,128]{2,1,0:T(8,128)}) custom-call(s32[4]{0:T(128)} %pad_add_fusion.bounds_ref, f32[5,8]{1,0:T(8,128)} %table_ref.1, f32[3,36,36,128]{3,2,1,0:T(8,128)} %copy-done.1), custom_call_target="tpu_custom_call" | custom-call | flops 16588800 | bytes 4644864 | tf_op jit(solution)/shard_map/pallas_call | solution.py:187
  31.7 1.7 %maximum_divide_fusion = f32[36,36,127]{2,1,0:T(8,128)S(1)} fusion(f32[36,36,128]{2,1,0:T(8,128)} %get-tuple-element.11), kind=kLoop, calls=%fused_computation.18 | loop fusion | flops 822960 | bytes 1975104 | tf_op jit(solution)/shard_map/div | solution.py:45
  33.6 0.9 copy-done.4
  34.8 0.8 fusion.5
  36.0 1.2 %slice_add_fusion.4 = (f32[32,32,128]{2,1,0:T(8,128)S(1)}, f32[32,32,128]{2,1,0:T(8,128)S(1)}) fusion(f32[34,34,128]{2,1,0:T(8,128)S(1)} %get-tuple-element.29, f32[34,34,128]{2,1,0:T(8,128)S(1)} %get-tuple-element.30, f32[32,32,127]{2,1,0:T(8,128)S(1)} %get-tuple-element.39, f32[32,32,1]{2,1,0:T(8,128)S(1)} %get-tuple-element.41, ...), kind=kLoop, calls=%fused_computation.52 | loop fusion | flops 3538944 | bytes 9046976 | tf_op jit(solution)/shard_map/add | solution.py:147
  37.6 0.9 copy-done.3
  38.9 0.8 fusion.337
  39.7 1.5 %convolution_multiply_fusion = f32[72,18,64]{2,1,0:T(8,128)S(1)} fusion(f32[72,36,64]{2,1,0:T(8,128)S(1)} %fusion.337, f32[18,36]{1,0:T(8,128)S(1)} %fusion.358), kind=kOutput, calls=%fused_computation.3 | convolution fusion | flops 35914752 | bytes 997920 | tf_op jit(solution)/shard_map/dot_general | solution.py:68
  41.6 1.2 %fusion.23 = f32[30,30,128]{2,1,0:T(8,128)S(1)} fusion(f32[34,34,128]{2,1,0:T(8,128)S(1)} %get-tuple-element.30, f32[32,32,128]{2,1,0:T(8,128)S(1)} %get-tuple-element.27, f32[36,35,128]{2,1,0:T(8,128)S(1)} %maximum_divide_fusion.1, f32[35,36,128]{2,1,0:T(8,128)S(1)} %maximum_divide_fusion.2, f32[36,36,128]{2,1,0:T(8,128)S(1)} %slice_bitcast_fusion, ...), kind=kLoop, calls=%fused_computation.56 | loop fusion | flops 3110400 | bytes 8031168 | tf_op jit(solution)/shard_map/add | solution.py:147
  43.1 0.9 fusion.41
  44.4 0.3 divide_multiply_fusion.3
  46.6 6.7 %collective-permute-start.10 = (f32[5,4,4,32]{3,2,1,0:T(4,128)S(1)}, f32[5,4,4,32]{3,2,1,0:T(4,128)S(1)}, u32[]{:S(2)}, u32[]{:S(2)}) collective-permute-start(f32[5,4,4,32]{3,2,1,0:T(4,128)S(1)} %pad_maximum_fusion.21), channel_id=1, source_target_pairs={{0,1},{1,2},{2,3},{3,0},{4,5},{5,6},{6,7},{7,4},{8,9},{9,10},{10,1... | collective-permute-start | bytes 30728 | tf_op jit(solution)/shard_map/ppermute | solution.py:242
  53.4 2.4 %collective-permute-start.9 = (f32[5,4,4,32]{3,2,1,0:T(4,128)S(1)}, f32[5,4,4,32]{3,2,1,0:T(4,128)S(1)}, u32[]{:S(2)}, u32[]{:S(2)}) collective-permute-start(f32[5,4,4,32]{3,2,1,0:T(4,128)S(1)} %pad_maximum_fusion.21), channel_id=1, source_target_pairs={{0,2},{1,3},{2,0},{3,1},{4,6},{5,7},{6,4},{7,5},{8,10},{9,11},{10,... | collective-permute-start | bytes 30728 | tf_op jit(solution)/shard_map/ppermute | solution.py:242
  55.8 1.4 %collective-permute-start.8 = (f32[5,4,4,32]{3,2,1,0:T(4,128)S(1)}, f32[5,4,4,32]{3,2,1,0:T(4,128)S(1)}, u32[]{:S(2)}, u32[]{:S(2)}) collective-permute-start(f32[5,4,4,32]{3,2,1,0:T(4,128)S(1)} %pad_maximum_fusion.21), channel_id=1, source_target_pairs={{0,3},{1,0},{2,1},{3,2},{4,7},{5,4},{6,5},{7,6},{8,11},{9,8},{10,9... | collective-permute-start | bytes 30728 | tf_op jit(solution)/shard_map/ppermute | solution.py:242
  57.2 1.3 %collective-permute-start.5 = (f32[2,8,5,64]{3,2,1,0:T(8,128)S(1)}, f32[2,8,5,64]{3,2,1,0:T(8,128)S(1)}, u32[]{:S(2)}, u32[]{:S(2)}) collective-permute-start(f32[2,8,5,64]{3,2,1,0:T(8,128)S(1)} %get-tuple-element.160), channel_id=1, source_target_pairs={{1,0},{2,1},{3,2},{5,4},{6,5},{7,6},{9,8},{10,9},{11,10},{13,12},{... | collective-permute-start | bytes 61448 | tf_op jit(solution)/shard_map/ppermute | solution.py:30
  58.5 3.0 %collective-permute-start.4 = (f32[2,8,5,64]{3,2,1,0:T(8,128)S(1)}, f32[2,8,5,64]{3,2,1,0:T(8,128)S(1)}, u32[]{:S(2)}, u32[]{:S(2)}) collective-permute-start(f32[2,8,5,64]{3,2,1,0:T(8,128)S(1)} %get-tuple-element.159), channel_id=1, source_target_pairs={{0,1},{1,2},{2,3},{4,5},{5,6},{6,7},{8,9},{9,10},{10,11},{12,13},{... | collective-permute-start | bytes 61448 | tf_op jit(solution)/shard_map/ppermute | solution.py:30
  61.6 3.5 %collective-permute-start.12 = (f32[5,4,16,32]{3,2,1,0:T(8,128)S(1)}, f32[5,4,16,32]{3,2,1,0:T(8,128)S(1)}, u32[]{:S(2)}, u32[]{:S(2)}) collective-permute-start(f32[5,4,16,32]{3,2,1,0:T(8,128)S(1)} %pad_maximum_fusion.7), channel_id=1, source_target_pairs={{0,8},{4,12},{8,16},{12,20},{16,24},{20,28},{1,9},{5,13},{9,17},{1... | collective-permute-start | bytes 122888 | tf_op jit(solution)/shard_map/ppermute | solution.py:30
  65.1 3.4 %collective-permute-start.11 = (f32[5,4,16,32]{3,2,1,0:T(8,128)S(1)}, f32[5,4,16,32]{3,2,1,0:T(8,128)S(1)}, u32[]{:S(2)}, u32[]{:S(2)}) collective-permute-start(f32[5,4,16,32]{3,2,1,0:T(8,128)S(1)} %pad_maximum_fusion.7), channel_id=1, source_target_pairs={{0,12},{4,16},{8,20},{12,24},{16,28},{1,13},{5,17},{9,21},{13,25},... | collective-permute-start | bytes 122888 | tf_op jit(solution)/shard_map/ppermute | solution.py:30
  68.6 2.9 %collective-permute-start.13 = (f32[5,4,16,32]{3,2,1,0:T(8,128)S(1)}, f32[5,4,16,32]{3,2,1,0:T(8,128)S(1)}, u32[]{:S(2)}, u32[]{:S(2)}) collective-permute-start(f32[5,4,16,32]{3,2,1,0:T(8,128)S(1)} %pad_maximum_fusion.7), channel_id=1, source_target_pairs={{0,4},{4,8},{8,12},{12,16},{16,20},{20,24},{24,28},{1,5},{5,9},{9,... | collective-permute-start | bytes 122888 | tf_op jit(solution)/shard_map/ppermute | solution.py:30
  71.5 3.0 %collective-permute-start.14 = (f32[5,4,16,32]{3,2,1,0:T(8,128)S(1)}, f32[5,4,16,32]{3,2,1,0:T(8,128)S(1)}, u32[]{:S(2)}, u32[]{:S(2)}) collective-permute-start(f32[5,4,16,32]{3,2,1,0:T(8,128)S(1)} %pad_maximum_fusion.7), channel_id=1, source_target_pairs={{4,0},{8,4},{12,8},{16,12},{20,16},{24,20},{28,24},{5,1},{9,5},{13... | collective-permute-start | bytes 122888 | tf_op jit(solution)/shard_map/ppermute | solution.py:30
  74.5 1.3 %collective-permute-start.15 = (f32[5,4,16,32]{3,2,1,0:T(8,128)S(1)}, f32[5,4,16,32]{3,2,1,0:T(8,128)S(1)}, u32[]{:S(2)}, u32[]{:S(2)}) collective-permute-start(f32[5,4,16,32]{3,2,1,0:T(8,128)S(1)} %pad_maximum_fusion.7), channel_id=1, source_target_pairs={{8,0},{12,4},{16,8},{20,12},{24,16},{28,20},{9,1},{13,5},{17,9},{2... | collective-permute-start | bytes 122888 | tf_op jit(solution)/shard_map/ppermute | solution.py:30
  75.8 1.3 %collective-permute-start.16 = (f32[5,4,16,32]{3,2,1,0:T(8,128)S(1)}, f32[5,4,16,32]{3,2,1,0:T(8,128)S(1)}, u32[]{:S(2)}, u32[]{:S(2)}) collective-permute-start(f32[5,4,16,32]{3,2,1,0:T(8,128)S(1)} %pad_maximum_fusion.7), channel_id=1, source_target_pairs={{12,0},{16,4},{20,8},{24,12},{28,16},{13,1},{17,5},{21,9},{25,13},... | collective-permute-start | bytes 122888 | tf_op jit(solution)/shard_map/ppermute | solution.py:30
  77.2 2.1 %collective-permute-start.7 = (f32[2,5,18,64]{3,2,1,0:T(8,128)S(1)}, f32[2,5,18,64]{3,2,1,0:T(8,128)S(1)}, u32[]{:S(2)}, u32[]{:S(2)}) collective-permute-start(f32[2,5,18,64]{3,2,1,0:T(8,128)S(1)} %get-tuple-element.77), channel_id=1, source_target_pairs={{4,0},{8,4},{12,8},{16,12},{20,16},{24,20},{28,24},{5,1},{9,5},{13... | collective-permute-start | bytes 138248 | tf_op jit(solution)/shard_map/ppermute | solution.py:30
  79.3 4.8 %collective-permute-start.6 = (f32[2,5,18,64]{3,2,1,0:T(8,128)S(1)}, f32[2,5,18,64]{3,2,1,0:T(8,128)S(1)}, u32[]{:S(2)}, u32[]{:S(2)}) collective-permute-start(f32[2,5,18,64]{3,2,1,0:T(8,128)S(1)} %get-tuple-element.76), channel_id=1, source_target_pairs={{0,4},{4,8},{8,12},{12,16},{16,20},{20,24},{24,28},{1,5},{5,9},{9,... | collective-permute-start | bytes 138248 | tf_op jit(solution)/shard_map/ppermute | solution.py:30
  84.3 7.3 %collective-permute-done.16 = f32[5,4,16,32]{3,2,1,0:T(8,128)S(1)} collective-permute-done((f32[5,4,16,32]{3,2,1,0:T(8,128)S(1)}, f32[5,4,16,32]{3,2,1,0:T(8,128)S(1)}, u32[]{:S(2)}, u32[]{:S(2)}) %collective-permute-start.16) | collective-permute-done | bytes 40992 | tf_op jit(solution)/shard_map/ppermute | solution.py:30
  92.8 0.5 fusion.88
  93.7 0.4 multiply_add_fusion
  94.3 0.4 multiply_add_fusion.1
  95.0 0.3 multiply_add_fusion.2
  95.6 0.3 multiply_add_fusion.3
  97.6 0.4 fusion.319
  98.4 0.3 slice_add_fusion.9
  99.4 0.4 fusion.259
  99.8 0.5 fusion.316
  100.7 0.4 slice_add_fusion.6
  101.4 0.5 slice_add_fusion.8
  102.1 1.0 fusion.182
  (160 shorter events, 11.6 us)
Async XLA Ops:
  0.0 17.8 %copy-start.5 = (f32[16,16,128]{2,1,0:T(8,128)S(1)}, f32[16,16,128]{2,1,0:T(8,128)}, u32[]{:S(2)}) copy-start(f32[16,16,128]{2,1,0:T(8,128)} %param.5) | copy-start | bytes 393220
  0.0 17.8 %copy-start.6 = (f32[16,16,128]{2,1,0:T(8,128)S(1)}, f32[16,16,128]{2,1,0:T(8,128)}, u32[]{:S(2)}) copy-start(f32[16,16,128]{2,1,0:T(8,128)} %param.4) | copy-start | bytes 393220
  2.0 10.6 %collective-permute-start.1 = (f32[3,10,16,128]{3,2,1,0:T(8,128)S(1)}, f32[3,10,16,128]{3,2,1,0:T(8,128)S(1)}, u32[]{:S(2)}, u32[]{:S(2)}) collective-permute-start(f32[3,10,16,128]{3,2,1,0:T(8,128)S(1)} %get-tuple-element.51), channel_id=1, source_target_pairs={{4,0},{8,4},{12,8},{16,12},{20,16},{24,20},{28,24},{5,1},{9,5},{13... | collective-permute-start | bytes 737288 | tf_op jit(solution)/shard_map/ppermute | solution.py:30
  3.9 13.8 %collective-permute-start = (f32[3,10,16,128]{3,2,1,0:T(8,128)S(1)}, f32[3,10,16,128]{3,2,1,0:T(8,128)S(1)}, u32[]{:S(2)}, u32[]{:S(2)}) collective-permute-start(f32[3,10,16,128]{3,2,1,0:T(8,128)S(1)} %get-tuple-element.50), channel_id=1, source_target_pairs={{0,4},{4,8},{8,12},{12,16},{16,20},{20,24},{24,28},{1,5},{5,9},{9,... | collective-permute-start | bytes 737288 | tf_op jit(solution)/shard_map/ppermute | solution.py:30
  18.2 5.2 %collective-permute-start.3 = (f32[3,36,10,128]{3,1,2,0:T(8,128)S(1)}, f32[3,36,10,128]{3,1,2,0:T(8,128)S(1)}, u32[]{:S(2)}, u32[]{:S(2)}) collective-permute-start(f32[3,36,10,128]{3,1,2,0:T(8,128)S(1)} %copy.20), channel_id=1, source_target_pairs={{1,0},{2,1},{3,2},{5,4},{6,5},{7,6},{9,8},{10,9},{11,10},{13,12},{... | collective-permute-start | bytes 1658888 | tf_op jit(solution)/shard_map/ppermute | solution.py:30
  19.7 4.7 %collective-permute-start.2 = (f32[3,36,10,128]{3,1,2,0:T(8,128)S(1)}, f32[3,36,10,128]{3,1,2,0:T(8,128)S(1)}, u32[]{:S(2)}, u32[]{:S(2)}) collective-permute-start(f32[3,36,10,128]{3,1,2,0:T(8,128)S(1)} %copy.19), channel_id=1, source_target_pairs={{0,1},{1,2},{2,3},{4,5},{5,6},{6,7},{8,9},{9,10},{10,11},{12,13},{... | collective-permute-start | bytes 1658888 | tf_op jit(solution)/shard_map/ppermute | solution.py:30
  24.7 1.3 %copy-start.1 = (f32[3,36,36,128]{3,2,1,0:T(8,128)}, f32[3,36,36,128]{3,2,1,0:T(8,128)S(1)}, u32[]{:S(2)}) copy-start(f32[3,36,36,128]{3,2,1,0:T(8,128)S(1)} %pad_maximum_fusion.1.ext_ref) | copy-start | bytes 5971972
  31.7 1.7 %copy-start.2 = (f32[36,36,128]{2,1,0:T(8,128)S(1)}, f32[36,36,128]{2,1,0:T(8,128)}, u32[]{:S(2)}) copy-start(f32[36,36,128]{2,1,0:T(8,128)} %get-tuple-element.10) | copy-start | bytes 1990660
  33.4 1.1 %copy-start.4 = (f32[36,36,128]{2,1,0:T(8,128)S(1)}, f32[36,36,128]{2,1,0:T(8,128)}, u32[]{:S(2)}) copy-start(f32[36,36,128]{2,1,0:T(8,128)} %get-tuple-element.9) | copy-start | bytes 1990660
  33.6 1.2 %copy-start = (f32[36,36,128]{2,1,0:T(8,128)S(1)}, f32[36,36,128]{2,1,0:T(8,128)}, u32[]{:S(2)}) copy-start(f32[36,36,128]{2,1,0:T(8,128)} %get-tuple-element.12) | copy-start | bytes 1990660
  37.4 1.1 %copy-start.3 = (f32[36,36,128]{2,1,0:T(8,128)S(1)}, f32[36,36,128]{2,1,0:T(8,128)}, u32[]{:S(2)}) copy-start(f32[36,36,128]{2,1,0:T(8,128)} %get-tuple-element.11) | copy-start | bytes 1990660
  46.6 14.9 %collective-permute-start.10 = (f32[5,4,4,32]{3,2,1,0:T(4,128)S(1)}, f32[5,4,4,32]{3,2,1,0:T(4,128)S(1)}, u32[]{:S(2)}, u32[]{:S(2)}) collective-permute-start(f32[5,4,4,32]{3,2,1,0:T(4,128)S(1)} %pad_maximum_fusion.21), channel_id=1, source_target_pairs={{0,1},{1,2},{2,3},{3,0},{4,5},{5,6},{6,7},{7,4},{8,9},{9,10},{10,1... | collective-permute-start | bytes 30728 | tf_op jit(solution)/shard_map/ppermute | solution.py:242
  53.4 8.2 %collective-permute-start.9 = (f32[5,4,4,32]{3,2,1,0:T(4,128)S(1)}, f32[5,4,4,32]{3,2,1,0:T(4,128)S(1)}, u32[]{:S(2)}, u32[]{:S(2)}) collective-permute-start(f32[5,4,4,32]{3,2,1,0:T(4,128)S(1)} %pad_maximum_fusion.21), channel_id=1, source_target_pairs={{0,2},{1,3},{2,0},{3,1},{4,6},{5,7},{6,4},{7,5},{8,10},{9,11},{10,... | collective-permute-start | bytes 30728 | tf_op jit(solution)/shard_map/ppermute | solution.py:242
  55.8 5.8 %collective-permute-start.8 = (f32[5,4,4,32]{3,2,1,0:T(4,128)S(1)}, f32[5,4,4,32]{3,2,1,0:T(4,128)S(1)}, u32[]{:S(2)}, u32[]{:S(2)}) collective-permute-start(f32[5,4,4,32]{3,2,1,0:T(4,128)S(1)} %pad_maximum_fusion.21), channel_id=1, source_target_pairs={{0,3},{1,0},{2,1},{3,2},{4,7},{5,4},{6,5},{7,6},{8,11},{9,8},{10,9... | collective-permute-start | bytes 30728 | tf_op jit(solution)/shard_map/ppermute | solution.py:242
  57.2 14.3 %collective-permute-start.5 = (f32[2,8,5,64]{3,2,1,0:T(8,128)S(1)}, f32[2,8,5,64]{3,2,1,0:T(8,128)S(1)}, u32[]{:S(2)}, u32[]{:S(2)}) collective-permute-start(f32[2,8,5,64]{3,2,1,0:T(8,128)S(1)} %get-tuple-element.160), channel_id=1, source_target_pairs={{1,0},{2,1},{3,2},{5,4},{6,5},{7,6},{9,8},{10,9},{11,10},{13,12},{... | collective-permute-start | bytes 61448 | tf_op jit(solution)/shard_map/ppermute | solution.py:30
  58.5 15.9 %collective-permute-start.4 = (f32[2,8,5,64]{3,2,1,0:T(8,128)S(1)}, f32[2,8,5,64]{3,2,1,0:T(8,128)S(1)}, u32[]{:S(2)}, u32[]{:S(2)}) collective-permute-start(f32[2,8,5,64]{3,2,1,0:T(8,128)S(1)} %get-tuple-element.159), channel_id=1, source_target_pairs={{0,1},{1,2},{2,3},{4,5},{5,6},{6,7},{8,9},{9,10},{10,11},{12,13},{... | collective-permute-start | bytes 61448 | tf_op jit(solution)/shard_map/ppermute | solution.py:30
  61.6 15.5 %collective-permute-start.12 = (f32[5,4,16,32]{3,2,1,0:T(8,128)S(1)}, f32[5,4,16,32]{3,2,1,0:T(8,128)S(1)}, u32[]{:S(2)}, u32[]{:S(2)}) collective-permute-start(f32[5,4,16,32]{3,2,1,0:T(8,128)S(1)} %pad_maximum_fusion.7), channel_id=1, source_target_pairs={{0,8},{4,12},{8,16},{12,20},{16,24},{20,28},{1,9},{5,13},{9,17},{1... | collective-permute-start | bytes 122888 | tf_op jit(solution)/shard_map/ppermute | solution.py:30
  65.1 10.7 %collective-permute-start.11 = (f32[5,4,16,32]{3,2,1,0:T(8,128)S(1)}, f32[5,4,16,32]{3,2,1,0:T(8,128)S(1)}, u32[]{:S(2)}, u32[]{:S(2)}) collective-permute-start(f32[5,4,16,32]{3,2,1,0:T(8,128)S(1)} %pad_maximum_fusion.7), channel_id=1, source_target_pairs={{0,12},{4,16},{8,20},{12,24},{16,28},{1,13},{5,17},{9,21},{13,25},... | collective-permute-start | bytes 122888 | tf_op jit(solution)/shard_map/ppermute | solution.py:30
  68.6 10.7 %collective-permute-start.13 = (f32[5,4,16,32]{3,2,1,0:T(8,128)S(1)}, f32[5,4,16,32]{3,2,1,0:T(8,128)S(1)}, u32[]{:S(2)}, u32[]{:S(2)}) collective-permute-start(f32[5,4,16,32]{3,2,1,0:T(8,128)S(1)} %pad_maximum_fusion.7), channel_id=1, source_target_pairs={{0,4},{4,8},{8,12},{12,16},{16,20},{20,24},{24,28},{1,5},{5,9},{9,... | collective-permute-start | bytes 122888 | tf_op jit(solution)/shard_map/ppermute | solution.py:30
  71.5 12.8 %collective-permute-start.14 = (f32[5,4,16,32]{3,2,1,0:T(8,128)S(1)}, f32[5,4,16,32]{3,2,1,0:T(8,128)S(1)}, u32[]{:S(2)}, u32[]{:S(2)}) collective-permute-start(f32[5,4,16,32]{3,2,1,0:T(8,128)S(1)} %pad_maximum_fusion.7), channel_id=1, source_target_pairs={{4,0},{8,4},{12,8},{16,12},{20,16},{24,20},{28,24},{5,1},{9,5},{13... | collective-permute-start | bytes 122888 | tf_op jit(solution)/shard_map/ppermute | solution.py:30
  74.5 9.8 %collective-permute-start.15 = (f32[5,4,16,32]{3,2,1,0:T(8,128)S(1)}, f32[5,4,16,32]{3,2,1,0:T(8,128)S(1)}, u32[]{:S(2)}, u32[]{:S(2)}) collective-permute-start(f32[5,4,16,32]{3,2,1,0:T(8,128)S(1)} %pad_maximum_fusion.7), channel_id=1, source_target_pairs={{8,0},{12,4},{16,8},{20,12},{24,16},{28,20},{9,1},{13,5},{17,9},{2... | collective-permute-start | bytes 122888 | tf_op jit(solution)/shard_map/ppermute | solution.py:30
  75.8 15.8 %collective-permute-start.16 = (f32[5,4,16,32]{3,2,1,0:T(8,128)S(1)}, f32[5,4,16,32]{3,2,1,0:T(8,128)S(1)}, u32[]{:S(2)}, u32[]{:S(2)}) collective-permute-start(f32[5,4,16,32]{3,2,1,0:T(8,128)S(1)} %pad_maximum_fusion.7), channel_id=1, source_target_pairs={{12,0},{16,4},{20,8},{24,12},{28,16},{13,1},{17,5},{21,9},{25,13},... | collective-permute-start | bytes 122888 | tf_op jit(solution)/shard_map/ppermute | solution.py:30
  77.2 20.9 %collective-permute-start.7 = (f32[2,5,18,64]{3,2,1,0:T(8,128)S(1)}, f32[2,5,18,64]{3,2,1,0:T(8,128)S(1)}, u32[]{:S(2)}, u32[]{:S(2)}) collective-permute-start(f32[2,5,18,64]{3,2,1,0:T(8,128)S(1)} %get-tuple-element.77), channel_id=1, source_target_pairs={{4,0},{8,4},{12,8},{16,12},{20,16},{24,20},{28,24},{5,1},{9,5},{13... | collective-permute-start | bytes 138248 | tf_op jit(solution)/shard_map/ppermute | solution.py:30
  79.3 18.8 %collective-permute-start.6 = (f32[2,5,18,64]{3,2,1,0:T(8,128)S(1)}, f32[2,5,18,64]{3,2,1,0:T(8,128)S(1)}, u32[]{:S(2)}, u32[]{:S(2)}) collective-permute-start(f32[2,5,18,64]{3,2,1,0:T(8,128)S(1)} %get-tuple-element.76), channel_id=1, source_target_pairs={{0,4},{4,8},{8,12},{12,16},{16,20},{20,24},{24,28},{1,5},{5,9},{9,... | collective-permute-start | bytes 138248 | tf_op jit(solution)/shard_map/ppermute | solution.py:30

commit v7 on v5

--- a/solution.py
+++ b/solution.py
@@ -242,10 +242,10 @@
     mext = jnp.concatenate([south, mpack, north], axis=2)
     full = jnp.concatenate(blocks, axis=2)
     reach = 3
-    parts = [shift_from(full, "gx", -d) for d in range(reach, 0, -1)]
-    parts += [full]
-    parts += [shift_from(full, "gx", d) for d in range(1, reach + 1)]
-    cpack = jnp.concatenate(parts, axis=1)
+    every = lax.all_gather(full, "gx", axis=0)
+    every = jnp.pad(every, ((reach, reach),) + ((0, 0),) * full.ndim)
+    near = lax.dynamic_slice_in_dim(every, ix, 2 * reach + 1, axis=0)
+    cpack = jnp.concatenate([near[k] for k in range(2 * reach + 1)], axis=1)
     west_m = shift_from(mext[:, nm - hm :], "gx", -1)
     east_m = shift_from(mext[:, :hm], "gx", 1)
     mext = jnp.concatenate([west_m, mext, east_m], axis=1)

time: 103 us -> 116 us (1.13)
  blocking collectives: 0 us -> 33 us
  starting transfers between devices: 48.1 us -> 32.7 us
  waiting for transfers between devices: 17.1 us -> 12.9 us
    all_gather x0 -> x1, blocking collectives: none -> 33 us  [local(): every = lax.all_gather(full, 'gx', axis=0)]
    ppermute x14 -> x8, starting transfers between devices: 37.5 us -> 22.2 us  [shift_from(): return lax.ppermute(cells, axis, pairs)]
    ppermute x14 -> x8, waiting for transfers between devices: 17.1 us -> 12.9 us  [shift_from(): return lax.ppermute(cells, axis, pairs)]
  transfers between devices with their start and end apart: 17 -> 11, of which waited for: 4 -> 5; matrix products, arithmetic and copies ran while one was open for 7% -> 6% of each run, Pallas kernels for 0% -> 0%
where the time goes in v7:
time: 116 us; the launch traced here: 115 us
  blocking collectives  33 us (28%)
  starting transfers between devices  32.7 us (28%)
  other arithmetic  14.5 us (12%)
  waiting for transfers between devices  12.9 us (11%)
  local copies, waits for them, and re-layouts  10.2 us (9%)
  Pallas kernels  5.46 us (5%)
  matrix products  5.19 us (4%)
    all_gather x1, blocking collectives, local(): every = lax.all_gather(full, 'gx', axis=0)  33 us
    ppermute x8, starting transfers between devices, shift_from(): return lax.ppermute(cells, axis, pairs)  22.2 us
    ppermute x8, waiting for transfers between devices, shift_from(): return lax.ppermute(cells, axis, pairs)  12.9 us
    ppermute x3, starting transfers between devices, local(): blocks.append(lax.ppermute(cpack, 'gy', pairs))  10.6 us
    pallas_call x1, Pallas kernels, soil_fields(): pl.pallas_call(fields_kernel, out_shape=jax.ShapeDtypeStruct((4,) + conc....  5.46 us
    add x7, other arithmetic, chebyshev(): iterate = win(iterate, n, cur, nxt) + update  4.58 us
    add x8, other arithmetic, local(): u = centre + jacobi_weight * ((csrc[sl] - applied) / cdiag[sl])  2.49 us
  transfers between devices with their start and end apart: 11, of which 5 were waited for; matrix products, arithmetic and copies ran while one was open for 6% of the time, Pallas kernels for 0%

profile of v7, /device:TPU:4, one launch (start us, length us, event | category | flops | bytes accessed | tf_op | source)
XLA Modules:
  0.0 115.0 jit_solution(6443909215869724878)
XLA Ops:
  0.0 1.0 convert_bitcast_fusion
  1.0 1.0 pad_maximum_fusion.4
  2.0 1.9 %collective-permute-start.1 = (f32[3,10,16,128]{3,2,1,0:T(8,128)S(1)}, f32[3,10,16,128]{3,2,1,0:T(8,128)S(1)}, u32[]{:S(2)}, u32[]{:S(2)}) collective-permute-start(f32[3,10,16,128]{3,2,1,0:T(8,128)S(1)} %get-tuple-element.57), channel_id=1, source_target_pairs={{4,0},{8,4},{12,8},{16,12},{20,16},{24,20},{28,24},{5,1},{9,5},{13... | collective-permute-start | bytes 737288 | tf_op jit(solution)/shard_map/ppermute | solution.py:30
  3.9 4.8 %collective-permute-start = (f32[3,10,16,128]{3,2,1,0:T(8,128)S(1)}, f32[3,10,16,128]{3,2,1,0:T(8,128)S(1)}, u32[]{:S(2)}, u32[]{:S(2)}) collective-permute-start(f32[3,10,16,128]{3,2,1,0:T(8,128)S(1)} %get-tuple-element.56), channel_id=1, source_target_pairs={{0,4},{4,8},{8,12},{12,16},{16,20},{20,24},{24,28},{1,5},{5,9},{9,... | collective-permute-start | bytes 737288 | tf_op jit(solution)/shard_map/ppermute | solution.py:30
  8.9 3.7 %collective-permute-done.1 = f32[3,10,16,128]{3,2,1,0:T(8,128)S(1)} collective-permute-done((f32[3,10,16,128]{3,2,1,0:T(8,128)S(1)}, f32[3,10,16,128]{3,2,1,0:T(8,128)S(1)}, u32[]{:S(2)}, u32[]{:S(2)}) %collective-permute-start.1) | collective-permute-done | bytes 245792 | tf_op jit(solution)/shard_map/ppermute | solution.py:30
  12.6 5.2 %collective-permute-done = f32[3,10,16,128]{3,2,1,0:T(8,128)S(1)} collective-permute-done((f32[3,10,16,128]{3,2,1,0:T(8,128)S(1)}, f32[3,10,16,128]{3,2,1,0:T(8,128)S(1)}, u32[]{:S(2)}, u32[]{:S(2)}) %collective-permute-start) | collective-permute-done | bytes 245792 | tf_op jit(solution)/shard_map/ppermute | solution.py:30
  18.2 1.3 %collective-permute-start.3 = (f32[3,36,10,128]{3,1,2,0:T(8,128)S(1)}, f32[3,36,10,128]{3,1,2,0:T(8,128)S(1)}, u32[]{:S(2)}, u32[]{:S(2)}) collective-permute-start(f32[3,36,10,128]{3,1,2,0:T(8,128)S(1)} %copy.20), channel_id=1, source_target_pairs={{1,0},{2,1},{3,2},{5,4},{6,5},{7,6},{9,8},{10,9},{11,10},{13,12},{... | collective-permute-start | bytes 1658888 | tf_op jit(solution)/shard_map/ppermute | solution.py:30
  19.7 3.1 %collective-permute-start.2 = (f32[3,36,10,128]{3,1,2,0:T(8,128)S(1)}, f32[3,36,10,128]{3,1,2,0:T(8,128)S(1)}, u32[]{:S(2)}, u32[]{:S(2)}) collective-permute-start(f32[3,36,10,128]{3,1,2,0:T(8,128)S(1)} %copy.19), channel_id=1, source_target_pairs={{0,1},{1,2},{2,3},{4,5},{5,6},{6,7},{8,9},{9,10},{10,11},{12,13},{... | collective-permute-start | bytes 1658888 | tf_op jit(solution)/shard_map/ppermute | solution.py:30
  22.7 0.6 pad_add_fusion.bounds_ref
  23.5 0.8 collective-permute-done.2
  24.5 0.2 pad_maximum_fusion
  24.7 1.3 %slice_bitcast_fusion.3 = (f32[36,36,128]{2,1,0:T(8,128)}, f32[36,36,128]{2,1,0:T(8,128)}, f32[36,36,128]{2,1,0:T(8,128)S(1)}) fusion(f32[3,36,36,128]{3,2,1,0:T(8,128)S(1)} %pad_maximum_fusion), kind=kLoop, calls=%fused_computation.26 | loop fusion | bytes 3981312 | tf_op jit(solution)/shard_map/squeeze | solution.py:210
  26.0 5.5 %shard_map.46 = f32[4,36,36,128]{3,2,1,0:T(8,128)} custom-call(s32[4]{0:T(128)} %pad_add_fusion.bounds_ref, f32[5,8]{1,0:T(8,128)} %table_ref.1, f32[36,36,128]{2,1,0:T(8,128)} %get-tuple-element.33.conc_ref, f32[36,36,128]{2,1,0:T(8,128)} %get-tuple-element.32.idf_ref), custom_call_target="tpu_custom_call" | custom-call | flops 16588800 | bytes 3981312 | tf_op jit(solution)/shard_map/pallas_call | solution.py:183
  31.5 1.9 %slice_bitcast_fusion.2 = (f32[36,36,128]{2,1,0:T(8,128)S(1)}, f32[36,36,128]{2,1,0:T(8,128)S(1)}, f32[36,36,128]{2,1,0:T(8,128)S(1)}) fusion(f32[4,36,36,128]{3,2,1,0:T(8,128)} %shard_map.46), kind=kLoop, calls=%fused_computation.25 | loop fusion | bytes 3981312 | tf_op jit(solution)/shard_map/squeeze | solution.py:83
  33.3 0.6 copy-done
  34.1 0.3 maximum_divide_fusion
  34.6 0.8 fusion.4
  35.8 1.2 %slice_add_fusion.5 = (f32[32,32,128]{2,1,0:T(8,128)S(1)}, f32[32,32,128]{2,1,0:T(8,128)S(1)}) fusion(f32[34,34,128]{2,1,0:T(8,128)S(1)} %get-tuple-element.27, f32[34,34,128]{2,1,0:T(8,128)S(1)} %get-tuple-element.28, f32[32,32,127]{2,1,0:T(8,128)S(1)} %get-tuple-element.45, f32[32,32,1]{2,1,0:T(8,128)S(1)} %get-tuple-element.47, ...), kind=kLoop, calls=%fused_computation.64 | loop fusion | flops 3538944 | bytes 9046976 | tf_op jit(solution)/shard_map/add | solution.py:147
  37.6 0.8 fusion.343
  38.4 1.5 %convolution_multiply_fusion = f32[72,18,64]{2,1,0:T(8,128)S(1)} fusion(f32[72,36,64]{2,1,0:T(8,128)S(1)} %fusion.343, f32[18,36]{1,0:T(8,128)S(1)} %fusion.364), kind=kOutput, calls=%fused_computation.9 | convolution fusion | flops 35914752 | bytes 997920 | tf_op jit(solution)/shard_map/dot_general | solution.py:68
  40.3 1.2 %fusion.22 = f32[30,30,128]{2,1,0:T(8,128)S(1)} fusion(f32[34,34,128]{2,1,0:T(8,128)S(1)} %get-tuple-element.28, f32[32,32,128]{2,1,0:T(8,128)S(1)} %get-tuple-element.25, f32[36,35,128]{2,1,0:T(8,128)S(1)} %maximum_divide_fusion.1, f32[35,36,128]{2,1,0:T(8,128)S(1)} %divide_bitcast_fusion, f32[36,36,128]{2,1,0:T(8,128)S(1)} %get-tuple-element.30, ...), kind=kLoop, calls=%fused_computation.68 | loop fusion | flops 3110400 | bytes 8031168 | tf_op jit(solution)/shard_map/add | solution.py:147
  41.9 0.9 fusion.40
  43.2 0.3 divide_multiply_fusion.3
  44.9 0.3 convolution_multiply_fusion.2
  45.4 6.7 %collective-permute-start.10 = (f32[5,4,4,32]{3,2,1,0:T(4,128)S(1)}, f32[5,4,4,32]{3,2,1,0:T(4,128)S(1)}, u32[]{:S(2)}, u32[]{:S(2)}) collective-permute-start(f32[5,4,4,32]{3,2,1,0:T(4,128)S(1)} %pad_maximum_fusion.11), channel_id=1, source_target_pairs={{0,1},{1,2},{2,3},{3,0},{4,5},{5,6},{6,7},{7,4},{8,9},{9,10},{10,1... | collective-permute-start | bytes 30728 | tf_op jit(solution)/shard_map/ppermute | solution.py:239
  52.1 2.4 %collective-permute-start.9 = (f32[5,4,4,32]{3,2,1,0:T(4,128)S(1)}, f32[5,4,4,32]{3,2,1,0:T(4,128)S(1)}, u32[]{:S(2)}, u32[]{:S(2)}) collective-permute-start(f32[5,4,4,32]{3,2,1,0:T(4,128)S(1)} %pad_maximum_fusion.11), channel_id=1, source_target_pairs={{0,2},{1,3},{2,0},{3,1},{4,6},{5,7},{6,4},{7,5},{8,10},{9,11},{10,... | collective-permute-start | bytes 30728 | tf_op jit(solution)/shard_map/ppermute | solution.py:239
  54.5 1.4 %collective-permute-start.8 = (f32[5,4,4,32]{3,2,1,0:T(4,128)S(1)}, f32[5,4,4,32]{3,2,1,0:T(4,128)S(1)}, u32[]{:S(2)}, u32[]{:S(2)}) collective-permute-start(f32[5,4,4,32]{3,2,1,0:T(4,128)S(1)} %pad_maximum_fusion.11), channel_id=1, source_target_pairs={{0,3},{1,0},{2,1},{3,2},{4,7},{5,4},{6,5},{7,6},{8,11},{9,8},{10,9... | collective-permute-start | bytes 30728 | tf_op jit(solution)/shard_map/ppermute | solution.py:239
  55.9 1.3 %collective-permute-start.5 = (f32[2,8,5,64]{3,2,1,0:T(8,128)S(1)}, f32[2,8,5,64]{3,2,1,0:T(8,128)S(1)}, u32[]{:S(2)}, u32[]{:S(2)}) collective-permute-start(f32[2,8,5,64]{3,2,1,0:T(8,128)S(1)} %get-tuple-element.156), channel_id=1, source_target_pairs={{1,0},{2,1},{3,2},{5,4},{6,5},{7,6},{9,8},{10,9},{11,10},{13,12},{... | collective-permute-start | bytes 61448 | tf_op jit(solution)/shard_map/ppermute | solution.py:30
  57.2 3.0 %collective-permute-start.4 = (f32[2,8,5,64]{3,2,1,0:T(8,128)S(1)}, f32[2,8,5,64]{3,2,1,0:T(8,128)S(1)}, u32[]{:S(2)}, u32[]{:S(2)}) collective-permute-start(f32[2,8,5,64]{3,2,1,0:T(8,128)S(1)} %get-tuple-element.155), channel_id=1, source_target_pairs={{0,1},{1,2},{2,3},{4,5},{5,6},{6,7},{8,9},{9,10},{10,11},{12,13},{... | collective-permute-start | bytes 61448 | tf_op jit(solution)/shard_map/ppermute | solution.py:30
  60.4 33.0 %all-gather = f32[40,4,16,32]{3,2,1,0:T(8,128)S(1)} all-gather(f32[5,4,16,32]{3,2,1,0:T(8,128)S(1)} %pad_maximum_fusion.7), channel_id=2, replica_groups=mesh['gx'=8,'gy'=4] {'gx'}, dimensions={0}, use_global_device_ids=true | all-gather | bytes 368640 | tf_op jit(solution)/shard_map/all_gather | solution.py:245
  94.9 0.5 fusion.87
  95.7 0.4 multiply_add_fusion
  96.4 0.3 multiply_add_fusion.1
  97.0 0.3 multiply_add_fusion.2
  97.6 0.3 multiply_add_fusion.3
  98.1 0.3 multiply_add_fusion.4
  99.7 3.6 %collective-permute-start.7 = (f32[2,5,18,64]{3,2,1,0:T(8,128)S(1)}, f32[2,5,18,64]{3,2,1,0:T(8,128)S(1)}, u32[]{:S(2)}, u32[]{:S(2)}) collective-permute-start(f32[2,5,18,64]{3,2,1,0:T(8,128)S(1)} %get-tuple-element.83), channel_id=1, source_target_pairs={{4,0},{8,4},{12,8},{16,12},{20,16},{24,20},{28,24},{5,1},{9,5},{13... | collective-permute-start | bytes 138248 | tf_op jit(solution)/shard_map/ppermute | solution.py:30
  103.3 3.1 %collective-permute-start.6 = (f32[2,5,18,64]{3,2,1,0:T(8,128)S(1)}, f32[2,5,18,64]{3,2,1,0:T(8,128)S(1)}, u32[]{:S(2)}, u32[]{:S(2)}) collective-permute-start(f32[2,5,18,64]{3,2,1,0:T(8,128)S(1)} %get-tuple-element.82), channel_id=1, source_target_pairs={{0,4},{4,8},{8,12},{12,16},{16,20},{20,24},{24,28},{1,5},{5,9},{9,... | collective-permute-start | bytes 138248 | tf_op jit(solution)/shard_map/ppermute | solution.py:30
  106.4 0.4 fusion.325
  106.9 0.5 collective-permute-done.7
  107.3 2.7 %collective-permute-done.6 = f32[2,5,18,64]{3,2,1,0:T(8,128)S(1)} collective-permute-done((f32[2,5,18,64]{3,2,1,0:T(8,128)S(1)}, f32[2,5,18,64]{3,2,1,0:T(8,128)S(1)}, u32[]{:S(2)}, u32[]{:S(2)}) %collective-permute-start.6) | collective-permute-done | bytes 46112 | tf_op jit(solution)/shard_map/ppermute | solution.py:30
  110.4 0.3 slice_add_fusion.10
  110.9 0.3 slice_add_fusion.11
  111.4 0.4 fusion.267
  111.8 0.5 fusion.322
  112.6 0.4 slice_add_fusion.7
  113.3 0.5 slice_add_fusion.9
  114.1 1.0 fusion.190
  (145 shorter events, 10.2 us)
Async XLA Ops:
  0.0 17.8 %copy-start.1 = (f32[16,16,128]{2,1,0:T(8,128)S(1)}, f32[16,16,128]{2,1,0:T(8,128)}, u32[]{:S(2)}) copy-start(f32[16,16,128]{2,1,0:T(8,128)} %param.5) | copy-start | bytes 393220
  0.0 17.8 %copy-start.2 = (f32[16,16,128]{2,1,0:T(8,128)S(1)}, f32[16,16,128]{2,1,0:T(8,128)}, u32[]{:S(2)}) copy-start(f32[16,16,128]{2,1,0:T(8,128)} %param.4) | copy-start | bytes 393220
  2.0 10.6 %collective-permute-start.1 = (f32[3,10,16,128]{3,2,1,0:T(8,128)S(1)}, f32[3,10,16,128]{3,2,1,0:T(8,128)S(1)}, u32[]{:S(2)}, u32[]{:S(2)}) collective-permute-start(f32[3,10,16,128]{3,2,1,0:T(8,128)S(1)} %get-tuple-element.57), channel_id=1, source_target_pairs={{4,0},{8,4},{12,8},{16,12},{20,16},{24,20},{28,24},{5,1},{9,5},{13... | collective-permute-start | bytes 737288 | tf_op jit(solution)/shard_map/ppermute | solution.py:30
  3.9 13.8 %collective-permute-start = (f32[3,10,16,128]{3,2,1,0:T(8,128)S(1)}, f32[3,10,16,128]{3,2,1,0:T(8,128)S(1)}, u32[]{:S(2)}, u32[]{:S(2)}) collective-permute-start(f32[3,10,16,128]{3,2,1,0:T(8,128)S(1)} %get-tuple-element.56), channel_id=1, source_target_pairs={{0,4},{4,8},{8,12},{12,16},{16,20},{20,24},{24,28},{1,5},{5,9},{9,... | collective-permute-start | bytes 737288 | tf_op jit(solution)/shard_map/ppermute | solution.py:30
  18.2 5.2 %collective-permute-start.3 = (f32[3,36,10,128]{3,1,2,0:T(8,128)S(1)}, f32[3,36,10,128]{3,1,2,0:T(8,128)S(1)}, u32[]{:S(2)}, u32[]{:S(2)}) collective-permute-start(f32[3,36,10,128]{3,1,2,0:T(8,128)S(1)} %copy.20), channel_id=1, source_target_pairs={{1,0},{2,1},{3,2},{5,4},{6,5},{7,6},{9,8},{10,9},{11,10},{13,12},{... | collective-permute-start | bytes 1658888 | tf_op jit(solution)/shard_map/ppermute | solution.py:30
  19.7 4.7 %collective-permute-start.2 = (f32[3,36,10,128]{3,1,2,0:T(8,128)S(1)}, f32[3,36,10,128]{3,1,2,0:T(8,128)S(1)}, u32[]{:S(2)}, u32[]{:S(2)}) collective-permute-start(f32[3,36,10,128]{3,1,2,0:T(8,128)S(1)} %copy.19), channel_id=1, source_target_pairs={{0,1},{1,2},{2,3},{4,5},{5,6},{6,7},{8,9},{9,10},{10,11},{12,13},{... | collective-permute-start | bytes 1658888 | tf_op jit(solution)/shard_map/ppermute | solution.py:30
  31.5 2.5 %copy-start = (f32[4,36,36,128]{3,2,1,0:T(8,128)S(1)}, f32[4,36,36,128]{3,2,1,0:T(8,128)}, u32[]{:S(2)}) copy-start(f32[4,36,36,128]{3,2,1,0:T(8,128)} %shard_map.46) | copy-start | bytes 7962628
  45.4 14.9 %collective-permute-start.10 = (f32[5,4,4,32]{3,2,1,0:T(4,128)S(1)}, f32[5,4,4,32]{3,2,1,0:T(4,128)S(1)}, u32[]{:S(2)}, u32[]{:S(2)}) collective-permute-start(f32[5,4,4,32]{3,2,1,0:T(4,128)S(1)} %pad_maximum_fusion.11), channel_id=1, source_target_pairs={{0,1},{1,2},{2,3},{3,0},{4,5},{5,6},{6,7},{7,4},{8,9},{9,10},{10,1... | collective-permute-start | bytes 30728 | tf_op jit(solution)/shard_map/ppermute | solution.py:239
  52.1 8.2 %collective-permute-start.9 = (f32[5,4,4,32]{3,2,1,0:T(4,128)S(1)}, f32[5,4,4,32]{3,2,1,0:T(4,128)S(1)}, u32[]{:S(2)}, u32[]{:S(2)}) collective-permute-start(f32[5,4,4,32]{3,2,1,0:T(4,128)S(1)} %pad_maximum_fusion.11), channel_id=1, source_target_pairs={{0,2},{1,3},{2,0},{3,1},{4,6},{5,7},{6,4},{7,5},{8,10},{9,11},{10,... | collective-permute-start | bytes 30728 | tf_op jit(solution)/shard_map/ppermute | solution.py:239
  54.5 5.8 %collective-permute-start.8 = (f32[5,4,4,32]{3,2,1,0:T(4,128)S(1)}, f32[5,4,4,32]{3,2,1,0:T(4,128)S(1)}, u32[]{:S(2)}, u32[]{:S(2)}) collective-permute-start(f32[5,4,4,32]{3,2,1,0:T(4,128)S(1)} %pad_maximum_fusion.11), channel_id=1, source_target_pairs={{0,3},{1,0},{2,1},{3,2},{4,7},{5,4},{6,5},{7,6},{8,11},{9,8},{10,9... | collective-permute-start | bytes 30728 | tf_op jit(solution)/shard_map/ppermute | solution.py:239
  55.9 43.6 %collective-permute-start.5 = (f32[2,8,5,64]{3,2,1,0:T(8,128)S(1)}, f32[2,8,5,64]{3,2,1,0:T(8,128)S(1)}, u32[]{:S(2)}, u32[]{:S(2)}) collective-permute-start(f32[2,8,5,64]{3,2,1,0:T(8,128)S(1)} %get-tuple-element.156), channel_id=1, source_target_pairs={{1,0},{2,1},{3,2},{5,4},{6,5},{7,6},{9,8},{10,9},{11,10},{13,12},{... | collective-permute-start | bytes 61448 | tf_op jit(solution)/shard_map/ppermute | solution.py:30
  57.2 42.3 %collective-permute-start.4 = (f32[2,8,5,64]{3,2,1,0:T(8,128)S(1)}, f32[2,8,5,64]{3,2,1,0:T(8,128)S(1)}, u32[]{:S(2)}, u32[]{:S(2)}) collective-permute-start(f32[2,8,5,64]{3,2,1,0:T(8,128)S(1)} %get-tuple-element.155), channel_id=1, source_target_pairs={{0,1},{1,2},{2,3},{4,5},{5,6},{6,7},{8,9},{9,10},{10,11},{12,13},{... | collective-permute-start | bytes 61448 | tf_op jit(solution)/shard_map/ppermute | solution.py:30
  99.7 7.7 %collective-permute-start.7 = (f32[2,5,18,64]{3,2,1,0:T(8,128)S(1)}, f32[2,5,18,64]{3,2,1,0:T(8,128)S(1)}, u32[]{:S(2)}, u32[]{:S(2)}) collective-permute-start(f32[2,5,18,64]{3,2,1,0:T(8,128)S(1)} %get-tuple-element.83), channel_id=1, source_target_pairs={{4,0},{8,4},{12,8},{16,12},{20,16},{24,20},{28,24},{5,1},{9,5},{13... | collective-permute-start | bytes 138248 | tf_op jit(solution)/shard_map/ppermute | solution.py:30
  103.3 6.8 %collective-permute-start.6 = (f32[2,5,18,64]{3,2,1,0:T(8,128)S(1)}, f32[2,5,18,64]{3,2,1,0:T(8,128)S(1)}, u32[]{:S(2)}, u32[]{:S(2)}) collective-permute-start(f32[2,5,18,64]{3,2,1,0:T(8,128)S(1)} %get-tuple-element.82), channel_id=1, source_target_pairs={{0,4},{4,8},{8,12},{12,16},{16,20},{20,24},{24,28},{1,5},{5,9},{9,... | collective-permute-start | bytes 138248 | tf_op jit(solution)/shard_map/ppermute | solution.py:30

commit v8 on v5

--- a/solution.py
+++ b/solution.py
@@ -39,6 +39,37 @@
             [shift_from(tail, axis, -1), cells, shift_from(head, axis, 1)], axis=dim
         )
     return cells
+
+
+def corner_from(cells, dx, dy):
+    cx, cy = lax.axis_size("gx"), lax.axis_size("gy")
+    pairs = []
+    for i in range(cx):
+        for j in range(cy):
+            si, sj = i + dx, j + dy
+            if 0 <= si < cx and 0 <= sj < cy:
+                pairs.append((si * cy + sj, i * cy + j))
+    if not pairs:
+        return jnp.zeros_like(cells)
+    return lax.ppermute(cells, ("gx", "gy"), pairs)
+
+
+def halo_once(cells, width):
+    sx, sy = cells.shape[1], cells.shape[2]
+    lo_x, hi_x = cells[:, sx - width :], cells[:, :width]
+    lo_y, hi_y = cells[:, :, sy - width :], cells[:, :, :width]
+    west = shift_from(lo_x, "gx", -1)
+    east = shift_from(hi_x, "gx", 1)
+    south = shift_from(lo_y, "gy", -1)
+    north = shift_from(hi_y, "gy", 1)
+    sw = corner_from(cells[:, sx - width :, sy - width :], -1, -1)
+    se = corner_from(cells[:, sx - width :, :width], -1, 1)
+    nw = corner_from(cells[:, :width, sy - width :], 1, -1)
+    ne = corner_from(cells[:, :width, :width], 1, 1)
+    top = jnp.concatenate([sw, west, se], axis=2)
+    mid = jnp.concatenate([south, cells, north], axis=2)
+    bottom = jnp.concatenate([nw, east, ne], axis=2)
+    return jnp.concatenate([top, mid, bottom], axis=1)
 
 
 def harmonic(first, second):
@@ -206,7 +237,7 @@
     iy = lax.axis_index("gy")
 
     stacked = jnp.stack([conc_prev, right_side, soil_id.astype(jnp.float32)])
-    ext = halo(stacked, (("gx", 1), ("gy", 2)), hf)
+    ext = halo_once(stacked, hf)
     conc, rhs, idf = ext[0], ext[1], ext[2]
     x_lo = hf - ix * n
     y_lo = hf - iy * ny

time: 103 us -> 112 us (1.087)
  starting transfers between devices: 48.1 us -> 56.3 us
  other arithmetic: 14.5 us -> 15.8 us
    ppermute x14, waiting for transfers between devices: 17.1 us -> 6.93 us  [shift_from(): return lax.ppermute(cells, axis, pairs)]
    ppermute x14, starting transfers between devices: 37.5 us -> 47.4 us  [shift_from(): return lax.ppermute(cells, axis, pairs)]
    ppermute x0 -> x4, waiting for transfers between devices: none -> 9.88 us  [corner_from(): return lax.ppermute(cells, ('gx', 'gy'), pairs)]
    ppermute x3, starting transfers between devices: 10.6 us -> 2.52 us  [local(): blocks.append(lax.ppermute(cpack, 'gy', pairs))]
    ppermute x0 -> x4, starting transfers between devices: none -> 6.36 us  [corner_from(): return lax.ppermute(cells, ('gx', 'gy'), pairs)]
    concatenate x2 -> x1, other arithmetic: 0.32 us -> 1.75 us  [halo_once(): return jnp.concatenate([top, mid, bottom], axis=1)]
  transfers between devices with their start and end apart: 17 -> 21, of which waited for: 4 -> 6; matrix products, arithmetic and copies ran while one was open for 7% -> 7% of each run, Pallas kernels for 0% -> 0%
where the time goes in v8:
time: 112 us
  starting transfers between devices  56.3 us (50%)
  waiting for transfers between devices  16.8 us (15%)
  other arithmetic  15.8 us (14%)
  local copies, waits for them, and re-layouts  10.9 us (10%)
  Pallas kernels  5.48 us (5%)
  matrix products  5.17 us (5%)
  between operations  1.19 us (1%)
    ppermute x14, starting transfers between devices, shift_from(): return lax.ppermute(cells, axis, pairs)  47.4 us
    ppermute x4, waiting for transfers between devices, corner_from(): return lax.ppermute(cells, ('gx', 'gy'), pairs)  9.88 us
    ppermute x14, waiting for transfers between devices, shift_from(): return lax.ppermute(cells, axis, pairs)  6.93 us
    ppermute x4, starting transfers between devices, corner_from(): return lax.ppermute(cells, ('gx', 'gy'), pairs)  6.36 us
    pallas_call x1, Pallas kernels, soil_fields(): pl.pallas_call(fields_kernel, out_shape=jax.ShapeDtypeStruct((4,) + conc....  5.48 us
    add x7, other arithmetic, chebyshev(): iterate = win(iterate, n, cur, nxt) + update  4.56 us
    ppermute x3, starting transfers between devices, local(): blocks.append(lax.ppermute(cpack, 'gy', pairs))  2.52 us
    add x8, other arithmetic, local(): u = centre + jacobi_weight * ((csrc[sl] - applied) / cdiag[sl])  2.5 us
  transfers between devices with their start and end apart: 21, of which 6 were waited for; matrix products, arithmetic and copies ran while one was open for 7% of the time, Pallas kernels for 0%

profile of v8, /device:TPU:4, one launch (start us, length us, event | category | flops | bytes accessed | tf_op | source)
XLA Modules:
  0.0 111.6 jit_solution(8819723218354284964)
XLA Ops:
  0.0 0.9 convert_bitcast_fusion
  0.9 1.0 pad_maximum_fusion.2
  2.0 1.4 %collective-permute-start.7 = (f32[3,10,10,128]{3,2,1,0:T(8,128)S(1)}, f32[3,10,10,128]{3,2,1,0:T(8,128)}, u32[]{:S(2)}, u32[]{:S(2)}) collective-permute-start(f32[3,10,10,128]{3,2,1,0:T(8,128)S(1)} %get-tuple-element.48), channel_id=1, source_target_pairs={{5,0},{6,1},{7,2},{9,4},{10,5},{11,6},{13,8},{14,9},{15,10},{17,12... | collective-permute-start | bytes 460808 | tf_op jit(solution)/shard_map/ppermute | solution.py:54
  3.5 0.8 fusion.387
  4.3 1.9 %collective-permute-start.6 = (f32[3,10,16,128]{3,2,1,0:T(8,128)}, f32[3,10,16,128]{3,2,1,0:T(8,128)}, u32[]{:S(2)}, u32[]{:S(2)}) collective-permute-start(f32[3,10,16,128]{3,2,1,0:T(8,128)} %get-tuple-element.51), channel_id=1, source_target_pairs={{4,0},{8,4},{12,8},{16,12},{20,16},{24,20},{28,24},{5,1},{9,5},{13... | collective-permute-start | bytes 737288 | tf_op jit(solution)/shard_map/ppermute | solution.py:30
  6.2 2.0 %collective-permute-start.5 = (f32[3,10,10,128]{3,2,1,0:T(8,128)S(1)}, f32[3,10,10,128]{3,2,1,0:T(8,128)}, u32[]{:S(2)}, u32[]{:S(2)}) collective-permute-start(f32[3,10,10,128]{3,2,1,0:T(8,128)S(1)} %get-tuple-element.47), channel_id=1, source_target_pairs={{4,1},{5,2},{6,3},{8,5},{9,6},{10,7},{12,9},{13,10},{14,11},{16,13... | collective-permute-start | bytes 460808 | tf_op jit(solution)/shard_map/ppermute | solution.py:54
  8.3 1.3 %collective-permute-start.4 = (f32[3,16,10,128]{3,2,1,0:T(8,128)S(1)}, f32[3,16,10,128]{3,2,1,0:T(8,128)S(1)}, u32[]{:S(2)}, u32[]{:S(2)}) collective-permute-start(f32[3,16,10,128]{3,2,1,0:T(8,128)S(1)} %get-tuple-element.53), channel_id=1, source_target_pairs={{1,0},{2,1},{3,2},{5,4},{6,5},{7,6},{9,8},{10,9},{11,10},{13,12},{... | collective-permute-start | bytes 737288 | tf_op jit(solution)/shard_map/ppermute | solution.py:30
  9.6 1.3 %collective-permute-start.2 = (f32[3,10,10,128]{3,2,1,0:T(8,128)S(1)}, f32[3,10,10,128]{3,2,1,0:T(8,128)S(1)}, u32[]{:S(2)}, u32[]{:S(2)}) collective-permute-start(f32[3,10,10,128]{3,2,1,0:T(8,128)S(1)} %get-tuple-element.49), channel_id=1, source_target_pairs={{1,4},{2,5},{3,6},{5,8},{6,9},{7,10},{9,12},{10,13},{11,14},{13,16... | collective-permute-start | bytes 460808 | tf_op jit(solution)/shard_map/ppermute | solution.py:54
  11.0 0.7 collective-permute-done.7
  11.7 5.6 %collective-permute-start.3 = (f32[3,16,10,128]{3,2,1,0:T(8,128)S(1)}, f32[3,16,10,128]{3,2,1,0:T(8,128)S(1)}, u32[]{:S(2)}, u32[]{:S(2)}) collective-permute-start(f32[3,16,10,128]{3,2,1,0:T(8,128)S(1)} %get-tuple-element.52), channel_id=1, source_target_pairs={{0,1},{1,2},{2,3},{4,5},{5,6},{6,7},{8,9},{9,10},{10,11},{12,13},{... | collective-permute-start | bytes 737288 | tf_op jit(solution)/shard_map/ppermute | solution.py:30
  17.5 8.2 %collective-permute-start.1 = (f32[3,10,16,128]{3,2,1,0:T(8,128)}, f32[3,10,16,128]{3,2,1,0:T(8,128)}, u32[]{:S(2)}, u32[]{:S(2)}) collective-permute-start(f32[3,10,16,128]{3,2,1,0:T(8,128)} %get-tuple-element.50), channel_id=1, source_target_pairs={{0,4},{4,8},{8,12},{12,16},{16,20},{20,24},{24,28},{1,5},{5,9},{9,... | collective-permute-start | bytes 737288 | tf_op jit(solution)/shard_map/ppermute | solution.py:30
  25.6 3.3 %collective-permute-done.2 = f32[3,10,10,128]{3,2,1,0:T(8,128)S(1)} collective-permute-done((f32[3,10,10,128]{3,2,1,0:T(8,128)S(1)}, f32[3,10,10,128]{3,2,1,0:T(8,128)S(1)}, u32[]{:S(2)}, u32[]{:S(2)}) %collective-permute-start.2) | collective-permute-done | bytes 153632 | tf_op jit(solution)/shard_map/ppermute | solution.py:54
  28.9 1.6 %collective-permute-start = (f32[3,10,10,128]{3,2,1,0:T(8,128)S(1)}, f32[3,10,10,128]{3,2,1,0:T(8,128)S(1)}, u32[]{:S(2)}, u32[]{:S(2)}) collective-permute-start(f32[3,10,10,128]{3,2,1,0:T(8,128)S(1)} %get-tuple-element.46), channel_id=1, source_target_pairs={{0,5},{1,6},{2,7},{4,9},{5,10},{6,11},{8,13},{9,14},{10,15},{12,17... | collective-permute-start | bytes 460808 | tf_op jit(solution)/shard_map/ppermute | solution.py:54
  30.6 0.6 pad_add_fusion.bounds_ref
  31.2 5.8 %collective-permute-done = f32[3,10,10,128]{3,2,1,0:T(8,128)S(1)} collective-permute-done((f32[3,10,10,128]{3,2,1,0:T(8,128)S(1)}, f32[3,10,10,128]{3,2,1,0:T(8,128)S(1)}, u32[]{:S(2)}, u32[]{:S(2)}) %collective-permute-start) | collective-permute-done | bytes 153632 | tf_op jit(solution)/shard_map/ppermute | solution.py:54
  37.0 0.7 copy-done.4
  37.6 1.8 %maximum_maximum_fusion = f32[3,36,36,128]{3,2,1,0:T(8,128)S(1)} fusion(f32[3,10,10,128]{3,2,1,0:T(8,128)} %collective-permute-done.7, f32[3,10,16,128]{3,2,1,0:T(8,128)} %collective-permute-done.6, f32[3,10,10,128]{3,2,1,0:T(8,128)} %collective-permute-done.5, f32[3,16,10,128]{3,2,1,0:T(8,128)S(1)} %collective-permute-done.4, ...), kind=kLoop, calls=%fused_computation | loop fusion | flops 4976640 | bytes 3981312 | tf_op jit(solution)/shard_map/concatenate | solution.py:72
  39.4 1.3 %slice_bitcast_fusion.3 = (f32[36,36,128]{2,1,0:T(8,128)}, f32[36,36,128]{2,1,0:T(8,128)}, f32[36,36,128]{2,1,0:T(8,128)S(1)}) fusion(f32[3,36,36,128]{3,2,1,0:T(8,128)S(1)} %maximum_maximum_fusion), kind=kLoop, calls=%fused_computation.18 | loop fusion | bytes 3981312 | tf_op jit(solution)/shard_map/squeeze | solution.py:241
  40.7 5.5 %shard_map.46 = f32[4,36,36,128]{3,2,1,0:T(8,128)} custom-call(s32[4]{0:T(128)} %pad_add_fusion.bounds_ref, f32[5,8]{1,0:T(8,128)} %table_ref.1, f32[36,36,128]{2,1,0:T(8,128)} %get-tuple-element.27.conc_ref, f32[36,36,128]{2,1,0:T(8,128)} %get-tuple-element.26.idf_ref), custom_call_target="tpu_custom_call" | custom-call | flops 16588800 | bytes 3981312 | tf_op jit(solution)/shard_map/pallas_call | solution.py:214
  46.2 1.9 %slice_bitcast_fusion.2 = (f32[36,36,128]{2,1,0:T(8,128)S(1)}, f32[36,36,128]{2,1,0:T(8,128)S(1)}, f32[36,36,128]{2,1,0:T(8,128)S(1)}) fusion(f32[4,36,36,128]{3,2,1,0:T(8,128)} %shard_map.46), kind=kLoop, calls=%fused_computation.17 | loop fusion | bytes 3981312 | tf_op jit(solution)/shard_map/squeeze | solution.py:114
  48.0 0.6 copy-done
  49.3 0.7 fusion.4
  50.5 1.2 %slice_add_fusion.5 = (f32[32,32,128]{2,1,0:T(8,128)S(1)}, f32[32,32,128]{2,1,0:T(8,128)S(1)}) fusion(f32[34,34,128]{2,1,0:T(8,128)S(1)} %get-tuple-element.21, f32[34,34,128]{2,1,0:T(8,128)S(1)} %get-tuple-element.22, f32[32,32,127]{2,1,0:T(8,128)S(1)} %get-tuple-element.35, f32[32,32,1]{2,1,0:T(8,128)S(1)} %get-tuple-element.37, ...), kind=kLoop, calls=%fused_computation.56 | loop fusion | flops 3538944 | bytes 9046976 | tf_op jit(solution)/shard_map/add | solution.py:178
  52.2 0.8 fusion.336
  53.0 1.5 %convolution_multiply_fusion = f32[72,18,64]{2,1,0:T(8,128)S(1)} fusion(f32[72,36,64]{2,1,0:T(8,128)S(1)} %fusion.336, f32[18,36]{1,0:T(8,128)S(1)} %fusion.357), kind=kOutput, calls=%fused_computation.2 | convolution fusion | flops 35914752 | bytes 997920 | tf_op jit(solution)/shard_map/dot_general | solution.py:99
  54.9 1.2 %fusion.22 = f32[30,30,128]{2,1,0:T(8,128)S(1)} fusion(f32[34,34,128]{2,1,0:T(8,128)S(1)} %get-tuple-element.22, f32[32,32,128]{2,1,0:T(8,128)S(1)} %get-tuple-element.19, f32[36,35,128]{2,1,0:T(8,128)S(1)} %maximum_divide_fusion.1, f32[35,36,128]{2,1,0:T(8,128)S(1)} %divide_bitcast_fusion, f32[36,36,128]{2,1,0:T(8,128)S(1)} %get-tuple-element.24, ...), kind=kLoop, calls=%fused_computation.60 | loop fusion | flops 3110400 | bytes 8031168 | tf_op jit(solution)/shard_map/add | solution.py:178
  56.5 0.9 fusion.40
  59.9 0.8 collective-permute-start.14
  60.8 1.7 %collective-permute-start.13 = (f32[5,4,4,32]{3,2,1,0:T(4,128)S(1)}, f32[5,4,4,32]{3,2,1,0:T(4,128)S(1)}, u32[]{:S(2)}, u32[]{:S(2)}) collective-permute-start(f32[5,4,4,32]{3,2,1,0:T(4,128)S(1)} %pad_maximum_fusion.18), channel_id=1, source_target_pairs={{0,2},{1,3},{2,0},{3,1},{4,6},{5,7},{6,4},{7,5},{8,10},{9,11},{10,... | collective-permute-start | bytes 30728 | tf_op jit(solution)/shard_map/ppermute | solution.py:270
  62.5 1.3 %collective-permute-start.9 = (f32[2,8,5,64]{3,2,1,0:T(8,128)S(1)}, f32[2,8,5,64]{3,2,1,0:T(8,128)S(1)}, u32[]{:S(2)}, u32[]{:S(2)}) collective-permute-start(f32[2,8,5,64]{3,2,1,0:T(8,128)S(1)} %get-tuple-element.162), channel_id=1, source_target_pairs={{1,0},{2,1},{3,2},{5,4},{6,5},{7,6},{9,8},{10,9},{11,10},{13,12},{... | collective-permute-start | bytes 61448 | tf_op jit(solution)/shard_map/ppermute | solution.py:30
  63.8 3.0 %collective-permute-start.8 = (f32[2,8,5,64]{3,2,1,0:T(8,128)S(1)}, f32[2,8,5,64]{3,2,1,0:T(8,128)S(1)}, u32[]{:S(2)}, u32[]{:S(2)}) collective-permute-start(f32[2,8,5,64]{3,2,1,0:T(8,128)S(1)} %get-tuple-element.161), channel_id=1, source_target_pairs={{0,1},{1,2},{2,3},{4,5},{5,6},{6,7},{8,9},{9,10},{10,11},{12,13},{... | collective-permute-start | bytes 61448 | tf_op jit(solution)/shard_map/ppermute | solution.py:30
  66.9 4.2 %collective-permute-start.16 = (f32[5,4,16,32]{3,2,1,0:T(8,128)S(1)}, f32[5,4,16,32]{3,2,1,0:T(8,128)S(1)}, u32[]{:S(2)}, u32[]{:S(2)}) collective-permute-start(f32[5,4,16,32]{3,2,1,0:T(8,128)S(1)} %pad_maximum_fusion.4), channel_id=1, source_target_pairs={{0,8},{4,12},{8,16},{12,20},{16,24},{20,28},{1,9},{5,13},{9,17},{1... | collective-permute-start | bytes 122888 | tf_op jit(solution)/shard_map/ppermute | solution.py:30
  71.1 7.0 %collective-permute-start.15 = (f32[5,4,16,32]{3,2,1,0:T(8,128)S(1)}, f32[5,4,16,32]{3,2,1,0:T(8,128)S(1)}, u32[]{:S(2)}, u32[]{:S(2)}) collective-permute-start(f32[5,4,16,32]{3,2,1,0:T(8,128)S(1)} %pad_maximum_fusion.4), channel_id=1, source_target_pairs={{0,12},{4,16},{8,20},{12,24},{16,28},{1,13},{5,17},{9,21},{13,25},... | collective-permute-start | bytes 122888 | tf_op jit(solution)/shard_map/ppermute | solution.py:30
  78.1 1.9 %collective-permute-start.17 = (f32[5,4,16,32]{3,2,1,0:T(8,128)S(1)}, f32[5,4,16,32]{3,2,1,0:T(8,128)S(1)}, u32[]{:S(2)}, u32[]{:S(2)}) collective-permute-start(f32[5,4,16,32]{3,2,1,0:T(8,128)S(1)} %pad_maximum_fusion.4), channel_id=1, source_target_pairs={{0,4},{4,8},{8,12},{12,16},{16,20},{20,24},{24,28},{1,5},{5,9},{9,... | collective-permute-start | bytes 122888 | tf_op jit(solution)/shard_map/ppermute | solution.py:30
  80.0 3.9 %collective-permute-start.18 = (f32[5,4,16,32]{3,2,1,0:T(8,128)S(1)}, f32[5,4,16,32]{3,2,1,0:T(8,128)S(1)}, u32[]{:S(2)}, u32[]{:S(2)}) collective-permute-start(f32[5,4,16,32]{3,2,1,0:T(8,128)S(1)} %pad_maximum_fusion.4), channel_id=1, source_target_pairs={{4,0},{8,4},{12,8},{16,12},{20,16},{24,20},{28,24},{5,1},{9,5},{13... | collective-permute-start | bytes 122888 | tf_op jit(solution)/shard_map/ppermute | solution.py:30
  84.0 1.3 %collective-permute-start.19 = (f32[5,4,16,32]{3,2,1,0:T(8,128)S(1)}, f32[5,4,16,32]{3,2,1,0:T(8,128)S(1)}, u32[]{:S(2)}, u32[]{:S(2)}) collective-permute-start(f32[5,4,16,32]{3,2,1,0:T(8,128)S(1)} %pad_maximum_fusion.4), channel_id=1, source_target_pairs={{8,0},{12,4},{16,8},{20,12},{24,16},{28,20},{9,1},{13,5},{17,9},{2... | collective-permute-start | bytes 122888 | tf_op jit(solution)/shard_map/ppermute | solution.py:30
  85.4 1.3 %collective-permute-start.20 = (f32[5,4,16,32]{3,2,1,0:T(8,128)S(1)}, f32[5,4,16,32]{3,2,1,0:T(8,128)S(1)}, u32[]{:S(2)}, u32[]{:S(2)}) collective-permute-start(f32[5,4,16,32]{3,2,1,0:T(8,128)S(1)} %pad_maximum_fusion.4), channel_id=1, source_target_pairs={{12,0},{16,4},{20,8},{24,12},{28,16},{13,1},{17,5},{21,9},{25,13},... | collective-permute-start | bytes 122888 | tf_op jit(solution)/shard_map/ppermute | solution.py:30
  86.7 1.9 %collective-permute-start.11 = (f32[2,5,18,64]{3,2,1,0:T(8,128)S(1)}, f32[2,5,18,64]{3,2,1,0:T(8,128)S(1)}, u32[]{:S(2)}, u32[]{:S(2)}) collective-permute-start(f32[2,5,18,64]{3,2,1,0:T(8,128)S(1)} %get-tuple-element.79), channel_id=1, source_target_pairs={{4,0},{8,4},{12,8},{16,12},{20,16},{24,20},{28,24},{5,1},{9,5},{13... | collective-permute-start | bytes 138248 | tf_op jit(solution)/shard_map/ppermute | solution.py:30
  88.9 4.6 %collective-permute-start.10 = (f32[2,5,18,64]{3,2,1,0:T(8,128)S(1)}, f32[2,5,18,64]{3,2,1,0:T(8,128)S(1)}, u32[]{:S(2)}, u32[]{:S(2)}) collective-permute-start(f32[2,5,18,64]{3,2,1,0:T(8,128)S(1)} %get-tuple-element.78), channel_id=1, source_target_pairs={{0,4},{4,8},{8,12},{12,16},{16,20},{20,24},{24,28},{1,5},{5,9},{9,... | collective-permute-start | bytes 138248 | tf_op jit(solution)/shard_map/ppermute | solution.py:30
  93.7 6.7 %collective-permute-done.20 = f32[5,4,16,32]{3,2,1,0:T(8,128)S(1)} collective-permute-done((f32[5,4,16,32]{3,2,1,0:T(8,128)S(1)}, f32[5,4,16,32]{3,2,1,0:T(8,128)S(1)}, u32[]{:S(2)}, u32[]{:S(2)}) %collective-permute-start.20) | collective-permute-done | bytes 40992 | tf_op jit(solution)/shard_map/ppermute | solution.py:30
  101.6 0.5 fusion.87
  102.4 0.4 multiply_add_fusion
  106.2 0.4 fusion.318
  108.0 0.4 fusion.258
  108.5 0.5 fusion.315
  109.3 0.4 slice_add_fusion.7
  110.0 0.5 slice_add_fusion.9
  110.7 1.0 fusion.181
  (160 shorter events, 12.4 us)
Async XLA Ops:
  2.0 35.6 %copy-start.1 = (f32[16,16,128]{2,1,0:T(8,128)S(1)}, f32[16,16,128]{2,1,0:T(8,128)}, u32[]{:S(2)}) copy-start(f32[16,16,128]{2,1,0:T(8,128)} %param.5) | copy-start | bytes 393220
  2.0 35.6 %copy-start.2 = (f32[16,16,128]{2,1,0:T(8,128)S(1)}, f32[16,16,128]{2,1,0:T(8,128)}, u32[]{:S(2)}) copy-start(f32[16,16,128]{2,1,0:T(8,128)} %param.4) | copy-start | bytes 393220
  2.0 9.7 %collective-permute-start.7 = (f32[3,10,10,128]{3,2,1,0:T(8,128)S(1)}, f32[3,10,10,128]{3,2,1,0:T(8,128)}, u32[]{:S(2)}, u32[]{:S(2)}) collective-permute-start(f32[3,10,10,128]{3,2,1,0:T(8,128)S(1)} %get-tuple-element.48), channel_id=1, source_target_pairs={{5,0},{6,1},{7,2},{9,4},{10,5},{11,6},{13,8},{14,9},{15,10},{17,12... | collective-permute-start | bytes 460808 | tf_op jit(solution)/shard_map/ppermute | solution.py:54
  4.3 32.7 %collective-permute-start.6 = (f32[3,10,16,128]{3,2,1,0:T(8,128)}, f32[3,10,16,128]{3,2,1,0:T(8,128)}, u32[]{:S(2)}, u32[]{:S(2)}) collective-permute-start(f32[3,10,16,128]{3,2,1,0:T(8,128)} %get-tuple-element.51), channel_id=1, source_target_pairs={{4,0},{8,4},{12,8},{16,12},{20,16},{24,20},{28,24},{5,1},{9,5},{13... | collective-permute-start | bytes 737288 | tf_op jit(solution)/shard_map/ppermute | solution.py:30
  6.2 11.3 %collective-permute-start.5 = (f32[3,10,10,128]{3,2,1,0:T(8,128)S(1)}, f32[3,10,10,128]{3,2,1,0:T(8,128)}, u32[]{:S(2)}, u32[]{:S(2)}) collective-permute-start(f32[3,10,10,128]{3,2,1,0:T(8,128)S(1)} %get-tuple-element.47), channel_id=1, source_target_pairs={{4,1},{5,2},{6,3},{8,5},{9,6},{10,7},{12,9},{13,10},{14,11},{16,13... | collective-permute-start | bytes 460808 | tf_op jit(solution)/shard_map/ppermute | solution.py:54
  8.3 28.7 %collective-permute-start.4 = (f32[3,16,10,128]{3,2,1,0:T(8,128)S(1)}, f32[3,16,10,128]{3,2,1,0:T(8,128)S(1)}, u32[]{:S(2)}, u32[]{:S(2)}) collective-permute-start(f32[3,16,10,128]{3,2,1,0:T(8,128)S(1)} %get-tuple-element.53), channel_id=1, source_target_pairs={{1,0},{2,1},{3,2},{5,4},{6,5},{7,6},{9,8},{10,9},{11,10},{13,12},{... | collective-permute-start | bytes 737288 | tf_op jit(solution)/shard_map/ppermute | solution.py:30
  9.6 19.3 %collective-permute-start.2 = (f32[3,10,10,128]{3,2,1,0:T(8,128)S(1)}, f32[3,10,10,128]{3,2,1,0:T(8,128)S(1)}, u32[]{:S(2)}, u32[]{:S(2)}) collective-permute-start(f32[3,10,10,128]{3,2,1,0:T(8,128)S(1)} %get-tuple-element.49), channel_id=1, source_target_pairs={{1,4},{2,5},{3,6},{5,8},{6,9},{7,10},{9,12},{10,13},{11,14},{13,16... | collective-permute-start | bytes 460808 | tf_op jit(solution)/shard_map/ppermute | solution.py:54
  11.7 25.2 %collective-permute-start.3 = (f32[3,16,10,128]{3,2,1,0:T(8,128)S(1)}, f32[3,16,10,128]{3,2,1,0:T(8,128)S(1)}, u32[]{:S(2)}, u32[]{:S(2)}) collective-permute-start(f32[3,16,10,128]{3,2,1,0:T(8,128)S(1)} %get-tuple-element.52), channel_id=1, source_target_pairs={{0,1},{1,2},{2,3},{4,5},{5,6},{6,7},{8,9},{9,10},{10,11},{12,13},{... | collective-permute-start | bytes 737288 | tf_op jit(solution)/shard_map/ppermute | solution.py:30
  17.5 20.2 %collective-permute-start.1 = (f32[3,10,16,128]{3,2,1,0:T(8,128)}, f32[3,10,16,128]{3,2,1,0:T(8,128)}, u32[]{:S(2)}, u32[]{:S(2)}) collective-permute-start(f32[3,10,16,128]{3,2,1,0:T(8,128)} %get-tuple-element.50), channel_id=1, source_target_pairs={{0,4},{4,8},{8,12},{12,16},{16,20},{20,24},{24,28},{1,5},{5,9},{9,... | collective-permute-start | bytes 737288 | tf_op jit(solution)/shard_map/ppermute | solution.py:30
  28.9 8.0 %copy-start.3 = (f32[3,10,10,128]{3,2,1,0:T(8,128)}, f32[3,10,10,128]{3,2,1,0:T(8,128)S(1)}, u32[]{:S(2)}) copy-start(f32[3,10,10,128]{3,2,1,0:T(8,128)S(1)} %collective-permute-done.2) | copy-start | bytes 460804
  28.9 8.0 %collective-permute-start = (f32[3,10,10,128]{3,2,1,0:T(8,128)S(1)}, f32[3,10,10,128]{3,2,1,0:T(8,128)S(1)}, u32[]{:S(2)}, u32[]{:S(2)}) collective-permute-start(f32[3,10,10,128]{3,2,1,0:T(8,128)S(1)} %get-tuple-element.46), channel_id=1, source_target_pairs={{0,5},{1,6},{2,7},{4,9},{5,10},{6,11},{8,13},{9,14},{10,15},{12,17... | collective-permute-start | bytes 460808 | tf_op jit(solution)/shard_map/ppermute | solution.py:54
  36.9 0.7 copy-start.4
  46.1 2.5 %copy-start = (f32[4,36,36,128]{3,2,1,0:T(8,128)S(1)}, f32[4,36,36,128]{3,2,1,0:T(8,128)}, u32[]{:S(2)}) copy-start(f32[4,36,36,128]{3,2,1,0:T(8,128)} %shard_map.46) | copy-start | bytes 7962628
  59.9 6.9 %collective-permute-start.14 = (f32[5,4,4,32]{3,2,1,0:T(4,128)S(1)}, f32[5,4,4,32]{3,2,1,0:T(4,128)S(1)}, u32[]{:S(2)}, u32[]{:S(2)}) collective-permute-start(f32[5,4,4,32]{3,2,1,0:T(4,128)S(1)} %pad_maximum_fusion.18), channel_id=1, source_target_pairs={{0,1},{1,2},{2,3},{3,0},{4,5},{5,6},{6,7},{7,4},{8,9},{9,10},{10,1... | collective-permute-start | bytes 30728 | tf_op jit(solution)/shard_map/ppermute | solution.py:270
  60.8 6.1 %collective-permute-start.13 = (f32[5,4,4,32]{3,2,1,0:T(4,128)S(1)}, f32[5,4,4,32]{3,2,1,0:T(4,128)S(1)}, u32[]{:S(2)}, u32[]{:S(2)}) collective-permute-start(f32[5,4,4,32]{3,2,1,0:T(4,128)S(1)} %pad_maximum_fusion.18), channel_id=1, source_target_pairs={{0,2},{1,3},{2,0},{3,1},{4,6},{5,7},{6,4},{7,5},{8,10},{9,11},{10,... | collective-permute-start | bytes 30728 | tf_op jit(solution)/shard_map/ppermute | solution.py:270
  62.4 4.4 %collective-permute-start.12 = (f32[5,4,4,32]{3,2,1,0:T(4,128)S(1)}, f32[5,4,4,32]{3,2,1,0:T(4,128)S(1)}, u32[]{:S(2)}, u32[]{:S(2)}) collective-permute-start(f32[5,4,4,32]{3,2,1,0:T(4,128)S(1)} %pad_maximum_fusion.18), channel_id=1, source_target_pairs={{0,3},{1,0},{2,1},{3,2},{4,7},{5,4},{6,5},{7,6},{8,11},{9,8},{10,9... | collective-permute-start | bytes 30728 | tf_op jit(solution)/shard_map/ppermute | solution.py:270
  62.5 17.6 %collective-permute-start.9 = (f32[2,8,5,64]{3,2,1,0:T(8,128)S(1)}, f32[2,8,5,64]{3,2,1,0:T(8,128)S(1)}, u32[]{:S(2)}, u32[]{:S(2)}) collective-permute-start(f32[2,8,5,64]{3,2,1,0:T(8,128)S(1)} %get-tuple-element.162), channel_id=1, source_target_pairs={{1,0},{2,1},{3,2},{5,4},{6,5},{7,6},{9,8},{10,9},{11,10},{13,12},{... | collective-permute-start | bytes 61448 | tf_op jit(solution)/shard_map/ppermute | solution.py:30
  63.8 20.2 %collective-permute-start.8 = (f32[2,8,5,64]{3,2,1,0:T(8,128)S(1)}, f32[2,8,5,64]{3,2,1,0:T(8,128)S(1)}, u32[]{:S(2)}, u32[]{:S(2)}) collective-permute-start(f32[2,8,5,64]{3,2,1,0:T(8,128)S(1)} %get-tuple-element.161), channel_id=1, source_target_pairs={{0,1},{1,2},{2,3},{4,5},{5,6},{6,7},{8,9},{9,10},{10,11},{12,13},{... | collective-permute-start | bytes 61448 | tf_op jit(solution)/shard_map/ppermute | solution.py:30
  66.9 19.8 %collective-permute-start.16 = (f32[5,4,16,32]{3,2,1,0:T(8,128)S(1)}, f32[5,4,16,32]{3,2,1,0:T(8,128)S(1)}, u32[]{:S(2)}, u32[]{:S(2)}) collective-permute-start(f32[5,4,16,32]{3,2,1,0:T(8,128)S(1)} %pad_maximum_fusion.4), channel_id=1, source_target_pairs={{0,8},{4,12},{8,16},{12,20},{16,24},{20,28},{1,9},{5,13},{9,17},{1... | collective-permute-start | bytes 122888 | tf_op jit(solution)/shard_map/ppermute | solution.py:30
  71.1 14.2 %collective-permute-start.15 = (f32[5,4,16,32]{3,2,1,0:T(8,128)S(1)}, f32[5,4,16,32]{3,2,1,0:T(8,128)S(1)}, u32[]{:S(2)}, u32[]{:S(2)}) collective-permute-start(f32[5,4,16,32]{3,2,1,0:T(8,128)S(1)} %pad_maximum_fusion.4), channel_id=1, source_target_pairs={{0,12},{4,16},{8,20},{12,24},{16,28},{1,13},{5,17},{9,21},{13,25},... | collective-permute-start | bytes 122888 | tf_op jit(solution)/shard_map/ppermute | solution.py:30
  78.1 10.8 %collective-permute-start.17 = (f32[5,4,16,32]{3,2,1,0:T(8,128)S(1)}, f32[5,4,16,32]{3,2,1,0:T(8,128)S(1)}, u32[]{:S(2)}, u32[]{:S(2)}) collective-permute-start(f32[5,4,16,32]{3,2,1,0:T(8,128)S(1)} %pad_maximum_fusion.4), channel_id=1, source_target_pairs={{0,4},{4,8},{8,12},{12,16},{16,20},{20,24},{24,28},{1,5},{5,9},{9,... | collective-permute-start | bytes 122888 | tf_op jit(solution)/shard_map/ppermute | solution.py:30
  80.0 13.6 %collective-permute-start.18 = (f32[5,4,16,32]{3,2,1,0:T(8,128)S(1)}, f32[5,4,16,32]{3,2,1,0:T(8,128)S(1)}, u32[]{:S(2)}, u32[]{:S(2)}) collective-permute-start(f32[5,4,16,32]{3,2,1,0:T(8,128)S(1)} %pad_maximum_fusion.4), channel_id=1, source_target_pairs={{4,0},{8,4},{12,8},{16,12},{20,16},{24,20},{28,24},{5,1},{9,5},{13... | collective-permute-start | bytes 122888 | tf_op jit(solution)/shard_map/ppermute | solution.py:30
  84.0 9.7 %collective-permute-start.19 = (f32[5,4,16,32]{3,2,1,0:T(8,128)S(1)}, f32[5,4,16,32]{3,2,1,0:T(8,128)S(1)}, u32[]{:S(2)}, u32[]{:S(2)}) collective-permute-start(f32[5,4,16,32]{3,2,1,0:T(8,128)S(1)} %pad_maximum_fusion.4), channel_id=1, source_target_pairs={{8,0},{12,4},{16,8},{20,12},{24,16},{28,20},{9,1},{13,5},{17,9},{2... | collective-permute-start | bytes 122888 | tf_op jit(solution)/shard_map/ppermute | solution.py:30
  85.4 15.0 %collective-permute-start.20 = (f32[5,4,16,32]{3,2,1,0:T(8,128)S(1)}, f32[5,4,16,32]{3,2,1,0:T(8,128)S(1)}, u32[]{:S(2)}, u32[]{:S(2)}) collective-permute-start(f32[5,4,16,32]{3,2,1,0:T(8,128)S(1)} %pad_maximum_fusion.4), channel_id=1, source_target_pairs={{12,0},{16,4},{20,8},{24,12},{28,16},{13,1},{17,5},{21,9},{25,13},... | collective-permute-start | bytes 122888 | tf_op jit(solution)/shard_map/ppermute | solution.py:30
  86.7 20.0 %collective-permute-start.11 = (f32[2,5,18,64]{3,2,1,0:T(8,128)S(1)}, f32[2,5,18,64]{3,2,1,0:T(8,128)S(1)}, u32[]{:S(2)}, u32[]{:S(2)}) collective-permute-start(f32[2,5,18,64]{3,2,1,0:T(8,128)S(1)} %get-tuple-element.79), channel_id=1, source_target_pairs={{4,0},{8,4},{12,8},{16,12},{20,16},{24,20},{28,24},{5,1},{9,5},{13... | collective-permute-start | bytes 138248 | tf_op jit(solution)/shard_map/ppermute | solution.py:30
  88.9 17.8 %collective-permute-start.10 = (f32[2,5,18,64]{3,2,1,0:T(8,128)S(1)}, f32[2,5,18,64]{3,2,1,0:T(8,128)S(1)}, u32[]{:S(2)}, u32[]{:S(2)}) collective-permute-start(f32[2,5,18,64]{3,2,1,0:T(8,128)S(1)} %get-tuple-element.78), channel_id=1, source_target_pairs={{0,4},{4,8},{8,12},{12,16},{16,20},{20,24},{24,28},{1,5},{5,9},{9,... | collective-permute-start | bytes 138248 | tf_op jit(solution)/shard_map/ppermute | solution.py:30

commit v9 on v5

--- a/solution.py
+++ b/solution.py
@@ -39,6 +39,25 @@
             [shift_from(tail, axis, -1), cells, shift_from(head, axis, 1)], axis=dim
         )
     return cells
+
+
+def joined(first, second):
+    tail = tuple(max(a, b) for a, b in zip(first.shape[-2:], second.shape[-2:]))
+
+    def fit(a):
+        pad = [(0, 0)] * (a.ndim - 2) + [(0, t - d) for t, d in zip(tail, a.shape[-2:])]
+        return jnp.pad(a, pad).reshape((-1,) + tail)
+
+    return jnp.concatenate([fit(first), fit(second)], axis=0)
+
+
+def split(both, first, second):
+    lead = first.size // (first.shape[-2] * first.shape[-1])
+    a = both[:lead].reshape(first.shape[:-2] + both.shape[-2:])
+    b = both[lead:].reshape(second.shape[:-2] + both.shape[-2:])
+    a = a[..., : first.shape[-2], : first.shape[-1]]
+    b = b[..., : second.shape[-2], : second.shape[-1]]
+    return a, b
 
 
 def harmonic(first, second):
@@ -233,21 +252,35 @@
     cpack = jnp.concatenate([b2[None], coarse_own], axis=0)
     mpack = jnp.stack([win(x1, nm, x1m, 0), win(b1, nm, b1m, 0)])
     hm = MID_HALO
+    north_slab = mpack[:, :, :hm]
+    south_slab = mpack[:, :, nm - hm :]
     blocks = [cpack]
+    north = south = None
     for step in range(1, gy_count):
         pairs = [(j, (j - step) % gy_count) for j in range(gy_count)]
-        blocks.append(lax.ppermute(cpack, "gy", pairs))
-    north = shift_from(mpack[:, :, :hm], "gy", 1)
-    south = shift_from(mpack[:, :, nm - hm :], "gy", -1)
+        if step == 1 and gy_count > 2:
+            got, north = split(lax.ppermute(joined(cpack, north_slab), "gy", pairs), cpack, north_slab)
+        elif step == gy_count - 1 and gy_count > 2:
+            got, south = split(lax.ppermute(joined(cpack, south_slab), "gy", pairs), cpack, south_slab)
+        else:
+            got = lax.ppermute(cpack, "gy", pairs)
+        blocks.append(got)
+    if north is None:
+        north = shift_from(north_slab, "gy", 1)
+        south = shift_from(south_slab, "gy", -1)
+    north = jnp.where(iy < gy_count - 1, north, 0.0)
+    south = jnp.where(iy > 0, south, 0.0)
     mext = jnp.concatenate([south, mpack, north], axis=2)
     full = jnp.concatenate(blocks, axis=2)
     reach = 3
-    parts = [shift_from(full, "gx", -d) for d in range(reach, 0, -1)]
-    parts += [full]
-    parts += [shift_from(full, "gx", d) for d in range(1, reach + 1)]
+    west_slab = mext[:, nm - hm :]
+    east_slab = mext[:, :hm]
+    low, west_m = split(shift_from(joined(full, west_slab), "gx", -1), full, west_slab)
+    high, east_m = split(shift_from(joined(full, east_slab), "gx", 1), full, east_slab)
+    parts = [shift_from(full, "gx", -d) for d in range(reach, 1, -1)]
+    parts += [low, full, high]
+    parts += [shift_from(full, "gx", d) for d in range(2, reach + 1)]
     cpack = jnp.concatenate(parts, axis=1)
-    west_m = shift_from(mext[:, nm - hm :], "gx", -1)
-    east_m = shift_from(mext[:, :hm], "gx", 1)
     mext = jnp.concatenate([west_m, mext, east_m], axis=1)
     source = cpack[0]
     cc = cpack[1:]

time: 103 us -> 120 us (1.17)
  the two profiles are of different devices: /device:TPU:4 before, /device:TPU:25 now
where the time goes in v9:
time: 120 us; the launch traced here: 119 us
  waiting for transfers between devices  35.9 us (30%)
  starting transfers between devices  30.9 us (26%)
  other arithmetic  24.6 us (20%)
  local copies, waits for them, and re-layouts  14.7 us (12%)
  matrix products  6.11 us (5%)
  Pallas kernels  5.47 us (5%)
  between operations  1.38 us (1%)
    ppermute x10, waiting for transfers between devices, shift_from(): return lax.ppermute(cells, axis, pairs)  30.5 us
    ppermute x10, starting transfers between devices, shift_from(): return lax.ppermute(cells, axis, pairs)  30.4 us
    add x7, other arithmetic, chebyshev(): iterate = win(iterate, n, cur, nxt) + update  5.54 us
    ppermute x1, waiting for transfers between devices, local(): lax.ppermute(joined(cpack, north_slab), 'gy', pairs)  5.47 us
    pallas_call x1, Pallas kernels, soil_fields(): pl.pallas_call(fields_kernel, out_shape=jax.ShapeDtypeStruct((4,) + conc....  5.47 us
    add x8, other arithmetic, local(): u = centre + jacobi_weight * ((csrc[sl] - applied) / cdiag[sl])  3.15 us
    unnamed x62, local copies, waits for them, and re-layouts  2.62 us
  transfers between devices with their start and end apart: 13, of which 7 were waited for; matrix products, arithmetic and copies ran while one was open for 8% of the time, Pallas kernels for 0%

profile of v9, /device:TPU:25, one launch (start us, length us, event | category | flops | bytes accessed | tf_op | source)
XLA Modules:
  0.0 119.1 jit_solution(11412849394357179314)
XLA Ops:
  0.0 1.0 convert_bitcast_fusion
  1.0 1.0 pad_maximum_fusion.6
  2.0 3.1 %collective-permute-start = (f32[3,10,16,128]{3,2,1,0:T(8,128)S(1)}, f32[3,10,16,128]{3,2,1,0:T(8,128)S(1)}, u32[]{:S(2)}, u32[]{:S(2)}) collective-permute-start(f32[3,10,16,128]{3,2,1,0:T(8,128)S(1)} %get-tuple-element.48), channel_id=1, source_target_pairs={{0,4},{4,8},{8,12},{12,16},{16,20},{20,24},{24,28},{1,5},{5,9},{9,... | collective-permute-start | bytes 737288 | tf_op jit(solution)/shard_map/ppermute | solution.py:30
  5.2 3.0 %collective-permute-start.1 = (f32[3,10,16,128]{3,2,1,0:T(8,128)S(1)}, f32[3,10,16,128]{3,2,1,0:T(8,128)S(1)}, u32[]{:S(2)}, u32[]{:S(2)}) collective-permute-start(f32[3,10,16,128]{3,2,1,0:T(8,128)S(1)} %get-tuple-element.49), channel_id=1, source_target_pairs={{4,0},{8,4},{12,8},{16,12},{20,16},{24,20},{28,24},{5,1},{9,5},{13... | collective-permute-start | bytes 737288 | tf_op jit(solution)/shard_map/ppermute | solution.py:30
  8.8 0.6 fusion.362
  10.0 0.6 fusion.363
  10.6 1.1 collective-permute-done
  11.7 6.3 %collective-permute-done.1 = f32[3,10,16,128]{3,2,1,0:T(8,128)S(1)} collective-permute-done((f32[3,10,16,128]{3,2,1,0:T(8,128)S(1)}, f32[3,10,16,128]{3,2,1,0:T(8,128)S(1)}, u32[]{:S(2)}, u32[]{:S(2)}) %collective-permute-start.1) | collective-permute-done | bytes 245792 | tf_op jit(solution)/shard_map/ppermute | solution.py:30
  18.4 3.5 %collective-permute-start.2 = (f32[3,36,10,128]{3,1,2,0:T(8,128)S(1)}, f32[3,36,10,128]{3,1,2,0:T(8,128)S(1)}, u32[]{:S(2)}, u32[]{:S(2)}) collective-permute-start(f32[3,36,10,128]{3,1,2,0:T(8,128)S(1)} %copy.19), channel_id=1, source_target_pairs={{0,1},{1,2},{2,3},{4,5},{5,6},{6,7},{8,9},{9,10},{10,11},{12,13},{... | collective-permute-start | bytes 1658888 | tf_op jit(solution)/shard_map/ppermute | solution.py:30
  22.1 1.9 %collective-permute-start.3 = (f32[3,36,10,128]{3,1,2,0:T(8,128)S(1)}, f32[3,36,10,128]{3,1,2,0:T(8,128)S(1)}, u32[]{:S(2)}, u32[]{:S(2)}) collective-permute-start(f32[3,36,10,128]{3,1,2,0:T(8,128)S(1)} %copy.20), channel_id=1, source_target_pairs={{1,0},{2,1},{3,2},{5,4},{6,5},{7,6},{9,8},{10,9},{11,10},{13,12},{... | collective-permute-start | bytes 1658888 | tf_op jit(solution)/shard_map/ppermute | solution.py:30
  24.0 0.6 pad_add_fusion.bounds_ref
  24.6 0.6 fusion.361
  25.2 3.8 %collective-permute-done.2 = f32[3,36,10,128]{3,1,2,0:T(8,128)S(1)} collective-permute-done((f32[3,36,10,128]{3,1,2,0:T(8,128)S(1)}, f32[3,36,10,128]{3,1,2,0:T(8,128)S(1)}, u32[]{:S(2)}, u32[]{:S(2)}) %collective-permute-start.2) | collective-permute-done | bytes 552992 | tf_op jit(solution)/shard_map/ppermute | solution.py:30
  29.1 4.4 %collective-permute-done.3 = f32[3,36,10,128]{3,1,2,0:T(8,128)S(1)} collective-permute-done((f32[3,36,10,128]{3,1,2,0:T(8,128)S(1)}, f32[3,36,10,128]{3,1,2,0:T(8,128)S(1)}, u32[]{:S(2)}, u32[]{:S(2)}) %collective-permute-start.3) | collective-permute-done | bytes 552992 | tf_op jit(solution)/shard_map/ppermute | solution.py:30
  34.0 1.3 %slice_bitcast_fusion.3 = (f32[36,36,128]{2,1,0:T(8,128)}, f32[36,36,128]{2,1,0:T(8,128)}, f32[36,36,128]{2,1,0:T(8,128)S(1)}) fusion(f32[3,36,36,128]{3,2,1,0:T(8,128)S(1)} %pad_maximum_fusion), kind=kLoop, calls=%fused_computation.19 | loop fusion | bytes 3981312 | tf_op jit(solution)/shard_map/squeeze | solution.py:229
  35.2 5.5 %shard_map.46 = f32[4,36,36,128]{3,2,1,0:T(8,128)} custom-call(s32[4]{0:T(128)} %pad_add_fusion.bounds_ref, f32[5,8]{1,0:T(8,128)} %table_ref.1, f32[36,36,128]{2,1,0:T(8,128)} %get-tuple-element.27.conc_ref, f32[36,36,128]{2,1,0:T(8,128)} %get-tuple-element.26.idf_ref), custom_call_target="tpu_custom_call" | custom-call | flops 16588800 | bytes 3981312 | tf_op jit(solution)/shard_map/pallas_call | solution.py:202
  40.7 1.9 %slice_bitcast_fusion.2 = (f32[36,36,128]{2,1,0:T(8,128)S(1)}, f32[36,36,128]{2,1,0:T(8,128)S(1)}, f32[36,36,128]{2,1,0:T(8,128)S(1)}) fusion(f32[4,36,36,128]{3,2,1,0:T(8,128)} %shard_map.46), kind=kLoop, calls=%fused_computation.18 | loop fusion | bytes 3981312 | tf_op jit(solution)/shard_map/squeeze | solution.py:102
  42.6 0.6 copy-done
  43.9 0.7 fusion.4
  45.1 1.2 %slice_add_fusion.5 = (f32[32,32,128]{2,1,0:T(8,128)S(1)}, f32[32,32,128]{2,1,0:T(8,128)S(1)}) fusion(f32[34,34,128]{2,1,0:T(8,128)S(1)} %get-tuple-element.21, f32[34,34,128]{2,1,0:T(8,128)S(1)} %get-tuple-element.22, f32[32,32,127]{2,1,0:T(8,128)S(1)} %get-tuple-element.37, f32[32,32,1]{2,1,0:T(8,128)S(1)} %get-tuple-element.39, ...), kind=kLoop, calls=%fused_computation.57 | loop fusion | flops 3538944 | bytes 9046976 | tf_op jit(solution)/shard_map/add | solution.py:166
  46.7 1.2 fusion.22
  48.5 0.8 fusion.336
  49.3 1.5 %convolution_multiply_fusion = f32[72,18,64]{2,1,0:T(8,128)S(1)} fusion(f32[72,36,64]{2,1,0:T(8,128)S(1)} %fusion.336, f32[18,36]{1,0:T(8,128)S(1)} %fusion.357), kind=kOutput, calls=%fused_computation.2 | convolution fusion | flops 35914752 | bytes 997920 | tf_op jit(solution)/shard_map/dot_general | solution.py:87
  51.1 0.9 fusion.40
  55.1 0.6 copy-done.14
  55.7 0.6 pad_maximum_fusion.24
  56.3 0.8 pad.16
  57.2 0.8 pad_maximum_fusion.16
  58.5 5.5 %collective-permute-done.4 = f32[36,5,64]{2,1,0:T(8,128)} collective-permute-done((f32[36,5,64]{2,1,0:T(8,128)}, f32[36,5,64]{2,1,0:T(8,128)}, u32[]{:S(2)}, u32[]{:S(2)}) %collective-permute-start.4) | collective-permute-done | bytes 46112 | tf_op jit(solution)/shard_map/ppermute | solution.py:262
  64.0 0.9 slice.2225
  64.9 0.9 slice.2227
  65.8 0.8 pad_maximum_fusion.8
  66.6 1.3 %collective-permute-start.9 = (f32[5,4,16,32]{3,2,1,0:T(8,128)S(1)}, f32[5,4,16,32]{3,2,1,0:T(8,128)S(1)}, u32[]{:S(2)}, u32[]{:S(2)}) collective-permute-start(f32[5,4,16,32]{3,2,1,0:T(8,128)S(1)} %pad_maximum_fusion.8), channel_id=1, source_target_pairs={{0,12},{4,16},{8,20},{12,24},{16,28},{1,13},{5,17},{9,21},{13,25},... | collective-permute-start | bytes 122888 | tf_op jit(solution)/shard_map/ppermute | solution.py:30
  67.9 1.3 %collective-permute-start.10 = (f32[5,4,16,32]{3,2,1,0:T(8,128)S(1)}, f32[5,4,16,32]{3,2,1,0:T(8,128)S(1)}, u32[]{:S(2)}, u32[]{:S(2)}) collective-permute-start(f32[5,4,16,32]{3,2,1,0:T(8,128)S(1)} %pad_maximum_fusion.8), channel_id=1, source_target_pairs={{0,8},{4,12},{8,16},{12,20},{16,24},{20,28},{1,9},{5,13},{9,17},{1... | collective-permute-start | bytes 122888 | tf_op jit(solution)/shard_map/ppermute | solution.py:30
  69.2 4.0 %collective-permute-start.11 = (f32[5,4,16,32]{3,2,1,0:T(8,128)S(1)}, f32[5,4,16,32]{3,2,1,0:T(8,128)S(1)}, u32[]{:S(2)}, u32[]{:S(2)}) collective-permute-start(f32[5,4,16,32]{3,2,1,0:T(8,128)S(1)} %pad_maximum_fusion.8), channel_id=1, source_target_pairs={{8,0},{12,4},{16,8},{20,12},{24,16},{28,20},{9,1},{13,5},{17,9},{2... | collective-permute-start | bytes 122888 | tf_op jit(solution)/shard_map/ppermute | solution.py:30
  73.3 6.0 %collective-permute-start.12 = (f32[5,4,16,32]{3,2,1,0:T(8,128)S(1)}, f32[5,4,16,32]{3,2,1,0:T(8,128)S(1)}, u32[]{:S(2)}, u32[]{:S(2)}) collective-permute-start(f32[5,4,16,32]{3,2,1,0:T(8,128)S(1)} %pad_maximum_fusion.8), channel_id=1, source_target_pairs={{12,0},{16,4},{20,8},{24,12},{28,16},{13,1},{17,5},{21,9},{25,13},... | collective-permute-start | bytes 122888 | tf_op jit(solution)/shard_map/ppermute | solution.py:30
  79.2 0.8 slice_select_fusion.1
  80.1 0.8 slice_select_fusion
  81.1 1.9 %collective-permute-start.7 = (f32[30,18,64]{2,1,0:T(8,128)S(1)}, f32[30,18,64]{2,1,0:T(8,128)S(1)}, u32[]{:S(2)}, u32[]{:S(2)}) collective-permute-start(f32[30,18,64]{2,1,0:T(8,128)S(1)} %get-tuple-element.65), channel_id=1, source_target_pairs={{0,4},{4,8},{8,12},{12,16},{16,20},{20,24},{24,28},{1,5},{5,9},{9,... | collective-permute-start | bytes 414728 | tf_op jit(solution)/shard_map/ppermute | solution.py:30
  83.0 4.3 %collective-permute-start.8 = (f32[30,18,64]{2,1,0:T(8,128)S(1)}, f32[30,18,64]{2,1,0:T(8,128)S(1)}, u32[]{:S(2)}, u32[]{:S(2)}) collective-permute-start(f32[30,18,64]{2,1,0:T(8,128)S(1)} %get-tuple-element.64), channel_id=1, source_target_pairs={{4,0},{8,4},{12,8},{16,12},{20,16},{24,20},{28,24},{5,1},{9,5},{13... | collective-permute-start | bytes 414728 | tf_op jit(solution)/shard_map/ppermute | solution.py:30
  87.4 6.4 %collective-permute-done.7 = f32[30,18,64]{2,1,0:T(8,128)S(1)} collective-permute-done((f32[30,18,64]{2,1,0:T(8,128)S(1)}, f32[30,18,64]{2,1,0:T(8,128)S(1)}, u32[]{:S(2)}, u32[]{:S(2)}) %collective-permute-start.7) | collective-permute-done | bytes 138272 | tf_op jit(solution)/shard_map/ppermute | solution.py:30
  93.8 8.5 %collective-permute-done.8 = f32[30,18,64]{2,1,0:T(8,128)S(1)} collective-permute-done((f32[30,18,64]{2,1,0:T(8,128)S(1)}, f32[30,18,64]{2,1,0:T(8,128)S(1)}, u32[]{:S(2)}, u32[]{:S(2)}) %collective-permute-start.8) | collective-permute-done | bytes 138272 | tf_op jit(solution)/shard_map/ppermute | solution.py:30
  102.3 0.9 fusion.285
  109.0 0.9 multiply_add_fusion.6
  111.2 1.2 %slice_add_fusion.10 = (f32[16,16,64]{2,1,0:T(8,128)S(1)}, f32[16,16,64]{2,1,0:T(8,128)S(1)}) fusion(f32[18,18,64]{2,1,0:T(8,128)S(1)} %slice_add_fusion.8, f32[16,16,64]{2,1,0:T(8,128)S(1)} %add_maximum_fusion.1, f32[16,16,63]{2,1,0:T(8,128)S(1)} %get-tuple-element.71, f32[16,16,1]{2,1,0:T(8,128)S(1)} %get-tuple-element.73, ...), kind=kLoop, calls=%fused_computation.400 | loop fusion | flops 409600 | bytes 1130224 | tf_op jit(solution)/shard_map/add | solution.py:156
  112.6 1.2 %slice_add_fusion.11 = (f32[14,14,64]{2,1,0:T(8,128)S(1)}, f32[14,14,64]{2,1,0:T(8,128)S(1)}) fusion(f32[16,16,64]{2,1,0:T(8,128)S(1)} %get-tuple-element.15, f32[16,16,64]{2,1,0:T(8,128)S(1)} %add_maximum_fusion.1, f32[14,14,63]{2,1,0:T(8,128)S(1)} %get-tuple-element.123, f32[14,14,1]{2,1,0:T(8,128)S(1)} %get-tuple-element.125, ...), kind=kLoop, calls=%fused_computation.453 | loop fusion | flops 338688 | bytes 934640 | tf_op jit(solution)/shard_map/add | solution.py:166
  114.0 1.3 %fusion.258 = f32[12,12,128]{2,1,0:T(8,128)S(1)} fusion(f32[14,14,64]{2,1,0:T(8,128)S(1)} %get-tuple-element.14, f32[14,14,64]{2,1,0:T(8,128)S(1)} %get-tuple-element.13, f32[18,18,64]{2,1,0:T(8,128)S(1)} %slice_bitcast_fusion.9, f32[12,12,1]{2,1,0:T(8,128)S(1)} %get-tuple-element.135, f32[12,12,63]{2,1,0:T(8,128)S(1)} %get-tuple-element.137, ...), kind=kOutput, calls=%fused_computation.483 | convolution fusion | flops 14412800 | bytes 1966592 | tf_op jit(solution)/shard_map/xyz,wz->xyw/dot_general | solution.py:94
  118.1 1.0 fusion.181
  (212 shorter events, 17.8 us)
Async XLA Ops:
  0.0 18.0 %copy-start.13 = (f32[16,16,128]{2,1,0:T(8,128)S(1)}, f32[16,16,128]{2,1,0:T(8,128)}, u32[]{:S(2)}) copy-start(f32[16,16,128]{2,1,0:T(8,128)} %param.4) | copy-start | bytes 393220
  0.0 18.0 %copy-start.12 = (f32[16,16,128]{2,1,0:T(8,128)S(1)}, f32[16,16,128]{2,1,0:T(8,128)}, u32[]{:S(2)}) copy-start(f32[16,16,128]{2,1,0:T(8,128)} %param.5) | copy-start | bytes 393220
  2.0 9.7 %collective-permute-start = (f32[3,10,16,128]{3,2,1,0:T(8,128)S(1)}, f32[3,10,16,128]{3,2,1,0:T(8,128)S(1)}, u32[]{:S(2)}, u32[]{:S(2)}) collective-permute-start(f32[3,10,16,128]{3,2,1,0:T(8,128)S(1)} %get-tuple-element.48), channel_id=1, source_target_pairs={{0,4},{4,8},{8,12},{12,16},{16,20},{20,24},{24,28},{1,5},{5,9},{9,... | collective-permute-start | bytes 737288 | tf_op jit(solution)/shard_map/ppermute | solution.py:30
  5.2 12.8 %collective-permute-start.1 = (f32[3,10,16,128]{3,2,1,0:T(8,128)S(1)}, f32[3,10,16,128]{3,2,1,0:T(8,128)S(1)}, u32[]{:S(2)}, u32[]{:S(2)}) collective-permute-start(f32[3,10,16,128]{3,2,1,0:T(8,128)S(1)} %get-tuple-element.49), channel_id=1, source_target_pairs={{4,0},{8,4},{12,8},{16,12},{20,16},{24,20},{28,24},{5,1},{9,5},{13... | collective-permute-start | bytes 737288 | tf_op jit(solution)/shard_map/ppermute | solution.py:30
  8.2 43.8 %copy-start.27 = (s32[128]{0:T(128)}, s32[128]{0:T(128)S(1)}, u32[]{:S(2)}) copy-start(s32[128]{0:T(128)S(1)} %and_select_fusion.4) | copy-start | bytes 1540
  18.4 10.6 %collective-permute-start.2 = (f32[3,36,10,128]{3,1,2,0:T(8,128)S(1)}, f32[3,36,10,128]{3,1,2,0:T(8,128)S(1)}, u32[]{:S(2)}, u32[]{:S(2)}) collective-permute-start(f32[3,36,10,128]{3,1,2,0:T(8,128)S(1)} %copy.19), channel_id=1, source_target_pairs={{0,1},{1,2},{2,3},{4,5},{5,6},{6,7},{8,9},{9,10},{10,11},{12,13},{... | collective-permute-start | bytes 1658888 | tf_op jit(solution)/shard_map/ppermute | solution.py:30
  22.1 11.5 %collective-permute-start.3 = (f32[3,36,10,128]{3,1,2,0:T(8,128)S(1)}, f32[3,36,10,128]{3,1,2,0:T(8,128)S(1)}, u32[]{:S(2)}, u32[]{:S(2)}) collective-permute-start(f32[3,36,10,128]{3,1,2,0:T(8,128)S(1)} %copy.20), channel_id=1, source_target_pairs={{1,0},{2,1},{3,2},{5,4},{6,5},{7,6},{9,8},{10,9},{11,10},{13,12},{... | collective-permute-start | bytes 1658888 | tf_op jit(solution)/shard_map/ppermute | solution.py:30
  40.7 2.5 %copy-start = (f32[4,36,36,128]{3,2,1,0:T(8,128)S(1)}, f32[4,36,36,128]{3,2,1,0:T(8,128)}, u32[]{:S(2)}) copy-start(f32[4,36,36,128]{3,2,1,0:T(8,128)} %shard_map.46) | copy-start | bytes 7962628
  43.2 7.9 %copy-start.1 = (f32[36,36,128]{2,1,0:T(8,128)}, f32[36,36,128]{2,1,0:T(8,128)S(1)}, u32[]{:S(2)}) copy-start(f32[36,36,128]{2,1,0:T(8,128)S(1)} %get-tuple-element.24) | copy-start | bytes 1990660
  44.6 2.1 %copy-start.10 = (f32[34,34,128]{2,1,0:T(8,128)}, f32[34,34,128]{2,1,0:T(8,128)S(1)}, u32[]{:S(2)}) copy-start(f32[34,34,128]{2,1,0:T(8,128)S(1)} %get-tuple-element.22) | copy-start | bytes 1775620
  50.8 3.2 %copy-start.5 = (f32[72,18,64]{2,1,0:T(8,128)}, f32[72,18,64]{2,1,0:T(8,128)S(1)}, u32[]{:S(2)}) copy-start(f32[72,18,64]{2,1,0:T(8,128)S(1)} %convolution_multiply_fusion) | copy-start | bytes 995332
  51.0 3.1 %copy-start.3 = (f32[18,18,63]{2,1,0:T(8,128)}, f32[18,18,63]{2,1,0:T(8,128)S(1)}, u32[]{:S(2)}) copy-start(f32[18,18,63]{2,1,0:T(8,128)S(1)} %divide_multiply_fusion) | copy-start | bytes 244948
  51.1 3.0 %copy-start.8 = (f32[18,17,64]{2,1,0:T(8,128)}, f32[18,17,64]{2,1,0:T(8,128)S(1)}, u32[]{:S(2)}) copy-start(f32[18,17,64]{2,1,0:T(8,128)S(1)} %divide_multiply_fusion.1) | copy-start | bytes 235012
  52.0 0.7 copy-start.22
  52.4 1.7 %copy-start.6 = (f32[17,18,64]{2,1,0:T(8,128)}, f32[17,18,64]{2,1,0:T(8,128)S(1)}, u32[]{:S(2)}) copy-start(f32[17,18,64]{2,1,0:T(8,128)S(1)} %multiply_bitcast_fusion) | copy-start | bytes 235012
  53.7 0.7 copy-start.25
  54.2 2.9 %copy-start.16 = (f32[1,8,8,64]{3,2,1,0:T(8,128)}, f32[1,8,8,64]{3,2,1,0:T(8,128)S(1)}, u32[]{:S(2)}) copy-start(f32[1,8,8,64]{3,2,1,0:T(8,128)S(1)} %get-tuple-element.146) | copy-start | bytes 49156
  54.2 2.9 %copy-start.18 = (f32[1,8,8,64]{3,2,1,0:T(8,128)}, f32[1,8,8,64]{3,2,1,0:T(8,128)S(1)}, u32[]{:S(2)}) copy-start(f32[1,8,8,64]{3,2,1,0:T(8,128)S(1)} %get-tuple-element.156) | copy-start | bytes 49156
  54.8 2.3 %copy-start.20 = (f32[1,4,4,32]{3,2,1,0:T(4,128)}, f32[1,4,4,32]{3,2,1,0:T(4,128)S(1)}, u32[]{:S(2)}) copy-start(f32[1,4,4,32]{3,2,1,0:T(4,128)S(1)} %fusion) | copy-start | bytes 6148
  55.1 0.6 copy-start.14
  56.3 9.5 %collective-permute-start.5 = (f32[5,4,4,32]{3,2,1,0:T(4,128)}, f32[5,4,4,32]{3,2,1,0:T(4,128)}, u32[]{:S(2)}, u32[]{:S(2)}) collective-permute-start(f32[5,4,4,32]{3,2,1,0:T(4,128)} %pad_maximum_fusion.24), channel_id=1, source_target_pairs={{0,2},{1,3},{2,0},{3,1},{4,6},{5,7},{6,4},{7,5},{8,10},{9,11},{10,... | collective-permute-start | bytes 30728 | tf_op jit(solution)/shard_map/ppermute | solution.py:266
  57.9 6.9 %collective-permute-start.6 = (f32[36,5,64]{2,1,0:T(8,128)}, f32[36,5,64]{2,1,0:T(8,128)}, u32[]{:S(2)}, u32[]{:S(2)}) collective-permute-start(f32[36,5,64]{2,1,0:T(8,128)} %get-tuple-element.158), channel_id=1, source_target_pairs={{0,1},{1,2},{2,3},{3,0},{4,5},{5,6},{6,7},{7,4},{8,9},{9,10},{10,1... | collective-permute-start | bytes 138248 | tf_op jit(solution)/shard_map/ppermute | solution.py:264
  57.9 6.0 %collective-permute-start.4 = (f32[36,5,64]{2,1,0:T(8,128)}, f32[36,5,64]{2,1,0:T(8,128)}, u32[]{:S(2)}, u32[]{:S(2)}) collective-permute-start(f32[36,5,64]{2,1,0:T(8,128)} %get-tuple-element.157), channel_id=1, source_target_pairs={{0,3},{1,0},{2,1},{3,2},{4,7},{5,4},{6,5},{7,6},{8,11},{9,8},{10,9... | collective-permute-start | bytes 138248 | tf_op jit(solution)/shard_map/ppermute | solution.py:262
  58.5 22.5 %copy-start.17 = (f32[1,8,8,64]{3,2,1,0:T(8,128)S(1)}, f32[1,8,8,64]{3,2,1,0:T(8,128)}, u32[]{:S(2)}) copy-start(f32[1,8,8,64]{3,2,1,0:T(8,128)} %copy-done.16) | copy-start | bytes 49156
  58.5 22.5 %copy-start.19 = (f32[1,8,8,64]{3,2,1,0:T(8,128)S(1)}, f32[1,8,8,64]{3,2,1,0:T(8,128)}, u32[]{:S(2)}) copy-start(f32[1,8,8,64]{3,2,1,0:T(8,128)} %copy-done.18) | copy-start | bytes 49156
  66.6 16.4 %collective-permute-start.9 = (f32[5,4,16,32]{3,2,1,0:T(8,128)S(1)}, f32[5,4,16,32]{3,2,1,0:T(8,128)S(1)}, u32[]{:S(2)}, u32[]{:S(2)}) collective-permute-start(f32[5,4,16,32]{3,2,1,0:T(8,128)S(1)} %pad_maximum_fusion.8), channel_id=1, source_target_pairs={{0,12},{4,16},{8,20},{12,24},{16,28},{1,13},{5,17},{9,21},{13,25},... | collective-permute-start | bytes 122888 | tf_op jit(solution)/shard_map/ppermute | solution.py:30
  67.9 19.4 %collective-permute-start.10 = (f32[5,4,16,32]{3,2,1,0:T(8,128)S(1)}, f32[5,4,16,32]{3,2,1,0:T(8,128)S(1)}, u32[]{:S(2)}, u32[]{:S(2)}) collective-permute-start(f32[5,4,16,32]{3,2,1,0:T(8,128)S(1)} %pad_maximum_fusion.8), channel_id=1, source_target_pairs={{0,8},{4,12},{8,16},{12,20},{16,24},{20,28},{1,9},{5,13},{9,17},{1... | collective-permute-start | bytes 122888 | tf_op jit(solution)/shard_map/ppermute | solution.py:30
  69.2 34.0 %collective-permute-start.11 = (f32[5,4,16,32]{3,2,1,0:T(8,128)S(1)}, f32[5,4,16,32]{3,2,1,0:T(8,128)S(1)}, u32[]{:S(2)}, u32[]{:S(2)}) collective-permute-start(f32[5,4,16,32]{3,2,1,0:T(8,128)S(1)} %pad_maximum_fusion.8), channel_id=1, source_target_pairs={{8,0},{12,4},{16,8},{20,12},{24,16},{28,20},{9,1},{13,5},{17,9},{2... | collective-permute-start | bytes 122888 | tf_op jit(solution)/shard_map/ppermute | solution.py:30
  73.3 30.1 %collective-permute-start.12 = (f32[5,4,16,32]{3,2,1,0:T(8,128)S(1)}, f32[5,4,16,32]{3,2,1,0:T(8,128)S(1)}, u32[]{:S(2)}, u32[]{:S(2)}) collective-permute-start(f32[5,4,16,32]{3,2,1,0:T(8,128)S(1)} %pad_maximum_fusion.8), channel_id=1, source_target_pairs={{12,0},{16,4},{20,8},{24,12},{28,16},{13,1},{17,5},{21,9},{25,13},... | collective-permute-start | bytes 122888 | tf_op jit(solution)/shard_map/ppermute | solution.py:30
  81.1 12.6 %collective-permute-start.7 = (f32[30,18,64]{2,1,0:T(8,128)S(1)}, f32[30,18,64]{2,1,0:T(8,128)S(1)}, u32[]{:S(2)}, u32[]{:S(2)}) collective-permute-start(f32[30,18,64]{2,1,0:T(8,128)S(1)} %get-tuple-element.65), channel_id=1, source_target_pairs={{0,4},{4,8},{8,12},{12,16},{16,20},{20,24},{24,28},{1,5},{5,9},{9,... | collective-permute-start | bytes 414728 | tf_op jit(solution)/shard_map/ppermute | solution.py:30
  83.0 19.3 %collective-permute-start.8 = (f32[30,18,64]{2,1,0:T(8,128)S(1)}, f32[30,18,64]{2,1,0:T(8,128)S(1)}, u32[]{:S(2)}, u32[]{:S(2)}) collective-permute-start(f32[30,18,64]{2,1,0:T(8,128)S(1)} %get-tuple-element.64), channel_id=1, source_target_pairs={{4,0},{8,4},{12,8},{16,12},{20,16},{24,20},{28,24},{5,1},{9,5},{13... | collective-permute-start | bytes 414728 | tf_op jit(solution)/shard_map/ppermute | solution.py:30
  103.2 0.6 copy-start.29
  108.2 0.8 copy-start.15
  108.2 0.8 copy-start.21
  109.0 1.1 copy-start.26
  109.0 1.4 %copy-start.24 = (f32[20,10]{0,1:T(8,128)S(1)}, f32[20,10]{0,1:T(8,128)}, u32[]{:S(2)}) copy-start(f32[20,10]{0,1:T(8,128)} %fusion.363) | copy-start | bytes 2404
  110.0 1.0 copy-start.4
  110.0 1.0 copy-start.7
  110.1 1.1 copy-start.9
  112.6 1.4 %copy-start.28 = (s32[128]{0:T(128)S(1)}, s32[128]{0:T(128)}, u32[]{:S(2)}) copy-start(s32[128]{0:T(128)} %copy-done.27) | copy-start | bytes 1540
  113.8 1.6 %copy-start.23 = (f32[24,12]{0,1:T(8,128)S(1)}, f32[24,12]{0,1:T(8,128)}, u32[]{:S(2)}) copy-start(f32[24,12]{0,1:T(8,128)} %fusion.361) | copy-start | bytes 3460
  115.4 1.1 copy-start.2
  115.4 1.3 %copy-start.11 = (f32[34,34,128]{2,1,0:T(8,128)S(1)}, f32[34,34,128]{2,1,0:T(8,128)}, u32[]{:S(2)}) copy-start(f32[34,34,128]{2,1,0:T(8,128)} %copy-done.10) | copy-start | bytes 1775620

commit v10 on v5

--- a/solution.py
+++ b/solution.py
@@ -1,3 +1,5 @@
+import functools
+
 import jax
 import jax.numpy as jnp
 from jax import lax
@@ -150,18 +152,23 @@
     return iterate, cur
 
 
-def fields_kernel(bounds_ref, table_ref, conc_ref, idf_ref, out_ref):
+def fields_kernel(frame, table_ref, conc_ref, idf_ref, out_ref):
     rows = conc_ref.shape[0]
     shape = conc_ref.shape[1:]
     mats = table_ref.shape[1]
+    nx, ny, hf = frame
+    x_lo = hf - lax.axis_index("gx") * nx
+    y_lo = hf - lax.axis_index("gy") * ny
+    x_hi = x_lo + lax.axis_size("gx") * nx
+    y_hi = y_lo + lax.axis_size("gy") * ny
     col = lax.broadcasted_iota(jnp.int32, shape, 0)
-    col_ok = (col >= bounds_ref[2]) & (col < bounds_ref[3])
+    col_ok = (col >= y_lo) & (col < y_hi)
 
     def body(i, carry):
         ids = idf_ref[i]
         conc = conc_ref[i]
         row = jnp.zeros(shape, jnp.int32) + i
-        ok = col_ok & (row >= bounds_ref[0]) & (row < bounds_ref[1])
+        ok = col_ok & (row >= x_lo) & (row < x_hi)
         vals = []
         for record in range(5):
             acc = jnp.zeros(shape, jnp.float32) + table_ref[record, mats - 1]
@@ -175,16 +182,15 @@
         out_ref[3, i] = jnp.where(ok, store, 0.0)
         return carry
 
-    lax.fori_loop(0, rows, body, 0)
-
-
-def soil_fields(bounds, soil_table, conc, idf):
+    lax.fori_loop(0, rows, body, 0, unroll=2)
+
+
+def soil_fields(frame, soil_table, conc, idf):
     cells = conc.size
     return pl.pallas_call(
-        fields_kernel,
+        functools.partial(fields_kernel, frame),
         out_shape=jax.ShapeDtypeStruct((4,) + conc.shape, jnp.float32),
         in_specs=[
-            pl.BlockSpec(memory_space=pltpu.SMEM),
             pl.BlockSpec(memory_space=pltpu.SMEM),
             pl.BlockSpec(memory_space=pltpu.VMEM),
             pl.BlockSpec(memory_space=pltpu.VMEM),
@@ -193,7 +199,7 @@
         cost_estimate=pl.CostEstimate(
             flops=100 * cells, transcendentals=2 * cells, bytes_accessed=24 * cells
         ),
-    )(bounds, soil_table, conc, idf)
+    )(soil_table, conc, idf)
 
 
 def local(conc_prev, right_side, soil_id, soil_table):
@@ -208,10 +214,7 @@
     stacked = jnp.stack([conc_prev, right_side, soil_id.astype(jnp.float32)])
     ext = halo(stacked, (("gx", 1), ("gy", 2)), hf)
     conc, rhs, idf = ext[0], ext[1], ext[2]
-    x_lo = hf - ix * n
-    y_lo = hf - iy * ny
-    bounds = jnp.stack([x_lo, x_lo + gx_count * n, y_lo, y_lo + gy_count * ny]).astype(jnp.int32)
-    fine_c = soil_fields(bounds, soil_table, conc, idf)
+    fine_c = soil_fields((n, ny, hf), soil_table, conc, idf)
     fine = build_level(fine_c, n, hf, 1.0)
 
     x0, x0m = chebyshev(rhs, hf, None, 0, fine)

time: 103 us -> 102 us (level)
  transfers between devices with their start and end apart: 17 -> 17, of which waited for: 4 -> 4; matrix products, arithmetic and copies ran while one was open for 7% -> 6% of each run, Pallas kernels for 0% -> 0%
where the time goes in v10:
time: 102 us
  starting transfers between devices  48.3 us (47%)
  waiting for transfers between devices  17.6 us (17%)
  other arithmetic  13.8 us (14%)
  local copies, waits for them, and re-layouts  10.7 us (10%)
  matrix products  5.17 us (5%)
  Pallas kernels  5.16 us (5%)
  between operations  1.18 us (1%)
    ppermute x14, starting transfers between devices, shift_from(): return lax.ppermute(cells, axis, pairs)  37.7 us
    ppermute x14, waiting for transfers between devices, shift_from(): return lax.ppermute(cells, axis, pairs)  17.6 us
    ppermute x3, starting transfers between devices, local(): blocks.append(lax.ppermute(cpack, 'gy', pairs))  10.6 us
    pallas_call x1, Pallas kernels, soil_fields(): pl.pallas_call(functools.partial(fields_kernel, frame), out_shape=jax.Sha...  5.16 us
    add x7, other arithmetic, chebyshev(): iterate = win(iterate, n, cur, nxt) + update  4.56 us
    add x8, other arithmetic, local(): u = centre + jacobi_weight * ((csrc[sl] - applied) / cdiag[sl])  2.49 us
    dot_general x4, matrix products, coarsen(): lax.dot_general(pick, rows, (((2,), (1,)), ((0,), (0,))), precision=HIGH)  2.25 us
  transfers between devices with their start and end apart: 17, of which 4 were waited for; matrix products, arithmetic and copies ran while one was open for 6% of the time, Pallas kernels for 0%

profile of v10, /device:TPU:4, one launch (start us, length us, event | category | flops | bytes accessed | tf_op | source)
XLA Modules:
  0.0 101.9 jit_solution(5060894548632727159)
XLA Ops:
  0.0 1.0 convert_bitcast_fusion
  1.0 1.0 pad_maximum_fusion.4
  2.0 1.9 %collective-permute-start.1 = (f32[3,10,16,128]{3,2,1,0:T(8,128)S(1)}, f32[3,10,16,128]{3,2,1,0:T(8,128)S(1)}, u32[]{:S(2)}, u32[]{:S(2)}) collective-permute-start(f32[3,10,16,128]{3,2,1,0:T(8,128)S(1)} %get-tuple-element.49), channel_id=1, source_target_pairs={{4,0},{8,4},{12,8},{16,12},{20,16},{24,20},{28,24},{5,1},{9,5},{13... | collective-permute-start | bytes 737288 | tf_op jit(solution)/shard_map/ppermute | solution.py:32
  4.0 4.8 %collective-permute-start = (f32[3,10,16,128]{3,2,1,0:T(8,128)S(1)}, f32[3,10,16,128]{3,2,1,0:T(8,128)S(1)}, u32[]{:S(2)}, u32[]{:S(2)}) collective-permute-start(f32[3,10,16,128]{3,2,1,0:T(8,128)S(1)} %get-tuple-element.48), channel_id=1, source_target_pairs={{0,4},{4,8},{8,12},{12,16},{16,20},{20,24},{24,28},{1,5},{5,9},{9,... | collective-permute-start | bytes 737288 | tf_op jit(solution)/shard_map/ppermute | solution.py:32
  8.9 3.7 %collective-permute-done.1 = f32[3,10,16,128]{3,2,1,0:T(8,128)S(1)} collective-permute-done((f32[3,10,16,128]{3,2,1,0:T(8,128)S(1)}, f32[3,10,16,128]{3,2,1,0:T(8,128)S(1)}, u32[]{:S(2)}, u32[]{:S(2)}) %collective-permute-start.1) | collective-permute-done | bytes 245792 | tf_op jit(solution)/shard_map/ppermute | solution.py:32
  12.6 5.2 %collective-permute-done = f32[3,10,16,128]{3,2,1,0:T(8,128)S(1)} collective-permute-done((f32[3,10,16,128]{3,2,1,0:T(8,128)S(1)}, f32[3,10,16,128]{3,2,1,0:T(8,128)S(1)}, u32[]{:S(2)}, u32[]{:S(2)}) %collective-permute-start) | collective-permute-done | bytes 245792 | tf_op jit(solution)/shard_map/ppermute | solution.py:32
  17.8 0.7 copy-done.3
  18.9 1.3 %collective-permute-start.3 = (f32[3,36,10,128]{3,1,2,0:T(8,128)S(1)}, f32[3,36,10,128]{3,1,2,0:T(8,128)S(1)}, u32[]{:S(2)}, u32[]{:S(2)}) collective-permute-start(f32[3,36,10,128]{3,1,2,0:T(8,128)S(1)} %copy.20), channel_id=1, source_target_pairs={{1,0},{2,1},{3,2},{5,4},{6,5},{7,6},{9,8},{10,9},{11,10},{13,12},{... | collective-permute-start | bytes 1658888 | tf_op jit(solution)/shard_map/ppermute | solution.py:32
  20.4 3.1 %collective-permute-start.2 = (f32[3,36,10,128]{3,1,2,0:T(8,128)S(1)}, f32[3,36,10,128]{3,1,2,0:T(8,128)S(1)}, u32[]{:S(2)}, u32[]{:S(2)}) collective-permute-start(f32[3,36,10,128]{3,1,2,0:T(8,128)S(1)} %copy.19), channel_id=1, source_target_pairs={{0,1},{1,2},{2,3},{4,5},{5,6},{6,7},{8,9},{9,10},{10,11},{12,13},{... | collective-permute-start | bytes 1658888 | tf_op jit(solution)/shard_map/ppermute | solution.py:32
  23.6 1.4 %collective-permute-done.2 = f32[3,36,10,128]{3,1,2,0:T(8,128)S(1)} collective-permute-done((f32[3,36,10,128]{3,1,2,0:T(8,128)S(1)}, f32[3,36,10,128]{3,1,2,0:T(8,128)S(1)}, u32[]{:S(2)}, u32[]{:S(2)}) %collective-permute-start.2) | collective-permute-done | bytes 552992 | tf_op jit(solution)/shard_map/ppermute | solution.py:32
  25.5 1.3 %slice_bitcast_fusion.3 = (f32[36,36,128]{2,1,0:T(8,128)}, f32[36,36,128]{2,1,0:T(8,128)}, f32[36,36,128]{2,1,0:T(8,128)S(1)}) fusion(f32[3,36,36,128]{3,2,1,0:T(8,128)S(1)} %pad_maximum_fusion), kind=kLoop, calls=%fused_computation.19 | loop fusion | bytes 3981312 | tf_op jit(solution)/shard_map/squeeze | solution.py:216
  26.7 5.2 %shard_map.46 = f32[4,36,36,128]{3,2,1,0:T(8,128)} custom-call(f32[5,8]{1,0:T(8,128)} %table_ref.1, f32[36,36,128]{2,1,0:T(8,128)} %get-tuple-element.27.conc_ref, f32[36,36,128]{2,1,0:T(8,128)} %get-tuple-element.26.idf_ref), custom_call_target="tpu_custom_call" | custom-call | flops 16588800 | bytes 3981312 | tf_op jit(solution)/shard_map/pallas_call | solution.py:190
  31.9 1.9 %slice_bitcast_fusion.2 = (f32[36,36,128]{2,1,0:T(8,128)S(1)}, f32[36,36,128]{2,1,0:T(8,128)S(1)}, f32[36,36,128]{2,1,0:T(8,128)S(1)}) fusion(f32[4,36,36,128]{3,2,1,0:T(8,128)} %shard_map.46), kind=kLoop, calls=%fused_computation.18 | loop fusion | bytes 3981312 | tf_op jit(solution)/shard_map/squeeze | solution.py:85
  33.8 0.6 copy-done
  35.0 0.7 fusion.4
  36.2 1.2 %slice_add_fusion.5 = (f32[32,32,128]{2,1,0:T(8,128)S(1)}, f32[32,32,128]{2,1,0:T(8,128)S(1)}) fusion(f32[34,34,128]{2,1,0:T(8,128)S(1)} %get-tuple-element.21, f32[34,34,128]{2,1,0:T(8,128)S(1)} %get-tuple-element.22, f32[32,32,127]{2,1,0:T(8,128)S(1)} %get-tuple-element.37, f32[32,32,1]{2,1,0:T(8,128)S(1)} %get-tuple-element.39, ...), kind=kLoop, calls=%fused_computation.57 | loop fusion | flops 3538944 | bytes 9046976 | tf_op jit(solution)/shard_map/add | solution.py:149
  38.0 0.8 fusion.336
  38.8 1.5 %convolution_multiply_fusion = f32[72,18,64]{2,1,0:T(8,128)S(1)} fusion(f32[72,36,64]{2,1,0:T(8,128)S(1)} %fusion.336, f32[18,36]{1,0:T(8,128)S(1)} %fusion.357), kind=kOutput, calls=%fused_computation.2 | convolution fusion | flops 35914752 | bytes 997920 | tf_op jit(solution)/shard_map/dot_general | solution.py:70
  40.6 1.2 %fusion.22 = f32[30,30,128]{2,1,0:T(8,128)S(1)} fusion(f32[34,34,128]{2,1,0:T(8,128)S(1)} %get-tuple-element.22, f32[32,32,128]{2,1,0:T(8,128)S(1)} %get-tuple-element.19, f32[36,35,128]{2,1,0:T(8,128)S(1)} %maximum_divide_fusion.1, f32[35,36,128]{2,1,0:T(8,128)S(1)} %divide_bitcast_fusion, f32[36,36,128]{2,1,0:T(8,128)S(1)} %get-tuple-element.24, ...), kind=kLoop, calls=%fused_computation.61 | loop fusion | flops 3110400 | bytes 8031168 | tf_op jit(solution)/shard_map/add | solution.py:149
  42.2 0.9 fusion.40
  43.5 0.3 divide_multiply_fusion.3
  45.7 6.7 %collective-permute-start.10 = (f32[5,4,4,32]{3,2,1,0:T(4,128)S(1)}, f32[5,4,4,32]{3,2,1,0:T(4,128)S(1)}, u32[]{:S(2)}, u32[]{:S(2)}) collective-permute-start(f32[5,4,4,32]{3,2,1,0:T(4,128)S(1)} %pad_maximum_fusion.20), channel_id=1, source_target_pairs={{0,1},{1,2},{2,3},{3,0},{4,5},{5,6},{6,7},{7,4},{8,9},{9,10},{10,1... | collective-permute-start | bytes 30728 | tf_op jit(solution)/shard_map/ppermute | solution.py:242
  52.4 2.4 %collective-permute-start.9 = (f32[5,4,4,32]{3,2,1,0:T(4,128)S(1)}, f32[5,4,4,32]{3,2,1,0:T(4,128)S(1)}, u32[]{:S(2)}, u32[]{:S(2)}) collective-permute-start(f32[5,4,4,32]{3,2,1,0:T(4,128)S(1)} %pad_maximum_fusion.20), channel_id=1, source_target_pairs={{0,2},{1,3},{2,0},{3,1},{4,6},{5,7},{6,4},{7,5},{8,10},{9,11},{10,... | collective-permute-start | bytes 30728 | tf_op jit(solution)/shard_map/ppermute | solution.py:242
  54.8 1.4 %collective-permute-start.8 = (f32[5,4,4,32]{3,2,1,0:T(4,128)S(1)}, f32[5,4,4,32]{3,2,1,0:T(4,128)S(1)}, u32[]{:S(2)}, u32[]{:S(2)}) collective-permute-start(f32[5,4,4,32]{3,2,1,0:T(4,128)S(1)} %pad_maximum_fusion.20), channel_id=1, source_target_pairs={{0,3},{1,0},{2,1},{3,2},{4,7},{5,4},{6,5},{7,6},{8,11},{9,8},{10,9... | collective-permute-start | bytes 30728 | tf_op jit(solution)/shard_map/ppermute | solution.py:242
  56.3 1.3 %collective-permute-start.5 = (f32[2,8,5,64]{3,2,1,0:T(8,128)S(1)}, f32[2,8,5,64]{3,2,1,0:T(8,128)S(1)}, u32[]{:S(2)}, u32[]{:S(2)}) collective-permute-start(f32[2,8,5,64]{3,2,1,0:T(8,128)S(1)} %get-tuple-element.158), channel_id=1, source_target_pairs={{1,0},{2,1},{3,2},{5,4},{6,5},{7,6},{9,8},{10,9},{11,10},{13,12},{... | collective-permute-start | bytes 61448 | tf_op jit(solution)/shard_map/ppermute | solution.py:32
  57.6 3.0 %collective-permute-start.4 = (f32[2,8,5,64]{3,2,1,0:T(8,128)S(1)}, f32[2,8,5,64]{3,2,1,0:T(8,128)S(1)}, u32[]{:S(2)}, u32[]{:S(2)}) collective-permute-start(f32[2,8,5,64]{3,2,1,0:T(8,128)S(1)} %get-tuple-element.157), channel_id=1, source_target_pairs={{0,1},{1,2},{2,3},{4,5},{5,6},{6,7},{8,9},{9,10},{10,11},{12,13},{... | collective-permute-start | bytes 61448 | tf_op jit(solution)/shard_map/ppermute | solution.py:32
  60.7 3.5 %collective-permute-start.12 = (f32[5,4,16,32]{3,2,1,0:T(8,128)S(1)}, f32[5,4,16,32]{3,2,1,0:T(8,128)S(1)}, u32[]{:S(2)}, u32[]{:S(2)}) collective-permute-start(f32[5,4,16,32]{3,2,1,0:T(8,128)S(1)} %pad_maximum_fusion.6), channel_id=1, source_target_pairs={{0,8},{4,12},{8,16},{12,20},{16,24},{20,28},{1,9},{5,13},{9,17},{1... | collective-permute-start | bytes 122888 | tf_op jit(solution)/shard_map/ppermute | solution.py:32
  64.2 3.4 %collective-permute-start.11 = (f32[5,4,16,32]{3,2,1,0:T(8,128)S(1)}, f32[5,4,16,32]{3,2,1,0:T(8,128)S(1)}, u32[]{:S(2)}, u32[]{:S(2)}) collective-permute-start(f32[5,4,16,32]{3,2,1,0:T(8,128)S(1)} %pad_maximum_fusion.6), channel_id=1, source_target_pairs={{0,12},{4,16},{8,20},{12,24},{16,28},{1,13},{5,17},{9,21},{13,25},... | collective-permute-start | bytes 122888 | tf_op jit(solution)/shard_map/ppermute | solution.py:32
  67.6 2.9 %collective-permute-start.13 = (f32[5,4,16,32]{3,2,1,0:T(8,128)S(1)}, f32[5,4,16,32]{3,2,1,0:T(8,128)S(1)}, u32[]{:S(2)}, u32[]{:S(2)}) collective-permute-start(f32[5,4,16,32]{3,2,1,0:T(8,128)S(1)} %pad_maximum_fusion.6), channel_id=1, source_target_pairs={{0,4},{4,8},{8,12},{12,16},{16,20},{20,24},{24,28},{1,5},{5,9},{9,... | collective-permute-start | bytes 122888 | tf_op jit(solution)/shard_map/ppermute | solution.py:32
  70.5 2.9 %collective-permute-start.14 = (f32[5,4,16,32]{3,2,1,0:T(8,128)S(1)}, f32[5,4,16,32]{3,2,1,0:T(8,128)S(1)}, u32[]{:S(2)}, u32[]{:S(2)}) collective-permute-start(f32[5,4,16,32]{3,2,1,0:T(8,128)S(1)} %pad_maximum_fusion.6), channel_id=1, source_target_pairs={{4,0},{8,4},{12,8},{16,12},{20,16},{24,20},{28,24},{5,1},{9,5},{13... | collective-permute-start | bytes 122888 | tf_op jit(solution)/shard_map/ppermute | solution.py:32
  73.5 1.3 %collective-permute-start.15 = (f32[5,4,16,32]{3,2,1,0:T(8,128)S(1)}, f32[5,4,16,32]{3,2,1,0:T(8,128)S(1)}, u32[]{:S(2)}, u32[]{:S(2)}) collective-permute-start(f32[5,4,16,32]{3,2,1,0:T(8,128)S(1)} %pad_maximum_fusion.6), channel_id=1, source_target_pairs={{8,0},{12,4},{16,8},{20,12},{24,16},{28,20},{9,1},{13,5},{17,9},{2... | collective-permute-start | bytes 122888 | tf_op jit(solution)/shard_map/ppermute | solution.py:32
  74.9 1.5 %collective-permute-start.16 = (f32[5,4,16,32]{3,2,1,0:T(8,128)S(1)}, f32[5,4,16,32]{3,2,1,0:T(8,128)S(1)}, u32[]{:S(2)}, u32[]{:S(2)}) collective-permute-start(f32[5,4,16,32]{3,2,1,0:T(8,128)S(1)} %pad_maximum_fusion.6), channel_id=1, source_target_pairs={{12,0},{16,4},{20,8},{24,12},{28,16},{13,1},{17,5},{21,9},{25,13},... | collective-permute-start | bytes 122888 | tf_op jit(solution)/shard_map/ppermute | solution.py:32
  76.4 1.9 %collective-permute-start.7 = (f32[2,5,18,64]{3,2,1,0:T(8,128)S(1)}, f32[2,5,18,64]{3,2,1,0:T(8,128)S(1)}, u32[]{:S(2)}, u32[]{:S(2)}) collective-permute-start(f32[2,5,18,64]{3,2,1,0:T(8,128)S(1)} %get-tuple-element.75), channel_id=1, source_target_pairs={{4,0},{8,4},{12,8},{16,12},{20,16},{24,20},{28,24},{5,1},{9,5},{13... | collective-permute-start | bytes 138248 | tf_op jit(solution)/shard_map/ppermute | solution.py:32
  78.4 4.8 %collective-permute-start.6 = (f32[2,5,18,64]{3,2,1,0:T(8,128)S(1)}, f32[2,5,18,64]{3,2,1,0:T(8,128)S(1)}, u32[]{:S(2)}, u32[]{:S(2)}) collective-permute-start(f32[2,5,18,64]{3,2,1,0:T(8,128)S(1)} %get-tuple-element.74), channel_id=1, source_target_pairs={{0,4},{4,8},{8,12},{12,16},{16,20},{20,24},{24,28},{1,5},{5,9},{9,... | collective-permute-start | bytes 138248 | tf_op jit(solution)/shard_map/ppermute | solution.py:32
  83.4 7.3 %collective-permute-done.16 = f32[5,4,16,32]{3,2,1,0:T(8,128)S(1)} collective-permute-done((f32[5,4,16,32]{3,2,1,0:T(8,128)S(1)}, f32[5,4,16,32]{3,2,1,0:T(8,128)S(1)}, u32[]{:S(2)}, u32[]{:S(2)}) %collective-permute-start.16) | collective-permute-done | bytes 40992 | tf_op jit(solution)/shard_map/ppermute | solution.py:32
  91.9 0.5 fusion.87
  92.7 0.4 multiply_add_fusion
  93.3 0.3 multiply_add_fusion.1
  94.0 0.3 multiply_add_fusion.2
  94.5 0.3 multiply_add_fusion.3
  96.5 0.4 fusion.318
  97.3 0.3 slice_add_fusion.10
  97.8 0.3 slice_add_fusion.11
  98.3 0.4 fusion.258
  98.7 0.5 fusion.315
  99.5 0.4 slice_add_fusion.7
  100.2 0.5 slice_add_fusion.9
  100.9 1.0 fusion.181
  (155 shorter events, 11.2 us)
Async XLA Ops:
  0.0 18.5 %copy-start.1 = (f32[16,16,128]{2,1,0:T(8,128)S(1)}, f32[16,16,128]{2,1,0:T(8,128)}, u32[]{:S(2)}) copy-start(f32[16,16,128]{2,1,0:T(8,128)} %param.5) | copy-start | bytes 393220
  0.0 18.5 %copy-start.2 = (f32[16,16,128]{2,1,0:T(8,128)S(1)}, f32[16,16,128]{2,1,0:T(8,128)}, u32[]{:S(2)}) copy-start(f32[16,16,128]{2,1,0:T(8,128)} %param.4) | copy-start | bytes 393220
  2.0 10.6 %collective-permute-start.1 = (f32[3,10,16,128]{3,2,1,0:T(8,128)S(1)}, f32[3,10,16,128]{3,2,1,0:T(8,128)S(1)}, u32[]{:S(2)}, u32[]{:S(2)}) collective-permute-start(f32[3,10,16,128]{3,2,1,0:T(8,128)S(1)} %get-tuple-element.49), channel_id=1, source_target_pairs={{4,0},{8,4},{12,8},{16,12},{20,16},{24,20},{28,24},{5,1},{9,5},{13... | collective-permute-start | bytes 737288 | tf_op jit(solution)/shard_map/ppermute | solution.py:32
  4.0 13.8 %collective-permute-start = (f32[3,10,16,128]{3,2,1,0:T(8,128)S(1)}, f32[3,10,16,128]{3,2,1,0:T(8,128)S(1)}, u32[]{:S(2)}, u32[]{:S(2)}) collective-permute-start(f32[3,10,16,128]{3,2,1,0:T(8,128)S(1)} %get-tuple-element.48), channel_id=1, source_target_pairs={{0,4},{4,8},{8,12},{12,16},{16,20},{20,24},{24,28},{1,5},{5,9},{9,... | collective-permute-start | bytes 737288 | tf_op jit(solution)/shard_map/ppermute | solution.py:32
  17.8 0.7 copy-start.3
  18.9 4.6 %collective-permute-start.3 = (f32[3,36,10,128]{3,1,2,0:T(8,128)S(1)}, f32[3,36,10,128]{3,1,2,0:T(8,128)S(1)}, u32[]{:S(2)}, u32[]{:S(2)}) collective-permute-start(f32[3,36,10,128]{3,1,2,0:T(8,128)S(1)} %copy.20), channel_id=1, source_target_pairs={{1,0},{2,1},{3,2},{5,4},{6,5},{7,6},{9,8},{10,9},{11,10},{13,12},{... | collective-permute-start | bytes 1658888 | tf_op jit(solution)/shard_map/ppermute | solution.py:32
  20.4 4.7 %collective-permute-start.2 = (f32[3,36,10,128]{3,1,2,0:T(8,128)S(1)}, f32[3,36,10,128]{3,1,2,0:T(8,128)S(1)}, u32[]{:S(2)}, u32[]{:S(2)}) collective-permute-start(f32[3,36,10,128]{3,1,2,0:T(8,128)S(1)} %copy.19), channel_id=1, source_target_pairs={{0,1},{1,2},{2,3},{4,5},{5,6},{6,7},{8,9},{9,10},{10,11},{12,13},{... | collective-permute-start | bytes 1658888 | tf_op jit(solution)/shard_map/ppermute | solution.py:32
  23.5 1.7 %copy-start.4 = (f32[3,10,16,128]{3,2,1,0:T(8,128)S(1)}, f32[3,10,16,128]{3,2,1,0:T(8,128)}, u32[]{:S(2)}) copy-start(f32[3,10,16,128]{3,2,1,0:T(8,128)} %copy-done.3) | copy-start | bytes 737284
  31.9 2.5 %copy-start = (f32[4,36,36,128]{3,2,1,0:T(8,128)S(1)}, f32[4,36,36,128]{3,2,1,0:T(8,128)}, u32[]{:S(2)}) copy-start(f32[4,36,36,128]{3,2,1,0:T(8,128)} %shard_map.46) | copy-start | bytes 7962628
  45.7 14.9 %collective-permute-start.10 = (f32[5,4,4,32]{3,2,1,0:T(4,128)S(1)}, f32[5,4,4,32]{3,2,1,0:T(4,128)S(1)}, u32[]{:S(2)}, u32[]{:S(2)}) collective-permute-start(f32[5,4,4,32]{3,2,1,0:T(4,128)S(1)} %pad_maximum_fusion.20), channel_id=1, source_target_pairs={{0,1},{1,2},{2,3},{3,0},{4,5},{5,6},{6,7},{7,4},{8,9},{9,10},{10,1... | collective-permute-start | bytes 30728 | tf_op jit(solution)/shard_map/ppermute | solution.py:242
  52.4 8.2 %collective-permute-start.9 = (f32[5,4,4,32]{3,2,1,0:T(4,128)S(1)}, f32[5,4,4,32]{3,2,1,0:T(4,128)S(1)}, u32[]{:S(2)}, u32[]{:S(2)}) collective-permute-start(f32[5,4,4,32]{3,2,1,0:T(4,128)S(1)} %pad_maximum_fusion.20), channel_id=1, source_target_pairs={{0,2},{1,3},{2,0},{3,1},{4,6},{5,7},{6,4},{7,5},{8,10},{9,11},{10,... | collective-permute-start | bytes 30728 | tf_op jit(solution)/shard_map/ppermute | solution.py:242
  54.8 5.8 %collective-permute-start.8 = (f32[5,4,4,32]{3,2,1,0:T(4,128)S(1)}, f32[5,4,4,32]{3,2,1,0:T(4,128)S(1)}, u32[]{:S(2)}, u32[]{:S(2)}) collective-permute-start(f32[5,4,4,32]{3,2,1,0:T(4,128)S(1)} %pad_maximum_fusion.20), channel_id=1, source_target_pairs={{0,3},{1,0},{2,1},{3,2},{4,7},{5,4},{6,5},{7,6},{8,11},{9,8},{10,9... | collective-permute-start | bytes 30728 | tf_op jit(solution)/shard_map/ppermute | solution.py:242
  56.3 14.3 %collective-permute-start.5 = (f32[2,8,5,64]{3,2,1,0:T(8,128)S(1)}, f32[2,8,5,64]{3,2,1,0:T(8,128)S(1)}, u32[]{:S(2)}, u32[]{:S(2)}) collective-permute-start(f32[2,8,5,64]{3,2,1,0:T(8,128)S(1)} %get-tuple-element.158), channel_id=1, source_target_pairs={{1,0},{2,1},{3,2},{5,4},{6,5},{7,6},{9,8},{10,9},{11,10},{13,12},{... | collective-permute-start | bytes 61448 | tf_op jit(solution)/shard_map/ppermute | solution.py:32
  57.6 15.9 %collective-permute-start.4 = (f32[2,8,5,64]{3,2,1,0:T(8,128)S(1)}, f32[2,8,5,64]{3,2,1,0:T(8,128)S(1)}, u32[]{:S(2)}, u32[]{:S(2)}) collective-permute-start(f32[2,8,5,64]{3,2,1,0:T(8,128)S(1)} %get-tuple-element.157), channel_id=1, source_target_pairs={{0,1},{1,2},{2,3},{4,5},{5,6},{6,7},{8,9},{9,10},{10,11},{12,13},{... | collective-permute-start | bytes 61448 | tf_op jit(solution)/shard_map/ppermute | solution.py:32
  60.7 15.7 %collective-permute-start.12 = (f32[5,4,16,32]{3,2,1,0:T(8,128)S(1)}, f32[5,4,16,32]{3,2,1,0:T(8,128)S(1)}, u32[]{:S(2)}, u32[]{:S(2)}) collective-permute-start(f32[5,4,16,32]{3,2,1,0:T(8,128)S(1)} %pad_maximum_fusion.6), channel_id=1, source_target_pairs={{0,8},{4,12},{8,16},{12,20},{16,24},{20,28},{1,9},{5,13},{9,17},{1... | collective-permute-start | bytes 122888 | tf_op jit(solution)/shard_map/ppermute | solution.py:32
  64.2 10.7 %collective-permute-start.11 = (f32[5,4,16,32]{3,2,1,0:T(8,128)S(1)}, f32[5,4,16,32]{3,2,1,0:T(8,128)S(1)}, u32[]{:S(2)}, u32[]{:S(2)}) collective-permute-start(f32[5,4,16,32]{3,2,1,0:T(8,128)S(1)} %pad_maximum_fusion.6), channel_id=1, source_target_pairs={{0,12},{4,16},{8,20},{12,24},{16,28},{1,13},{5,17},{9,21},{13,25},... | collective-permute-start | bytes 122888 | tf_op jit(solution)/shard_map/ppermute | solution.py:32
  67.6 10.7 %collective-permute-start.13 = (f32[5,4,16,32]{3,2,1,0:T(8,128)S(1)}, f32[5,4,16,32]{3,2,1,0:T(8,128)S(1)}, u32[]{:S(2)}, u32[]{:S(2)}) collective-permute-start(f32[5,4,16,32]{3,2,1,0:T(8,128)S(1)} %pad_maximum_fusion.6), channel_id=1, source_target_pairs={{0,4},{4,8},{8,12},{12,16},{16,20},{20,24},{24,28},{1,5},{5,9},{9,... | collective-permute-start | bytes 122888 | tf_op jit(solution)/shard_map/ppermute | solution.py:32
  70.5 12.8 %collective-permute-start.14 = (f32[5,4,16,32]{3,2,1,0:T(8,128)S(1)}, f32[5,4,16,32]{3,2,1,0:T(8,128)S(1)}, u32[]{:S(2)}, u32[]{:S(2)}) collective-permute-start(f32[5,4,16,32]{3,2,1,0:T(8,128)S(1)} %pad_maximum_fusion.6), channel_id=1, source_target_pairs={{4,0},{8,4},{12,8},{16,12},{20,16},{24,20},{28,24},{5,1},{9,5},{13... | collective-permute-start | bytes 122888 | tf_op jit(solution)/shard_map/ppermute | solution.py:32
  73.5 9.8 %collective-permute-start.15 = (f32[5,4,16,32]{3,2,1,0:T(8,128)S(1)}, f32[5,4,16,32]{3,2,1,0:T(8,128)S(1)}, u32[]{:S(2)}, u32[]{:S(2)}) collective-permute-start(f32[5,4,16,32]{3,2,1,0:T(8,128)S(1)} %pad_maximum_fusion.6), channel_id=1, source_target_pairs={{8,0},{12,4},{16,8},{20,12},{24,16},{28,20},{9,1},{13,5},{17,9},{2... | collective-permute-start | bytes 122888 | tf_op jit(solution)/shard_map/ppermute | solution.py:32
  74.9 15.8 %collective-permute-start.16 = (f32[5,4,16,32]{3,2,1,0:T(8,128)S(1)}, f32[5,4,16,32]{3,2,1,0:T(8,128)S(1)}, u32[]{:S(2)}, u32[]{:S(2)}) collective-permute-start(f32[5,4,16,32]{3,2,1,0:T(8,128)S(1)} %pad_maximum_fusion.6), channel_id=1, source_target_pairs={{12,0},{16,4},{20,8},{24,12},{28,16},{13,1},{17,5},{21,9},{25,13},... | collective-permute-start | bytes 122888 | tf_op jit(solution)/shard_map/ppermute | solution.py:32
  76.4 20.6 %collective-permute-start.7 = (f32[2,5,18,64]{3,2,1,0:T(8,128)S(1)}, f32[2,5,18,64]{3,2,1,0:T(8,128)S(1)}, u32[]{:S(2)}, u32[]{:S(2)}) collective-permute-start(f32[2,5,18,64]{3,2,1,0:T(8,128)S(1)} %get-tuple-element.75), channel_id=1, source_target_pairs={{4,0},{8,4},{12,8},{16,12},{20,16},{24,20},{28,24},{5,1},{9,5},{13... | collective-permute-start | bytes 138248 | tf_op jit(solution)/shard_map/ppermute | solution.py:32
  78.4 18.6 %collective-permute-start.6 = (f32[2,5,18,64]{3,2,1,0:T(8,128)S(1)}, f32[2,5,18,64]{3,2,1,0:T(8,128)S(1)}, u32[]{:S(2)}, u32[]{:S(2)}) collective-permute-start(f32[2,5,18,64]{3,2,1,0:T(8,128)S(1)} %get-tuple-element.74), channel_id=1, source_target_pairs={{0,4},{4,8},{8,12},{12,16},{16,20},{20,24},{24,28},{1,5},{5,9},{9,... | collective-permute-start | bytes 138248 | tf_op jit(solution)/shard_map/ppermute | solution.py:32

commit v11 on v10

--- a/solution.py
+++ b/solution.py
@@ -212,7 +212,7 @@
     iy = lax.axis_index("gy")
 
     stacked = jnp.stack([conc_prev, right_side, soil_id.astype(jnp.float32)])
-    ext = halo(stacked, (("gx", 1), ("gy", 2)), hf)
+    ext = halo(stacked, (("gy", 2), ("gx", 1)), hf)
     conc, rhs, idf = ext[0], ext[1], ext[2]
     fine_c = soil_fields((n, ny, hf), soil_table, conc, idf)
     fine = build_level(fine_c, n, hf, 1.0)

time: 102 us -> 110 us (1.078)
  waiting for transfers between devices: 17.6 us -> 34.5 us
  starting transfers between devices: 48.3 us -> 40.4 us
  local copies, waits for them, and re-layouts: 10.7 us -> 9.39 us
    ppermute x14, waiting for transfers between devices: 17.6 us -> 34.5 us  [shift_from(): return lax.ppermute(cells, axis, pairs)]
    ppermute x3, starting transfers between devices: 10.6 us -> 2.53 us  [local(): blocks.append(lax.ppermute(cpack, 'gy', pairs))]
where the time goes in v11:
time: 110 us
  starting transfers between devices  40.4 us (37%)
  waiting for transfers between devices  34.5 us (31%)
  other arithmetic  13.8 us (13%)
  local copies, waits for them, and re-layouts  9.39 us (9%)
  Pallas kernels  5.17 us (5%)
  matrix products  5.17 us (5%)
  between operations  1.15 us (1%)
    ppermute x14, starting transfers between devices, shift_from(): return lax.ppermute(cells, axis, pairs)  37.8 us
    ppermute x14, waiting for transfers between devices, shift_from(): return lax.ppermute(cells, axis, pairs)  34.5 us
    pallas_call x1, Pallas kernels, soil_fields(): pl.pallas_call(functools.partial(fields_kernel, frame), out_shape=jax.Sha...  5.17 us
    add x7, other arithmetic, chebyshev(): iterate = win(iterate, n, cur, nxt) + update  4.56 us
    ppermute x3, starting transfers between devices, local(): blocks.append(lax.ppermute(cpack, 'gy', pairs))  2.53 us
    add x8, other arithmetic, local(): u = centre + jacobi_weight * ((csrc[sl] - applied) / cdiag[sl])  2.5 us
    dot_general x4, matrix products, coarsen(): lax.dot_general(pick, rows, (((2,), (1,)), ((0,), (0,))), precision=HIGH)  2.25 us
  transfers between devices with their start and end apart: 17, of which 4 were waited for; matrix products, arithmetic and copies ran while one was open for 6% of the time, Pallas kernels for 0%

profile of v11, /device:TPU:4, one launch (start us, length us, event | category | flops | bytes accessed | tf_op | source)
XLA Modules:
  0.0 109.5 jit_solution(1162429314629118172)
XLA Ops:
  0.0 1.0 convert_bitcast_fusion
  1.0 1.0 pad_maximum_fusion.4
  2.0 1.3 %collective-permute-start.1 = (f32[3,16,10,128]{3,2,1,0:T(8,128)S(1)}, f32[3,16,10,128]{3,2,1,0:T(8,128)S(1)}, u32[]{:S(2)}, u32[]{:S(2)}) collective-permute-start(f32[3,16,10,128]{3,2,1,0:T(8,128)S(1)} %get-tuple-element.49), channel_id=1, source_target_pairs={{1,0},{2,1},{3,2},{5,4},{6,5},{7,6},{9,8},{10,9},{11,10},{13,12},{... | collective-permute-start | bytes 737288 | tf_op jit(solution)/shard_map/ppermute | solution.py:32
  3.3 3.1 %collective-permute-start = (f32[3,16,10,128]{3,2,1,0:T(8,128)S(1)}, f32[3,16,10,128]{3,2,1,0:T(8,128)S(1)}, u32[]{:S(2)}, u32[]{:S(2)}) collective-permute-start(f32[3,16,10,128]{3,2,1,0:T(8,128)S(1)} %get-tuple-element.48), channel_id=1, source_target_pairs={{0,1},{1,2},{2,3},{4,5},{5,6},{6,7},{8,9},{9,10},{10,11},{12,13},{... | collective-permute-start | bytes 737288 | tf_op jit(solution)/shard_map/ppermute | solution.py:32
  6.5 1.2 %collective-permute-done = f32[3,16,10,128]{3,2,1,0:T(8,128)S(1)} collective-permute-done((f32[3,16,10,128]{3,2,1,0:T(8,128)S(1)}, f32[3,16,10,128]{3,2,1,0:T(8,128)S(1)}, u32[]{:S(2)}, u32[]{:S(2)}) %collective-permute-start) | collective-permute-done | bytes 245792 | tf_op jit(solution)/shard_map/ppermute | solution.py:32
  7.9 1.9 %collective-permute-start.3 = (f32[3,10,36,128]{3,2,1,0:T(8,128)S(1)}, f32[3,10,36,128]{3,2,1,0:T(8,128)S(1)}, u32[]{:S(2)}, u32[]{:S(2)}) collective-permute-start(f32[3,10,36,128]{3,2,1,0:T(8,128)S(1)} %get-tuple-element.35), channel_id=1, source_target_pairs={{4,0},{8,4},{12,8},{16,12},{20,16},{24,20},{28,24},{5,1},{9,5},{13... | collective-permute-start | bytes 1658888 | tf_op jit(solution)/shard_map/ppermute | solution.py:32
  9.8 4.8 %collective-permute-start.2 = (f32[3,10,36,128]{3,2,1,0:T(8,128)S(1)}, f32[3,10,36,128]{3,2,1,0:T(8,128)S(1)}, u32[]{:S(2)}, u32[]{:S(2)}) collective-permute-start(f32[3,10,36,128]{3,2,1,0:T(8,128)S(1)} %get-tuple-element.34), channel_id=1, source_target_pairs={{0,4},{4,8},{8,12},{12,16},{16,20},{20,24},{24,28},{1,5},{5,9},{9,... | collective-permute-start | bytes 1658888 | tf_op jit(solution)/shard_map/ppermute | solution.py:32
  14.7 9.3 %collective-permute-done.3 = f32[3,10,36,128]{3,2,1,0:T(8,128)S(1)} collective-permute-done((f32[3,10,36,128]{3,2,1,0:T(8,128)S(1)}, f32[3,10,36,128]{3,2,1,0:T(8,128)S(1)}, u32[]{:S(2)}, u32[]{:S(2)}) %collective-permute-start.3) | collective-permute-done | bytes 552992 | tf_op jit(solution)/shard_map/ppermute | solution.py:32
  24.0 16.5 %collective-permute-done.2 = f32[3,10,36,128]{3,2,1,0:T(8,128)S(1)} collective-permute-done((f32[3,10,36,128]{3,2,1,0:T(8,128)S(1)}, f32[3,10,36,128]{3,2,1,0:T(8,128)S(1)}, u32[]{:S(2)}, u32[]{:S(2)}) %collective-permute-start.2) | collective-permute-done | bytes 552992 | tf_op jit(solution)/shard_map/ppermute | solution.py:32
  40.7 1.3 %slice_bitcast_fusion.3 = (f32[36,36,128]{2,1,0:T(8,128)}, f32[36,36,128]{2,1,0:T(8,128)}, f32[36,36,128]{2,1,0:T(8,128)S(1)}) fusion(f32[3,36,36,128]{3,2,1,0:T(8,128)S(1)} %pad_maximum_fusion), kind=kLoop, calls=%fused_computation.19 | loop fusion | bytes 3981312 | tf_op jit(solution)/shard_map/squeeze | solution.py:216
  42.0 5.2 %shard_map.46 = f32[4,36,36,128]{3,2,1,0:T(8,128)} custom-call(f32[5,8]{1,0:T(8,128)} %table_ref.1, f32[36,36,128]{2,1,0:T(8,128)} %get-tuple-element.27.conc_ref, f32[36,36,128]{2,1,0:T(8,128)} %get-tuple-element.26.idf_ref), custom_call_target="tpu_custom_call" | custom-call | flops 16588800 | bytes 3981312 | tf_op jit(solution)/shard_map/pallas_call | solution.py:190
  47.2 1.9 %slice_bitcast_fusion.2 = (f32[36,36,128]{2,1,0:T(8,128)S(1)}, f32[36,36,128]{2,1,0:T(8,128)S(1)}, f32[36,36,128]{2,1,0:T(8,128)S(1)}) fusion(f32[4,36,36,128]{3,2,1,0:T(8,128)} %shard_map.46), kind=kLoop, calls=%fused_computation.18 | loop fusion | bytes 3981312 | tf_op jit(solution)/shard_map/squeeze | solution.py:85
  49.0 0.6 copy-done
  49.8 0.3 maximum_divide_fusion
  50.3 0.7 fusion.4
  51.5 1.2 %slice_add_fusion.5 = (f32[32,32,128]{2,1,0:T(8,128)S(1)}, f32[32,32,128]{2,1,0:T(8,128)S(1)}) fusion(f32[34,34,128]{2,1,0:T(8,128)S(1)} %get-tuple-element.21, f32[34,34,128]{2,1,0:T(8,128)S(1)} %get-tuple-element.22, f32[32,32,127]{2,1,0:T(8,128)S(1)} %get-tuple-element.37, f32[32,32,1]{2,1,0:T(8,128)S(1)} %get-tuple-element.39, ...), kind=kLoop, calls=%fused_computation.57 | loop fusion | flops 3538944 | bytes 9046976 | tf_op jit(solution)/shard_map/add | solution.py:149
  53.3 0.8 fusion.336
  54.1 1.5 %convolution_multiply_fusion = f32[72,18,64]{2,1,0:T(8,128)S(1)} fusion(f32[72,36,64]{2,1,0:T(8,128)S(1)} %fusion.336, f32[18,36]{1,0:T(8,128)S(1)} %fusion.357), kind=kOutput, calls=%fused_computation.2 | convolution fusion | flops 35914752 | bytes 997920 | tf_op jit(solution)/shard_map/dot_general | solution.py:70
  55.9 1.2 %fusion.22 = f32[30,30,128]{2,1,0:T(8,128)S(1)} fusion(f32[34,34,128]{2,1,0:T(8,128)S(1)} %get-tuple-element.22, f32[32,32,128]{2,1,0:T(8,128)S(1)} %get-tuple-element.19, f32[36,35,128]{2,1,0:T(8,128)S(1)} %maximum_divide_fusion.1, f32[35,36,128]{2,1,0:T(8,128)S(1)} %divide_bitcast_fusion, f32[36,36,128]{2,1,0:T(8,128)S(1)} %get-tuple-element.24, ...), kind=kLoop, calls=%fused_computation.61 | loop fusion | flops 3110400 | bytes 8031168 | tf_op jit(solution)/shard_map/add | solution.py:149
  57.5 0.9 fusion.40
  58.8 0.3 divide_multiply_fusion.3
  60.5 0.3 convolution_multiply_fusion.2
  61.1 1.0 collective-permute-start.9
  62.1 1.4 %collective-permute-start.8 = (f32[5,4,4,32]{3,2,1,0:T(4,128)S(1)}, f32[5,4,4,32]{3,2,1,0:T(4,128)S(1)}, u32[]{:S(2)}, u32[]{:S(2)}) collective-permute-start(f32[5,4,4,32]{3,2,1,0:T(4,128)S(1)} %pad_maximum_fusion.20), channel_id=1, source_target_pairs={{0,3},{1,0},{2,1},{3,2},{4,7},{5,4},{6,5},{7,6},{8,11},{9,8},{10,9... | collective-permute-start | bytes 30728 | tf_op jit(solution)/shard_map/ppermute | solution.py:242
  63.5 1.5 %collective-permute-start.5 = (f32[2,8,5,64]{3,2,1,0:T(8,128)S(1)}, f32[2,8,5,64]{3,2,1,0:T(8,128)S(1)}, u32[]{:S(2)}, u32[]{:S(2)}) collective-permute-start(f32[2,8,5,64]{3,2,1,0:T(8,128)S(1)} %get-tuple-element.158), channel_id=1, source_target_pairs={{1,0},{2,1},{3,2},{5,4},{6,5},{7,6},{9,8},{10,9},{11,10},{13,12},{... | collective-permute-start | bytes 61448 | tf_op jit(solution)/shard_map/ppermute | solution.py:32
  65.0 3.0 %collective-permute-start.4 = (f32[2,8,5,64]{3,2,1,0:T(8,128)S(1)}, f32[2,8,5,64]{3,2,1,0:T(8,128)S(1)}, u32[]{:S(2)}, u32[]{:S(2)}) collective-permute-start(f32[2,8,5,64]{3,2,1,0:T(8,128)S(1)} %get-tuple-element.157), channel_id=1, source_target_pairs={{0,1},{1,2},{2,3},{4,5},{5,6},{6,7},{8,9},{9,10},{10,11},{12,13},{... | collective-permute-start | bytes 61448 | tf_op jit(solution)/shard_map/ppermute | solution.py:32
  68.1 3.5 %collective-permute-start.12 = (f32[5,4,16,32]{3,2,1,0:T(8,128)S(1)}, f32[5,4,16,32]{3,2,1,0:T(8,128)S(1)}, u32[]{:S(2)}, u32[]{:S(2)}) collective-permute-start(f32[5,4,16,32]{3,2,1,0:T(8,128)S(1)} %pad_maximum_fusion.6), channel_id=1, source_target_pairs={{0,8},{4,12},{8,16},{12,20},{16,24},{20,28},{1,9},{5,13},{9,17},{1... | collective-permute-start | bytes 122888 | tf_op jit(solution)/shard_map/ppermute | solution.py:32
  71.6 3.6 %collective-permute-start.11 = (f32[5,4,16,32]{3,2,1,0:T(8,128)S(1)}, f32[5,4,16,32]{3,2,1,0:T(8,128)S(1)}, u32[]{:S(2)}, u32[]{:S(2)}) collective-permute-start(f32[5,4,16,32]{3,2,1,0:T(8,128)S(1)} %pad_maximum_fusion.6), channel_id=1, source_target_pairs={{0,12},{4,16},{8,20},{12,24},{16,28},{1,13},{5,17},{9,21},{13,25},... | collective-permute-start | bytes 122888 | tf_op jit(solution)/shard_map/ppermute | solution.py:32
  75.2 2.7 %collective-permute-start.13 = (f32[5,4,16,32]{3,2,1,0:T(8,128)S(1)}, f32[5,4,16,32]{3,2,1,0:T(8,128)S(1)}, u32[]{:S(2)}, u32[]{:S(2)}) collective-permute-start(f32[5,4,16,32]{3,2,1,0:T(8,128)S(1)} %pad_maximum_fusion.6), channel_id=1, source_target_pairs={{0,4},{4,8},{8,12},{12,16},{16,20},{20,24},{24,28},{1,5},{5,9},{9,... | collective-permute-start | bytes 122888 | tf_op jit(solution)/shard_map/ppermute | solution.py:32
  77.9 3.1 %collective-permute-start.14 = (f32[5,4,16,32]{3,2,1,0:T(8,128)S(1)}, f32[5,4,16,32]{3,2,1,0:T(8,128)S(1)}, u32[]{:S(2)}, u32[]{:S(2)}) collective-permute-start(f32[5,4,16,32]{3,2,1,0:T(8,128)S(1)} %pad_maximum_fusion.6), channel_id=1, source_target_pairs={{4,0},{8,4},{12,8},{16,12},{20,16},{24,20},{28,24},{5,1},{9,5},{13... | collective-permute-start | bytes 122888 | tf_op jit(solution)/shard_map/ppermute | solution.py:32
  81.1 1.3 %collective-permute-start.15 = (f32[5,4,16,32]{3,2,1,0:T(8,128)S(1)}, f32[5,4,16,32]{3,2,1,0:T(8,128)S(1)}, u32[]{:S(2)}, u32[]{:S(2)}) collective-permute-start(f32[5,4,16,32]{3,2,1,0:T(8,128)S(1)} %pad_maximum_fusion.6), channel_id=1, source_target_pairs={{8,0},{12,4},{16,8},{20,12},{24,16},{28,20},{9,1},{13,5},{17,9},{2... | collective-permute-start | bytes 122888 | tf_op jit(solution)/shard_map/ppermute | solution.py:32
  82.4 1.3 %collective-permute-start.16 = (f32[5,4,16,32]{3,2,1,0:T(8,128)S(1)}, f32[5,4,16,32]{3,2,1,0:T(8,128)S(1)}, u32[]{:S(2)}, u32[]{:S(2)}) collective-permute-start(f32[5,4,16,32]{3,2,1,0:T(8,128)S(1)} %pad_maximum_fusion.6), channel_id=1, source_target_pairs={{12,0},{16,4},{20,8},{24,12},{28,16},{13,1},{17,5},{21,9},{25,13},... | collective-permute-start | bytes 122888 | tf_op jit(solution)/shard_map/ppermute | solution.py:32
  83.8 1.9 %collective-permute-start.7 = (f32[2,5,18,64]{3,2,1,0:T(8,128)S(1)}, f32[2,5,18,64]{3,2,1,0:T(8,128)S(1)}, u32[]{:S(2)}, u32[]{:S(2)}) collective-permute-start(f32[2,5,18,64]{3,2,1,0:T(8,128)S(1)} %get-tuple-element.75), channel_id=1, source_target_pairs={{4,0},{8,4},{12,8},{16,12},{20,16},{24,20},{28,24},{5,1},{9,5},{13... | collective-permute-start | bytes 138248 | tf_op jit(solution)/shard_map/ppermute | solution.py:32
  85.8 4.8 %collective-permute-start.6 = (f32[2,5,18,64]{3,2,1,0:T(8,128)S(1)}, f32[2,5,18,64]{3,2,1,0:T(8,128)S(1)}, u32[]{:S(2)}, u32[]{:S(2)}) collective-permute-start(f32[2,5,18,64]{3,2,1,0:T(8,128)S(1)} %get-tuple-element.74), channel_id=1, source_target_pairs={{0,4},{4,8},{8,12},{12,16},{16,20},{20,24},{24,28},{1,5},{5,9},{9,... | collective-permute-start | bytes 138248 | tf_op jit(solution)/shard_map/ppermute | solution.py:32
  90.8 7.5 %collective-permute-done.16 = f32[5,4,16,32]{3,2,1,0:T(8,128)S(1)} collective-permute-done((f32[5,4,16,32]{3,2,1,0:T(8,128)S(1)}, f32[5,4,16,32]{3,2,1,0:T(8,128)S(1)}, u32[]{:S(2)}, u32[]{:S(2)}) %collective-permute-start.16) | collective-permute-done | bytes 40992 | tf_op jit(solution)/shard_map/ppermute | solution.py:32
  99.5 0.5 fusion.87
  100.3 0.4 multiply_add_fusion
  100.9 0.3 multiply_add_fusion.1
  101.5 0.3 multiply_add_fusion.2
  102.1 0.3 multiply_add_fusion.3
  104.1 0.4 fusion.318
  104.9 0.3 slice_add_fusion.10
  105.4 0.3 slice_add_fusion.11
  105.9 0.4 fusion.258
  106.3 0.5 fusion.315
  107.1 0.4 slice_add_fusion.7
  107.8 0.5 slice_add_fusion.9
  108.5 1.0 fusion.181
  (147 shorter events, 10.1 us)
Async XLA Ops:
  0.0 7.7 %copy-start.1 = (f32[16,16,128]{2,1,0:T(8,128)S(1)}, f32[16,16,128]{2,1,0:T(8,128)}, u32[]{:S(2)}) copy-start(f32[16,16,128]{2,1,0:T(8,128)} %param.5) | copy-start | bytes 393220
  0.0 7.7 %copy-start.2 = (f32[16,16,128]{2,1,0:T(8,128)S(1)}, f32[16,16,128]{2,1,0:T(8,128)}, u32[]{:S(2)}) copy-start(f32[16,16,128]{2,1,0:T(8,128)} %param.4) | copy-start | bytes 393220
  2.0 4.5 %collective-permute-start.1 = (f32[3,16,10,128]{3,2,1,0:T(8,128)S(1)}, f32[3,16,10,128]{3,2,1,0:T(8,128)S(1)}, u32[]{:S(2)}, u32[]{:S(2)}) collective-permute-start(f32[3,16,10,128]{3,2,1,0:T(8,128)S(1)} %get-tuple-element.49), channel_id=1, source_target_pairs={{1,0},{2,1},{3,2},{5,4},{6,5},{7,6},{9,8},{10,9},{11,10},{13,12},{... | collective-permute-start | bytes 737288 | tf_op jit(solution)/shard_map/ppermute | solution.py:32
  3.3 4.4 %collective-permute-start = (f32[3,16,10,128]{3,2,1,0:T(8,128)S(1)}, f32[3,16,10,128]{3,2,1,0:T(8,128)S(1)}, u32[]{:S(2)}, u32[]{:S(2)}) collective-permute-start(f32[3,16,10,128]{3,2,1,0:T(8,128)S(1)} %get-tuple-element.48), channel_id=1, source_target_pairs={{0,1},{1,2},{2,3},{4,5},{5,6},{6,7},{8,9},{9,10},{10,11},{12,13},{... | collective-permute-start | bytes 737288 | tf_op jit(solution)/shard_map/ppermute | solution.py:32
  7.9 16.1 %collective-permute-start.3 = (f32[3,10,36,128]{3,2,1,0:T(8,128)S(1)}, f32[3,10,36,128]{3,2,1,0:T(8,128)S(1)}, u32[]{:S(2)}, u32[]{:S(2)}) collective-permute-start(f32[3,10,36,128]{3,2,1,0:T(8,128)S(1)} %get-tuple-element.35), channel_id=1, source_target_pairs={{4,0},{8,4},{12,8},{16,12},{20,16},{24,20},{28,24},{5,1},{9,5},{13... | collective-permute-start | bytes 1658888 | tf_op jit(solution)/shard_map/ppermute | solution.py:32
  9.8 30.7 %collective-permute-start.2 = (f32[3,10,36,128]{3,2,1,0:T(8,128)S(1)}, f32[3,10,36,128]{3,2,1,0:T(8,128)S(1)}, u32[]{:S(2)}, u32[]{:S(2)}) collective-permute-start(f32[3,10,36,128]{3,2,1,0:T(8,128)S(1)} %get-tuple-element.34), channel_id=1, source_target_pairs={{0,4},{4,8},{8,12},{12,16},{16,20},{20,24},{24,28},{1,5},{5,9},{9,... | collective-permute-start | bytes 1658888 | tf_op jit(solution)/shard_map/ppermute | solution.py:32
  47.2 2.5 %copy-start = (f32[4,36,36,128]{3,2,1,0:T(8,128)S(1)}, f32[4,36,36,128]{3,2,1,0:T(8,128)}, u32[]{:S(2)}) copy-start(f32[4,36,36,128]{3,2,1,0:T(8,128)} %shard_map.46) | copy-start | bytes 7962628
  60.9 7.1 %collective-permute-start.10 = (f32[5,4,4,32]{3,2,1,0:T(4,128)S(1)}, f32[5,4,4,32]{3,2,1,0:T(4,128)S(1)}, u32[]{:S(2)}, u32[]{:S(2)}) collective-permute-start(f32[5,4,4,32]{3,2,1,0:T(4,128)S(1)} %pad_maximum_fusion.20), channel_id=1, source_target_pairs={{0,1},{1,2},{2,3},{3,0},{4,5},{5,6},{6,7},{7,4},{8,9},{9,10},{10,1... | collective-permute-start | bytes 30728 | tf_op jit(solution)/shard_map/ppermute | solution.py:242
  61.1 6.9 %collective-permute-start.9 = (f32[5,4,4,32]{3,2,1,0:T(4,128)S(1)}, f32[5,4,4,32]{3,2,1,0:T(4,128)S(1)}, u32[]{:S(2)}, u32[]{:S(2)}) collective-permute-start(f32[5,4,4,32]{3,2,1,0:T(4,128)S(1)} %pad_maximum_fusion.20), channel_id=1, source_target_pairs={{0,2},{1,3},{2,0},{3,1},{4,6},{5,7},{6,4},{7,5},{8,10},{9,11},{10,... | collective-permute-start | bytes 30728 | tf_op jit(solution)/shard_map/ppermute | solution.py:242
  62.1 6.0 %collective-permute-start.8 = (f32[5,4,4,32]{3,2,1,0:T(4,128)S(1)}, f32[5,4,4,32]{3,2,1,0:T(4,128)S(1)}, u32[]{:S(2)}, u32[]{:S(2)}) collective-permute-start(f32[5,4,4,32]{3,2,1,0:T(4,128)S(1)} %pad_maximum_fusion.20), channel_id=1, source_target_pairs={{0,3},{1,0},{2,1},{3,2},{4,7},{5,4},{6,5},{7,6},{8,11},{9,8},{10,9... | collective-permute-start | bytes 30728 | tf_op jit(solution)/shard_map/ppermute | solution.py:242
  63.5 14.4 %collective-permute-start.5 = (f32[2,8,5,64]{3,2,1,0:T(8,128)S(1)}, f32[2,8,5,64]{3,2,1,0:T(8,128)S(1)}, u32[]{:S(2)}, u32[]{:S(2)}) collective-permute-start(f32[2,8,5,64]{3,2,1,0:T(8,128)S(1)} %get-tuple-element.158), channel_id=1, source_target_pairs={{1,0},{2,1},{3,2},{5,4},{6,5},{7,6},{9,8},{10,9},{11,10},{13,12},{... | collective-permute-start | bytes 61448 | tf_op jit(solution)/shard_map/ppermute | solution.py:32
  65.0 16.1 %collective-permute-start.4 = (f32[2,8,5,64]{3,2,1,0:T(8,128)S(1)}, f32[2,8,5,64]{3,2,1,0:T(8,128)S(1)}, u32[]{:S(2)}, u32[]{:S(2)}) collective-permute-start(f32[2,8,5,64]{3,2,1,0:T(8,128)S(1)} %get-tuple-element.157), channel_id=1, source_target_pairs={{0,1},{1,2},{2,3},{4,5},{5,6},{6,7},{8,9},{9,10},{10,11},{12,13},{... | collective-permute-start | bytes 61448 | tf_op jit(solution)/shard_map/ppermute | solution.py:32
  68.1 15.7 %collective-permute-start.12 = (f32[5,4,16,32]{3,2,1,0:T(8,128)S(1)}, f32[5,4,16,32]{3,2,1,0:T(8,128)S(1)}, u32[]{:S(2)}, u32[]{:S(2)}) collective-permute-start(f32[5,4,16,32]{3,2,1,0:T(8,128)S(1)} %pad_maximum_fusion.6), channel_id=1, source_target_pairs={{0,8},{4,12},{8,16},{12,20},{16,24},{20,28},{1,9},{5,13},{9,17},{1... | collective-permute-start | bytes 122888 | tf_op jit(solution)/shard_map/ppermute | solution.py:32
  71.6 10.8 %collective-permute-start.11 = (f32[5,4,16,32]{3,2,1,0:T(8,128)S(1)}, f32[5,4,16,32]{3,2,1,0:T(8,128)S(1)}, u32[]{:S(2)}, u32[]{:S(2)}) collective-permute-start(f32[5,4,16,32]{3,2,1,0:T(8,128)S(1)} %pad_maximum_fusion.6), channel_id=1, source_target_pairs={{0,12},{4,16},{8,20},{12,24},{16,28},{1,13},{5,17},{9,21},{13,25},... | collective-permute-start | bytes 122888 | tf_op jit(solution)/shard_map/ppermute | solution.py:32
  75.2 10.6 %collective-permute-start.13 = (f32[5,4,16,32]{3,2,1,0:T(8,128)S(1)}, f32[5,4,16,32]{3,2,1,0:T(8,128)S(1)}, u32[]{:S(2)}, u32[]{:S(2)}) collective-permute-start(f32[5,4,16,32]{3,2,1,0:T(8,128)S(1)} %pad_maximum_fusion.6), channel_id=1, source_target_pairs={{0,4},{4,8},{8,12},{12,16},{16,20},{20,24},{24,28},{1,5},{5,9},{9,... | collective-permute-start | bytes 122888 | tf_op jit(solution)/shard_map/ppermute | solution.py:32
  77.9 12.7 %collective-permute-start.14 = (f32[5,4,16,32]{3,2,1,0:T(8,128)S(1)}, f32[5,4,16,32]{3,2,1,0:T(8,128)S(1)}, u32[]{:S(2)}, u32[]{:S(2)}) collective-permute-start(f32[5,4,16,32]{3,2,1,0:T(8,128)S(1)} %pad_maximum_fusion.6), channel_id=1, source_target_pairs={{4,0},{8,4},{12,8},{16,12},{20,16},{24,20},{28,24},{5,1},{9,5},{13... | collective-permute-start | bytes 122888 | tf_op jit(solution)/shard_map/ppermute | solution.py:32
  81.1 9.7 %collective-permute-start.15 = (f32[5,4,16,32]{3,2,1,0:T(8,128)S(1)}, f32[5,4,16,32]{3,2,1,0:T(8,128)S(1)}, u32[]{:S(2)}, u32[]{:S(2)}) collective-permute-start(f32[5,4,16,32]{3,2,1,0:T(8,128)S(1)} %pad_maximum_fusion.6), channel_id=1, source_target_pairs={{8,0},{12,4},{16,8},{20,12},{24,16},{28,20},{9,1},{13,5},{17,9},{2... | collective-permute-start | bytes 122888 | tf_op jit(solution)/shard_map/ppermute | solution.py:32
  82.4 15.8 %collective-permute-start.16 = (f32[5,4,16,32]{3,2,1,0:T(8,128)S(1)}, f32[5,4,16,32]{3,2,1,0:T(8,128)S(1)}, u32[]{:S(2)}, u32[]{:S(2)}) collective-permute-start(f32[5,4,16,32]{3,2,1,0:T(8,128)S(1)} %pad_maximum_fusion.6), channel_id=1, source_target_pairs={{12,0},{16,4},{20,8},{24,12},{28,16},{13,1},{17,5},{21,9},{25,13},... | collective-permute-start | bytes 122888 | tf_op jit(solution)/shard_map/ppermute | solution.py:32
  83.8 20.8 %collective-permute-start.7 = (f32[2,5,18,64]{3,2,1,0:T(8,128)S(1)}, f32[2,5,18,64]{3,2,1,0:T(8,128)S(1)}, u32[]{:S(2)}, u32[]{:S(2)}) collective-permute-start(f32[2,5,18,64]{3,2,1,0:T(8,128)S(1)} %get-tuple-element.75), channel_id=1, source_target_pairs={{4,0},{8,4},{12,8},{16,12},{20,16},{24,20},{28,24},{5,1},{9,5},{13... | collective-permute-start | bytes 138248 | tf_op jit(solution)/shard_map/ppermute | solution.py:32
  85.8 18.8 %collective-permute-start.6 = (f32[2,5,18,64]{3,2,1,0:T(8,128)S(1)}, f32[2,5,18,64]{3,2,1,0:T(8,128)S(1)}, u32[]{:S(2)}, u32[]{:S(2)}) collective-permute-start(f32[2,5,18,64]{3,2,1,0:T(8,128)S(1)} %get-tuple-element.74), channel_id=1, source_target_pairs={{0,4},{4,8},{8,12},{12,16},{16,20},{20,24},{24,28},{1,5},{5,9},{9,... | collective-permute-start | bytes 138248 | tf_op jit(solution)/shard_map/ppermute | solution.py:32

commit v12 on v11

--- a/solution.py
+++ b/solution.py
@@ -41,6 +41,20 @@
             [shift_from(tail, axis, -1), cells, shift_from(head, axis, 1)], axis=dim
         )
     return cells
+
+
+def halo_overlapped(cells, width):
+    sx, sy = cells.shape[1], cells.shape[2]
+    west = shift_from(cells[:, sx - width :], "gx", -1)
+    east = shift_from(cells[:, :width], "gx", 1)
+    south = shift_from(cells[:, :, sy - width :], "gy", -1)
+    north = shift_from(cells[:, :, :width], "gy", 1)
+    low = shift_from(jnp.concatenate([west[:, :, sy - width :], east[:, :, sy - width :]], axis=1), "gy", -1)
+    high = shift_from(jnp.concatenate([west[:, :, :width], east[:, :, :width]], axis=1), "gy", 1)
+    top = jnp.concatenate([low[:, :width], west, high[:, :width]], axis=2)
+    mid = jnp.concatenate([south, cells, north], axis=2)
+    bottom = jnp.concatenate([low[:, width:], east, high[:, width:]], axis=2)
+    return jnp.concatenate([top, mid, bottom], axis=1)
 
 
 def harmonic(first, second):
@@ -212,7 +226,7 @@
     iy = lax.axis_index("gy")
 
     stacked = jnp.stack([conc_prev, right_side, soil_id.astype(jnp.float32)])
-    ext = halo(stacked, (("gy", 2), ("gx", 1)), hf)
+    ext = halo_overlapped(stacked, hf)
     conc, rhs, idf = ext[0], ext[1], ext[2]
     fine_c = soil_fields((n, ny, hf), soil_table, conc, idf)
     fine = build_level(fine_c, n, hf, 1.0)

time: 110 us -> 101 us (0.918)
  waiting for transfers between devices: 34.5 us -> 11.7 us
  starting transfers between devices: 40.4 us -> 52.4 us
    ppermute x14 -> x16, waiting for transfers between devices: 34.5 us -> 11.7 us  [shift_from(): return lax.ppermute(cells, axis, pairs)]
    ppermute x3, starting transfers between devices: 2.53 us -> 9.6 us  [local(): blocks.append(lax.ppermute(cpack, 'gy', pairs))]
    ppermute x14 -> x16, starting transfers between devices: 37.8 us -> 42.8 us  [shift_from(): return lax.ppermute(cells, axis, pairs)]
  transfers between devices with their start and end apart: 17 -> 19, of which waited for: 4 -> 3; matrix products, arithmetic and copies ran while one was open for 6% -> 7% of each run, Pallas kernels for 0% -> 0%
where the time goes in v12:
time: 101 us
  starting transfers between devices  52.4 us (52%)
  other arithmetic  14.8 us (15%)
  waiting for transfers between devices  11.7 us (12%)
  local copies, waits for them, and re-layouts  10.3 us (10%)
  Pallas kernels  5.18 us (5%)
  matrix products  5.17 us (5%)
  between operations  1.21 us (1%)
    ppermute x16, starting transfers between devices, shift_from(): return lax.ppermute(cells, axis, pairs)  42.8 us
    ppermute x16, waiting for transfers between devices, shift_from(): return lax.ppermute(cells, axis, pairs)  11.7 us
    ppermute x3, starting transfers between devices, local(): blocks.append(lax.ppermute(cpack, 'gy', pairs))  9.6 us
    pallas_call x1, Pallas kernels, soil_fields(): pl.pallas_call(functools.partial(fields_kernel, frame), out_shape=jax.Sha...  5.18 us
    add x7, other arithmetic, chebyshev(): iterate = win(iterate, n, cur, nxt) + update  4.56 us
    add x8, other arithmetic, local(): u = centre + jacobi_weight * ((csrc[sl] - applied) / cdiag[sl])  2.49 us
    dot_general x4, matrix products, coarsen(): lax.dot_general(pick, rows, (((2,), (1,)), ((0,), (0,))), precision=HIGH)  2.25 us
  transfers between devices with their start and end apart: 19, of which 3 were waited for; matrix products, arithmetic and copies ran while one was open for 7% of the time, Pallas kernels for 0%

profile of v12, /device:TPU:4, one launch (start us, length us, event | category | flops | bytes accessed | tf_op | source)
XLA Modules:
  0.0 100.7 jit_solution(8257437887783749725)
XLA Ops:
  0.0 0.9 convert_bitcast_fusion
  0.9 1.0 pad_maximum_fusion.4
  2.0 1.9 %collective-permute-start.1 = (f32[3,10,16,128]{3,2,1,0:T(8,128)S(1)}, f32[3,10,16,128]{3,2,1,0:T(8,128)S(1)}, u32[]{:S(2)}, u32[]{:S(2)}) collective-permute-start(f32[3,10,16,128]{3,2,1,0:T(8,128)S(1)} %get-tuple-element.53), channel_id=1, source_target_pairs={{4,0},{8,4},{12,8},{16,12},{20,16},{24,20},{28,24},{5,1},{9,5},{13... | collective-permute-start | bytes 737288 | tf_op jit(solution)/shard_map/ppermute | solution.py:32
  3.9 4.8 %collective-permute-start = (f32[3,10,16,128]{3,2,1,0:T(8,128)S(1)}, f32[3,10,16,128]{3,2,1,0:T(8,128)S(1)}, u32[]{:S(2)}, u32[]{:S(2)}) collective-permute-start(f32[3,10,16,128]{3,2,1,0:T(8,128)S(1)} %get-tuple-element.52), channel_id=1, source_target_pairs={{0,4},{4,8},{8,12},{12,16},{16,20},{20,24},{24,28},{1,5},{5,9},{9,... | collective-permute-start | bytes 737288 | tf_op jit(solution)/shard_map/ppermute | solution.py:32
  8.7 0.9 fusion.388
  9.6 1.3 %collective-permute-start.5 = (f32[3,16,10,128]{3,2,1,0:T(8,128)}, f32[3,16,10,128]{3,2,1,0:T(8,128)S(1)}, u32[]{:S(2)}, u32[]{:S(2)}) collective-permute-start(f32[3,16,10,128]{3,2,1,0:T(8,128)} %get-tuple-element.51), channel_id=1, source_target_pairs={{1,0},{2,1},{3,2},{5,4},{6,5},{7,6},{9,8},{10,9},{11,10},{13,12},{... | collective-permute-start | bytes 737288 | tf_op jit(solution)/shard_map/ppermute | solution.py:32
  10.9 3.8 %collective-permute-start.4 = (f32[3,16,10,128]{3,2,1,0:T(8,128)}, f32[3,16,10,128]{3,2,1,0:T(8,128)}, u32[]{:S(2)}, u32[]{:S(2)}) collective-permute-start(f32[3,16,10,128]{3,2,1,0:T(8,128)} %get-tuple-element.50), channel_id=1, source_target_pairs={{0,1},{1,2},{2,3},{4,5},{5,6},{6,7},{8,9},{9,10},{10,11},{12,13},{... | collective-permute-start | bytes 737288 | tf_op jit(solution)/shard_map/ppermute | solution.py:32
  14.9 2.8 %collective-permute-done = f32[3,10,16,128]{3,2,1,0:T(8,128)S(1)} collective-permute-done((f32[3,10,16,128]{3,2,1,0:T(8,128)S(1)}, f32[3,10,16,128]{3,2,1,0:T(8,128)S(1)}, u32[]{:S(2)}, u32[]{:S(2)}) %collective-permute-start) | collective-permute-done | bytes 245792 | tf_op jit(solution)/shard_map/ppermute | solution.py:32
  17.8 1.3 %collective-permute-start.3 = (f32[3,20,10,128]{3,2,1,0:T(8,128)S(1)}, f32[3,20,10,128]{3,2,1,0:T(8,128)S(1)}, u32[]{:S(2)}, u32[]{:S(2)}) collective-permute-start(f32[3,20,10,128]{3,2,1,0:T(8,128)S(1)} %pad_maximum_fusion.2), channel_id=1, source_target_pairs={{1,0},{2,1},{3,2},{5,4},{6,5},{7,6},{9,8},{10,9},{11,10},{13,12},{... | collective-permute-start | bytes 921608 | tf_op jit(solution)/shard_map/ppermute | solution.py:32
  19.2 3.2 %collective-permute-start.2 = (f32[3,20,10,128]{3,2,1,0:T(8,128)S(1)}, f32[3,20,10,128]{3,2,1,0:T(8,128)S(1)}, u32[]{:S(2)}, u32[]{:S(2)}) collective-permute-start(f32[3,20,10,128]{3,2,1,0:T(8,128)S(1)} %pad_maximum_fusion.1), channel_id=1, source_target_pairs={{0,1},{1,2},{2,3},{4,5},{5,6},{6,7},{8,9},{9,10},{10,11},{12,13},{... | collective-permute-start | bytes 921608 | tf_op jit(solution)/shard_map/ppermute | solution.py:32
  22.5 1.4 %collective-permute-done.2 = f32[3,20,10,128]{3,2,1,0:T(8,128)S(1)} collective-permute-done((f32[3,20,10,128]{3,2,1,0:T(8,128)S(1)}, f32[3,20,10,128]{3,2,1,0:T(8,128)S(1)}, u32[]{:S(2)}, u32[]{:S(2)}) %collective-permute-start.2) | collective-permute-done | bytes 307232 | tf_op jit(solution)/shard_map/ppermute | solution.py:32
  23.9 1.3 %maximum_maximum_fusion = f32[3,36,36,128]{3,2,1,0:T(8,128)S(1)} fusion(f32[3,10,10,128]{3,2,1,0:T(8,128)S(1)} %get-tuple-element.49, f32[3,10,16,128]{3,2,1,0:T(8,128)S(1)} %collective-permute-done.1, f32[3,10,10,128]{3,2,1,0:T(8,128)S(1)} %get-tuple-element.47, f32[3,16,10,128]{3,2,1,0:T(8,128)S(1)} %collective-permute-done.5, ...), kind=kLoop, calls=%fused_computation | loop fusion | flops 4976640 | bytes 3981312 | tf_op jit(solution)/shard_map/concatenate | solution.py:57
  25.2 1.3 %slice_bitcast_fusion.3 = (f32[36,36,128]{2,1,0:T(8,128)}, f32[36,36,128]{2,1,0:T(8,128)}, f32[36,36,128]{2,1,0:T(8,128)S(1)}) fusion(f32[3,36,36,128]{3,2,1,0:T(8,128)S(1)} %maximum_maximum_fusion), kind=kLoop, calls=%fused_computation.18 | loop fusion | bytes 3981312 | tf_op jit(solution)/shard_map/squeeze | solution.py:230
  26.5 5.2 %shard_map.46 = f32[4,36,36,128]{3,2,1,0:T(8,128)} custom-call(f32[5,8]{1,0:T(8,128)} %table_ref.1, f32[36,36,128]{2,1,0:T(8,128)} %get-tuple-element.27.conc_ref, f32[36,36,128]{2,1,0:T(8,128)} %get-tuple-element.26.idf_ref), custom_call_target="tpu_custom_call" | custom-call | flops 16588800 | bytes 3981312 | tf_op jit(solution)/shard_map/pallas_call | solution.py:204
  31.7 1.9 %slice_bitcast_fusion.2 = (f32[36,36,128]{2,1,0:T(8,128)S(1)}, f32[36,36,128]{2,1,0:T(8,128)S(1)}, f32[36,36,128]{2,1,0:T(8,128)S(1)}) fusion(f32[4,36,36,128]{3,2,1,0:T(8,128)} %shard_map.46), kind=kLoop, calls=%fused_computation.17 | loop fusion | bytes 3981312 | tf_op jit(solution)/shard_map/squeeze | solution.py:99
  33.5 0.6 copy-done
  34.8 0.7 fusion.4
  36.0 1.2 %slice_add_fusion.5 = (f32[32,32,128]{2,1,0:T(8,128)S(1)}, f32[32,32,128]{2,1,0:T(8,128)S(1)}) fusion(f32[34,34,128]{2,1,0:T(8,128)S(1)} %get-tuple-element.21, f32[34,34,128]{2,1,0:T(8,128)S(1)} %get-tuple-element.22, f32[32,32,127]{2,1,0:T(8,128)S(1)} %get-tuple-element.35, f32[32,32,1]{2,1,0:T(8,128)S(1)} %get-tuple-element.37, ...), kind=kLoop, calls=%fused_computation.56 | loop fusion | flops 3538944 | bytes 9046976 | tf_op jit(solution)/shard_map/add | solution.py:163
  37.7 0.8 fusion.336
  38.5 1.5 %convolution_multiply_fusion = f32[72,18,64]{2,1,0:T(8,128)S(1)} fusion(f32[72,36,64]{2,1,0:T(8,128)S(1)} %fusion.336, f32[18,36]{1,0:T(8,128)S(1)} %fusion.357), kind=kOutput, calls=%fused_computation.2 | convolution fusion | flops 35914752 | bytes 997920 | tf_op jit(solution)/shard_map/dot_general | solution.py:84
  40.4 1.2 %fusion.22 = f32[30,30,128]{2,1,0:T(8,128)S(1)} fusion(f32[34,34,128]{2,1,0:T(8,128)S(1)} %get-tuple-element.22, f32[32,32,128]{2,1,0:T(8,128)S(1)} %get-tuple-element.19, f32[36,35,128]{2,1,0:T(8,128)S(1)} %maximum_divide_fusion.1, f32[35,36,128]{2,1,0:T(8,128)S(1)} %divide_bitcast_fusion, f32[36,36,128]{2,1,0:T(8,128)S(1)} %get-tuple-element.24, ...), kind=kLoop, calls=%fused_computation.60 | loop fusion | flops 3110400 | bytes 8031168 | tf_op jit(solution)/shard_map/add | solution.py:163
  42.0 0.9 fusion.40
  43.2 0.3 divide_multiply_fusion.3
  45.4 5.8 %collective-permute-start.12 = (f32[5,4,4,32]{3,2,1,0:T(4,128)S(1)}, f32[5,4,4,32]{3,2,1,0:T(4,128)S(1)}, u32[]{:S(2)}, u32[]{:S(2)}) collective-permute-start(f32[5,4,4,32]{3,2,1,0:T(4,128)S(1)} %pad_maximum_fusion.20), channel_id=1, source_target_pairs={{0,1},{1,2},{2,3},{3,0},{4,5},{5,6},{6,7},{7,4},{8,9},{9,10},{10,1... | collective-permute-start | bytes 30728 | tf_op jit(solution)/shard_map/ppermute | solution.py:256
  51.2 2.4 %collective-permute-start.11 = (f32[5,4,4,32]{3,2,1,0:T(4,128)S(1)}, f32[5,4,4,32]{3,2,1,0:T(4,128)S(1)}, u32[]{:S(2)}, u32[]{:S(2)}) collective-permute-start(f32[5,4,4,32]{3,2,1,0:T(4,128)S(1)} %pad_maximum_fusion.20), channel_id=1, source_target_pairs={{0,2},{1,3},{2,0},{3,1},{4,6},{5,7},{6,4},{7,5},{8,10},{9,11},{10,... | collective-permute-start | bytes 30728 | tf_op jit(solution)/shard_map/ppermute | solution.py:256
  53.6 1.4 %collective-permute-start.10 = (f32[5,4,4,32]{3,2,1,0:T(4,128)S(1)}, f32[5,4,4,32]{3,2,1,0:T(4,128)S(1)}, u32[]{:S(2)}, u32[]{:S(2)}) collective-permute-start(f32[5,4,4,32]{3,2,1,0:T(4,128)S(1)} %pad_maximum_fusion.20), channel_id=1, source_target_pairs={{0,3},{1,0},{2,1},{3,2},{4,7},{5,4},{6,5},{7,6},{8,11},{9,8},{10,9... | collective-permute-start | bytes 30728 | tf_op jit(solution)/shard_map/ppermute | solution.py:256
  55.0 1.3 %collective-permute-start.7 = (f32[2,8,5,64]{3,2,1,0:T(8,128)S(1)}, f32[2,8,5,64]{3,2,1,0:T(8,128)S(1)}, u32[]{:S(2)}, u32[]{:S(2)}) collective-permute-start(f32[2,8,5,64]{3,2,1,0:T(8,128)S(1)} %get-tuple-element.166), channel_id=1, source_target_pairs={{1,0},{2,1},{3,2},{5,4},{6,5},{7,6},{9,8},{10,9},{11,10},{13,12},{... | collective-permute-start | bytes 61448 | tf_op jit(solution)/shard_map/ppermute | solution.py:32
  56.3 3.0 %collective-permute-start.6 = (f32[2,8,5,64]{3,2,1,0:T(8,128)S(1)}, f32[2,8,5,64]{3,2,1,0:T(8,128)S(1)}, u32[]{:S(2)}, u32[]{:S(2)}) collective-permute-start(f32[2,8,5,64]{3,2,1,0:T(8,128)S(1)} %get-tuple-element.165), channel_id=1, source_target_pairs={{0,1},{1,2},{2,3},{4,5},{5,6},{6,7},{8,9},{9,10},{10,11},{12,13},{... | collective-permute-start | bytes 61448 | tf_op jit(solution)/shard_map/ppermute | solution.py:32
  59.5 3.5 %collective-permute-start.14 = (f32[5,4,16,32]{3,2,1,0:T(8,128)S(1)}, f32[5,4,16,32]{3,2,1,0:T(8,128)S(1)}, u32[]{:S(2)}, u32[]{:S(2)}) collective-permute-start(f32[5,4,16,32]{3,2,1,0:T(8,128)S(1)} %pad_maximum_fusion.6), channel_id=1, source_target_pairs={{0,8},{4,12},{8,16},{12,20},{16,24},{20,28},{1,9},{5,13},{9,17},{1... | collective-permute-start | bytes 122888 | tf_op jit(solution)/shard_map/ppermute | solution.py:32
  63.0 3.5 %collective-permute-start.13 = (f32[5,4,16,32]{3,2,1,0:T(8,128)S(1)}, f32[5,4,16,32]{3,2,1,0:T(8,128)S(1)}, u32[]{:S(2)}, u32[]{:S(2)}) collective-permute-start(f32[5,4,16,32]{3,2,1,0:T(8,128)S(1)} %pad_maximum_fusion.6), channel_id=1, source_target_pairs={{0,12},{4,16},{8,20},{12,24},{16,28},{1,13},{5,17},{9,21},{13,25},... | collective-permute-start | bytes 122888 | tf_op jit(solution)/shard_map/ppermute | solution.py:32
  66.4 2.8 %collective-permute-start.15 = (f32[5,4,16,32]{3,2,1,0:T(8,128)S(1)}, f32[5,4,16,32]{3,2,1,0:T(8,128)S(1)}, u32[]{:S(2)}, u32[]{:S(2)}) collective-permute-start(f32[5,4,16,32]{3,2,1,0:T(8,128)S(1)} %pad_maximum_fusion.6), channel_id=1, source_target_pairs={{0,4},{4,8},{8,12},{12,16},{16,20},{20,24},{24,28},{1,5},{5,9},{9,... | collective-permute-start | bytes 122888 | tf_op jit(solution)/shard_map/ppermute | solution.py:32
  69.3 3.0 %collective-permute-start.16 = (f32[5,4,16,32]{3,2,1,0:T(8,128)S(1)}, f32[5,4,16,32]{3,2,1,0:T(8,128)S(1)}, u32[]{:S(2)}, u32[]{:S(2)}) collective-permute-start(f32[5,4,16,32]{3,2,1,0:T(8,128)S(1)} %pad_maximum_fusion.6), channel_id=1, source_target_pairs={{4,0},{8,4},{12,8},{16,12},{20,16},{24,20},{28,24},{5,1},{9,5},{13... | collective-permute-start | bytes 122888 | tf_op jit(solution)/shard_map/ppermute | solution.py:32
  72.3 1.3 %collective-permute-start.17 = (f32[5,4,16,32]{3,2,1,0:T(8,128)S(1)}, f32[5,4,16,32]{3,2,1,0:T(8,128)S(1)}, u32[]{:S(2)}, u32[]{:S(2)}) collective-permute-start(f32[5,4,16,32]{3,2,1,0:T(8,128)S(1)} %pad_maximum_fusion.6), channel_id=1, source_target_pairs={{8,0},{12,4},{16,8},{20,12},{24,16},{28,20},{9,1},{13,5},{17,9},{2... | collective-permute-start | bytes 122888 | tf_op jit(solution)/shard_map/ppermute | solution.py:32
  73.7 1.3 %collective-permute-start.18 = (f32[5,4,16,32]{3,2,1,0:T(8,128)S(1)}, f32[5,4,16,32]{3,2,1,0:T(8,128)S(1)}, u32[]{:S(2)}, u32[]{:S(2)}) collective-permute-start(f32[5,4,16,32]{3,2,1,0:T(8,128)S(1)} %pad_maximum_fusion.6), channel_id=1, source_target_pairs={{12,0},{16,4},{20,8},{24,12},{28,16},{13,1},{17,5},{21,9},{25,13},... | collective-permute-start | bytes 122888 | tf_op jit(solution)/shard_map/ppermute | solution.py:32
  75.0 1.9 %collective-permute-start.9 = (f32[2,5,18,64]{3,2,1,0:T(8,128)S(1)}, f32[2,5,18,64]{3,2,1,0:T(8,128)S(1)}, u32[]{:S(2)}, u32[]{:S(2)}) collective-permute-start(f32[2,5,18,64]{3,2,1,0:T(8,128)S(1)} %get-tuple-element.83), channel_id=1, source_target_pairs={{4,0},{8,4},{12,8},{16,12},{20,16},{24,20},{28,24},{5,1},{9,5},{13... | collective-permute-start | bytes 138248 | tf_op jit(solution)/shard_map/ppermute | solution.py:32
  77.0 4.8 %collective-permute-start.8 = (f32[2,5,18,64]{3,2,1,0:T(8,128)S(1)}, f32[2,5,18,64]{3,2,1,0:T(8,128)S(1)}, u32[]{:S(2)}, u32[]{:S(2)}) collective-permute-start(f32[2,5,18,64]{3,2,1,0:T(8,128)S(1)} %get-tuple-element.82), channel_id=1, source_target_pairs={{0,4},{4,8},{8,12},{12,16},{16,20},{20,24},{24,28},{1,5},{5,9},{9,... | collective-permute-start | bytes 138248 | tf_op jit(solution)/shard_map/ppermute | solution.py:32
  82.0 7.4 %collective-permute-done.18 = f32[5,4,16,32]{3,2,1,0:T(8,128)S(1)} collective-permute-done((f32[5,4,16,32]{3,2,1,0:T(8,128)S(1)}, f32[5,4,16,32]{3,2,1,0:T(8,128)S(1)}, u32[]{:S(2)}, u32[]{:S(2)}) %collective-permute-start.18) | collective-permute-done | bytes 40992 | tf_op jit(solution)/shard_map/ppermute | solution.py:32
  90.7 0.5 fusion.87
  91.5 0.4 multiply_add_fusion
  92.1 0.3 multiply_add_fusion.1
  92.7 0.3 multiply_add_fusion.2
  95.3 0.4 fusion.318
  96.1 0.3 slice_add_fusion.10
  97.1 0.4 fusion.258
  97.5 0.5 fusion.315
  98.3 0.4 slice_add_fusion.7
  99.0 0.5 slice_add_fusion.9
  99.7 1.0 fusion.181
  (156 shorter events, 10.9 us)
Async XLA Ops:
  2.0 12.9 %collective-permute-start.1 = (f32[3,10,16,128]{3,2,1,0:T(8,128)S(1)}, f32[3,10,16,128]{3,2,1,0:T(8,128)S(1)}, u32[]{:S(2)}, u32[]{:S(2)}) collective-permute-start(f32[3,10,16,128]{3,2,1,0:T(8,128)S(1)} %get-tuple-element.53), channel_id=1, source_target_pairs={{4,0},{8,4},{12,8},{16,12},{20,16},{24,20},{28,24},{5,1},{9,5},{13... | collective-permute-start | bytes 737288 | tf_op jit(solution)/shard_map/ppermute | solution.py:32
  3.9 13.8 %collective-permute-start = (f32[3,10,16,128]{3,2,1,0:T(8,128)S(1)}, f32[3,10,16,128]{3,2,1,0:T(8,128)S(1)}, u32[]{:S(2)}, u32[]{:S(2)}) collective-permute-start(f32[3,10,16,128]{3,2,1,0:T(8,128)S(1)} %get-tuple-element.52), channel_id=1, source_target_pairs={{0,4},{4,8},{8,12},{12,16},{16,20},{20,24},{24,28},{1,5},{5,9},{9,... | collective-permute-start | bytes 737288 | tf_op jit(solution)/shard_map/ppermute | solution.py:32
  9.6 14.2 %collective-permute-start.5 = (f32[3,16,10,128]{3,2,1,0:T(8,128)}, f32[3,16,10,128]{3,2,1,0:T(8,128)S(1)}, u32[]{:S(2)}, u32[]{:S(2)}) collective-permute-start(f32[3,16,10,128]{3,2,1,0:T(8,128)} %get-tuple-element.51), channel_id=1, source_target_pairs={{1,0},{2,1},{3,2},{5,4},{6,5},{7,6},{9,8},{10,9},{11,10},{13,12},{... | collective-permute-start | bytes 737288 | tf_op jit(solution)/shard_map/ppermute | solution.py:32
  10.9 13.0 %collective-permute-start.4 = (f32[3,16,10,128]{3,2,1,0:T(8,128)}, f32[3,16,10,128]{3,2,1,0:T(8,128)}, u32[]{:S(2)}, u32[]{:S(2)}) collective-permute-start(f32[3,16,10,128]{3,2,1,0:T(8,128)} %get-tuple-element.50), channel_id=1, source_target_pairs={{0,1},{1,2},{2,3},{4,5},{5,6},{6,7},{8,9},{9,10},{10,11},{12,13},{... | collective-permute-start | bytes 737288 | tf_op jit(solution)/shard_map/ppermute | solution.py:32
  17.8 4.6 %collective-permute-start.3 = (f32[3,20,10,128]{3,2,1,0:T(8,128)S(1)}, f32[3,20,10,128]{3,2,1,0:T(8,128)S(1)}, u32[]{:S(2)}, u32[]{:S(2)}) collective-permute-start(f32[3,20,10,128]{3,2,1,0:T(8,128)S(1)} %pad_maximum_fusion.2), channel_id=1, source_target_pairs={{1,0},{2,1},{3,2},{5,4},{6,5},{7,6},{9,8},{10,9},{11,10},{13,12},{... | collective-permute-start | bytes 921608 | tf_op jit(solution)/shard_map/ppermute | solution.py:32
  19.1 4.8 %copy-start.1 = (f32[16,16,128]{2,1,0:T(8,128)S(1)}, f32[16,16,128]{2,1,0:T(8,128)}, u32[]{:S(2)}) copy-start(f32[16,16,128]{2,1,0:T(8,128)} %param.5) | copy-start | bytes 393220
  19.1 4.8 %copy-start.2 = (f32[16,16,128]{2,1,0:T(8,128)S(1)}, f32[16,16,128]{2,1,0:T(8,128)}, u32[]{:S(2)}) copy-start(f32[16,16,128]{2,1,0:T(8,128)} %param.4) | copy-start | bytes 393220
  19.2 4.6 %collective-permute-start.2 = (f32[3,20,10,128]{3,2,1,0:T(8,128)S(1)}, f32[3,20,10,128]{3,2,1,0:T(8,128)S(1)}, u32[]{:S(2)}, u32[]{:S(2)}) collective-permute-start(f32[3,20,10,128]{3,2,1,0:T(8,128)S(1)} %pad_maximum_fusion.1), channel_id=1, source_target_pairs={{0,1},{1,2},{2,3},{4,5},{5,6},{6,7},{8,9},{9,10},{10,11},{12,13},{... | collective-permute-start | bytes 921608 | tf_op jit(solution)/shard_map/ppermute | solution.py:32
  31.7 2.5 %copy-start = (f32[4,36,36,128]{3,2,1,0:T(8,128)S(1)}, f32[4,36,36,128]{3,2,1,0:T(8,128)}, u32[]{:S(2)}) copy-start(f32[4,36,36,128]{3,2,1,0:T(8,128)} %shard_map.46) | copy-start | bytes 7962628
  45.4 14.0 %collective-permute-start.12 = (f32[5,4,4,32]{3,2,1,0:T(4,128)S(1)}, f32[5,4,4,32]{3,2,1,0:T(4,128)S(1)}, u32[]{:S(2)}, u32[]{:S(2)}) collective-permute-start(f32[5,4,4,32]{3,2,1,0:T(4,128)S(1)} %pad_maximum_fusion.20), channel_id=1, source_target_pairs={{0,1},{1,2},{2,3},{3,0},{4,5},{5,6},{6,7},{7,4},{8,9},{9,10},{10,1... | collective-permute-start | bytes 30728 | tf_op jit(solution)/shard_map/ppermute | solution.py:256
  51.2 8.2 %collective-permute-start.11 = (f32[5,4,4,32]{3,2,1,0:T(4,128)S(1)}, f32[5,4,4,32]{3,2,1,0:T(4,128)S(1)}, u32[]{:S(2)}, u32[]{:S(2)}) collective-permute-start(f32[5,4,4,32]{3,2,1,0:T(4,128)S(1)} %pad_maximum_fusion.20), channel_id=1, source_target_pairs={{0,2},{1,3},{2,0},{3,1},{4,6},{5,7},{6,4},{7,5},{8,10},{9,11},{10,... | collective-permute-start | bytes 30728 | tf_op jit(solution)/shard_map/ppermute | solution.py:256
  53.6 5.8 %collective-permute-start.10 = (f32[5,4,4,32]{3,2,1,0:T(4,128)S(1)}, f32[5,4,4,32]{3,2,1,0:T(4,128)S(1)}, u32[]{:S(2)}, u32[]{:S(2)}) collective-permute-start(f32[5,4,4,32]{3,2,1,0:T(4,128)S(1)} %pad_maximum_fusion.20), channel_id=1, source_target_pairs={{0,3},{1,0},{2,1},{3,2},{4,7},{5,4},{6,5},{7,6},{8,11},{9,8},{10,9... | collective-permute-start | bytes 30728 | tf_op jit(solution)/shard_map/ppermute | solution.py:256
  55.0 14.3 %collective-permute-start.7 = (f32[2,8,5,64]{3,2,1,0:T(8,128)S(1)}, f32[2,8,5,64]{3,2,1,0:T(8,128)S(1)}, u32[]{:S(2)}, u32[]{:S(2)}) collective-permute-start(f32[2,8,5,64]{3,2,1,0:T(8,128)S(1)} %get-tuple-element.166), channel_id=1, source_target_pairs={{1,0},{2,1},{3,2},{5,4},{6,5},{7,6},{9,8},{10,9},{11,10},{13,12},{... | collective-permute-start | bytes 61448 | tf_op jit(solution)/shard_map/ppermute | solution.py:32
  56.3 16.0 %collective-permute-start.6 = (f32[2,8,5,64]{3,2,1,0:T(8,128)S(1)}, f32[2,8,5,64]{3,2,1,0:T(8,128)S(1)}, u32[]{:S(2)}, u32[]{:S(2)}) collective-permute-start(f32[2,8,5,64]{3,2,1,0:T(8,128)S(1)} %get-tuple-element.165), channel_id=1, source_target_pairs={{0,1},{1,2},{2,3},{4,5},{5,6},{6,7},{8,9},{9,10},{10,11},{12,13},{... | collective-permute-start | bytes 61448 | tf_op jit(solution)/shard_map/ppermute | solution.py:32
  59.5 15.6 %collective-permute-start.14 = (f32[5,4,16,32]{3,2,1,0:T(8,128)S(1)}, f32[5,4,16,32]{3,2,1,0:T(8,128)S(1)}, u32[]{:S(2)}, u32[]{:S(2)}) collective-permute-start(f32[5,4,16,32]{3,2,1,0:T(8,128)S(1)} %pad_maximum_fusion.6), channel_id=1, source_target_pairs={{0,8},{4,12},{8,16},{12,20},{16,24},{20,28},{1,9},{5,13},{9,17},{1... | collective-permute-start | bytes 122888 | tf_op jit(solution)/shard_map/ppermute | solution.py:32
  63.0 10.7 %collective-permute-start.13 = (f32[5,4,16,32]{3,2,1,0:T(8,128)S(1)}, f32[5,4,16,32]{3,2,1,0:T(8,128)S(1)}, u32[]{:S(2)}, u32[]{:S(2)}) collective-permute-start(f32[5,4,16,32]{3,2,1,0:T(8,128)S(1)} %pad_maximum_fusion.6), channel_id=1, source_target_pairs={{0,12},{4,16},{8,20},{12,24},{16,28},{1,13},{5,17},{9,21},{13,25},... | collective-permute-start | bytes 122888 | tf_op jit(solution)/shard_map/ppermute | solution.py:32
  66.4 10.6 %collective-permute-start.15 = (f32[5,4,16,32]{3,2,1,0:T(8,128)S(1)}, f32[5,4,16,32]{3,2,1,0:T(8,128)S(1)}, u32[]{:S(2)}, u32[]{:S(2)}) collective-permute-start(f32[5,4,16,32]{3,2,1,0:T(8,128)S(1)} %pad_maximum_fusion.6), channel_id=1, source_target_pairs={{0,4},{4,8},{8,12},{12,16},{16,20},{20,24},{24,28},{1,5},{5,9},{9,... | collective-permute-start | bytes 122888 | tf_op jit(solution)/shard_map/ppermute | solution.py:32
  69.3 12.6 %collective-permute-start.16 = (f32[5,4,16,32]{3,2,1,0:T(8,128)S(1)}, f32[5,4,16,32]{3,2,1,0:T(8,128)S(1)}, u32[]{:S(2)}, u32[]{:S(2)}) collective-permute-start(f32[5,4,16,32]{3,2,1,0:T(8,128)S(1)} %pad_maximum_fusion.6), channel_id=1, source_target_pairs={{4,0},{8,4},{12,8},{16,12},{20,16},{24,20},{28,24},{5,1},{9,5},{13... | collective-permute-start | bytes 122888 | tf_op jit(solution)/shard_map/ppermute | solution.py:32
  72.3 9.7 %collective-permute-start.17 = (f32[5,4,16,32]{3,2,1,0:T(8,128)S(1)}, f32[5,4,16,32]{3,2,1,0:T(8,128)S(1)}, u32[]{:S(2)}, u32[]{:S(2)}) collective-permute-start(f32[5,4,16,32]{3,2,1,0:T(8,128)S(1)} %pad_maximum_fusion.6), channel_id=1, source_target_pairs={{8,0},{12,4},{16,8},{20,12},{24,16},{28,20},{9,1},{13,5},{17,9},{2... | collective-permute-start | bytes 122888 | tf_op jit(solution)/shard_map/ppermute | solution.py:32
  73.7 15.7 %collective-permute-start.18 = (f32[5,4,16,32]{3,2,1,0:T(8,128)S(1)}, f32[5,4,16,32]{3,2,1,0:T(8,128)S(1)}, u32[]{:S(2)}, u32[]{:S(2)}) collective-permute-start(f32[5,4,16,32]{3,2,1,0:T(8,128)S(1)} %pad_maximum_fusion.6), channel_id=1, source_target_pairs={{12,0},{16,4},{20,8},{24,12},{28,16},{13,1},{17,5},{21,9},{25,13},... | collective-permute-start | bytes 122888 | tf_op jit(solution)/shard_map/ppermute | solution.py:32
  75.0 20.7 %collective-permute-start.9 = (f32[2,5,18,64]{3,2,1,0:T(8,128)S(1)}, f32[2,5,18,64]{3,2,1,0:T(8,128)S(1)}, u32[]{:S(2)}, u32[]{:S(2)}) collective-permute-start(f32[2,5,18,64]{3,2,1,0:T(8,128)S(1)} %get-tuple-element.83), channel_id=1, source_target_pairs={{4,0},{8,4},{12,8},{16,12},{20,16},{24,20},{28,24},{5,1},{9,5},{13... | collective-permute-start | bytes 138248 | tf_op jit(solution)/shard_map/ppermute | solution.py:32
  77.0 18.7 %collective-permute-start.8 = (f32[2,5,18,64]{3,2,1,0:T(8,128)S(1)}, f32[2,5,18,64]{3,2,1,0:T(8,128)S(1)}, u32[]{:S(2)}, u32[]{:S(2)}) collective-permute-start(f32[2,5,18,64]{3,2,1,0:T(8,128)S(1)} %get-tuple-element.82), channel_id=1, source_target_pairs={{0,4},{4,8},{8,12},{12,16},{16,20},{20,24},{24,28},{1,5},{5,9},{9,... | collective-permute-start | bytes 138248 | tf_op jit(solution)/shard_map/ppermute | solution.py:32

commit v13 on v12

--- a/solution.py
+++ b/solution.py
@@ -55,6 +55,28 @@
     mid = jnp.concatenate([south, cells, north], axis=2)
     bottom = jnp.concatenate([low[:, width:], east, high[:, width:]], axis=2)
     return jnp.concatenate([top, mid, bottom], axis=1)
+
+
+def frames_overlapped(fields, width):
+    sx, sy = fields[0].shape[0], fields[0].shape[1]
+
+    def slab(xs, ys):
+        return jnp.stack([f[xs, ys] for f in fields])
+
+    every = slice(None)
+    west = shift_from(slab(slice(sx - width, sx), every), "gx", -1)
+    east = shift_from(slab(slice(0, width), every), "gx", 1)
+    south = shift_from(slab(every, slice(sy - width, sy)), "gy", -1)
+    north = shift_from(slab(every, slice(0, width)), "gy", 1)
+    low = shift_from(jnp.concatenate([west[:, :, sy - width :], east[:, :, sy - width :]], axis=1), "gy", -1)
+    high = shift_from(jnp.concatenate([west[:, :, :width], east[:, :, :width]], axis=1), "gy", 1)
+    out = []
+    for k, f in enumerate(fields):
+        top = jnp.concatenate([low[k, :width], west[k], high[k, :width]], axis=1)
+        mid = jnp.concatenate([south[k], f, north[k]], axis=1)
+        bottom = jnp.concatenate([low[k, width:], east[k], high[k, width:]], axis=1)
+        out.append(jnp.concatenate([top, mid, bottom], axis=0))
+    return out
 
 
 def harmonic(first, second):
@@ -225,9 +247,7 @@
     ix = lax.axis_index("gx")
     iy = lax.axis_index("gy")
 
-    stacked = jnp.stack([conc_prev, right_side, soil_id.astype(jnp.float32)])
-    ext = halo_overlapped(stacked, hf)
-    conc, rhs, idf = ext[0], ext[1], ext[2]
+    conc, rhs, idf = frames_overlapped([conc_prev, right_side, soil_id.astype(jnp.float32)], hf)
     fine_c = soil_fields((n, ny, hf), soil_table, conc, idf)
     fine = build_level(fine_c, n, hf, 1.0)
 

time: 101 us -> 100 us (0.990)
  waiting for transfers between devices: 11.7 us -> 10.2 us
    ppermute x16, waiting for transfers between devices: 11.7 us -> 10.2 us  [shift_from(): return lax.ppermute(cells, axis, pairs)]
    another operation x0 -> x4, local copies, waits for them, and re-layouts: none -> 1.14 us  [slab(): return jnp.stack([f[xs, ys] for f in fields])]
    another operation x2 -> x4, other arithmetic: 1.91 us -> 0.86 us  [slab(): return jnp.stack([f[xs, ys] for f in fields])]
    slice x6 -> x2, local copies, waits for them, and re-layouts: 1.09 us -> 0.07 us  [the longest x1 0.03 us: frames_overlapped(): east[:, :, sy - width:]]
    concatenate x3 -> x5, other arithmetic: 1.34 us -> 2.08 us  [the longest x3 2.02 us: frames_overlapped(): out.append(jnp.concatenate([top, mid, bottom], axis=0))]
  transfers between devices with their start and end apart: 19 -> 19, of which waited for: 3 -> 3; matrix products, arithmetic and copies ran while one was open for 7% -> 8% of each run, Pallas kernels for 0% -> 0%
where the time goes in v13:
time: 100 us; the launch traced here: 99.8 us
  starting transfers between devices  52.2 us (52%)
  other arithmetic  15.4 us (15%)
  local copies, waits for them, and re-layouts  10.4 us (10%)
  waiting for transfers between devices  10.2 us (10%)
  matrix products  5.17 us (5%)
  Pallas kernels  5.15 us (5%)
  between operations  1.27 us (1%)
    ppermute x16, starting transfers between devices, shift_from(): return lax.ppermute(cells, axis, pairs)  42.8 us
    ppermute x16, waiting for transfers between devices, shift_from(): return lax.ppermute(cells, axis, pairs)  10.2 us
    ppermute x3, starting transfers between devices, local(): blocks.append(lax.ppermute(cpack, 'gy', pairs))  9.42 us
    pallas_call x1, Pallas kernels, soil_fields(): pl.pallas_call(functools.partial(fields_kernel, frame), out_shape=jax.Sha...  5.15 us
    add x7, other arithmetic, chebyshev(): iterate = win(iterate, n, cur, nxt) + update  4.54 us
    add x8, other arithmetic, local(): u = centre + jacobi_weight * ((csrc[sl] - applied) / cdiag[sl])  2.5 us
    dot_general x4, matrix products, coarsen(): lax.dot_general(pick, rows, (((2,), (1,)), ((0,), (0,))), precision=HIGH)  2.25 us
    concatenate x3, other arithmetic, frames_overlapped(): out.append(jnp.concatenate([top, mid, bottom], axis=0))  2.02 us
  transfers between devices with their start and end apart: 19, of which 3 were waited for; matrix products, arithmetic and copies ran while one was open for 8% of the time, Pallas kernels for 0%

profile of v13, /device:TPU:4, one launch (start us, length us, event | category | flops | bytes accessed | tf_op | source)
XLA Modules:
  0.0 99.8 jit_solution(11625367044621651796)
XLA Ops:
  0.0 0.9 convert_element_type.30
  1.0 1.1 %slice_bitcast_fusion.58 = (f32[1,10,16,128]{3,2,1,0:T(8,128)S(1)}, f32[1,10,16,128]{3,2,1,0:T(8,128)S(1)}, f32[1,10,16,128]{3,2,1,0:T(8,128)S(1)}, f32[1,10,16,128]{3,2,1,0:T(8,128)S(1)}) fusion(f32[16,16,128]{2,1,0:T(8,128)} %param.5, f32[16,16,128]{2,1,0:T(8,128)} %param.4), kind=kLoop, calls=%fused_computation.601 | loop fusion | bytes 655360 | tf_op jit(solution)/shard_map/stack | solution.py:64
  2.1 1.9 %collective-permute-start.1 = (f32[3,10,16,128]{3,2,1,0:T(8,128)S(1)}, f32[3,10,16,128]{3,2,1,0:T(8,128)S(1)}, u32[]{:S(2)}, u32[]{:S(2)}) collective-permute-start(f32[3,10,16,128]{3,2,1,0:T(8,128)S(1)} %pad_maximum_fusion.7), channel_id=1, source_target_pairs={{4,0},{8,4},{12,8},{16,12},{20,16},{24,20},{28,24},{5,1},{9,5},{13... | collective-permute-start | bytes 737288 | tf_op jit(solution)/shard_map/ppermute | solution.py:32
  4.0 4.8 %collective-permute-start = (f32[3,10,16,128]{3,2,1,0:T(8,128)S(1)}, f32[3,10,16,128]{3,2,1,0:T(8,128)S(1)}, u32[]{:S(2)}, u32[]{:S(2)}) collective-permute-start(f32[3,10,16,128]{3,2,1,0:T(8,128)S(1)} %pad_maximum_fusion.6), channel_id=1, source_target_pairs={{0,4},{4,8},{8,12},{12,16},{16,20},{20,24},{24,28},{1,5},{5,9},{9,... | collective-permute-start | bytes 737288 | tf_op jit(solution)/shard_map/ppermute | solution.py:32
  9.0 1.3 %collective-permute-start.5 = (f32[3,16,10,128]{3,2,1,0:T(8,128)S(1)}, f32[3,16,10,128]{3,2,1,0:T(8,128)S(1)}, u32[]{:S(2)}, u32[]{:S(2)}) collective-permute-start(f32[3,16,10,128]{3,2,1,0:T(8,128)S(1)} %pad_maximum_fusion.5), channel_id=1, source_target_pairs={{1,0},{2,1},{3,2},{5,4},{6,5},{7,6},{9,8},{10,9},{11,10},{13,12},{... | collective-permute-start | bytes 737288 | tf_op jit(solution)/shard_map/ppermute | solution.py:32
  10.3 0.8 pad_maximum_fusion.4
  11.1 3.8 %collective-permute-start.4 = (f32[3,16,10,128]{3,2,1,0:T(8,128)}, f32[3,16,10,128]{3,2,1,0:T(8,128)}, u32[]{:S(2)}, u32[]{:S(2)}) collective-permute-start(f32[3,16,10,128]{3,2,1,0:T(8,128)} %pad_maximum_fusion.4), channel_id=1, source_target_pairs={{0,1},{1,2},{2,3},{4,5},{5,6},{6,7},{8,9},{9,10},{10,11},{12,13},{... | collective-permute-start | bytes 737288 | tf_op jit(solution)/shard_map/ppermute | solution.py:32
  15.1 2.7 %collective-permute-done = f32[3,10,16,128]{3,2,1,0:T(8,128)S(1)} collective-permute-done((f32[3,10,16,128]{3,2,1,0:T(8,128)S(1)}, f32[3,10,16,128]{3,2,1,0:T(8,128)S(1)}, u32[]{:S(2)}, u32[]{:S(2)}) %collective-permute-start) | collective-permute-done | bytes 245792 | tf_op jit(solution)/shard_map/ppermute | solution.py:32
  17.9 1.3 %collective-permute-start.3 = (f32[3,20,10,128]{3,2,1,0:T(8,128)S(1)}, f32[3,20,10,128]{3,2,1,0:T(8,128)S(1)}, u32[]{:S(2)}, u32[]{:S(2)}) collective-permute-start(f32[3,20,10,128]{3,2,1,0:T(8,128)S(1)} %pad_maximum_fusion.2), channel_id=1, source_target_pairs={{1,0},{2,1},{3,2},{5,4},{6,5},{7,6},{9,8},{10,9},{11,10},{13,12},{... | collective-permute-start | bytes 921608 | tf_op jit(solution)/shard_map/ppermute | solution.py:32
  19.2 3.1 %collective-permute-start.2 = (f32[3,20,10,128]{3,2,1,0:T(8,128)S(1)}, f32[3,20,10,128]{3,2,1,0:T(8,128)S(1)}, u32[]{:S(2)}, u32[]{:S(2)}) collective-permute-start(f32[3,20,10,128]{3,2,1,0:T(8,128)S(1)} %pad_maximum_fusion.1), channel_id=1, source_target_pairs={{0,1},{1,2},{2,3},{4,5},{5,6},{6,7},{8,9},{9,10},{10,11},{12,13},{... | collective-permute-start | bytes 921608 | tf_op jit(solution)/shard_map/ppermute | solution.py:32
  22.4 1.1 %slice_bitcast_fusion.23 = (f32[16,10,128]{2,1,0:T(8,128)S(1)}, f32[16,10,128]{2,1,0:T(8,128)S(1)}, f32[16,10,128]{2,1,0:T(8,128)S(1)}) fusion(f32[3,16,10,128]{3,2,1,0:T(8,128)} %collective-permute-done.4), kind=kLoop, calls=%fused_computation.384 | loop fusion | bytes 491520 | tf_op jit(solution)/shard_map/squeeze | solution.py:76
  23.8 1.0 maximum_maximum_fusion.1.conc_ref
  24.7 1.0 maximum_maximum_fusion.2.idf_ref
  25.7 5.2 %shard_map.46 = f32[4,36,36,128]{3,2,1,0:T(8,128)} custom-call(f32[5,8]{1,0:T(8,128)} %table_ref.1, f32[36,36,128]{2,1,0:T(8,128)} %maximum_maximum_fusion.1.conc_ref, f32[36,36,128]{2,1,0:T(8,128)} %maximum_maximum_fusion.2.idf_ref), custom_call_target="tpu_custom_call" | custom-call | flops 16588800 | bytes 3981312 | tf_op jit(solution)/shard_map/pallas_call | solution.py:226
  30.9 1.9 %slice_bitcast_fusion.2 = (f32[36,36,128]{2,1,0:T(8,128)S(1)}, f32[36,36,128]{2,1,0:T(8,128)S(1)}, f32[36,36,128]{2,1,0:T(8,128)S(1)}) fusion(f32[4,36,36,128]{3,2,1,0:T(8,128)} %shard_map.46), kind=kLoop, calls=%fused_computation.16 | loop fusion | bytes 3981312 | tf_op jit(solution)/shard_map/squeeze | solution.py:121
  32.7 0.6 copy-done
  34.1 0.7 fusion.4
  35.3 1.2 %slice_add_fusion.5 = (f32[32,32,128]{2,1,0:T(8,128)S(1)}, f32[32,32,128]{2,1,0:T(8,128)S(1)}) fusion(f32[34,34,128]{2,1,0:T(8,128)S(1)} %get-tuple-element.21, f32[34,34,128]{2,1,0:T(8,128)S(1)} %get-tuple-element.22, f32[32,32,127]{2,1,0:T(8,128)S(1)} %get-tuple-element.32, f32[32,32,1]{2,1,0:T(8,128)S(1)} %get-tuple-element.34, ...), kind=kLoop, calls=%fused_computation.55 | loop fusion | flops 3538944 | bytes 9046976 | tf_op jit(solution)/shard_map/add | solution.py:185
  37.0 0.8 fusion.336
  37.9 1.5 %convolution_multiply_fusion = f32[72,18,64]{2,1,0:T(8,128)S(1)} fusion(f32[72,36,64]{2,1,0:T(8,128)S(1)} %fusion.336, f32[18,36]{1,0:T(8,128)S(1)} %fusion.357), kind=kOutput, calls=%fused_computation.1 | convolution fusion | flops 35914752 | bytes 997920 | tf_op jit(solution)/shard_map/dot_general | solution.py:106
  39.7 1.2 %fusion.22 = f32[30,30,128]{2,1,0:T(8,128)S(1)} fusion(f32[34,34,128]{2,1,0:T(8,128)S(1)} %get-tuple-element.22, f32[32,32,128]{2,1,0:T(8,128)S(1)} %get-tuple-element.19, f32[36,35,128]{2,1,0:T(8,128)S(1)} %maximum_divide_fusion.1, f32[35,36,128]{2,1,0:T(8,128)S(1)} %divide_bitcast_fusion, f32[36,36,128]{2,1,0:T(8,128)S(1)} %get-tuple-element.24, ...), kind=kLoop, calls=%fused_computation.59 | loop fusion | flops 3110400 | bytes 8031168 | tf_op jit(solution)/shard_map/add | solution.py:185
  41.3 0.9 fusion.40
  42.5 0.3 divide_multiply_fusion.3
  44.7 5.6 %collective-permute-start.12 = (f32[5,4,4,32]{3,2,1,0:T(4,128)S(1)}, f32[5,4,4,32]{3,2,1,0:T(4,128)S(1)}, u32[]{:S(2)}, u32[]{:S(2)}) collective-permute-start(f32[5,4,4,32]{3,2,1,0:T(4,128)S(1)} %pad_maximum_fusion.23), channel_id=1, source_target_pairs={{0,1},{1,2},{2,3},{3,0},{4,5},{5,6},{6,7},{7,4},{8,9},{9,10},{10,1... | collective-permute-start | bytes 30728 | tf_op jit(solution)/shard_map/ppermute | solution.py:276
  50.3 2.4 %collective-permute-start.11 = (f32[5,4,4,32]{3,2,1,0:T(4,128)S(1)}, f32[5,4,4,32]{3,2,1,0:T(4,128)S(1)}, u32[]{:S(2)}, u32[]{:S(2)}) collective-permute-start(f32[5,4,4,32]{3,2,1,0:T(4,128)S(1)} %pad_maximum_fusion.23), channel_id=1, source_target_pairs={{0,2},{1,3},{2,0},{3,1},{4,6},{5,7},{6,4},{7,5},{8,10},{9,11},{10,... | collective-permute-start | bytes 30728 | tf_op jit(solution)/shard_map/ppermute | solution.py:276
  52.8 1.4 %collective-permute-start.10 = (f32[5,4,4,32]{3,2,1,0:T(4,128)S(1)}, f32[5,4,4,32]{3,2,1,0:T(4,128)S(1)}, u32[]{:S(2)}, u32[]{:S(2)}) collective-permute-start(f32[5,4,4,32]{3,2,1,0:T(4,128)S(1)} %pad_maximum_fusion.23), channel_id=1, source_target_pairs={{0,3},{1,0},{2,1},{3,2},{4,7},{5,4},{6,5},{7,6},{8,11},{9,8},{10,9... | collective-permute-start | bytes 30728 | tf_op jit(solution)/shard_map/ppermute | solution.py:276
  54.2 1.3 %collective-permute-start.7 = (f32[2,8,5,64]{3,2,1,0:T(8,128)S(1)}, f32[2,8,5,64]{3,2,1,0:T(8,128)S(1)}, u32[]{:S(2)}, u32[]{:S(2)}) collective-permute-start(f32[2,8,5,64]{3,2,1,0:T(8,128)S(1)} %get-tuple-element.191), channel_id=1, source_target_pairs={{1,0},{2,1},{3,2},{5,4},{6,5},{7,6},{9,8},{10,9},{11,10},{13,12},{... | collective-permute-start | bytes 61448 | tf_op jit(solution)/shard_map/ppermute | solution.py:32
  55.5 3.0 %collective-permute-start.6 = (f32[2,8,5,64]{3,2,1,0:T(8,128)S(1)}, f32[2,8,5,64]{3,2,1,0:T(8,128)S(1)}, u32[]{:S(2)}, u32[]{:S(2)}) collective-permute-start(f32[2,8,5,64]{3,2,1,0:T(8,128)S(1)} %get-tuple-element.190), channel_id=1, source_target_pairs={{0,1},{1,2},{2,3},{4,5},{5,6},{6,7},{8,9},{9,10},{10,11},{12,13},{... | collective-permute-start | bytes 61448 | tf_op jit(solution)/shard_map/ppermute | solution.py:32
  58.6 3.5 %collective-permute-start.14 = (f32[5,4,16,32]{3,2,1,0:T(8,128)S(1)}, f32[5,4,16,32]{3,2,1,0:T(8,128)S(1)}, u32[]{:S(2)}, u32[]{:S(2)}) collective-permute-start(f32[5,4,16,32]{3,2,1,0:T(8,128)S(1)} %pad_maximum_fusion.9), channel_id=1, source_target_pairs={{0,8},{4,12},{8,16},{12,20},{16,24},{20,28},{1,9},{5,13},{9,17},{1... | collective-permute-start | bytes 122888 | tf_op jit(solution)/shard_map/ppermute | solution.py:32
  62.1 3.5 %collective-permute-start.13 = (f32[5,4,16,32]{3,2,1,0:T(8,128)S(1)}, f32[5,4,16,32]{3,2,1,0:T(8,128)S(1)}, u32[]{:S(2)}, u32[]{:S(2)}) collective-permute-start(f32[5,4,16,32]{3,2,1,0:T(8,128)S(1)} %pad_maximum_fusion.9), channel_id=1, source_target_pairs={{0,12},{4,16},{8,20},{12,24},{16,28},{1,13},{5,17},{9,21},{13,25},... | collective-permute-start | bytes 122888 | tf_op jit(solution)/shard_map/ppermute | solution.py:32
  65.6 2.9 %collective-permute-start.15 = (f32[5,4,16,32]{3,2,1,0:T(8,128)S(1)}, f32[5,4,16,32]{3,2,1,0:T(8,128)S(1)}, u32[]{:S(2)}, u32[]{:S(2)}) collective-permute-start(f32[5,4,16,32]{3,2,1,0:T(8,128)S(1)} %pad_maximum_fusion.9), channel_id=1, source_target_pairs={{0,4},{4,8},{8,12},{12,16},{16,20},{20,24},{24,28},{1,5},{5,9},{9,... | collective-permute-start | bytes 122888 | tf_op jit(solution)/shard_map/ppermute | solution.py:32
  68.5 3.0 %collective-permute-start.16 = (f32[5,4,16,32]{3,2,1,0:T(8,128)S(1)}, f32[5,4,16,32]{3,2,1,0:T(8,128)S(1)}, u32[]{:S(2)}, u32[]{:S(2)}) collective-permute-start(f32[5,4,16,32]{3,2,1,0:T(8,128)S(1)} %pad_maximum_fusion.9), channel_id=1, source_target_pairs={{4,0},{8,4},{12,8},{16,12},{20,16},{24,20},{28,24},{5,1},{9,5},{13... | collective-permute-start | bytes 122888 | tf_op jit(solution)/shard_map/ppermute | solution.py:32
  71.5 1.3 %collective-permute-start.17 = (f32[5,4,16,32]{3,2,1,0:T(8,128)S(1)}, f32[5,4,16,32]{3,2,1,0:T(8,128)S(1)}, u32[]{:S(2)}, u32[]{:S(2)}) collective-permute-start(f32[5,4,16,32]{3,2,1,0:T(8,128)S(1)} %pad_maximum_fusion.9), channel_id=1, source_target_pairs={{8,0},{12,4},{16,8},{20,12},{24,16},{28,20},{9,1},{13,5},{17,9},{2... | collective-permute-start | bytes 122888 | tf_op jit(solution)/shard_map/ppermute | solution.py:32
  72.9 1.3 %collective-permute-start.18 = (f32[5,4,16,32]{3,2,1,0:T(8,128)S(1)}, f32[5,4,16,32]{3,2,1,0:T(8,128)S(1)}, u32[]{:S(2)}, u32[]{:S(2)}) collective-permute-start(f32[5,4,16,32]{3,2,1,0:T(8,128)S(1)} %pad_maximum_fusion.9), channel_id=1, source_target_pairs={{12,0},{16,4},{20,8},{24,12},{28,16},{13,1},{17,5},{21,9},{25,13},... | collective-permute-start | bytes 122888 | tf_op jit(solution)/shard_map/ppermute | solution.py:32
  74.2 1.9 %collective-permute-start.9 = (f32[2,5,18,64]{3,2,1,0:T(8,128)S(1)}, f32[2,5,18,64]{3,2,1,0:T(8,128)S(1)}, u32[]{:S(2)}, u32[]{:S(2)}) collective-permute-start(f32[2,5,18,64]{3,2,1,0:T(8,128)S(1)} %get-tuple-element.96), channel_id=1, source_target_pairs={{4,0},{8,4},{12,8},{16,12},{20,16},{24,20},{28,24},{5,1},{9,5},{13... | collective-permute-start | bytes 138248 | tf_op jit(solution)/shard_map/ppermute | solution.py:32
  76.2 5.0 %collective-permute-start.8 = (f32[2,5,18,64]{3,2,1,0:T(8,128)S(1)}, f32[2,5,18,64]{3,2,1,0:T(8,128)S(1)}, u32[]{:S(2)}, u32[]{:S(2)}) collective-permute-start(f32[2,5,18,64]{3,2,1,0:T(8,128)S(1)} %get-tuple-element.95), channel_id=1, source_target_pairs={{0,4},{4,8},{8,12},{12,16},{16,20},{20,24},{24,28},{1,5},{5,9},{9,... | collective-permute-start | bytes 138248 | tf_op jit(solution)/shard_map/ppermute | solution.py:32
  81.3 7.2 %collective-permute-done.18 = f32[5,4,16,32]{3,2,1,0:T(8,128)S(1)} collective-permute-done((f32[5,4,16,32]{3,2,1,0:T(8,128)S(1)}, f32[5,4,16,32]{3,2,1,0:T(8,128)S(1)}, u32[]{:S(2)}, u32[]{:S(2)}) %collective-permute-start.18) | collective-permute-done | bytes 40992 | tf_op jit(solution)/shard_map/ppermute | solution.py:32
  89.8 0.5 fusion.87
  90.6 0.4 multiply_add_fusion
  91.3 0.3 multiply_add_fusion.1
  91.9 0.3 multiply_add_fusion.2
  94.4 0.4 fusion.318
  95.3 0.3 slice_add_fusion.10
  96.2 0.4 fusion.258
  96.7 0.5 fusion.315
  97.5 0.4 slice_add_fusion.7
  98.2 0.5 slice_add_fusion.9
  98.9 1.0 fusion.181
  (166 shorter events, 11.3 us)
Async XLA Ops:
  0.9 7.9 %copy-start.1 = (f32[16,16,128]{2,1,0:T(8,128)S(1)}, f32[16,16,128]{2,1,0:T(8,128)}, u32[]{:S(2)}) copy-start(f32[16,16,128]{2,1,0:T(8,128)} %param.5) | copy-start | bytes 393220
  1.0 7.9 %copy-start.2 = (f32[16,16,128]{2,1,0:T(8,128)S(1)}, f32[16,16,128]{2,1,0:T(8,128)}, u32[]{:S(2)}) copy-start(f32[16,16,128]{2,1,0:T(8,128)} %param.4) | copy-start | bytes 393220
  2.1 13.0 %collective-permute-start.1 = (f32[3,10,16,128]{3,2,1,0:T(8,128)S(1)}, f32[3,10,16,128]{3,2,1,0:T(8,128)S(1)}, u32[]{:S(2)}, u32[]{:S(2)}) collective-permute-start(f32[3,10,16,128]{3,2,1,0:T(8,128)S(1)} %pad_maximum_fusion.7), channel_id=1, source_target_pairs={{4,0},{8,4},{12,8},{16,12},{20,16},{24,20},{28,24},{5,1},{9,5},{13... | collective-permute-start | bytes 737288 | tf_op jit(solution)/shard_map/ppermute | solution.py:32
  4.0 13.8 %collective-permute-start = (f32[3,10,16,128]{3,2,1,0:T(8,128)S(1)}, f32[3,10,16,128]{3,2,1,0:T(8,128)S(1)}, u32[]{:S(2)}, u32[]{:S(2)}) collective-permute-start(f32[3,10,16,128]{3,2,1,0:T(8,128)S(1)} %pad_maximum_fusion.6), channel_id=1, source_target_pairs={{0,4},{4,8},{8,12},{12,16},{16,20},{20,24},{24,28},{1,5},{5,9},{9,... | collective-permute-start | bytes 737288 | tf_op jit(solution)/shard_map/ppermute | solution.py:32
  9.0 13.3 %collective-permute-start.5 = (f32[3,16,10,128]{3,2,1,0:T(8,128)S(1)}, f32[3,16,10,128]{3,2,1,0:T(8,128)S(1)}, u32[]{:S(2)}, u32[]{:S(2)}) collective-permute-start(f32[3,16,10,128]{3,2,1,0:T(8,128)S(1)} %pad_maximum_fusion.5), channel_id=1, source_target_pairs={{1,0},{2,1},{3,2},{5,4},{6,5},{7,6},{9,8},{10,9},{11,10},{13,12},{... | collective-permute-start | bytes 737288 | tf_op jit(solution)/shard_map/ppermute | solution.py:32
  11.1 11.3 %collective-permute-start.4 = (f32[3,16,10,128]{3,2,1,0:T(8,128)}, f32[3,16,10,128]{3,2,1,0:T(8,128)}, u32[]{:S(2)}, u32[]{:S(2)}) collective-permute-start(f32[3,16,10,128]{3,2,1,0:T(8,128)} %pad_maximum_fusion.4), channel_id=1, source_target_pairs={{0,1},{1,2},{2,3},{4,5},{5,6},{6,7},{8,9},{9,10},{10,11},{12,13},{... | collective-permute-start | bytes 737288 | tf_op jit(solution)/shard_map/ppermute | solution.py:32
  17.9 5.6 %collective-permute-start.3 = (f32[3,20,10,128]{3,2,1,0:T(8,128)S(1)}, f32[3,20,10,128]{3,2,1,0:T(8,128)S(1)}, u32[]{:S(2)}, u32[]{:S(2)}) collective-permute-start(f32[3,20,10,128]{3,2,1,0:T(8,128)S(1)} %pad_maximum_fusion.2), channel_id=1, source_target_pairs={{1,0},{2,1},{3,2},{5,4},{6,5},{7,6},{9,8},{10,9},{11,10},{13,12},{... | collective-permute-start | bytes 921608 | tf_op jit(solution)/shard_map/ppermute | solution.py:32
  19.2 4.5 %collective-permute-start.2 = (f32[3,20,10,128]{3,2,1,0:T(8,128)S(1)}, f32[3,20,10,128]{3,2,1,0:T(8,128)S(1)}, u32[]{:S(2)}, u32[]{:S(2)}) collective-permute-start(f32[3,20,10,128]{3,2,1,0:T(8,128)S(1)} %pad_maximum_fusion.1), channel_id=1, source_target_pairs={{0,1},{1,2},{2,3},{4,5},{5,6},{6,7},{8,9},{9,10},{10,11},{12,13},{... | collective-permute-start | bytes 921608 | tf_op jit(solution)/shard_map/ppermute | solution.py:32
  30.9 2.5 %copy-start = (f32[4,36,36,128]{3,2,1,0:T(8,128)S(1)}, f32[4,36,36,128]{3,2,1,0:T(8,128)}, u32[]{:S(2)}) copy-start(f32[4,36,36,128]{3,2,1,0:T(8,128)} %shard_map.46) | copy-start | bytes 7962628
  44.7 13.8 %collective-permute-start.12 = (f32[5,4,4,32]{3,2,1,0:T(4,128)S(1)}, f32[5,4,4,32]{3,2,1,0:T(4,128)S(1)}, u32[]{:S(2)}, u32[]{:S(2)}) collective-permute-start(f32[5,4,4,32]{3,2,1,0:T(4,128)S(1)} %pad_maximum_fusion.23), channel_id=1, source_target_pairs={{0,1},{1,2},{2,3},{3,0},{4,5},{5,6},{6,7},{7,4},{8,9},{9,10},{10,1... | collective-permute-start | bytes 30728 | tf_op jit(solution)/shard_map/ppermute | solution.py:276
  50.3 8.2 %collective-permute-start.11 = (f32[5,4,4,32]{3,2,1,0:T(4,128)S(1)}, f32[5,4,4,32]{3,2,1,0:T(4,128)S(1)}, u32[]{:S(2)}, u32[]{:S(2)}) collective-permute-start(f32[5,4,4,32]{3,2,1,0:T(4,128)S(1)} %pad_maximum_fusion.23), channel_id=1, source_target_pairs={{0,2},{1,3},{2,0},{3,1},{4,6},{5,7},{6,4},{7,5},{8,10},{9,11},{10,... | collective-permute-start | bytes 30728 | tf_op jit(solution)/shard_map/ppermute | solution.py:276
  52.8 5.8 %collective-permute-start.10 = (f32[5,4,4,32]{3,2,1,0:T(4,128)S(1)}, f32[5,4,4,32]{3,2,1,0:T(4,128)S(1)}, u32[]{:S(2)}, u32[]{:S(2)}) collective-permute-start(f32[5,4,4,32]{3,2,1,0:T(4,128)S(1)} %pad_maximum_fusion.23), channel_id=1, source_target_pairs={{0,3},{1,0},{2,1},{3,2},{4,7},{5,4},{6,5},{7,6},{8,11},{9,8},{10,9... | collective-permute-start | bytes 30728 | tf_op jit(solution)/shard_map/ppermute | solution.py:276
  54.2 14.3 %collective-permute-start.7 = (f32[2,8,5,64]{3,2,1,0:T(8,128)S(1)}, f32[2,8,5,64]{3,2,1,0:T(8,128)S(1)}, u32[]{:S(2)}, u32[]{:S(2)}) collective-permute-start(f32[2,8,5,64]{3,2,1,0:T(8,128)S(1)} %get-tuple-element.191), channel_id=1, source_target_pairs={{1,0},{2,1},{3,2},{5,4},{6,5},{7,6},{9,8},{10,9},{11,10},{13,12},{... | collective-permute-start | bytes 61448 | tf_op jit(solution)/shard_map/ppermute | solution.py:32
  55.5 16.0 %collective-permute-start.6 = (f32[2,8,5,64]{3,2,1,0:T(8,128)S(1)}, f32[2,8,5,64]{3,2,1,0:T(8,128)S(1)}, u32[]{:S(2)}, u32[]{:S(2)}) collective-permute-start(f32[2,8,5,64]{3,2,1,0:T(8,128)S(1)} %get-tuple-element.190), channel_id=1, source_target_pairs={{0,1},{1,2},{2,3},{4,5},{5,6},{6,7},{8,9},{9,10},{10,11},{12,13},{... | collective-permute-start | bytes 61448 | tf_op jit(solution)/shard_map/ppermute | solution.py:32
  58.6 15.6 %collective-permute-start.14 = (f32[5,4,16,32]{3,2,1,0:T(8,128)S(1)}, f32[5,4,16,32]{3,2,1,0:T(8,128)S(1)}, u32[]{:S(2)}, u32[]{:S(2)}) collective-permute-start(f32[5,4,16,32]{3,2,1,0:T(8,128)S(1)} %pad_maximum_fusion.9), channel_id=1, source_target_pairs={{0,8},{4,12},{8,16},{12,20},{16,24},{20,28},{1,9},{5,13},{9,17},{1... | collective-permute-start | bytes 122888 | tf_op jit(solution)/shard_map/ppermute | solution.py:32
  62.1 10.7 %collective-permute-start.13 = (f32[5,4,16,32]{3,2,1,0:T(8,128)S(1)}, f32[5,4,16,32]{3,2,1,0:T(8,128)S(1)}, u32[]{:S(2)}, u32[]{:S(2)}) collective-permute-start(f32[5,4,16,32]{3,2,1,0:T(8,128)S(1)} %pad_maximum_fusion.9), channel_id=1, source_target_pairs={{0,12},{4,16},{8,20},{12,24},{16,28},{1,13},{5,17},{9,21},{13,25},... | collective-permute-start | bytes 122888 | tf_op jit(solution)/shard_map/ppermute | solution.py:32
  65.6 10.6 %collective-permute-start.15 = (f32[5,4,16,32]{3,2,1,0:T(8,128)S(1)}, f32[5,4,16,32]{3,2,1,0:T(8,128)S(1)}, u32[]{:S(2)}, u32[]{:S(2)}) collective-permute-start(f32[5,4,16,32]{3,2,1,0:T(8,128)S(1)} %pad_maximum_fusion.9), channel_id=1, source_target_pairs={{0,4},{4,8},{8,12},{12,16},{16,20},{20,24},{24,28},{1,5},{5,9},{9,... | collective-permute-start | bytes 122888 | tf_op jit(solution)/shard_map/ppermute | solution.py:32
  68.5 12.8 %collective-permute-start.16 = (f32[5,4,16,32]{3,2,1,0:T(8,128)S(1)}, f32[5,4,16,32]{3,2,1,0:T(8,128)S(1)}, u32[]{:S(2)}, u32[]{:S(2)}) collective-permute-start(f32[5,4,16,32]{3,2,1,0:T(8,128)S(1)} %pad_maximum_fusion.9), channel_id=1, source_target_pairs={{4,0},{8,4},{12,8},{16,12},{20,16},{24,20},{28,24},{5,1},{9,5},{13... | collective-permute-start | bytes 122888 | tf_op jit(solution)/shard_map/ppermute | solution.py:32
  71.5 9.8 %collective-permute-start.17 = (f32[5,4,16,32]{3,2,1,0:T(8,128)S(1)}, f32[5,4,16,32]{3,2,1,0:T(8,128)S(1)}, u32[]{:S(2)}, u32[]{:S(2)}) collective-permute-start(f32[5,4,16,32]{3,2,1,0:T(8,128)S(1)} %pad_maximum_fusion.9), channel_id=1, source_target_pairs={{8,0},{12,4},{16,8},{20,12},{24,16},{28,20},{9,1},{13,5},{17,9},{2... | collective-permute-start | bytes 122888 | tf_op jit(solution)/shard_map/ppermute | solution.py:32
  72.9 15.7 %collective-permute-start.18 = (f32[5,4,16,32]{3,2,1,0:T(8,128)S(1)}, f32[5,4,16,32]{3,2,1,0:T(8,128)S(1)}, u32[]{:S(2)}, u32[]{:S(2)}) collective-permute-start(f32[5,4,16,32]{3,2,1,0:T(8,128)S(1)} %pad_maximum_fusion.9), channel_id=1, source_target_pairs={{12,0},{16,4},{20,8},{24,12},{28,16},{13,1},{17,5},{21,9},{25,13},... | collective-permute-start | bytes 122888 | tf_op jit(solution)/shard_map/ppermute | solution.py:32
  74.2 20.7 %collective-permute-start.9 = (f32[2,5,18,64]{3,2,1,0:T(8,128)S(1)}, f32[2,5,18,64]{3,2,1,0:T(8,128)S(1)}, u32[]{:S(2)}, u32[]{:S(2)}) collective-permute-start(f32[2,5,18,64]{3,2,1,0:T(8,128)S(1)} %get-tuple-element.96), channel_id=1, source_target_pairs={{4,0},{8,4},{12,8},{16,12},{20,16},{24,20},{28,24},{5,1},{9,5},{13... | collective-permute-start | bytes 138248 | tf_op jit(solution)/shard_map/ppermute | solution.py:32
  76.2 18.7 %collective-permute-start.8 = (f32[2,5,18,64]{3,2,1,0:T(8,128)S(1)}, f32[2,5,18,64]{3,2,1,0:T(8,128)S(1)}, u32[]{:S(2)}, u32[]{:S(2)}) collective-permute-start(f32[2,5,18,64]{3,2,1,0:T(8,128)S(1)} %get-tuple-element.95), channel_id=1, source_target_pairs={{0,4},{4,8},{8,12},{12,16},{16,20},{20,24},{24,28},{1,5},{5,9},{9,... | collective-permute-start | bytes 138248 | tf_op jit(solution)/shard_map/ppermute | solution.py:32

commit v14 on v13

--- a/solution.py
+++ b/solution.py
@@ -61,7 +61,7 @@
     sx, sy = fields[0].shape[0], fields[0].shape[1]
 
     def slab(xs, ys):
-        return jnp.stack([f[xs, ys] for f in fields])
+        return jnp.stack([f[xs, ys].astype(jnp.float32) for f in fields])
 
     every = slice(None)
     west = shift_from(slab(slice(sx - width, sx), every), "gx", -1)
@@ -73,7 +73,7 @@
     out = []
     for k, f in enumerate(fields):
         top = jnp.concatenate([low[k, :width], west[k], high[k, :width]], axis=1)
-        mid = jnp.concatenate([south[k], f, north[k]], axis=1)
+        mid = jnp.concatenate([south[k], f.astype(jnp.float32), north[k]], axis=1)
         bottom = jnp.concatenate([low[k, width:], east[k], high[k, width:]], axis=1)
         out.append(jnp.concatenate([top, mid, bottom], axis=0))
     return out
@@ -247,7 +247,7 @@
     ix = lax.axis_index("gx")
     iy = lax.axis_index("gy")
 
-    conc, rhs, idf = frames_overlapped([conc_prev, right_side, soil_id.astype(jnp.float32)], hf)
+    conc, rhs, idf = frames_overlapped([conc_prev, right_side, soil_id], hf)
     fine_c = soil_fields((n, ny, hf), soil_table, conc, idf)
     fine = build_level(fine_c, n, hf, 1.0)
 

time: 100 us -> 101 us (1.010)
    another operation x4 -> x6, other arithmetic: 0.86 us -> 1.91 us  [slab(): return jnp.stack([f[xs, ys].astype(jnp.float32) for f in fields])]
where the time goes in v14:
time: 101 us; the launch traced here: 99.9 us
  starting transfers between devices  52.3 us (52%)
  other arithmetic  15.5 us (15%)
  local copies, waits for them, and re-layouts  10.3 us (10%)
  waiting for transfers between devices  10.2 us (10%)
  matrix products  5.17 us (5%)
  Pallas kernels  5.15 us (5%)
  between operations  1.28 us (1%)
    ppermute x16, starting transfers between devices, shift_from(): return lax.ppermute(cells, axis, pairs)  42.8 us
    ppermute x16, waiting for transfers between devices, shift_from(): return lax.ppermute(cells, axis, pairs)  10.2 us
    ppermute x3, starting transfers between devices, local(): blocks.append(lax.ppermute(cpack, 'gy', pairs))  9.42 us
    pallas_call x1, Pallas kernels, soil_fields(): pl.pallas_call(functools.partial(fields_kernel, frame), out_shape=jax.Sha...  5.15 us
    add x7, other arithmetic, chebyshev(): iterate = win(iterate, n, cur, nxt) + update  4.54 us
    add x8, other arithmetic, local(): u = centre + jacobi_weight * ((csrc[sl] - applied) / cdiag[sl])  2.5 us
    dot_general x4, matrix products, coarsen(): lax.dot_general(pick, rows, (((2,), (1,)), ((0,), (0,))), precision=HIGH)  2.25 us
    concatenate x3, other arithmetic, frames_overlapped(): out.append(jnp.concatenate([top, mid, bottom], axis=0))  2.03 us
  transfers between devices with their start and end apart: 19, of which 3 were waited for; matrix products, arithmetic and copies ran while one was open for 8% of the time, Pallas kernels for 0%

profile of v14, /device:TPU:4, one launch (start us, length us, event | category | flops | bytes accessed | tf_op | source)
XLA Modules:
  0.0 99.9 jit_solution(6115258021414864094)
XLA Ops:
  0.0 1.0 %convert_bitcast_fusion.3 = (f32[1,10,16,128]{3,2,1,0:T(8,128)S(1)}, f32[1,10,16,128]{3,2,1,0:T(8,128)S(1)}) fusion(s32[16,16,128]{2,1,0:T(8,128)} %param.6), kind=kLoop, calls=%fused_computation.600 | loop fusion | flops 40960 | bytes 327680 | tf_op jit(solution)/shard_map/stack | solution.py:64
  1.1 1.1 %slice_bitcast_fusion.54 = (f32[1,10,16,128]{3,2,1,0:T(8,128)S(1)}, f32[1,10,16,128]{3,2,1,0:T(8,128)S(1)}, f32[1,10,16,128]{3,2,1,0:T(8,128)S(1)}, f32[1,10,16,128]{3,2,1,0:T(8,128)S(1)}) fusion(f32[16,16,128]{2,1,0:T(8,128)} %param.5, f32[16,16,128]{2,1,0:T(8,128)} %param.4), kind=kLoop, calls=%fused_computation.601 | loop fusion | bytes 655360 | tf_op jit(solution)/shard_map/stack | solution.py:64
  2.2 1.9 %collective-permute-start.1 = (f32[3,10,16,128]{3,2,1,0:T(8,128)S(1)}, f32[3,10,16,128]{3,2,1,0:T(8,128)S(1)}, u32[]{:S(2)}, u32[]{:S(2)}) collective-permute-start(f32[3,10,16,128]{3,2,1,0:T(8,128)S(1)} %pad_maximum_fusion.7), channel_id=1, source_target_pairs={{4,0},{8,4},{12,8},{16,12},{20,16},{24,20},{28,24},{5,1},{9,5},{13... | collective-permute-start | bytes 737288 | tf_op jit(solution)/shard_map/ppermute | solution.py:32
  4.1 4.8 %collective-permute-start = (f32[3,10,16,128]{3,2,1,0:T(8,128)S(1)}, f32[3,10,16,128]{3,2,1,0:T(8,128)S(1)}, u32[]{:S(2)}, u32[]{:S(2)}) collective-permute-start(f32[3,10,16,128]{3,2,1,0:T(8,128)S(1)} %pad_maximum_fusion.6), channel_id=1, source_target_pairs={{0,4},{4,8},{8,12},{12,16},{16,20},{20,24},{24,28},{1,5},{5,9},{9,... | collective-permute-start | bytes 737288 | tf_op jit(solution)/shard_map/ppermute | solution.py:32
  9.1 1.3 %collective-permute-start.5 = (f32[3,16,10,128]{3,2,1,0:T(8,128)S(1)}, f32[3,16,10,128]{3,2,1,0:T(8,128)S(1)}, u32[]{:S(2)}, u32[]{:S(2)}) collective-permute-start(f32[3,16,10,128]{3,2,1,0:T(8,128)S(1)} %pad_maximum_fusion.5), channel_id=1, source_target_pairs={{1,0},{2,1},{3,2},{5,4},{6,5},{7,6},{9,8},{10,9},{11,10},{13,12},{... | collective-permute-start | bytes 737288 | tf_op jit(solution)/shard_map/ppermute | solution.py:32
  10.4 0.8 pad_maximum_fusion.4
  11.2 3.8 %collective-permute-start.4 = (f32[3,16,10,128]{3,2,1,0:T(8,128)}, f32[3,16,10,128]{3,2,1,0:T(8,128)}, u32[]{:S(2)}, u32[]{:S(2)}) collective-permute-start(f32[3,16,10,128]{3,2,1,0:T(8,128)} %pad_maximum_fusion.4), channel_id=1, source_target_pairs={{0,1},{1,2},{2,3},{4,5},{5,6},{6,7},{8,9},{9,10},{10,11},{12,13},{... | collective-permute-start | bytes 737288 | tf_op jit(solution)/shard_map/ppermute | solution.py:32
  15.2 2.7 %collective-permute-done = f32[3,10,16,128]{3,2,1,0:T(8,128)S(1)} collective-permute-done((f32[3,10,16,128]{3,2,1,0:T(8,128)S(1)}, f32[3,10,16,128]{3,2,1,0:T(8,128)S(1)}, u32[]{:S(2)}, u32[]{:S(2)}) %collective-permute-start) | collective-permute-done | bytes 245792 | tf_op jit(solution)/shard_map/ppermute | solution.py:32
  18.0 1.3 %collective-permute-start.3 = (f32[3,20,10,128]{3,2,1,0:T(8,128)S(1)}, f32[3,20,10,128]{3,2,1,0:T(8,128)S(1)}, u32[]{:S(2)}, u32[]{:S(2)}) collective-permute-start(f32[3,20,10,128]{3,2,1,0:T(8,128)S(1)} %pad_maximum_fusion.2), channel_id=1, source_target_pairs={{1,0},{2,1},{3,2},{5,4},{6,5},{7,6},{9,8},{10,9},{11,10},{13,12},{... | collective-permute-start | bytes 921608 | tf_op jit(solution)/shard_map/ppermute | solution.py:32
  19.4 3.1 %collective-permute-start.2 = (f32[3,20,10,128]{3,2,1,0:T(8,128)S(1)}, f32[3,20,10,128]{3,2,1,0:T(8,128)S(1)}, u32[]{:S(2)}, u32[]{:S(2)}) collective-permute-start(f32[3,20,10,128]{3,2,1,0:T(8,128)S(1)} %pad_maximum_fusion.1), channel_id=1, source_target_pairs={{0,1},{1,2},{2,3},{4,5},{5,6},{6,7},{8,9},{9,10},{10,11},{12,13},{... | collective-permute-start | bytes 921608 | tf_op jit(solution)/shard_map/ppermute | solution.py:32
  22.5 1.1 %slice_bitcast_fusion.23 = (f32[16,10,128]{2,1,0:T(8,128)S(1)}, f32[16,10,128]{2,1,0:T(8,128)S(1)}, f32[16,10,128]{2,1,0:T(8,128)S(1)}) fusion(f32[3,16,10,128]{3,2,1,0:T(8,128)} %collective-permute-done.4), kind=kLoop, calls=%fused_computation.384 | loop fusion | bytes 491520 | tf_op jit(solution)/shard_map/squeeze | solution.py:76
  23.9 1.0 maximum_maximum_fusion.1.conc_ref
  24.9 1.0 maximum_maximum_fusion.2.idf_ref
  25.8 5.1 %shard_map.46 = f32[4,36,36,128]{3,2,1,0:T(8,128)} custom-call(f32[5,8]{1,0:T(8,128)} %table_ref.1, f32[36,36,128]{2,1,0:T(8,128)} %maximum_maximum_fusion.1.conc_ref, f32[36,36,128]{2,1,0:T(8,128)} %maximum_maximum_fusion.2.idf_ref), custom_call_target="tpu_custom_call" | custom-call | flops 16588800 | bytes 3981312 | tf_op jit(solution)/shard_map/pallas_call | solution.py:226
  31.0 1.9 %slice_bitcast_fusion.2 = (f32[36,36,128]{2,1,0:T(8,128)S(1)}, f32[36,36,128]{2,1,0:T(8,128)S(1)}, f32[36,36,128]{2,1,0:T(8,128)S(1)}) fusion(f32[4,36,36,128]{3,2,1,0:T(8,128)} %shard_map.46), kind=kLoop, calls=%fused_computation.16 | loop fusion | bytes 3981312 | tf_op jit(solution)/shard_map/squeeze | solution.py:121
  32.8 0.6 copy-done
  34.2 0.7 fusion.4
  35.4 1.2 %slice_add_fusion.5 = (f32[32,32,128]{2,1,0:T(8,128)S(1)}, f32[32,32,128]{2,1,0:T(8,128)S(1)}) fusion(f32[34,34,128]{2,1,0:T(8,128)S(1)} %get-tuple-element.21, f32[34,34,128]{2,1,0:T(8,128)S(1)} %get-tuple-element.22, f32[32,32,127]{2,1,0:T(8,128)S(1)} %get-tuple-element.32, f32[32,32,1]{2,1,0:T(8,128)S(1)} %get-tuple-element.34, ...), kind=kLoop, calls=%fused_computation.55 | loop fusion | flops 3538944 | bytes 9046976 | tf_op jit(solution)/shard_map/add | solution.py:185
  37.2 0.8 fusion.336
  38.0 1.5 %convolution_multiply_fusion = f32[72,18,64]{2,1,0:T(8,128)S(1)} fusion(f32[72,36,64]{2,1,0:T(8,128)S(1)} %fusion.336, f32[18,36]{1,0:T(8,128)S(1)} %fusion.357), kind=kOutput, calls=%fused_computation.1 | convolution fusion | flops 35914752 | bytes 997920 | tf_op jit(solution)/shard_map/dot_general | solution.py:106
  39.8 1.2 %fusion.22 = f32[30,30,128]{2,1,0:T(8,128)S(1)} fusion(f32[34,34,128]{2,1,0:T(8,128)S(1)} %get-tuple-element.22, f32[32,32,128]{2,1,0:T(8,128)S(1)} %get-tuple-element.19, f32[36,35,128]{2,1,0:T(8,128)S(1)} %maximum_divide_fusion.1, f32[35,36,128]{2,1,0:T(8,128)S(1)} %divide_bitcast_fusion, f32[36,36,128]{2,1,0:T(8,128)S(1)} %get-tuple-element.24, ...), kind=kLoop, calls=%fused_computation.59 | loop fusion | flops 3110400 | bytes 8031168 | tf_op jit(solution)/shard_map/add | solution.py:185
  41.4 0.9 fusion.40
  42.7 0.3 divide_multiply_fusion.3
  44.9 5.6 %collective-permute-start.12 = (f32[5,4,4,32]{3,2,1,0:T(4,128)S(1)}, f32[5,4,4,32]{3,2,1,0:T(4,128)S(1)}, u32[]{:S(2)}, u32[]{:S(2)}) collective-permute-start(f32[5,4,4,32]{3,2,1,0:T(4,128)S(1)} %pad_maximum_fusion.23), channel_id=1, source_target_pairs={{0,1},{1,2},{2,3},{3,0},{4,5},{5,6},{6,7},{7,4},{8,9},{9,10},{10,1... | collective-permute-start | bytes 30728 | tf_op jit(solution)/shard_map/ppermute | solution.py:276
  50.4 2.4 %collective-permute-start.11 = (f32[5,4,4,32]{3,2,1,0:T(4,128)S(1)}, f32[5,4,4,32]{3,2,1,0:T(4,128)S(1)}, u32[]{:S(2)}, u32[]{:S(2)}) collective-permute-start(f32[5,4,4,32]{3,2,1,0:T(4,128)S(1)} %pad_maximum_fusion.23), channel_id=1, source_target_pairs={{0,2},{1,3},{2,0},{3,1},{4,6},{5,7},{6,4},{7,5},{8,10},{9,11},{10,... | collective-permute-start | bytes 30728 | tf_op jit(solution)/shard_map/ppermute | solution.py:276
  52.9 1.4 %collective-permute-start.10 = (f32[5,4,4,32]{3,2,1,0:T(4,128)S(1)}, f32[5,4,4,32]{3,2,1,0:T(4,128)S(1)}, u32[]{:S(2)}, u32[]{:S(2)}) collective-permute-start(f32[5,4,4,32]{3,2,1,0:T(4,128)S(1)} %pad_maximum_fusion.23), channel_id=1, source_target_pairs={{0,3},{1,0},{2,1},{3,2},{4,7},{5,4},{6,5},{7,6},{8,11},{9,8},{10,9... | collective-permute-start | bytes 30728 | tf_op jit(solution)/shard_map/ppermute | solution.py:276
  54.3 1.3 %collective-permute-start.7 = (f32[2,8,5,64]{3,2,1,0:T(8,128)S(1)}, f32[2,8,5,64]{3,2,1,0:T(8,128)S(1)}, u32[]{:S(2)}, u32[]{:S(2)}) collective-permute-start(f32[2,8,5,64]{3,2,1,0:T(8,128)S(1)} %get-tuple-element.191), channel_id=1, source_target_pairs={{1,0},{2,1},{3,2},{5,4},{6,5},{7,6},{9,8},{10,9},{11,10},{13,12},{... | collective-permute-start | bytes 61448 | tf_op jit(solution)/shard_map/ppermute | solution.py:32
  55.6 3.0 %collective-permute-start.6 = (f32[2,8,5,64]{3,2,1,0:T(8,128)S(1)}, f32[2,8,5,64]{3,2,1,0:T(8,128)S(1)}, u32[]{:S(2)}, u32[]{:S(2)}) collective-permute-start(f32[2,8,5,64]{3,2,1,0:T(8,128)S(1)} %get-tuple-element.190), channel_id=1, source_target_pairs={{0,1},{1,2},{2,3},{4,5},{5,6},{6,7},{8,9},{9,10},{10,11},{12,13},{... | collective-permute-start | bytes 61448 | tf_op jit(solution)/shard_map/ppermute | solution.py:32
  58.7 3.5 %collective-permute-start.14 = (f32[5,4,16,32]{3,2,1,0:T(8,128)S(1)}, f32[5,4,16,32]{3,2,1,0:T(8,128)S(1)}, u32[]{:S(2)}, u32[]{:S(2)}) collective-permute-start(f32[5,4,16,32]{3,2,1,0:T(8,128)S(1)} %pad_maximum_fusion.9), channel_id=1, source_target_pairs={{0,8},{4,12},{8,16},{12,20},{16,24},{20,28},{1,9},{5,13},{9,17},{1... | collective-permute-start | bytes 122888 | tf_op jit(solution)/shard_map/ppermute | solution.py:32
  62.2 3.5 %collective-permute-start.13 = (f32[5,4,16,32]{3,2,1,0:T(8,128)S(1)}, f32[5,4,16,32]{3,2,1,0:T(8,128)S(1)}, u32[]{:S(2)}, u32[]{:S(2)}) collective-permute-start(f32[5,4,16,32]{3,2,1,0:T(8,128)S(1)} %pad_maximum_fusion.9), channel_id=1, source_target_pairs={{0,12},{4,16},{8,20},{12,24},{16,28},{1,13},{5,17},{9,21},{13,25},... | collective-permute-start | bytes 122888 | tf_op jit(solution)/shard_map/ppermute | solution.py:32
  65.7 2.8 %collective-permute-start.15 = (f32[5,4,16,32]{3,2,1,0:T(8,128)S(1)}, f32[5,4,16,32]{3,2,1,0:T(8,128)S(1)}, u32[]{:S(2)}, u32[]{:S(2)}) collective-permute-start(f32[5,4,16,32]{3,2,1,0:T(8,128)S(1)} %pad_maximum_fusion.9), channel_id=1, source_target_pairs={{0,4},{4,8},{8,12},{12,16},{16,20},{20,24},{24,28},{1,5},{5,9},{9,... | collective-permute-start | bytes 122888 | tf_op jit(solution)/shard_map/ppermute | solution.py:32
  68.6 3.0 %collective-permute-start.16 = (f32[5,4,16,32]{3,2,1,0:T(8,128)S(1)}, f32[5,4,16,32]{3,2,1,0:T(8,128)S(1)}, u32[]{:S(2)}, u32[]{:S(2)}) collective-permute-start(f32[5,4,16,32]{3,2,1,0:T(8,128)S(1)} %pad_maximum_fusion.9), channel_id=1, source_target_pairs={{4,0},{8,4},{12,8},{16,12},{20,16},{24,20},{28,24},{5,1},{9,5},{13... | collective-permute-start | bytes 122888 | tf_op jit(solution)/shard_map/ppermute | solution.py:32
  71.6 1.3 %collective-permute-start.17 = (f32[5,4,16,32]{3,2,1,0:T(8,128)S(1)}, f32[5,4,16,32]{3,2,1,0:T(8,128)S(1)}, u32[]{:S(2)}, u32[]{:S(2)}) collective-permute-start(f32[5,4,16,32]{3,2,1,0:T(8,128)S(1)} %pad_maximum_fusion.9), channel_id=1, source_target_pairs={{8,0},{12,4},{16,8},{20,12},{24,16},{28,20},{9,1},{13,5},{17,9},{2... | collective-permute-start | bytes 122888 | tf_op jit(solution)/shard_map/ppermute | solution.py:32
  73.0 1.3 %collective-permute-start.18 = (f32[5,4,16,32]{3,2,1,0:T(8,128)S(1)}, f32[5,4,16,32]{3,2,1,0:T(8,128)S(1)}, u32[]{:S(2)}, u32[]{:S(2)}) collective-permute-start(f32[5,4,16,32]{3,2,1,0:T(8,128)S(1)} %pad_maximum_fusion.9), channel_id=1, source_target_pairs={{12,0},{16,4},{20,8},{24,12},{28,16},{13,1},{17,5},{21,9},{25,13},... | collective-permute-start | bytes 122888 | tf_op jit(solution)/shard_map/ppermute | solution.py:32
  74.3 1.9 %collective-permute-start.9 = (f32[2,5,18,64]{3,2,1,0:T(8,128)S(1)}, f32[2,5,18,64]{3,2,1,0:T(8,128)S(1)}, u32[]{:S(2)}, u32[]{:S(2)}) collective-permute-start(f32[2,5,18,64]{3,2,1,0:T(8,128)S(1)} %get-tuple-element.96), channel_id=1, source_target_pairs={{4,0},{8,4},{12,8},{16,12},{20,16},{24,20},{28,24},{5,1},{9,5},{13... | collective-permute-start | bytes 138248 | tf_op jit(solution)/shard_map/ppermute | solution.py:32
  76.3 5.0 %collective-permute-start.8 = (f32[2,5,18,64]{3,2,1,0:T(8,128)S(1)}, f32[2,5,18,64]{3,2,1,0:T(8,128)S(1)}, u32[]{:S(2)}, u32[]{:S(2)}) collective-permute-start(f32[2,5,18,64]{3,2,1,0:T(8,128)S(1)} %get-tuple-element.95), channel_id=1, source_target_pairs={{0,4},{4,8},{8,12},{12,16},{16,20},{20,24},{24,28},{1,5},{5,9},{9,... | collective-permute-start | bytes 138248 | tf_op jit(solution)/shard_map/ppermute | solution.py:32
  81.5 7.2 %collective-permute-done.18 = f32[5,4,16,32]{3,2,1,0:T(8,128)S(1)} collective-permute-done((f32[5,4,16,32]{3,2,1,0:T(8,128)S(1)}, f32[5,4,16,32]{3,2,1,0:T(8,128)S(1)}, u32[]{:S(2)}, u32[]{:S(2)}) %collective-permute-start.18) | collective-permute-done | bytes 40992 | tf_op jit(solution)/shard_map/ppermute | solution.py:32
  89.9 0.5 fusion.87
  90.7 0.4 multiply_add_fusion
  91.4 0.3 multiply_add_fusion.1
  92.0 0.3 multiply_add_fusion.2
  94.6 0.4 fusion.318
  95.4 0.3 slice_add_fusion.10
  96.3 0.4 fusion.258
  96.8 0.5 fusion.315
  97.6 0.4 slice_add_fusion.7
  98.3 0.5 slice_add_fusion.9
  99.0 1.0 fusion.181
  (168 shorter events, 11.3 us)
Async XLA Ops:
  0.0 9.0 %copy-start.2 = (s32[16,16,128]{2,1,0:T(8,128)S(1)}, s32[16,16,128]{2,1,0:T(8,128)}, u32[]{:S(2)}) copy-start(s32[16,16,128]{2,1,0:T(8,128)} %param.6) | copy-start | bytes 393220
  1.1 7.9 %copy-start.1 = (f32[16,16,128]{2,1,0:T(8,128)S(1)}, f32[16,16,128]{2,1,0:T(8,128)}, u32[]{:S(2)}) copy-start(f32[16,16,128]{2,1,0:T(8,128)} %param.5) | copy-start | bytes 393220
  1.1 7.9 %copy-start.3 = (f32[16,16,128]{2,1,0:T(8,128)S(1)}, f32[16,16,128]{2,1,0:T(8,128)}, u32[]{:S(2)}) copy-start(f32[16,16,128]{2,1,0:T(8,128)} %param.4) | copy-start | bytes 393220
  2.2 13.0 %collective-permute-start.1 = (f32[3,10,16,128]{3,2,1,0:T(8,128)S(1)}, f32[3,10,16,128]{3,2,1,0:T(8,128)S(1)}, u32[]{:S(2)}, u32[]{:S(2)}) collective-permute-start(f32[3,10,16,128]{3,2,1,0:T(8,128)S(1)} %pad_maximum_fusion.7), channel_id=1, source_target_pairs={{4,0},{8,4},{12,8},{16,12},{20,16},{24,20},{28,24},{5,1},{9,5},{13... | collective-permute-start | bytes 737288 | tf_op jit(solution)/shard_map/ppermute | solution.py:32
  4.1 13.8 %collective-permute-start = (f32[3,10,16,128]{3,2,1,0:T(8,128)S(1)}, f32[3,10,16,128]{3,2,1,0:T(8,128)S(1)}, u32[]{:S(2)}, u32[]{:S(2)}) collective-permute-start(f32[3,10,16,128]{3,2,1,0:T(8,128)S(1)} %pad_maximum_fusion.6), channel_id=1, source_target_pairs={{0,4},{4,8},{8,12},{12,16},{16,20},{20,24},{24,28},{1,5},{5,9},{9,... | collective-permute-start | bytes 737288 | tf_op jit(solution)/shard_map/ppermute | solution.py:32
  9.1 13.3 %collective-permute-start.5 = (f32[3,16,10,128]{3,2,1,0:T(8,128)S(1)}, f32[3,16,10,128]{3,2,1,0:T(8,128)S(1)}, u32[]{:S(2)}, u32[]{:S(2)}) collective-permute-start(f32[3,16,10,128]{3,2,1,0:T(8,128)S(1)} %pad_maximum_fusion.5), channel_id=1, source_target_pairs={{1,0},{2,1},{3,2},{5,4},{6,5},{7,6},{9,8},{10,9},{11,10},{13,12},{... | collective-permute-start | bytes 737288 | tf_op jit(solution)/shard_map/ppermute | solution.py:32
  11.2 11.3 %collective-permute-start.4 = (f32[3,16,10,128]{3,2,1,0:T(8,128)}, f32[3,16,10,128]{3,2,1,0:T(8,128)}, u32[]{:S(2)}, u32[]{:S(2)}) collective-permute-start(f32[3,16,10,128]{3,2,1,0:T(8,128)} %pad_maximum_fusion.4), channel_id=1, source_target_pairs={{0,1},{1,2},{2,3},{4,5},{5,6},{6,7},{8,9},{9,10},{10,11},{12,13},{... | collective-permute-start | bytes 737288 | tf_op jit(solution)/shard_map/ppermute | solution.py:32
  18.0 5.6 %collective-permute-start.3 = (f32[3,20,10,128]{3,2,1,0:T(8,128)S(1)}, f32[3,20,10,128]{3,2,1,0:T(8,128)S(1)}, u32[]{:S(2)}, u32[]{:S(2)}) collective-permute-start(f32[3,20,10,128]{3,2,1,0:T(8,128)S(1)} %pad_maximum_fusion.2), channel_id=1, source_target_pairs={{1,0},{2,1},{3,2},{5,4},{6,5},{7,6},{9,8},{10,9},{11,10},{13,12},{... | collective-permute-start | bytes 921608 | tf_op jit(solution)/shard_map/ppermute | solution.py:32
  19.4 4.5 %collective-permute-start.2 = (f32[3,20,10,128]{3,2,1,0:T(8,128)S(1)}, f32[3,20,10,128]{3,2,1,0:T(8,128)S(1)}, u32[]{:S(2)}, u32[]{:S(2)}) collective-permute-start(f32[3,20,10,128]{3,2,1,0:T(8,128)S(1)} %pad_maximum_fusion.1), channel_id=1, source_target_pairs={{0,1},{1,2},{2,3},{4,5},{5,6},{6,7},{8,9},{9,10},{10,11},{12,13},{... | collective-permute-start | bytes 921608 | tf_op jit(solution)/shard_map/ppermute | solution.py:32
  31.0 2.5 %copy-start = (f32[4,36,36,128]{3,2,1,0:T(8,128)S(1)}, f32[4,36,36,128]{3,2,1,0:T(8,128)}, u32[]{:S(2)}) copy-start(f32[4,36,36,128]{3,2,1,0:T(8,128)} %shard_map.46) | copy-start | bytes 7962628
  44.9 13.8 %collective-permute-start.12 = (f32[5,4,4,32]{3,2,1,0:T(4,128)S(1)}, f32[5,4,4,32]{3,2,1,0:T(4,128)S(1)}, u32[]{:S(2)}, u32[]{:S(2)}) collective-permute-start(f32[5,4,4,32]{3,2,1,0:T(4,128)S(1)} %pad_maximum_fusion.23), channel_id=1, source_target_pairs={{0,1},{1,2},{2,3},{3,0},{4,5},{5,6},{6,7},{7,4},{8,9},{9,10},{10,1... | collective-permute-start | bytes 30728 | tf_op jit(solution)/shard_map/ppermute | solution.py:276
  50.4 8.2 %collective-permute-start.11 = (f32[5,4,4,32]{3,2,1,0:T(4,128)S(1)}, f32[5,4,4,32]{3,2,1,0:T(4,128)S(1)}, u32[]{:S(2)}, u32[]{:S(2)}) collective-permute-start(f32[5,4,4,32]{3,2,1,0:T(4,128)S(1)} %pad_maximum_fusion.23), channel_id=1, source_target_pairs={{0,2},{1,3},{2,0},{3,1},{4,6},{5,7},{6,4},{7,5},{8,10},{9,11},{10,... | collective-permute-start | bytes 30728 | tf_op jit(solution)/shard_map/ppermute | solution.py:276
  52.9 5.8 %collective-permute-start.10 = (f32[5,4,4,32]{3,2,1,0:T(4,128)S(1)}, f32[5,4,4,32]{3,2,1,0:T(4,128)S(1)}, u32[]{:S(2)}, u32[]{:S(2)}) collective-permute-start(f32[5,4,4,32]{3,2,1,0:T(4,128)S(1)} %pad_maximum_fusion.23), channel_id=1, source_target_pairs={{0,3},{1,0},{2,1},{3,2},{4,7},{5,4},{6,5},{7,6},{8,11},{9,8},{10,9... | collective-permute-start | bytes 30728 | tf_op jit(solution)/shard_map/ppermute | solution.py:276
  54.3 14.3 %collective-permute-start.7 = (f32[2,8,5,64]{3,2,1,0:T(8,128)S(1)}, f32[2,8,5,64]{3,2,1,0:T(8,128)S(1)}, u32[]{:S(2)}, u32[]{:S(2)}) collective-permute-start(f32[2,8,5,64]{3,2,1,0:T(8,128)S(1)} %get-tuple-element.191), channel_id=1, source_target_pairs={{1,0},{2,1},{3,2},{5,4},{6,5},{7,6},{9,8},{10,9},{11,10},{13,12},{... | collective-permute-start | bytes 61448 | tf_op jit(solution)/shard_map/ppermute | solution.py:32
  55.6 16.0 %collective-permute-start.6 = (f32[2,8,5,64]{3,2,1,0:T(8,128)S(1)}, f32[2,8,5,64]{3,2,1,0:T(8,128)S(1)}, u32[]{:S(2)}, u32[]{:S(2)}) collective-permute-start(f32[2,8,5,64]{3,2,1,0:T(8,128)S(1)} %get-tuple-element.190), channel_id=1, source_target_pairs={{0,1},{1,2},{2,3},{4,5},{5,6},{6,7},{8,9},{9,10},{10,11},{12,13},{... | collective-permute-start | bytes 61448 | tf_op jit(solution)/shard_map/ppermute | solution.py:32
  58.7 15.6 %collective-permute-start.14 = (f32[5,4,16,32]{3,2,1,0:T(8,128)S(1)}, f32[5,4,16,32]{3,2,1,0:T(8,128)S(1)}, u32[]{:S(2)}, u32[]{:S(2)}) collective-permute-start(f32[5,4,16,32]{3,2,1,0:T(8,128)S(1)} %pad_maximum_fusion.9), channel_id=1, source_target_pairs={{0,8},{4,12},{8,16},{12,20},{16,24},{20,28},{1,9},{5,13},{9,17},{1... | collective-permute-start | bytes 122888 | tf_op jit(solution)/shard_map/ppermute | solution.py:32
  62.2 10.7 %collective-permute-start.13 = (f32[5,4,16,32]{3,2,1,0:T(8,128)S(1)}, f32[5,4,16,32]{3,2,1,0:T(8,128)S(1)}, u32[]{:S(2)}, u32[]{:S(2)}) collective-permute-start(f32[5,4,16,32]{3,2,1,0:T(8,128)S(1)} %pad_maximum_fusion.9), channel_id=1, source_target_pairs={{0,12},{4,16},{8,20},{12,24},{16,28},{1,13},{5,17},{9,21},{13,25},... | collective-permute-start | bytes 122888 | tf_op jit(solution)/shard_map/ppermute | solution.py:32
  65.7 10.6 %collective-permute-start.15 = (f32[5,4,16,32]{3,2,1,0:T(8,128)S(1)}, f32[5,4,16,32]{3,2,1,0:T(8,128)S(1)}, u32[]{:S(2)}, u32[]{:S(2)}) collective-permute-start(f32[5,4,16,32]{3,2,1,0:T(8,128)S(1)} %pad_maximum_fusion.9), channel_id=1, source_target_pairs={{0,4},{4,8},{8,12},{12,16},{16,20},{20,24},{24,28},{1,5},{5,9},{9,... | collective-permute-start | bytes 122888 | tf_op jit(solution)/shard_map/ppermute | solution.py:32
  68.6 12.8 %collective-permute-start.16 = (f32[5,4,16,32]{3,2,1,0:T(8,128)S(1)}, f32[5,4,16,32]{3,2,1,0:T(8,128)S(1)}, u32[]{:S(2)}, u32[]{:S(2)}) collective-permute-start(f32[5,4,16,32]{3,2,1,0:T(8,128)S(1)} %pad_maximum_fusion.9), channel_id=1, source_target_pairs={{4,0},{8,4},{12,8},{16,12},{20,16},{24,20},{28,24},{5,1},{9,5},{13... | collective-permute-start | bytes 122888 | tf_op jit(solution)/shard_map/ppermute | solution.py:32
  71.6 9.8 %collective-permute-start.17 = (f32[5,4,16,32]{3,2,1,0:T(8,128)S(1)}, f32[5,4,16,32]{3,2,1,0:T(8,128)S(1)}, u32[]{:S(2)}, u32[]{:S(2)}) collective-permute-start(f32[5,4,16,32]{3,2,1,0:T(8,128)S(1)} %pad_maximum_fusion.9), channel_id=1, source_target_pairs={{8,0},{12,4},{16,8},{20,12},{24,16},{28,20},{9,1},{13,5},{17,9},{2... | collective-permute-start | bytes 122888 | tf_op jit(solution)/shard_map/ppermute | solution.py:32
  73.0 15.7 %collective-permute-start.18 = (f32[5,4,16,32]{3,2,1,0:T(8,128)S(1)}, f32[5,4,16,32]{3,2,1,0:T(8,128)S(1)}, u32[]{:S(2)}, u32[]{:S(2)}) collective-permute-start(f32[5,4,16,32]{3,2,1,0:T(8,128)S(1)} %pad_maximum_fusion.9), channel_id=1, source_target_pairs={{12,0},{16,4},{20,8},{24,12},{28,16},{13,1},{17,5},{21,9},{25,13},... | collective-permute-start | bytes 122888 | tf_op jit(solution)/shard_map/ppermute | solution.py:32
  74.3 20.7 %collective-permute-start.9 = (f32[2,5,18,64]{3,2,1,0:T(8,128)S(1)}, f32[2,5,18,64]{3,2,1,0:T(8,128)S(1)}, u32[]{:S(2)}, u32[]{:S(2)}) collective-permute-start(f32[2,5,18,64]{3,2,1,0:T(8,128)S(1)} %get-tuple-element.96), channel_id=1, source_target_pairs={{4,0},{8,4},{12,8},{16,12},{20,16},{24,20},{28,24},{5,1},{9,5},{13... | collective-permute-start | bytes 138248 | tf_op jit(solution)/shard_map/ppermute | solution.py:32
  76.3 18.7 %collective-permute-start.8 = (f32[2,5,18,64]{3,2,1,0:T(8,128)S(1)}, f32[2,5,18,64]{3,2,1,0:T(8,128)S(1)}, u32[]{:S(2)}, u32[]{:S(2)}) collective-permute-start(f32[2,5,18,64]{3,2,1,0:T(8,128)S(1)} %get-tuple-element.95), channel_id=1, source_target_pairs={{0,4},{4,8},{8,12},{12,16},{16,20},{20,24},{24,28},{1,5},{5,9},{9,... | collective-permute-start | bytes 138248 | tf_op jit(solution)/shard_map/ppermute | solution.py:32

commit v15 on v14

--- a/solution.py
+++ b/solution.py
@@ -218,7 +218,7 @@
         out_ref[3, i] = jnp.where(ok, store, 0.0)
         return carry
 
-    lax.fori_loop(0, rows, body, 0, unroll=2)
+    lax.fori_loop(0, rows, body, 0, unroll=4)
 
 
 def soil_fields(frame, soil_table, conc, idf):

time: 101 us -> 100 us (0.990)
  no operation moved by 1% of the time
where the time goes in v15:
time: 100 us; the launch traced here: 99.8 us
  starting transfers between devices  52.1 us (52%)
  other arithmetic  15.5 us (16%)
  waiting for transfers between devices  10.4 us (10%)
  local copies, waits for them, and re-layouts  10.3 us (10%)
  matrix products  5.17 us (5%)
  Pallas kernels  5.02 us (5%)
  between operations  1.28 us (1%)
    ppermute x16, starting transfers between devices, shift_from(): return lax.ppermute(cells, axis, pairs)  42.7 us
    ppermute x16, waiting for transfers between devices, shift_from(): return lax.ppermute(cells, axis, pairs)  10.4 us
    ppermute x3, starting transfers between devices, local(): blocks.append(lax.ppermute(cpack, 'gy', pairs))  9.42 us
    pallas_call x1, Pallas kernels, soil_fields(): pl.pallas_call(functools.partial(fields_kernel, frame), out_shape=jax.Sha...  5.02 us
    add x7, other arithmetic, chebyshev(): iterate = win(iterate, n, cur, nxt) + update  4.54 us
    add x8, other arithmetic, local(): u = centre + jacobi_weight * ((csrc[sl] - applied) / cdiag[sl])  2.5 us
    dot_general x4, matrix products, coarsen(): lax.dot_general(pick, rows, (((2,), (1,)), ((0,), (0,))), precision=HIGH)  2.25 us
    concatenate x3, other arithmetic, frames_overlapped(): out.append(jnp.concatenate([top, mid, bottom], axis=0))  2.03 us
  transfers between devices with their start and end apart: 19, of which 3 were waited for; matrix products, arithmetic and copies ran while one was open for 8% of the time, Pallas kernels for 0%

profile of v15, /device:TPU:4, one launch (start us, length us, event | category | flops | bytes accessed | tf_op | source)
XLA Modules:
  0.0 99.8 jit_solution(9935272381076378616)
XLA Ops:
  0.0 1.0 %convert_bitcast_fusion.3 = (f32[1,10,16,128]{3,2,1,0:T(8,128)S(1)}, f32[1,10,16,128]{3,2,1,0:T(8,128)S(1)}) fusion(s32[16,16,128]{2,1,0:T(8,128)} %param.6), kind=kLoop, calls=%fused_computation.600 | loop fusion | flops 40960 | bytes 327680 | tf_op jit(solution)/shard_map/stack | solution.py:64
  1.1 1.1 %slice_bitcast_fusion.54 = (f32[1,10,16,128]{3,2,1,0:T(8,128)S(1)}, f32[1,10,16,128]{3,2,1,0:T(8,128)S(1)}, f32[1,10,16,128]{3,2,1,0:T(8,128)S(1)}, f32[1,10,16,128]{3,2,1,0:T(8,128)S(1)}) fusion(f32[16,16,128]{2,1,0:T(8,128)} %param.5, f32[16,16,128]{2,1,0:T(8,128)} %param.4), kind=kLoop, calls=%fused_computation.601 | loop fusion | bytes 655360 | tf_op jit(solution)/shard_map/stack | solution.py:64
  2.2 1.9 %collective-permute-start.1 = (f32[3,10,16,128]{3,2,1,0:T(8,128)S(1)}, f32[3,10,16,128]{3,2,1,0:T(8,128)S(1)}, u32[]{:S(2)}, u32[]{:S(2)}) collective-permute-start(f32[3,10,16,128]{3,2,1,0:T(8,128)S(1)} %pad_maximum_fusion.7), channel_id=1, source_target_pairs={{4,0},{8,4},{12,8},{16,12},{20,16},{24,20},{28,24},{5,1},{9,5},{13... | collective-permute-start | bytes 737288 | tf_op jit(solution)/shard_map/ppermute | solution.py:32
  4.1 4.8 %collective-permute-start = (f32[3,10,16,128]{3,2,1,0:T(8,128)S(1)}, f32[3,10,16,128]{3,2,1,0:T(8,128)S(1)}, u32[]{:S(2)}, u32[]{:S(2)}) collective-permute-start(f32[3,10,16,128]{3,2,1,0:T(8,128)S(1)} %pad_maximum_fusion.6), channel_id=1, source_target_pairs={{0,4},{4,8},{8,12},{12,16},{16,20},{20,24},{24,28},{1,5},{5,9},{9,... | collective-permute-start | bytes 737288 | tf_op jit(solution)/shard_map/ppermute | solution.py:32
  9.1 1.3 %collective-permute-start.5 = (f32[3,16,10,128]{3,2,1,0:T(8,128)S(1)}, f32[3,16,10,128]{3,2,1,0:T(8,128)S(1)}, u32[]{:S(2)}, u32[]{:S(2)}) collective-permute-start(f32[3,16,10,128]{3,2,1,0:T(8,128)S(1)} %pad_maximum_fusion.5), channel_id=1, source_target_pairs={{1,0},{2,1},{3,2},{5,4},{6,5},{7,6},{9,8},{10,9},{11,10},{13,12},{... | collective-permute-start | bytes 737288 | tf_op jit(solution)/shard_map/ppermute | solution.py:32
  10.4 0.8 pad_maximum_fusion.4
  11.2 3.8 %collective-permute-start.4 = (f32[3,16,10,128]{3,2,1,0:T(8,128)}, f32[3,16,10,128]{3,2,1,0:T(8,128)}, u32[]{:S(2)}, u32[]{:S(2)}) collective-permute-start(f32[3,16,10,128]{3,2,1,0:T(8,128)} %pad_maximum_fusion.4), channel_id=1, source_target_pairs={{0,1},{1,2},{2,3},{4,5},{5,6},{6,7},{8,9},{9,10},{10,11},{12,13},{... | collective-permute-start | bytes 737288 | tf_op jit(solution)/shard_map/ppermute | solution.py:32
  15.2 2.7 %collective-permute-done = f32[3,10,16,128]{3,2,1,0:T(8,128)S(1)} collective-permute-done((f32[3,10,16,128]{3,2,1,0:T(8,128)S(1)}, f32[3,10,16,128]{3,2,1,0:T(8,128)S(1)}, u32[]{:S(2)}, u32[]{:S(2)}) %collective-permute-start) | collective-permute-done | bytes 245792 | tf_op jit(solution)/shard_map/ppermute | solution.py:32
  18.0 1.3 %collective-permute-start.3 = (f32[3,20,10,128]{3,2,1,0:T(8,128)S(1)}, f32[3,20,10,128]{3,2,1,0:T(8,128)S(1)}, u32[]{:S(2)}, u32[]{:S(2)}) collective-permute-start(f32[3,20,10,128]{3,2,1,0:T(8,128)S(1)} %pad_maximum_fusion.2), channel_id=1, source_target_pairs={{1,0},{2,1},{3,2},{5,4},{6,5},{7,6},{9,8},{10,9},{11,10},{13,12},{... | collective-permute-start | bytes 921608 | tf_op jit(solution)/shard_map/ppermute | solution.py:32
  19.4 3.1 %collective-permute-start.2 = (f32[3,20,10,128]{3,2,1,0:T(8,128)S(1)}, f32[3,20,10,128]{3,2,1,0:T(8,128)S(1)}, u32[]{:S(2)}, u32[]{:S(2)}) collective-permute-start(f32[3,20,10,128]{3,2,1,0:T(8,128)S(1)} %pad_maximum_fusion.1), channel_id=1, source_target_pairs={{0,1},{1,2},{2,3},{4,5},{5,6},{6,7},{8,9},{9,10},{10,11},{12,13},{... | collective-permute-start | bytes 921608 | tf_op jit(solution)/shard_map/ppermute | solution.py:32
  22.5 1.1 %slice_bitcast_fusion.23 = (f32[16,10,128]{2,1,0:T(8,128)S(1)}, f32[16,10,128]{2,1,0:T(8,128)S(1)}, f32[16,10,128]{2,1,0:T(8,128)S(1)}) fusion(f32[3,16,10,128]{3,2,1,0:T(8,128)} %collective-permute-done.4), kind=kLoop, calls=%fused_computation.384 | loop fusion | bytes 491520 | tf_op jit(solution)/shard_map/squeeze | solution.py:76
  23.9 1.0 maximum_maximum_fusion.1.conc_ref
  24.9 1.0 maximum_maximum_fusion.2.idf_ref
  25.8 5.0 %shard_map.46 = f32[4,36,36,128]{3,2,1,0:T(8,128)} custom-call(f32[5,8]{1,0:T(8,128)} %table_ref.1, f32[36,36,128]{2,1,0:T(8,128)} %maximum_maximum_fusion.1.conc_ref, f32[36,36,128]{2,1,0:T(8,128)} %maximum_maximum_fusion.2.idf_ref), custom_call_target="tpu_custom_call" | custom-call | flops 16588800 | bytes 3981312 | tf_op jit(solution)/shard_map/pallas_call | solution.py:226
  30.9 1.9 %slice_bitcast_fusion.2 = (f32[36,36,128]{2,1,0:T(8,128)S(1)}, f32[36,36,128]{2,1,0:T(8,128)S(1)}, f32[36,36,128]{2,1,0:T(8,128)S(1)}) fusion(f32[4,36,36,128]{3,2,1,0:T(8,128)} %shard_map.46), kind=kLoop, calls=%fused_computation.16 | loop fusion | bytes 3981312 | tf_op jit(solution)/shard_map/squeeze | solution.py:121
  32.7 0.6 copy-done
  34.1 0.7 fusion.4
  35.3 1.2 %slice_add_fusion.5 = (f32[32,32,128]{2,1,0:T(8,128)S(1)}, f32[32,32,128]{2,1,0:T(8,128)S(1)}) fusion(f32[34,34,128]{2,1,0:T(8,128)S(1)} %get-tuple-element.21, f32[34,34,128]{2,1,0:T(8,128)S(1)} %get-tuple-element.22, f32[32,32,127]{2,1,0:T(8,128)S(1)} %get-tuple-element.32, f32[32,32,1]{2,1,0:T(8,128)S(1)} %get-tuple-element.34, ...), kind=kLoop, calls=%fused_computation.55 | loop fusion | flops 3538944 | bytes 9046976 | tf_op jit(solution)/shard_map/add | solution.py:185
  37.0 0.8 fusion.336
  37.9 1.5 %convolution_multiply_fusion = f32[72,18,64]{2,1,0:T(8,128)S(1)} fusion(f32[72,36,64]{2,1,0:T(8,128)S(1)} %fusion.336, f32[18,36]{1,0:T(8,128)S(1)} %fusion.357), kind=kOutput, calls=%fused_computation.1 | convolution fusion | flops 35914752 | bytes 997920 | tf_op jit(solution)/shard_map/dot_general | solution.py:106
  39.7 1.2 %fusion.22 = f32[30,30,128]{2,1,0:T(8,128)S(1)} fusion(f32[34,34,128]{2,1,0:T(8,128)S(1)} %get-tuple-element.22, f32[32,32,128]{2,1,0:T(8,128)S(1)} %get-tuple-element.19, f32[36,35,128]{2,1,0:T(8,128)S(1)} %maximum_divide_fusion.1, f32[35,36,128]{2,1,0:T(8,128)S(1)} %divide_bitcast_fusion, f32[36,36,128]{2,1,0:T(8,128)S(1)} %get-tuple-element.24, ...), kind=kLoop, calls=%fused_computation.59 | loop fusion | flops 3110400 | bytes 8031168 | tf_op jit(solution)/shard_map/add | solution.py:185
  41.3 0.9 fusion.40
  42.5 0.3 divide_multiply_fusion.3
  44.7 5.6 %collective-permute-start.12 = (f32[5,4,4,32]{3,2,1,0:T(4,128)S(1)}, f32[5,4,4,32]{3,2,1,0:T(4,128)S(1)}, u32[]{:S(2)}, u32[]{:S(2)}) collective-permute-start(f32[5,4,4,32]{3,2,1,0:T(4,128)S(1)} %pad_maximum_fusion.23), channel_id=1, source_target_pairs={{0,1},{1,2},{2,3},{3,0},{4,5},{5,6},{6,7},{7,4},{8,9},{9,10},{10,1... | collective-permute-start | bytes 30728 | tf_op jit(solution)/shard_map/ppermute | solution.py:276
  50.3 2.4 %collective-permute-start.11 = (f32[5,4,4,32]{3,2,1,0:T(4,128)S(1)}, f32[5,4,4,32]{3,2,1,0:T(4,128)S(1)}, u32[]{:S(2)}, u32[]{:S(2)}) collective-permute-start(f32[5,4,4,32]{3,2,1,0:T(4,128)S(1)} %pad_maximum_fusion.23), channel_id=1, source_target_pairs={{0,2},{1,3},{2,0},{3,1},{4,6},{5,7},{6,4},{7,5},{8,10},{9,11},{10,... | collective-permute-start | bytes 30728 | tf_op jit(solution)/shard_map/ppermute | solution.py:276
  52.8 1.4 %collective-permute-start.10 = (f32[5,4,4,32]{3,2,1,0:T(4,128)S(1)}, f32[5,4,4,32]{3,2,1,0:T(4,128)S(1)}, u32[]{:S(2)}, u32[]{:S(2)}) collective-permute-start(f32[5,4,4,32]{3,2,1,0:T(4,128)S(1)} %pad_maximum_fusion.23), channel_id=1, source_target_pairs={{0,3},{1,0},{2,1},{3,2},{4,7},{5,4},{6,5},{7,6},{8,11},{9,8},{10,9... | collective-permute-start | bytes 30728 | tf_op jit(solution)/shard_map/ppermute | solution.py:276
  54.2 1.3 %collective-permute-start.7 = (f32[2,8,5,64]{3,2,1,0:T(8,128)S(1)}, f32[2,8,5,64]{3,2,1,0:T(8,128)S(1)}, u32[]{:S(2)}, u32[]{:S(2)}) collective-permute-start(f32[2,8,5,64]{3,2,1,0:T(8,128)S(1)} %get-tuple-element.191), channel_id=1, source_target_pairs={{1,0},{2,1},{3,2},{5,4},{6,5},{7,6},{9,8},{10,9},{11,10},{13,12},{... | collective-permute-start | bytes 61448 | tf_op jit(solution)/shard_map/ppermute | solution.py:32
  55.5 3.0 %collective-permute-start.6 = (f32[2,8,5,64]{3,2,1,0:T(8,128)S(1)}, f32[2,8,5,64]{3,2,1,0:T(8,128)S(1)}, u32[]{:S(2)}, u32[]{:S(2)}) collective-permute-start(f32[2,8,5,64]{3,2,1,0:T(8,128)S(1)} %get-tuple-element.190), channel_id=1, source_target_pairs={{0,1},{1,2},{2,3},{4,5},{5,6},{6,7},{8,9},{9,10},{10,11},{12,13},{... | collective-permute-start | bytes 61448 | tf_op jit(solution)/shard_map/ppermute | solution.py:32
  58.6 3.5 %collective-permute-start.14 = (f32[5,4,16,32]{3,2,1,0:T(8,128)S(1)}, f32[5,4,16,32]{3,2,1,0:T(8,128)S(1)}, u32[]{:S(2)}, u32[]{:S(2)}) collective-permute-start(f32[5,4,16,32]{3,2,1,0:T(8,128)S(1)} %pad_maximum_fusion.9), channel_id=1, source_target_pairs={{0,8},{4,12},{8,16},{12,20},{16,24},{20,28},{1,9},{5,13},{9,17},{1... | collective-permute-start | bytes 122888 | tf_op jit(solution)/shard_map/ppermute | solution.py:32
  62.1 3.5 %collective-permute-start.13 = (f32[5,4,16,32]{3,2,1,0:T(8,128)S(1)}, f32[5,4,16,32]{3,2,1,0:T(8,128)S(1)}, u32[]{:S(2)}, u32[]{:S(2)}) collective-permute-start(f32[5,4,16,32]{3,2,1,0:T(8,128)S(1)} %pad_maximum_fusion.9), channel_id=1, source_target_pairs={{0,12},{4,16},{8,20},{12,24},{16,28},{1,13},{5,17},{9,21},{13,25},... | collective-permute-start | bytes 122888 | tf_op jit(solution)/shard_map/ppermute | solution.py:32
  65.6 2.9 %collective-permute-start.15 = (f32[5,4,16,32]{3,2,1,0:T(8,128)S(1)}, f32[5,4,16,32]{3,2,1,0:T(8,128)S(1)}, u32[]{:S(2)}, u32[]{:S(2)}) collective-permute-start(f32[5,4,16,32]{3,2,1,0:T(8,128)S(1)} %pad_maximum_fusion.9), channel_id=1, source_target_pairs={{0,4},{4,8},{8,12},{12,16},{16,20},{20,24},{24,28},{1,5},{5,9},{9,... | collective-permute-start | bytes 122888 | tf_op jit(solution)/shard_map/ppermute | solution.py:32
  68.5 3.0 %collective-permute-start.16 = (f32[5,4,16,32]{3,2,1,0:T(8,128)S(1)}, f32[5,4,16,32]{3,2,1,0:T(8,128)S(1)}, u32[]{:S(2)}, u32[]{:S(2)}) collective-permute-start(f32[5,4,16,32]{3,2,1,0:T(8,128)S(1)} %pad_maximum_fusion.9), channel_id=1, source_target_pairs={{4,0},{8,4},{12,8},{16,12},{20,16},{24,20},{28,24},{5,1},{9,5},{13... | collective-permute-start | bytes 122888 | tf_op jit(solution)/shard_map/ppermute | solution.py:32
  71.5 1.3 %collective-permute-start.17 = (f32[5,4,16,32]{3,2,1,0:T(8,128)S(1)}, f32[5,4,16,32]{3,2,1,0:T(8,128)S(1)}, u32[]{:S(2)}, u32[]{:S(2)}) collective-permute-start(f32[5,4,16,32]{3,2,1,0:T(8,128)S(1)} %pad_maximum_fusion.9), channel_id=1, source_target_pairs={{8,0},{12,4},{16,8},{20,12},{24,16},{28,20},{9,1},{13,5},{17,9},{2... | collective-permute-start | bytes 122888 | tf_op jit(solution)/shard_map/ppermute | solution.py:32
  72.8 1.3 %collective-permute-start.18 = (f32[5,4,16,32]{3,2,1,0:T(8,128)S(1)}, f32[5,4,16,32]{3,2,1,0:T(8,128)S(1)}, u32[]{:S(2)}, u32[]{:S(2)}) collective-permute-start(f32[5,4,16,32]{3,2,1,0:T(8,128)S(1)} %pad_maximum_fusion.9), channel_id=1, source_target_pairs={{12,0},{16,4},{20,8},{24,12},{28,16},{13,1},{17,5},{21,9},{25,13},... | collective-permute-start | bytes 122888 | tf_op jit(solution)/shard_map/ppermute | solution.py:32
  74.2 1.9 %collective-permute-start.9 = (f32[2,5,18,64]{3,2,1,0:T(8,128)S(1)}, f32[2,5,18,64]{3,2,1,0:T(8,128)S(1)}, u32[]{:S(2)}, u32[]{:S(2)}) collective-permute-start(f32[2,5,18,64]{3,2,1,0:T(8,128)S(1)} %get-tuple-element.96), channel_id=1, source_target_pairs={{4,0},{8,4},{12,8},{16,12},{20,16},{24,20},{28,24},{5,1},{9,5},{13... | collective-permute-start | bytes 138248 | tf_op jit(solution)/shard_map/ppermute | solution.py:32
  76.1 4.8 %collective-permute-start.8 = (f32[2,5,18,64]{3,2,1,0:T(8,128)S(1)}, f32[2,5,18,64]{3,2,1,0:T(8,128)S(1)}, u32[]{:S(2)}, u32[]{:S(2)}) collective-permute-start(f32[2,5,18,64]{3,2,1,0:T(8,128)S(1)} %get-tuple-element.95), channel_id=1, source_target_pairs={{0,4},{4,8},{8,12},{12,16},{16,20},{20,24},{24,28},{1,5},{5,9},{9,... | collective-permute-start | bytes 138248 | tf_op jit(solution)/shard_map/ppermute | solution.py:32
  81.2 7.4 %collective-permute-done.18 = f32[5,4,16,32]{3,2,1,0:T(8,128)S(1)} collective-permute-done((f32[5,4,16,32]{3,2,1,0:T(8,128)S(1)}, f32[5,4,16,32]{3,2,1,0:T(8,128)S(1)}, u32[]{:S(2)}, u32[]{:S(2)}) %collective-permute-start.18) | collective-permute-done | bytes 40992 | tf_op jit(solution)/shard_map/ppermute | solution.py:32
  89.8 0.5 fusion.87
  90.6 0.4 multiply_add_fusion
  91.3 0.3 multiply_add_fusion.1
  91.9 0.3 multiply_add_fusion.2
  94.4 0.4 fusion.318
  95.3 0.3 slice_add_fusion.10
  96.2 0.4 fusion.258
  96.7 0.5 fusion.315
  97.5 0.4 slice_add_fusion.7
  98.2 0.5 slice_add_fusion.9
  98.9 1.0 fusion.181
  (168 shorter events, 11.3 us)
Async XLA Ops:
  0.0 9.0 %copy-start.2 = (s32[16,16,128]{2,1,0:T(8,128)S(1)}, s32[16,16,128]{2,1,0:T(8,128)}, u32[]{:S(2)}) copy-start(s32[16,16,128]{2,1,0:T(8,128)} %param.6) | copy-start | bytes 393220
  1.1 7.9 %copy-start.1 = (f32[16,16,128]{2,1,0:T(8,128)S(1)}, f32[16,16,128]{2,1,0:T(8,128)}, u32[]{:S(2)}) copy-start(f32[16,16,128]{2,1,0:T(8,128)} %param.5) | copy-start | bytes 393220
  1.1 7.9 %copy-start.3 = (f32[16,16,128]{2,1,0:T(8,128)S(1)}, f32[16,16,128]{2,1,0:T(8,128)}, u32[]{:S(2)}) copy-start(f32[16,16,128]{2,1,0:T(8,128)} %param.4) | copy-start | bytes 393220
  2.2 13.0 %collective-permute-start.1 = (f32[3,10,16,128]{3,2,1,0:T(8,128)S(1)}, f32[3,10,16,128]{3,2,1,0:T(8,128)S(1)}, u32[]{:S(2)}, u32[]{:S(2)}) collective-permute-start(f32[3,10,16,128]{3,2,1,0:T(8,128)S(1)} %pad_maximum_fusion.7), channel_id=1, source_target_pairs={{4,0},{8,4},{12,8},{16,12},{20,16},{24,20},{28,24},{5,1},{9,5},{13... | collective-permute-start | bytes 737288 | tf_op jit(solution)/shard_map/ppermute | solution.py:32
  4.1 13.8 %collective-permute-start = (f32[3,10,16,128]{3,2,1,0:T(8,128)S(1)}, f32[3,10,16,128]{3,2,1,0:T(8,128)S(1)}, u32[]{:S(2)}, u32[]{:S(2)}) collective-permute-start(f32[3,10,16,128]{3,2,1,0:T(8,128)S(1)} %pad_maximum_fusion.6), channel_id=1, source_target_pairs={{0,4},{4,8},{8,12},{12,16},{16,20},{20,24},{24,28},{1,5},{5,9},{9,... | collective-permute-start | bytes 737288 | tf_op jit(solution)/shard_map/ppermute | solution.py:32
  9.1 13.3 %collective-permute-start.5 = (f32[3,16,10,128]{3,2,1,0:T(8,128)S(1)}, f32[3,16,10,128]{3,2,1,0:T(8,128)S(1)}, u32[]{:S(2)}, u32[]{:S(2)}) collective-permute-start(f32[3,16,10,128]{3,2,1,0:T(8,128)S(1)} %pad_maximum_fusion.5), channel_id=1, source_target_pairs={{1,0},{2,1},{3,2},{5,4},{6,5},{7,6},{9,8},{10,9},{11,10},{13,12},{... | collective-permute-start | bytes 737288 | tf_op jit(solution)/shard_map/ppermute | solution.py:32
  11.2 11.3 %collective-permute-start.4 = (f32[3,16,10,128]{3,2,1,0:T(8,128)}, f32[3,16,10,128]{3,2,1,0:T(8,128)}, u32[]{:S(2)}, u32[]{:S(2)}) collective-permute-start(f32[3,16,10,128]{3,2,1,0:T(8,128)} %pad_maximum_fusion.4), channel_id=1, source_target_pairs={{0,1},{1,2},{2,3},{4,5},{5,6},{6,7},{8,9},{9,10},{10,11},{12,13},{... | collective-permute-start | bytes 737288 | tf_op jit(solution)/shard_map/ppermute | solution.py:32
  18.0 5.6 %collective-permute-start.3 = (f32[3,20,10,128]{3,2,1,0:T(8,128)S(1)}, f32[3,20,10,128]{3,2,1,0:T(8,128)S(1)}, u32[]{:S(2)}, u32[]{:S(2)}) collective-permute-start(f32[3,20,10,128]{3,2,1,0:T(8,128)S(1)} %pad_maximum_fusion.2), channel_id=1, source_target_pairs={{1,0},{2,1},{3,2},{5,4},{6,5},{7,6},{9,8},{10,9},{11,10},{13,12},{... | collective-permute-start | bytes 921608 | tf_op jit(solution)/shard_map/ppermute | solution.py:32
  19.4 4.5 %collective-permute-start.2 = (f32[3,20,10,128]{3,2,1,0:T(8,128)S(1)}, f32[3,20,10,128]{3,2,1,0:T(8,128)S(1)}, u32[]{:S(2)}, u32[]{:S(2)}) collective-permute-start(f32[3,20,10,128]{3,2,1,0:T(8,128)S(1)} %pad_maximum_fusion.1), channel_id=1, source_target_pairs={{0,1},{1,2},{2,3},{4,5},{5,6},{6,7},{8,9},{9,10},{10,11},{12,13},{... | collective-permute-start | bytes 921608 | tf_op jit(solution)/shard_map/ppermute | solution.py:32
  30.9 2.5 %copy-start = (f32[4,36,36,128]{3,2,1,0:T(8,128)S(1)}, f32[4,36,36,128]{3,2,1,0:T(8,128)}, u32[]{:S(2)}) copy-start(f32[4,36,36,128]{3,2,1,0:T(8,128)} %shard_map.46) | copy-start | bytes 7962628
  44.7 13.8 %collective-permute-start.12 = (f32[5,4,4,32]{3,2,1,0:T(4,128)S(1)}, f32[5,4,4,32]{3,2,1,0:T(4,128)S(1)}, u32[]{:S(2)}, u32[]{:S(2)}) collective-permute-start(f32[5,4,4,32]{3,2,1,0:T(4,128)S(1)} %pad_maximum_fusion.23), channel_id=1, source_target_pairs={{0,1},{1,2},{2,3},{3,0},{4,5},{5,6},{6,7},{7,4},{8,9},{9,10},{10,1... | collective-permute-start | bytes 30728 | tf_op jit(solution)/shard_map/ppermute | solution.py:276
  50.3 8.2 %collective-permute-start.11 = (f32[5,4,4,32]{3,2,1,0:T(4,128)S(1)}, f32[5,4,4,32]{3,2,1,0:T(4,128)S(1)}, u32[]{:S(2)}, u32[]{:S(2)}) collective-permute-start(f32[5,4,4,32]{3,2,1,0:T(4,128)S(1)} %pad_maximum_fusion.23), channel_id=1, source_target_pairs={{0,2},{1,3},{2,0},{3,1},{4,6},{5,7},{6,4},{7,5},{8,10},{9,11},{10,... | collective-permute-start | bytes 30728 | tf_op jit(solution)/shard_map/ppermute | solution.py:276
  52.8 5.8 %collective-permute-start.10 = (f32[5,4,4,32]{3,2,1,0:T(4,128)S(1)}, f32[5,4,4,32]{3,2,1,0:T(4,128)S(1)}, u32[]{:S(2)}, u32[]{:S(2)}) collective-permute-start(f32[5,4,4,32]{3,2,1,0:T(4,128)S(1)} %pad_maximum_fusion.23), channel_id=1, source_target_pairs={{0,3},{1,0},{2,1},{3,2},{4,7},{5,4},{6,5},{7,6},{8,11},{9,8},{10,9... | collective-permute-start | bytes 30728 | tf_op jit(solution)/shard_map/ppermute | solution.py:276
  54.2 14.3 %collective-permute-start.7 = (f32[2,8,5,64]{3,2,1,0:T(8,128)S(1)}, f32[2,8,5,64]{3,2,1,0:T(8,128)S(1)}, u32[]{:S(2)}, u32[]{:S(2)}) collective-permute-start(f32[2,8,5,64]{3,2,1,0:T(8,128)S(1)} %get-tuple-element.191), channel_id=1, source_target_pairs={{1,0},{2,1},{3,2},{5,4},{6,5},{7,6},{9,8},{10,9},{11,10},{13,12},{... | collective-permute-start | bytes 61448 | tf_op jit(solution)/shard_map/ppermute | solution.py:32
  55.5 16.0 %collective-permute-start.6 = (f32[2,8,5,64]{3,2,1,0:T(8,128)S(1)}, f32[2,8,5,64]{3,2,1,0:T(8,128)S(1)}, u32[]{:S(2)}, u32[]{:S(2)}) collective-permute-start(f32[2,8,5,64]{3,2,1,0:T(8,128)S(1)} %get-tuple-element.190), channel_id=1, source_target_pairs={{0,1},{1,2},{2,3},{4,5},{5,6},{6,7},{8,9},{9,10},{10,11},{12,13},{... | collective-permute-start | bytes 61448 | tf_op jit(solution)/shard_map/ppermute | solution.py:32
  58.6 15.6 %collective-permute-start.14 = (f32[5,4,16,32]{3,2,1,0:T(8,128)S(1)}, f32[5,4,16,32]{3,2,1,0:T(8,128)S(1)}, u32[]{:S(2)}, u32[]{:S(2)}) collective-permute-start(f32[5,4,16,32]{3,2,1,0:T(8,128)S(1)} %pad_maximum_fusion.9), channel_id=1, source_target_pairs={{0,8},{4,12},{8,16},{12,20},{16,24},{20,28},{1,9},{5,13},{9,17},{1... | collective-permute-start | bytes 122888 | tf_op jit(solution)/shard_map/ppermute | solution.py:32
  62.1 10.7 %collective-permute-start.13 = (f32[5,4,16,32]{3,2,1,0:T(8,128)S(1)}, f32[5,4,16,32]{3,2,1,0:T(8,128)S(1)}, u32[]{:S(2)}, u32[]{:S(2)}) collective-permute-start(f32[5,4,16,32]{3,2,1,0:T(8,128)S(1)} %pad_maximum_fusion.9), channel_id=1, source_target_pairs={{0,12},{4,16},{8,20},{12,24},{16,28},{1,13},{5,17},{9,21},{13,25},... | collective-permute-start | bytes 122888 | tf_op jit(solution)/shard_map/ppermute | solution.py:32
  65.6 10.6 %collective-permute-start.15 = (f32[5,4,16,32]{3,2,1,0:T(8,128)S(1)}, f32[5,4,16,32]{3,2,1,0:T(8,128)S(1)}, u32[]{:S(2)}, u32[]{:S(2)}) collective-permute-start(f32[5,4,16,32]{3,2,1,0:T(8,128)S(1)} %pad_maximum_fusion.9), channel_id=1, source_target_pairs={{0,4},{4,8},{8,12},{12,16},{16,20},{20,24},{24,28},{1,5},{5,9},{9,... | collective-permute-start | bytes 122888 | tf_op jit(solution)/shard_map/ppermute | solution.py:32
  68.5 12.6 %collective-permute-start.16 = (f32[5,4,16,32]{3,2,1,0:T(8,128)S(1)}, f32[5,4,16,32]{3,2,1,0:T(8,128)S(1)}, u32[]{:S(2)}, u32[]{:S(2)}) collective-permute-start(f32[5,4,16,32]{3,2,1,0:T(8,128)S(1)} %pad_maximum_fusion.9), channel_id=1, source_target_pairs={{4,0},{8,4},{12,8},{16,12},{20,16},{24,20},{28,24},{5,1},{9,5},{13... | collective-permute-start | bytes 122888 | tf_op jit(solution)/shard_map/ppermute | solution.py:32
  71.5 9.7 %collective-permute-start.17 = (f32[5,4,16,32]{3,2,1,0:T(8,128)S(1)}, f32[5,4,16,32]{3,2,1,0:T(8,128)S(1)}, u32[]{:S(2)}, u32[]{:S(2)}) collective-permute-start(f32[5,4,16,32]{3,2,1,0:T(8,128)S(1)} %pad_maximum_fusion.9), channel_id=1, source_target_pairs={{8,0},{12,4},{16,8},{20,12},{24,16},{28,20},{9,1},{13,5},{17,9},{2... | collective-permute-start | bytes 122888 | tf_op jit(solution)/shard_map/ppermute | solution.py:32
  72.8 15.7 %collective-permute-start.18 = (f32[5,4,16,32]{3,2,1,0:T(8,128)S(1)}, f32[5,4,16,32]{3,2,1,0:T(8,128)S(1)}, u32[]{:S(2)}, u32[]{:S(2)}) collective-permute-start(f32[5,4,16,32]{3,2,1,0:T(8,128)S(1)} %pad_maximum_fusion.9), channel_id=1, source_target_pairs={{12,0},{16,4},{20,8},{24,12},{28,16},{13,1},{17,5},{21,9},{25,13},... | collective-permute-start | bytes 122888 | tf_op jit(solution)/shard_map/ppermute | solution.py:32
  74.2 20.7 %collective-permute-start.9 = (f32[2,5,18,64]{3,2,1,0:T(8,128)S(1)}, f32[2,5,18,64]{3,2,1,0:T(8,128)S(1)}, u32[]{:S(2)}, u32[]{:S(2)}) collective-permute-start(f32[2,5,18,64]{3,2,1,0:T(8,128)S(1)} %get-tuple-element.96), channel_id=1, source_target_pairs={{4,0},{8,4},{12,8},{16,12},{20,16},{24,20},{28,24},{5,1},{9,5},{13... | collective-permute-start | bytes 138248 | tf_op jit(solution)/shard_map/ppermute | solution.py:32
  76.1 18.7 %collective-permute-start.8 = (f32[2,5,18,64]{3,2,1,0:T(8,128)S(1)}, f32[2,5,18,64]{3,2,1,0:T(8,128)S(1)}, u32[]{:S(2)}, u32[]{:S(2)}) collective-permute-start(f32[2,5,18,64]{3,2,1,0:T(8,128)S(1)} %get-tuple-element.95), channel_id=1, source_target_pairs={{0,4},{4,8},{8,12},{12,16},{16,20},{20,24},{24,28},{1,5},{5,9},{9,... | collective-permute-start | bytes 138248 | tf_op jit(solution)/shard_map/ppermute | solution.py:32
